TPU v7x, 32 devices: a whole 2x2x4 slice. The times are simulated.
32 devices in a mesh: groups: 2 (over y), blk: 4 (over z), cls: 4 (over x, core).
Axes of the slice: x: 2, y: 2, z: 4, core: 2. Of those that a mesh axis runs over, the one named last changes fastest.
Arguments:
- particles: bfloat16 [64, 4096], P(('groups', 'blk')), parts along dimension 0
- references: bfloat16 [4, 400, 4096], P('blk', ('groups', 'cls')), parts along dimension 1
- ctf_table: float32 [32, 2048], P('groups'), parts along dimension 0, may hold values from 0.05 to 1
- spectral_reg: float32 [4096], P('groups'), parts along dimension 0, may hold values from 0.002 to 0.02
- defocus_bin: int32 [64], P(('groups', 'blk')), parts along dimension 0, may hold values from 0 to 15
- group_counts: int32 [32], P(('groups', 'blk')), parts along dimension 0, may hold values from 0 to 8, as said below
- group_scale: float32 [32], P(('groups', 'blk')), parts along dimension 0, may hold values from 0.5 to 2
Outputs:
- class_average: float32 [4, 400, 4096], P('blk', ('groups', 'cls')), parts along dimension 1
- log_evidence: float32 [64], P(('groups', 'blk')), parts along dimension 0
There are 2 independent parts, one for each index of `groups`. A program takes and returns all parts, laid end to end along the dimension named above; each array names one. Nothing has to cross between parts.
Inputs may be any that keep to these rules, and one draw needn't show every extreme that they name: `group_counts`: the 4 groups of one block of 8 slots hold at most 8 particles together, filling the block's first slots; in every draw some single group holds exactly 8.
All inputs are finite; a program needn't handle non-finite values.
Results may differ from a plain program's by a relative error of at most 0.013.
Values may be sent and summed in bfloat16 or wider, within the bound.
No kernel may reach another device: no remote copies, remote signals or barrier semaphores. Data moves between devices by JAX's collectives and lax.ppermute only.
A program may use at most 64 MiB of HBM per device.

v0:
```python
import math

import jax
import jax.numpy as jnp
from jax import lax
from jax.sharding import PartitionSpec as P

KX = 32
KY = 64
IMG = 128
SIDE = 4
BINS = 16


HIGHEST = lax.Precision.HIGHEST


def combined_all(value, axis, join):
    pieces = jax.tree.map(lambda part: lax.all_gather(part, axis), value)
    head = jax.tree.map(lambda part: part[0], pieces)
    tail = jax.tree.map(lambda part: part[1:], pieces)
    running, _ = lax.scan(lambda running, section: (join(running, section), None), head, tail)
    return running


def phase_tables():
    column = jnp.arange(KX * KY, dtype=jnp.int32)
    freq_x = (column % KX).astype(jnp.float32)
    freq_y = (column // KX - KY // 2).astype(jnp.float32)
    offsets = jnp.arange(SIDE, dtype=jnp.float32) - (SIDE - 1) / 2.0
    shift_x = jnp.tile(offsets, SIDE)
    shift_y = jnp.repeat(offsets, SIDE)
    phases = (
        2.0
        * math.pi
        / IMG
        * (shift_x[:, None] * freq_x[None, :] + shift_y[:, None] * freq_y[None, :])
    )
    return (jnp.cos(phases), jnp.sin(phases))


def bin_matrix(bin_values):
    return (bin_values[:, None] == jnp.arange(BINS, dtype=jnp.float32)[None, :]).astype(jnp.float32)


def slot_weights(group_sizes, scale_rows, slots):
    group_ends = jnp.cumsum(group_sizes, axis=1)
    group_starts = group_ends - group_sizes
    slot_index = jnp.arange(slots, dtype=jnp.int32)
    membership = (
        (slot_index[None, :, None] >= group_starts[:, None, :])
        & (slot_index[None, :, None] < group_ends[:, None, :])
    ).astype(jnp.float32)
    gain_rows = jnp.sum(membership * scale_rows[:, None, :], axis=2)
    live_mask = jnp.sum(membership, axis=2)
    return (gain_rows.reshape(-1), live_mask.reshape(-1))


def shifted_rows(images, ctf_rows, cosine_table, sine_table):
    half_width = ctf_rows.shape[1]
    real_part = images[:, :half_width].astype(jnp.float32)[:, None, :]
    imag_part = images[:, half_width:].astype(jnp.float32)[:, None, :]
    ctf_wide = ctf_rows[:, None, :]
    new_real = (real_part * cosine_table + imag_part * sine_table) * ctf_wide
    new_imag = (imag_part * cosine_table - real_part * sine_table) * ctf_wide
    joined = jnp.concatenate([new_real, new_imag], axis=2).astype(jnp.bfloat16)
    return joined.reshape(images.shape[0] * cosine_table.shape[0], 2 * half_width)


def tile_norms(ref_rows, ctf_square):
    half_width = ctf_square.shape[1]
    values = ref_rows.astype(jnp.float32)
    power_sum = (
        values[:, :half_width] * values[:, :half_width]
        + values[:, half_width:] * values[:, half_width:]
    )
    return lax.dot_general(ctf_square, power_sum, (((1,), (1,)), ((), ())), precision=HIGHEST)


def tile_scores(shifted, ref_rows, norms, gain_rows, bin_rows):
    count_here = gain_rows.shape[0]
    products = lax.dot_general(
        shifted, ref_rows, (((1,), (1,)), ((), ())), preferred_element_type=jnp.float32
    )
    products = products.reshape(count_here, shifted.shape[0] // count_here, ref_rows.shape[0])
    norm_term = jnp.dot(bin_rows, norms, precision=HIGHEST)
    return (
        gain_rows[:, None, None] * products
        - 0.5 * (gain_rows * gain_rows)[:, None, None] * norm_term[:, None, :]
    )


def combine_stats(former, latter):
    new_peak = jnp.maximum(former[0], latter[0])
    return (
        new_peak,
        former[1] * jnp.exp(former[0] - new_peak) + latter[1] * jnp.exp(latter[0] - new_peak),
    )


def accumulate(running, shifted, scores, gain_rows, bin_rows, live_mask, peak_score, totals):
    weights = (
        jnp.exp(scores - peak_score[:, None, None])
        / totals[:, None, None]
        * live_mask[:, None, None]
    )
    scaled = (weights * gain_rows[:, None, None]).astype(jnp.bfloat16).reshape(shifted.shape[0], -1)
    numerator = running[0] + lax.dot_general(
        scaled, shifted, (((0,), (0,)), ((), ())), preferred_element_type=jnp.float32
    )
    summed = jnp.sum(weights, axis=1) * (gain_rows * gain_rows)[:, None]
    bin_weight = running[1] + lax.dot_general(
        summed, bin_rows, (((0,), (0,)), ((), ())), precision=HIGHEST
    )
    return (numerator, bin_weight)


def per_device(
    particles, references, ctf_table, spectral_reg, defocus_bin, group_counts, group_scale
):
    cosine_table, sine_table = phase_tables()
    ctf_square = ctf_table * ctf_table
    batch_size = particles.shape[0]
    gain_rows, live_mask = slot_weights(
        group_counts.reshape(1, -1), group_scale.reshape(1, -1), batch_size
    )
    bin_values = defocus_bin.astype(jnp.float32)
    ref_tile = references[0]
    own_norms = tile_norms(ref_tile, ctf_square)
    classes_here = ref_tile.shape[0]
    zero_sums = (
        jnp.zeros((classes_here, ref_tile.shape[1]), jnp.float32),
        jnp.zeros((classes_here, ctf_table.shape[0]), jnp.float32),
    )

    def batch_rows(images, bins_part):
        bin_rows = bin_matrix(bins_part)
        ctf_rows = jnp.dot(bin_rows, ctf_table, precision=HIGHEST)
        return (shifted_rows(images, ctf_rows, cosine_table, sine_table), bin_rows)

    everyone = lax.all_gather(particles, "blk", axis=0, tiled=True)
    gain_all, bins_all, live_all = (
        lax.all_gather(gain_rows, "blk", axis=0, tiled=True),
        lax.all_gather(bin_values, "blk", axis=0, tiled=True),
        lax.all_gather(live_mask, "blk", axis=0, tiled=True),
    )
    whole_count = everyone.shape[0]
    block_size = math.gcd(whole_count, 32)
    block_count = whole_count // block_size

    def block_inputs(block_index):
        offset = block_index * block_size
        images = lax.dynamic_slice_in_dim(everyone, offset, block_size)
        gains_part = lax.dynamic_slice_in_dim(gain_all, offset, block_size)
        shifted, bin_rows = batch_rows(
            images, lax.dynamic_slice_in_dim(bins_all, offset, block_size)
        )
        return (offset, shifted, bin_rows, gains_part)

    def block_scores(block_index):
        offset, shifted, bin_rows, gains_part = block_inputs(block_index)
        return tile_scores(shifted, ref_tile, own_norms, gains_part, bin_rows)

    all_scores = lax.map(block_scores, jnp.arange(block_count, dtype=jnp.int32))
    all_scores = all_scores.reshape(whole_count, cosine_table.shape[0], classes_here)
    flattened = all_scores.reshape(whole_count, -1)
    peak_all = jnp.max(flattened, axis=1)
    totals_all = jnp.sum(jnp.exp(flattened - peak_all[:, None]), axis=1)
    peak_all, totals_all = combined_all((peak_all, totals_all), ("blk", "cls"), combine_stats)

    def block_sums(block_index, running):
        offset, shifted, bin_rows, gains_part = block_inputs(block_index)
        scores = lax.dynamic_slice_in_dim(all_scores, offset, block_size)
        live_part = lax.dynamic_slice_in_dim(live_all, offset, block_size)
        peak_part = lax.dynamic_slice_in_dim(peak_all, offset, block_size)
        totals_part = lax.dynamic_slice_in_dim(totals_all, offset, block_size)
        return accumulate(
            running, shifted, scores, gains_part, bin_rows, live_part, peak_part, totals_part
        )

    numerator, bin_weight = lax.fori_loop(0, block_count, block_sums, zero_sums)
    own_offset = lax.axis_index("blk") * batch_size
    peak_score = lax.dynamic_slice_in_dim(peak_all, own_offset, batch_size)
    totals = lax.dynamic_slice_in_dim(totals_all, own_offset, batch_size)
    log_evidence = jnp.where(live_mask > 0.5, peak_score + jnp.log(totals), 0.0)
    denominator = jnp.dot(bin_weight, ctf_square, precision=HIGHEST)
    denominator = (
        jnp.concatenate([denominator, denominator], axis=1)
        + jnp.concatenate([spectral_reg, spectral_reg])[None, :]
    )
    class_average = (numerator / denominator)[None]
    return (class_average, log_evidence)


def solution(mesh):
    placed = (
        P(("groups", "blk"), None),
        P("blk", ("groups", "cls"), None),
        P("groups", None),
        P("groups"),
        P(("groups", "blk")),
        P(("groups", "blk")),
        P(("groups", "blk")),
    )
    return jax.shard_map(
        per_device,
        mesh=mesh,
        in_specs=placed,
        out_specs=(P("blk", ("groups", "cls"), None), P(("groups", "blk"))),
        check_vma=False,
    )
```

profile of v0, /device:TPU:0, one launch (start us, length us, event | category | flops | bytes accessed | tf_op | source)
XLA Modules:
  0.0 79.3 jit_solution(13035143194727210498)
XLA Ops:
  0.6 0.0 copy-start.1
  0.6 0.0 copy-start.2
  0.7 1.3 %dynamic-slice.2 = u32[1]{0:T(128)} dynamic-slice(u32[32]{0:T(128)} %constant.106, u32[]{:T(128)S(6)} %add.107), dynamic_slice_sizes={1} | dynamic-slice | bytes 12
  2.6 1.2 %dynamic-slice = u32[1]{0:T(128)} dynamic-slice(u32[32]{0:T(128)} %constant.96, u32[]{:T(128)S(6)} %add.107), dynamic_slice_sizes={1} | dynamic-slice | bytes 12
  4.5 0.8 %reduce-window.7 = s32[4,1]{0,1:T(1,128)S(1)} reduce-window(s32[4,1]{0,1:T(1,128)} %bitcast.39, s32[]{:T(128)} %copy.31), window={size=4x1 pad=3_0x0_0}, to_apply=%region_0.1 | reduce-window | flops 12 | bytes 36 | tf_op jit(solution)/shard_map/reduce-window.2
  5.3 0.7 bitcast_subtract_fusion
  6.0 0.7 select_reduce_fusion
  6.7 0.2 dynamic-update-slice.4
  7.0 0.7 convert_dynamic-update-slice_fusion
  7.7 0.2 dynamic-update-slice
  7.9 13.4 %all-reduce.6 = (f32[32]{0:T(128)S(1)}, f32[32]{0:T(128)S(1)}, f32[32]{0:T(128)S(1)}) all-reduce(f32[32]{0:T(128)S(1)} %convert_dynamic-update-slice_fusion, f32[32]{0:T(128)S(1)} %dynamic-update-slice.4, f32[32]{0:T(128)S(1)} %dynamic-update-slice), channel_id=1, replica_groups=mesh['groups'=2,'blk'=4,'cls'=4] {'blk'}, use_global_device_ids=true, to_apply=%add.1 | all-reduce | flops 96 | bytes 768
  21.4 0.1 broadcast_in_dim.50
  21.4 0.1 mul.359
  21.5 0.1 mul.355
  21.6 0.8 pad_maximum_fusion.7
  22.4 0.5 fusion.15
  22.9 1.2 %fusion.22 = f32[32,2048]{1,0:T(8,128)S(1)} fusion(f32[16,2048]{1,0:T(8,128)} %param.11, f32[32]{0:T(128)S(1)} %get-tuple-element.122), kind=kOutput, calls=%fused_computation.40 | convolution fusion | flops 12583424 | bytes 393344 | tf_op jit(solution)/shard_map/while/body/eval_jaxpr/dot_general | solution.py:138
  24.2 14.1 %all_gather.25 = bf16[32,4096]{1,0:T(8,128)(2,1)S(1)} all-gather(bf16[8,4096]{1,0:T(8,128)(2,1)} %param.9), channel_id=1, replica_groups=mesh['groups'=2,'blk'=4,'cls'=4] {'blk'}, dimensions={0}, use_global_device_ids=true | all-gather | bytes 327680 | tf_op jit(solution)/shard_map/all_gather | solution.py:141
  38.3 0.0 copy-done.2
  38.3 0.1 bitcast_convert_fusion
  38.4 0.0 copy-done.1
  38.4 0.5 fusion.11
  38.8 0.2 convolution_multiply_fusion
  39.1 1.5 %multiply_convert_fusion.1 = (bf16[32,16,2048]{2,1,0:T(8,128)(2,1)S(1)}, bf16[32,16,2048]{2,1,0:T(8,128)(2,1)S(1)}) fusion(f32[32,2048]{1,0:T(8,128)S(1)} %fusion.22, f32[16,2048]{1,0:T(8,128)S(1)} %get-tuple-element.132, f32[32,2048]{1,0:T(8,128)S(1)} %get-tuple-element.130, f32[16,2048]{1,0:T(8,128)S(1)} %get-tuple-element.131, ...), kind=kLoop, calls=%fused_computation.12 | loop fusion | flops 10485760 | bytes 5242880 | tf_op jit(solution)/shard_map/convert
  40.6 0.0 copy-start
  40.6 1.4 %fusion.40 = (f32[32]{0:T(128)S(1)}, f32[32,16,50]{2,1,0:T(8,128)S(1)}) fusion(f32[32,50]{1,0:T(8,128)S(1)} %convolution_multiply_fusion, bf16[1,50,4096]{2,1,0:T(8,128)(2,1)S(1)} %copy-done.2, bf16[32,16,2048]{2,1,0:T(8,128)(2,1)S(1)} %get-tuple-element.128, bf16[32,16,2048]{2,1,0:T(8,128)(2,1)S(1)} %get-tuple-element.127, f32[32]{0:T(128)S(1)} %get-tuple-element.124), kind=kOutput, calls=%fused_computation.71 | convolution fusion | flops 218180576 | bytes 4712960 | tf_op jit(solution)/shard_map/while/body/eval_jaxpr/dot_general | solution.py:82
  42.1 0.0 copy-done
  42.1 0.2 dynamic-update-slice.2
  42.3 0.5 exponential_reduce_fusion
  42.8 0.2 dynamic-update-slice.3
  43.0 29.5 %all-reduce.5 = (f32[512]{0:T(512)S(1)}, f32[512]{0:T(512)S(1)}) all-reduce(f32[512]{0:T(512)S(1)} %dynamic-update-slice.2, f32[512]{0:T(512)S(1)} %dynamic-update-slice.3), channel_id=2, replica_groups=mesh['groups'=2,'blk'=4,'cls'=4] {'blk','cls'}, use_global_device_ids=true, to_apply=%add.2 | all-reduce | flops 1024 | bytes 8192
  72.5 0.1 slice.42
  72.6 0.1 slice.43
  72.7 0.1 reshape.391
  72.7 0.1 reshape.390
  72.8 0.6 while.2
  73.4 0.6 compare_select_fusion
  74.0 0.2 fusion.38
  74.2 0.3 fusion.20
  74.5 0.5 fusion.17
  75.0 2.6 %fusion.6 = f32[1,50,4096]{2,1,0:T(8,128)S(1)} fusion(bf16[32,16,2048]{2,1,0:T(8,128)(2,1)} %copy-done, bf16[32,16,2048]{2,1,0:T(8,128)(2,1)S(1)} %get-tuple-element.127, f32[50,2048]{1,0:T(8,128)S(1)} %fusion.17, f32[4096]{0:T(1024)S(1)} %pad_maximum_fusion.7, f32[32]{0:T(128)S(1)} %get-tuple-element.124, f32[32,16,50]{2,1,0:T(8,128)S(1)} %get-tuple-element.136, ...), kind=kOutput, calls=%fused_computation.9 | convolution fusion | flops 218846208 | bytes 5542400 | tf_op jit(solution)/shard_map/while/body/eval_jaxpr/dot_general | solution.py:108
  77.6 1.7 %copy.14 = f32[1,50,4096]{2,0,1:T(1,128)} copy(f32[1,50,4096]{2,1,0:T(8,128)S(1)} %fusion.6) | data formatting | bytes 1638400
  (27 shorter events, 0.5 us)
Async XLA Ops:
  0.6 37.7 %copy-start.1 = (f32[16,2048]{1,0:T(8,128)S(1)}, f32[16,2048]{1,0:T(8,128)}, u32[]{:S(2)}) copy-start(f32[16,2048]{1,0:T(8,128)} %param.11) | copy-start | bytes 393220
  0.6 37.6 %copy-start.2 = (bf16[1,50,4096]{2,1,0:T(8,128)(2,1)S(1)}, bf16[1,50,4096]{2,1,0:T(8,128)(2,1)}, u32[]{:S(2)}) copy-start(bf16[1,50,4096]{2,1,0:T(8,128)(2,1)} %param.10) | copy-start | bytes 1228804
  40.6 1.5 %copy-start = (bf16[32,16,2048]{2,1,0:T(8,128)(2,1)}, bf16[32,16,2048]{2,1,0:T(8,128)(2,1)S(1)}, u32[]{:S(2)}) copy-start(bf16[32,16,2048]{2,1,0:T(8,128)(2,1)S(1)} %get-tuple-element.128) | copy-start | bytes 6291460
where the time goes:
time: 79.7 us; the launch traced here: 79.3 us
  blocking collectives  57 us (72%)
  other arithmetic  7.63 us (10%)
  matrix products  6.69 us (8%)
  local copies, waits for them, and re-layouts  5.77 us (7%)
  between operations  2.08 us (3%)
    unnamed x2, blocking collectives  42.9 us
    all_gather x1, blocking collectives, per_device(): everyone = lax.all_gather(particles, 'blk', axis=0, tiled=True)  14.1 us
    unnamed x18, local copies, waits for them, and re-layouts  5.22 us
    dot_general x1, matrix products, accumulate(): lax.dot_general(scaled, shifted, (((0,), (0,)), ((), ())), preferred_elem...  2.57 us
    another operation x2, other arithmetic  2.37 us

commit v1 on v0

v1 whole, which is shorter than its diff:
```python
import math

import jax
import jax.numpy as jnp
from jax import lax
from jax.sharding import PartitionSpec as P

KX = 32
KY = 64
IMG = 128
SIDE = 4
BINS = 16
META = 128


HIGHEST = lax.Precision.HIGHEST


def phase_tables():
    column = jnp.arange(KX * KY, dtype=jnp.int32)
    freq_x = (column % KX).astype(jnp.float32)
    freq_y = (column // KX - KY // 2).astype(jnp.float32)
    offsets = jnp.arange(SIDE, dtype=jnp.float32) - (SIDE - 1) / 2.0
    shift_x = jnp.tile(offsets, SIDE)
    shift_y = jnp.repeat(offsets, SIDE)
    phases = (
        2.0
        * math.pi
        / IMG
        * (shift_x[:, None] * freq_x[None, :] + shift_y[:, None] * freq_y[None, :])
    )
    return (jnp.cos(phases), jnp.sin(phases))


def bin_matrix(bin_values):
    return (bin_values[:, None] == jnp.arange(BINS, dtype=jnp.float32)[None, :]).astype(jnp.float32)


def slot_weights(group_sizes, scale_rows, slots):
    group_ends = jnp.cumsum(group_sizes, axis=1)
    group_starts = group_ends - group_sizes
    slot_index = jnp.arange(slots, dtype=jnp.int32)
    membership = (
        (slot_index[None, :, None] >= group_starts[:, None, :])
        & (slot_index[None, :, None] < group_ends[:, None, :])
    ).astype(jnp.float32)
    gain_rows = jnp.sum(membership * scale_rows[:, None, :], axis=2)
    live_mask = jnp.sum(membership, axis=2)
    return (gain_rows.reshape(-1), live_mask.reshape(-1))


def shifted_rows(images, ctf_rows, cosine_table, sine_table):
    half_width = ctf_rows.shape[1]
    real_part = images[:, :half_width].astype(jnp.float32)[:, None, :]
    imag_part = images[:, half_width:].astype(jnp.float32)[:, None, :]
    ctf_wide = ctf_rows[:, None, :]
    new_real = (real_part * cosine_table + imag_part * sine_table) * ctf_wide
    new_imag = (imag_part * cosine_table - real_part * sine_table) * ctf_wide
    joined = jnp.concatenate([new_real, new_imag], axis=2).astype(jnp.bfloat16)
    return joined.reshape(images.shape[0] * cosine_table.shape[0], 2 * half_width)


def tile_norms(ref_rows, ctf_square):
    half_width = ctf_square.shape[1]
    values = ref_rows.astype(jnp.float32)
    power_sum = (
        values[:, :half_width] * values[:, :half_width]
        + values[:, half_width:] * values[:, half_width:]
    )
    return lax.dot_general(ctf_square, power_sum, (((1,), (1,)), ((), ())), precision=HIGHEST)


def tile_scores(shifted, ref_rows, norms, gain_rows, bin_rows):
    count_here = gain_rows.shape[0]
    products = lax.dot_general(
        shifted, ref_rows, (((1,), (1,)), ((), ())), preferred_element_type=jnp.float32
    )
    products = products.reshape(count_here, shifted.shape[0] // count_here, ref_rows.shape[0])
    norm_term = jnp.dot(bin_rows, norms, precision=HIGHEST)
    return (
        gain_rows[:, None, None] * products
        - 0.5 * (gain_rows * gain_rows)[:, None, None] * norm_term[:, None, :]
    )


def combine_stats(former, latter):
    new_peak = jnp.maximum(former[0], latter[0])
    return (
        new_peak,
        former[1] * jnp.exp(former[0] - new_peak) + latter[1] * jnp.exp(latter[0] - new_peak),
    )


def combine_many(peaks, totals):
    new_peak = jnp.max(peaks, axis=0)
    return (new_peak, jnp.sum(totals * jnp.exp(peaks - new_peak[None]), axis=0))


def split_exact(value):
    high = lax.reduce_precision(value, exponent_bits=8, mantissa_bits=7)
    rest = value - high
    middle = lax.reduce_precision(rest, exponent_bits=8, mantissa_bits=7)
    return (high, middle, rest - middle)


def shift_gather(value, axis, size):
    pieces = [value] + [
        lax.ppermute(value, axis, [(i, (i + k) % size) for i in range(size)])
        for k in range(1, size)
    ]
    return jnp.concatenate(pieces, axis=0)


def xor_butterfly(stats, axis, size):
    step = 1
    while step < size:
        other = jax.tree.map(
            lambda part: lax.ppermute(part, axis, [(i, i ^ step) for i in range(size)]), stats
        )
        stats = combine_stats(stats, other)
        step *= 2
    return stats


def accumulate(shifted, scores, gain_rows, bin_rows, live_mask, peak_score, totals):
    weights = (
        jnp.exp(scores - peak_score[:, None, None])
        / totals[:, None, None]
        * live_mask[:, None, None]
    )
    scaled = (weights * gain_rows[:, None, None]).astype(jnp.bfloat16).reshape(shifted.shape[0], -1)
    numerator = lax.dot_general(
        scaled, shifted, (((0,), (0,)), ((), ())), preferred_element_type=jnp.float32
    )
    summed = jnp.sum(weights, axis=1) * (gain_rows * gain_rows)[:, None]
    bin_weight = lax.dot_general(summed, bin_rows, (((0,), (0,)), ((), ())), precision=HIGHEST)
    return (numerator, bin_weight)


def per_device(
    particles, references, ctf_table, spectral_reg, defocus_bin, group_counts, group_scale,
    *, n_blk, n_cls,
):
    cosine_table, sine_table = phase_tables()
    ctf_square = ctf_table * ctf_table
    batch_size, width = particles.shape
    gain_rows, live_mask = slot_weights(
        group_counts.reshape(1, -1), group_scale.reshape(1, -1), batch_size
    )
    ref_tile = references[0]
    own_norms = tile_norms(ref_tile, ctf_square)
    classes_here = ref_tile.shape[0]
    shifts_count = cosine_table.shape[0]

    small = n_blk <= 4
    if small:
        meta = jnp.stack(
            [*split_exact(gain_rows), live_mask, defocus_bin.astype(jnp.float32)], axis=1
        )
        meta = jnp.pad(meta, ((0, 0), (0, META - meta.shape[1]))).astype(jnp.bfloat16)
        packed = jnp.concatenate([particles, meta], axis=1)
        everyone = shift_gather(packed, "blk", n_blk)
        images = everyone[:, :width]
        meta_all = everyone[:, width : width + 5].astype(jnp.float32)
        gain_all = (meta_all[:, 0] + meta_all[:, 1]) + meta_all[:, 2]
        live_all = meta_all[:, 3]
        bins_all = meta_all[:, 4]
    else:
        images = lax.all_gather(particles, "blk", axis=0, tiled=True)
        gain_all, bins_all, live_all = (
            lax.all_gather(gain_rows, "blk", axis=0, tiled=True),
            lax.all_gather(defocus_bin.astype(jnp.float32), "blk", axis=0, tiled=True),
            lax.all_gather(live_mask, "blk", axis=0, tiled=True),
        )
    whole_count = images.shape[0]

    bin_rows = bin_matrix(bins_all)
    ctf_rows = jnp.dot(bin_rows, ctf_table, precision=HIGHEST)
    shifted = shifted_rows(images, ctf_rows, cosine_table, sine_table)
    all_scores = tile_scores(shifted, ref_tile, own_norms, gain_all, bin_rows)
    flattened = all_scores.reshape(whole_count, -1)
    peak_all = jnp.max(flattened, axis=1)
    totals_all = jnp.sum(jnp.exp(flattened - peak_all[:, None]), axis=1)

    if small and n_cls & (n_cls - 1) == 0:
        peak_all, totals_all = xor_butterfly((peak_all, totals_all), "cls", n_cls)
        stats = jnp.stack([peak_all, totals_all]).reshape(2, n_blk, batch_size)
        parts = [stats] + [
            jnp.roll(lax.ppermute(stats, "blk", [(i, (i + k) % n_blk) for i in range(n_blk)]), k, axis=1)
            for k in range(1, n_blk)
        ]
        parts = jnp.stack(parts)
        peak_all, totals_all = combine_many(parts[:, 0], parts[:, 1])
        peak_all = peak_all.reshape(-1)
        totals_all = totals_all.reshape(-1)
        peak_score = peak_all[:batch_size]
        totals = totals_all[:batch_size]
    else:
        gathered = lax.all_gather(jnp.stack([peak_all, totals_all]), ("blk", "cls"))
        peak_all, totals_all = combine_many(gathered[:, 0], gathered[:, 1])
        if small:
            own_offset = 0
        else:
            own_offset = lax.axis_index("blk") * batch_size
        peak_score = lax.dynamic_slice_in_dim(peak_all, own_offset, batch_size)
        totals = lax.dynamic_slice_in_dim(totals_all, own_offset, batch_size)

    numerator, bin_weight = accumulate(
        shifted, all_scores, gain_all, bin_rows, live_all, peak_all, totals_all
    )
    log_evidence = jnp.where(live_mask > 0.5, peak_score + jnp.log(totals), 0.0)
    denominator = jnp.dot(bin_weight, ctf_square, precision=HIGHEST)
    denominator = (
        jnp.concatenate([denominator, denominator], axis=1)
        + jnp.concatenate([spectral_reg, spectral_reg])[None, :]
    )
    class_average = (numerator / denominator)[None]
    return (class_average, log_evidence)


def solution(mesh):
    placed = (
        P(("groups", "blk"), None),
        P("blk", ("groups", "cls"), None),
        P("groups", None),
        P("groups"),
        P(("groups", "blk")),
        P(("groups", "blk")),
        P(("groups", "blk")),
    )
    body = lambda *args: per_device(*args, n_blk=mesh.shape["blk"], n_cls=mesh.shape["cls"])
    return jax.shard_map(
        body,
        mesh=mesh,
        in_specs=placed,
        out_specs=(P("blk", ("groups", "cls"), None), P(("groups", "blk"))),
        check_vma=False,
    )
```

time: 79.7 us -> 41.2 us (0.52)
  blocking collectives: 57 us -> 0 us
  starting transfers between devices: 0 us -> 12.5 us
  waiting for transfers between devices: 0 us -> 9.66 us
  local copies, waits for them, and re-layouts: 5.77 us -> 2.66 us
  between operations: 2.08 us -> 0.82 us
  other arithmetic: 7.63 us -> 8.55 us
    unnamed x2 -> x0, blocking collectives: 42.9 us -> none
    all_gather x1 -> x0, blocking collectives: 14.1 us -> none  [per_device(): everyone = lax.all_gather(particles, 'blk', axis=0, tiled=True)]
    ppermute x0 -> x10, starting transfers between devices: none -> 12.5 us  [the longest x3 6.06 us: shift_gather(): lax.ppermute(value, axis, [(i, (i + k) % size) for i in range(size)])]
    ppermute x0 -> x10, waiting for transfers between devices: none -> 9.66 us  [the longest x4 3.82 us: xor_butterfly(): lax.ppermute(part, axis, [(i, i ^ step) for i in range(size)])]
    unnamed x18 -> x13, local copies, waits for them, and re-layouts: 5.22 us -> 1.87 us
    convert_element_type x1, other arithmetic: 0.06 us -> 1.08 us  [tile_norms(): values = ref_rows.astype(jnp.float32)]
    dot_general x1, matrix products: 0.48 us -> 1.38 us  [tile_norms(): lax.dot_general(ctf_square, power_sum, (((1,), (1,)), ((), ())), precisio...]
    dot_general x1, matrix products: 1.21 us -> 0.31 us  [per_device(): ctf_rows = jnp.dot(bin_rows, ctf_table, precision=HIGHEST)]
  transfers between devices with their start and end apart: 0 -> 10, of which waited for: 0 -> 7; matrix products, arithmetic and copies ran while one was open for 0% -> 8% of each run, Pallas kernels for 0% -> 0%
where the time goes in v1:
time: 41.2 us; the launch traced here: 40.9 us
  starting transfers between devices  12.5 us (30%)
  waiting for transfers between devices  9.66 us (23%)
  other arithmetic  8.55 us (21%)
  matrix products  6.73 us (16%)
  local copies, waits for them, and re-layouts  2.66 us (6%)
  between operations  0.82 us (2%)
    ppermute x3, starting transfers between devices, shift_gather(): lax.ppermute(value, axis, [(i, (i + k) % size) for i in range(size)])  6.06 us
    ppermute x4, waiting for transfers between devices, xor_butterfly(): lax.ppermute(part, axis, [(i, i ^ step) for i in range(size)])  3.82 us
    ppermute x3, starting transfers between devices, per_device(): lax.ppermute(stats, 'blk', [(i, (i + k) % n_blk) for i in range(n_blk)])  3.79 us
    ppermute x3, waiting for transfers between devices, per_device(): lax.ppermute(stats, 'blk', [(i, (i + k) % n_blk) for i in range(n_blk)])  3.49 us
    ppermute x4, starting transfers between devices, xor_butterfly(): lax.ppermute(part, axis, [(i, i ^ step) for i in range(size)])  2.61 us
    dot_general x1, matrix products, accumulate(): lax.dot_general(scaled, shifted, (((0,), (0,)), ((), ())), preferred_elem...  2.57 us
    another operation x3, other arithmetic  2.42 us
    ppermute x3, waiting for transfers between devices, shift_gather(): lax.ppermute(value, axis, [(i, (i + k) % size) for i in range(size)])  2.35 us
  transfers between devices with their start and end apart: 10, of which 7 were waited for; matrix products, arithmetic and copies ran while one was open for 8% of the time, Pallas kernels for 0%

profile of v1, /device:TPU:0, one launch (start us, length us, event | category | flops | bytes accessed | tf_op | source)
XLA Modules:
  0.0 40.9 jit_solution(12313942731739047112)
XLA Ops:
  0.6 0.0 copy-start.1
  0.6 0.0 copy-start.2
  0.7 0.9 %reduce-window.7 = s32[4,1]{0,1:T(1,128)S(1)} reduce-window(s32[4,1]{0,1:T(1,128)} %bitcast.55, s32[]{:T(128)} %constant.41.clone.1), window={size=4x1 pad=3_0x0_0}, to_apply=%region_0.1 | reduce-window | flops 12 | bytes 36 | tf_op jit(solution)/shard_map/reduce-window.2
  1.5 0.7 %bitcast_subtract_fusion.1 = s32[4]{0:T(128)S(1)} fusion(s32[4]{0:T(128)} %param.12, s32[4,1]{0,1:T(1,128)S(1)} %reduce-window.7), kind=kLoop, calls=%fused_computation.93 | loop fusion | flops 4 | bytes 48 | tf_op jit(solution)/shard_map/sub | solution.py:41
  2.2 0.7 %convert_reduce_fusion = (f32[8]{0:T(128)S(1)}, f32[8]{0:T(128)S(1)}) fusion(s32[4]{0:T(128)S(1)} %bitcast.54, s32[4]{0:T(128)S(1)} %bitcast_subtract_fusion.1, f32[4]{0:T(128)} %param.13), kind=kLoop, calls=%fused_computation.74 | loop fusion | flops 208 | bytes 112 | tf_op jit(solution)/shard_map/reduce_sum | solution.py:48
  2.9 0.7 %convert_bitcast_fusion = bf16[8,1]{0,1:T(2,128)(2,1)S(1)} fusion(s32[8]{0:T(128)} %param.11), kind=kLoop, calls=%fused_computation.89 | loop fusion | flops 16 | bytes 48 | tf_op jit(solution)/shard_map/stack | solution.py:157
  3.6 0.1 copy.19
  3.7 0.8 %pad_maximum_fusion.11 = bf16[8,4224]{1,0:T(8,128)(2,1)S(1)} fusion(bf16[8,128]{1,0:T(8,128)(2,1)S(1)} %pad.5.clone, bf16[8,4096]{1,0:T(8,128)(2,1)} %param.7), kind=kLoop, calls=%fused_computation.33 | loop fusion | flops 135168 | bytes 135168 | tf_op jit(solution)/shard_map/concatenate | solution.py:161
  4.6 5.0 %collective-permute-start.2 = (bf16[8,4224]{1,0:T(8,128)(2,1)S(1)}, bf16[8,4224]{1,0:T(8,128)(2,1)S(1)}, u32[]{:S(2)}, u32[]{:S(2)}) collective-permute-start(bf16[8,4224]{1,0:T(8,128)(2,1)S(1)} %pad_maximum_fusion.11), channel_id=1, source_target_pairs={{0,12},{4,0},{8,4},{12,8},{1,13},{5,1},{9,5},{13,9},{2,14},{6,2},{... | collective-permute-start | bytes 202760 | tf_op jit(solution)/shard_map/ppermute | solution.py:108
  9.6 0.0 collective-permute-start.1
  9.6 1.0 %collective-permute-start = (bf16[8,4224]{1,0:T(8,128)(2,1)S(1)}, bf16[8,4224]{1,0:T(8,128)(2,1)S(1)}, u32[]{:S(2)}, u32[]{:S(2)}) collective-permute-start(bf16[8,4224]{1,0:T(8,128)(2,1)S(1)} %pad_maximum_fusion.11), channel_id=1, source_target_pairs={{0,4},{4,8},{8,12},{12,0},{1,5},{5,9},{9,13},{13,1},{2,6},{6,10},{... | collective-permute-start | bytes 202760 | tf_op jit(solution)/shard_map/ppermute | solution.py:108
  10.7 0.1 broadcast_in_dim.13
  10.7 0.1 mul.278
  10.8 0.1 mul.274
  10.9 1.1 %bitcast_convert_fusion = f32[50,4096]{1,0:T(8,128)S(1)} fusion(bf16[1,50,4096]{2,1,0:T(8,128)(2,1)} %param.8), kind=kLoop, calls=%fused_computation.16 | loop fusion | flops 204800 | bytes 1228800 | tf_op jit(solution)/shard_map/convert_element_type | solution.py:65
  12.0 0.5 %fusion.11 = (f32[16,2048]{1,0:T(8,128)S(1)}, f32[16,2048]{1,0:T(8,128)S(1)}) fusion(f32[2048]{0:T(1024)S(1)} %get-tuple-element.32, f32[16]{0:T(128)S(1)} %mul.278, f32[2048]{0:T(1024)S(1)} %get-tuple-element.31, f32[16]{0:T(128)S(1)} %mul.274), kind=kLoop, calls=%fused_computation.28 | loop fusion | flops 131072 | bytes 278656 | tf_op jit(solution)/shard_map/cos | solution.py:32
  12.5 1.4 %fusion.6 = f32[16,50]{1,0:T(8,128)S(1)} fusion(f32[50,4096]{1,0:T(8,128)S(1)} %bitcast_convert_fusion, f32[16,2048]{1,0:T(8,128)} %param.9), kind=kOutput, calls=%fused_computation.13 | convolution fusion | flops 20000768 | bytes 953472 | tf_op jit(solution)/shard_map/dot_general | solution.py:70
  13.9 0.0 collective-permute-done.2
  13.9 2.3 %collective-permute-done.1 = bf16[8,4224]{1,0:T(8,128)(2,1)S(1)} collective-permute-done((bf16[8,4224]{1,0:T(8,128)(2,1)S(1)}, bf16[8,4224]{1,0:T(8,128)(2,1)S(1)}, u32[]{:S(2)}, u32[]{:S(2)}) %collective-permute-start.1) | collective-permute-done | bytes 67616 | tf_op jit(solution)/shard_map/ppermute | solution.py:108
  16.3 0.0 collective-permute-done
  16.3 0.0 copy-done.1
  16.3 0.2 multiply_reduce_fusion
  16.5 0.0 copy-done.2
  16.5 0.3 fusion.18
  16.8 0.2 convolution_multiply_fusion
  17.1 0.0 copy-start.3
  17.1 1.5 %multiply_convert_fusion.1 = (bf16[32,16,2048]{2,1,0:T(8,128)(2,1)S(1)}, bf16[32,16,2048]{2,1,0:T(8,128)(2,1)S(1)}) fusion(f32[32,2048]{1,0:T(8,128)S(1)} %fusion.18, f32[16,2048]{1,0:T(8,128)S(1)} %get-tuple-element.23, f32[32,2048]{1,0:T(8,128)S(1)} %get-tuple-element.21, f32[16,2048]{1,0:T(8,128)S(1)} %get-tuple-element.22, ...), kind=kLoop, calls=%fused_computation.5 | loop fusion | flops 10485760 | bytes 5242880 | tf_op jit(solution)/shard_map/convert
  18.7 0.0 copy-start
  18.7 0.0 copy-done.3
  18.7 0.0 copy-start.4
  18.7 1.4 %fusion.41 = (f32[32]{0:T(128)S(1)}, f32[32,16,50]{2,1,0:T(8,128)S(1)}) fusion(f32[32,50]{1,0:T(8,128)S(1)} %convolution_multiply_fusion, bf16[1,50,4096]{2,1,0:T(8,128)(2,1)S(1)} %copy-done.3, bf16[32,16,2048]{2,1,0:T(8,128)(2,1)S(1)} %get-tuple-element.19, bf16[32,16,2048]{2,1,0:T(8,128)(2,1)S(1)} %get-tuple-element.18, f32[32]{0:T(128)S(1)} %get-tuple-element.9), kind=kOutput, calls=%fused_computation.97 | convolution fusion | flops 218180576 | bytes 4712960 | tf_op jit(solution)/shard_map/dot_general | solution.py:75
  20.1 0.0 copy-done
  20.1 0.5 %exponential_reduce_fusion = f32[32]{0:T(128)S(1)} fusion(f32[32,16,50]{2,1,0:T(8,128)S(1)} %get-tuple-element.30, f32[32]{0:T(128)S(1)} %get-tuple-element.29), kind=kLoop, calls=%fused_computation.19 | loop fusion | flops 51168 | bytes 102656 | tf_op jit(solution)/shard_map/reduce_sum | solution.py:183
  20.6 0.1 collective-permute-start.5
  20.7 0.5 %collective-permute-start.3 = (f32[32]{0:T(128)S(1)}, f32[32]{0:T(128)S(1)}, u32[]{:S(2)}, u32[]{:S(2)}) collective-permute-start(f32[32]{0:T(128)S(1)} %get-tuple-element.29), channel_id=1, source_target_pairs={{0,1},{1,0},{2,3},{3,2},{4,5},{5,4},{6,7},{7,6},{8,9},{9,8},{10,11... | collective-permute-start | bytes 392 | tf_op jit(solution)/shard_map/ppermute | solution.py:118
  21.2 0.6 %collective-permute-done.5 = f32[32]{0:T(128)S(1)} collective-permute-done((f32[32]{0:T(128)S(1)}, f32[32]{0:T(128)S(1)}, u32[]{:S(2)}, u32[]{:S(2)}) %collective-permute-start.5) | collective-permute-done | bytes 160 | tf_op jit(solution)/shard_map/ppermute | solution.py:118
  21.8 0.2 collective-permute-done.3
  22.0 1.5 %collective-permute-start.6 = (f32[32]{0:T(128)S(1)}, f32[32]{0:T(128)S(1)}, u32[]{:S(2)}, u32[]{:S(2)}) collective-permute-start(f32[32]{0:T(128)S(1)} %get-tuple-element.16), channel_id=1, source_target_pairs={{0,2},{1,3},{2,0},{3,1},{4,6},{5,7},{6,4},{7,5},{8,10},{9,11},{10,... | collective-permute-start | bytes 392 | tf_op jit(solution)/shard_map/ppermute | solution.py:118
  23.5 0.5 %collective-permute-start.4 = (f32[32]{0:T(128)S(1)}, f32[32]{0:T(128)S(1)}, u32[]{:S(2)}, u32[]{:S(2)}) collective-permute-start(f32[32]{0:T(128)S(1)} %get-tuple-element.17), channel_id=1, source_target_pairs={{0,2},{1,3},{2,0},{3,1},{4,6},{5,7},{6,4},{7,5},{8,10},{9,11},{10,... | collective-permute-start | bytes 392 | tf_op jit(solution)/shard_map/ppermute | solution.py:118
  24.1 1.5 %collective-permute-done.6 = f32[32]{0:T(128)S(1)} collective-permute-done((f32[32]{0:T(128)S(1)}, f32[32]{0:T(128)S(1)}, u32[]{:S(2)}, u32[]{:S(2)}) %collective-permute-start.6) | collective-permute-done | bytes 160 | tf_op jit(solution)/shard_map/ppermute | solution.py:118
  25.6 1.5 %collective-permute-done.4 = f32[32]{0:T(128)S(1)} collective-permute-done((f32[32]{0:T(128)S(1)}, f32[32]{0:T(128)S(1)}, u32[]{:S(2)}, u32[]{:S(2)}) %collective-permute-start.4) | collective-permute-done | bytes 160 | tf_op jit(solution)/shard_map/ppermute | solution.py:118
  27.1 0.1 stack.44
  27.2 0.1 stack.43
  27.3 1.9 %collective-permute-start.9 = (f32[2,4,8]{2,1,0:T(4,128)S(1)}, f32[2,4,8]{2,1,0:T(4,128)S(1)}, u32[]{:S(2)}, u32[]{:S(2)}) collective-permute-start(f32[2,4,8]{2,1,0:T(4,128)S(1)} %constant_dynamic-update-slice_fusion), channel_id=1, source_target_pairs={{0,12},{4,0},{8,4},{12,8},{1,13},{5,1},{9,5},{13,9},{2,14},{6,2},{... | collective-permute-start | bytes 776 | tf_op jit(solution)/shard_map/ppermute | solution.py:189
  29.1 0.0 copy-done.4
  29.1 0.1 stack.41
  29.2 0.1 stack.40
  29.3 0.0 collective-permute-start.8
  29.3 1.9 %collective-permute-start.7 = (f32[2,4,8]{2,1,0:T(4,128)S(1)}, f32[2,4,8]{2,1,0:T(4,128)S(1)}, u32[]{:S(2)}, u32[]{:S(2)}) collective-permute-start(f32[2,4,8]{2,1,0:T(4,128)S(1)} %constant_dynamic-update-slice_fusion), channel_id=1, source_target_pairs={{0,4},{4,8},{8,12},{12,0},{1,5},{5,9},{9,13},{13,1},{2,6},{6,10},{... | collective-permute-start | bytes 776 | tf_op jit(solution)/shard_map/ppermute | solution.py:189
  31.2 0.0 collective-permute-done.9
  31.3 2.6 %collective-permute-done.8 = f32[2,4,8]{2,1,0:T(4,128)S(1)} collective-permute-done((f32[2,4,8]{2,1,0:T(4,128)S(1)}, f32[2,4,8]{2,1,0:T(4,128)S(1)}, u32[]{:S(2)}, u32[]{:S(2)}) %collective-permute-start.8) | collective-permute-done | bytes 288 | tf_op jit(solution)/shard_map/ppermute | solution.py:189
  33.8 0.9 %collective-permute-done.7 = f32[2,4,8]{2,1,0:T(4,128)S(1)} collective-permute-done((f32[2,4,8]{2,1,0:T(4,128)S(1)}, f32[2,4,8]{2,1,0:T(4,128)S(1)}, u32[]{:S(2)}, u32[]{:S(2)}) %collective-permute-start.7) | collective-permute-done | bytes 288 | tf_op jit(solution)/shard_map/ppermute | solution.py:189
  34.8 0.1 sub.124
  34.9 0.5 %compare_select_fusion = f32[8]{0:T(128)} fusion(f32[8]{0:T(128)S(1)} %get-tuple-element.12, f32[4,8]{1,0:T(4,128)S(1)} %fusion.24, f32[4,8]{1,0:T(4,128)S(1)} %slice_reduce_fusion.2), kind=kLoop, calls=%fused_computation.79 | loop fusion | flops 24 | bytes 128 | tf_op jit(solution)/shard_map/jit(_where)/select_n | solution.py:211
  35.4 0.1 div.29
  35.5 0.2 fusion.39
  35.7 0.3 fusion.16
  36.0 0.6 %fusion.13 = f32[50,2048]{1,0:T(8,128)S(1)} fusion(f32[50,16]{0,1:T(8,128)S(1)} %fusion.16, f32[16,2048]{1,0:T(8,128)S(1)} %copy-done.2), kind=kOutput, calls=%fused_computation.30 | convolution fusion | flops 19693568 | bytes 543872 | tf_op jit(solution)/shard_map/dot_general | solution.py:212
  36.6 2.6 %fusion.1 = f32[1,50,4096]{2,1,0:T(8,128)S(1)} fusion(bf16[32,16,2048]{2,1,0:T(8,128)(2,1)} %copy-done, bf16[32,16,2048]{2,1,0:T(8,128)(2,1)S(1)} %get-tuple-element.18, f32[50,2048]{1,0:T(8,128)S(1)} %fusion.13, f32[4096]{0:T(1024)S(1)} %pad_maximum_fusion.13, f32[32]{0:T(128)S(1)} %get-tuple-element.9, f32[32,16,50]{2,1,0:T(8,128)S(1)} %get-tuple-element.30, ...), kind=kOutput, calls=%fused_computation.2 | convolution fusion | flops 218846208 | bytes 5542400 | tf_op jit(solution)/shard_map/dot_general | solution.py:132
  39.2 1.7 %copy.18 = f32[1,50,4096]{2,0,1:T(1,128)} copy(f32[1,50,4096]{2,1,0:T(8,128)S(1)} %fusion.1) | data formatting | bytes 1638400
  (25 shorter events, 0.2 us)
Async XLA Ops:
  0.6 15.7 %copy-start.1 = (bf16[8,4096]{1,0:T(8,128)(2,1)S(1)}, bf16[8,4096]{1,0:T(8,128)(2,1)}, u32[]{:S(2)}) copy-start(bf16[8,4096]{1,0:T(8,128)(2,1)} %param.7) | copy-start | bytes 196612
  0.6 15.9 %copy-start.2 = (f32[16,2048]{1,0:T(8,128)S(1)}, f32[16,2048]{1,0:T(8,128)}, u32[]{:S(2)}) copy-start(f32[16,2048]{1,0:T(8,128)} %param.9) | copy-start | bytes 393220
  4.6 9.4 %collective-permute-start.2 = (bf16[8,4224]{1,0:T(8,128)(2,1)S(1)}, bf16[8,4224]{1,0:T(8,128)(2,1)S(1)}, u32[]{:S(2)}, u32[]{:S(2)}) collective-permute-start(bf16[8,4224]{1,0:T(8,128)(2,1)S(1)} %pad_maximum_fusion.11), channel_id=1, source_target_pairs={{0,12},{4,0},{8,4},{12,8},{1,13},{5,1},{9,5},{13,9},{2,14},{6,2},{... | collective-permute-start | bytes 202760 | tf_op jit(solution)/shard_map/ppermute | solution.py:108
  9.6 6.6 %collective-permute-start.1 = (bf16[8,4224]{1,0:T(8,128)(2,1)S(1)}, bf16[8,4224]{1,0:T(8,128)(2,1)S(1)}, u32[]{:S(2)}, u32[]{:S(2)}) collective-permute-start(bf16[8,4224]{1,0:T(8,128)(2,1)S(1)} %pad_maximum_fusion.11), channel_id=1, source_target_pairs={{0,8},{4,12},{8,0},{12,4},{1,9},{5,13},{9,1},{13,5},{2,10},{6,14},... | collective-permute-start | bytes 202760 | tf_op jit(solution)/shard_map/ppermute | solution.py:108
  9.6 6.6 %collective-permute-start = (bf16[8,4224]{1,0:T(8,128)(2,1)S(1)}, bf16[8,4224]{1,0:T(8,128)(2,1)S(1)}, u32[]{:S(2)}, u32[]{:S(2)}) collective-permute-start(bf16[8,4224]{1,0:T(8,128)(2,1)S(1)} %pad_maximum_fusion.11), channel_id=1, source_target_pairs={{0,4},{4,8},{8,12},{12,0},{1,5},{5,9},{9,13},{13,1},{2,6},{6,10},{... | collective-permute-start | bytes 202760 | tf_op jit(solution)/shard_map/ppermute | solution.py:108
  17.1 1.6 %copy-start.3 = (bf16[1,50,4096]{2,1,0:T(8,128)(2,1)S(1)}, bf16[1,50,4096]{2,1,0:T(8,128)(2,1)}, u32[]{:S(2)}) copy-start(bf16[1,50,4096]{2,1,0:T(8,128)(2,1)} %param.8) | copy-start | bytes 1228804
  18.7 1.5 %copy-start = (bf16[32,16,2048]{2,1,0:T(8,128)(2,1)}, bf16[32,16,2048]{2,1,0:T(8,128)(2,1)S(1)}, u32[]{:S(2)}) copy-start(bf16[32,16,2048]{2,1,0:T(8,128)(2,1)S(1)} %get-tuple-element.19) | copy-start | bytes 6291460
  18.7 10.5 %copy-start.4 = (f32[2048]{0:T(1024)S(1)}, f32[2048]{0:T(1024)}, u32[]{:S(2)}) copy-start(f32[2048]{0:T(1024)} %param.10) | copy-start | bytes 24580
  20.6 1.2 %collective-permute-start.5 = (f32[32]{0:T(128)S(1)}, f32[32]{0:T(128)S(1)}, u32[]{:S(2)}, u32[]{:S(2)}) collective-permute-start(f32[32]{0:T(128)S(1)} %exponential_reduce_fusion), channel_id=1, source_target_pairs={{0,1},{1,0},{2,3},{3,2},{4,5},{5,4},{6,7},{7,6},{8,9},{9,8},{10,11... | collective-permute-start | bytes 392 | tf_op jit(solution)/shard_map/ppermute | solution.py:118
  20.7 1.3 %collective-permute-start.3 = (f32[32]{0:T(128)S(1)}, f32[32]{0:T(128)S(1)}, u32[]{:S(2)}, u32[]{:S(2)}) collective-permute-start(f32[32]{0:T(128)S(1)} %get-tuple-element.29), channel_id=1, source_target_pairs={{0,1},{1,0},{2,3},{3,2},{4,5},{5,4},{6,7},{7,6},{8,9},{9,8},{10,11... | collective-permute-start | bytes 392 | tf_op jit(solution)/shard_map/ppermute | solution.py:118
  22.0 3.6 %collective-permute-start.6 = (f32[32]{0:T(128)S(1)}, f32[32]{0:T(128)S(1)}, u32[]{:S(2)}, u32[]{:S(2)}) collective-permute-start(f32[32]{0:T(128)S(1)} %get-tuple-element.16), channel_id=1, source_target_pairs={{0,2},{1,3},{2,0},{3,1},{4,6},{5,7},{6,4},{7,5},{8,10},{9,11},{10,... | collective-permute-start | bytes 392 | tf_op jit(solution)/shard_map/ppermute | solution.py:118
  23.5 3.5 %collective-permute-start.4 = (f32[32]{0:T(128)S(1)}, f32[32]{0:T(128)S(1)}, u32[]{:S(2)}, u32[]{:S(2)}) collective-permute-start(f32[32]{0:T(128)S(1)} %get-tuple-element.17), channel_id=1, source_target_pairs={{0,2},{1,3},{2,0},{3,1},{4,6},{5,7},{6,4},{7,5},{8,10},{9,11},{10,... | collective-permute-start | bytes 392 | tf_op jit(solution)/shard_map/ppermute | solution.py:118
  27.3 4.0 %collective-permute-start.9 = (f32[2,4,8]{2,1,0:T(4,128)S(1)}, f32[2,4,8]{2,1,0:T(4,128)S(1)}, u32[]{:S(2)}, u32[]{:S(2)}) collective-permute-start(f32[2,4,8]{2,1,0:T(4,128)S(1)} %constant_dynamic-update-slice_fusion), channel_id=1, source_target_pairs={{0,12},{4,0},{8,4},{12,8},{1,13},{5,1},{9,5},{13,9},{2,14},{6,2},{... | collective-permute-start | bytes 776 | tf_op jit(solution)/shard_map/ppermute | solution.py:189
  29.3 4.5 %collective-permute-start.8 = (f32[2,4,8]{2,1,0:T(4,128)S(1)}, f32[2,4,8]{2,1,0:T(4,128)S(1)}, u32[]{:S(2)}, u32[]{:S(2)}) collective-permute-start(f32[2,4,8]{2,1,0:T(4,128)S(1)} %constant_dynamic-update-slice_fusion), channel_id=1, source_target_pairs={{0,8},{4,12},{8,0},{12,4},{1,9},{5,13},{9,1},{13,5},{2,10},{6,14},... | collective-permute-start | bytes 776 | tf_op jit(solution)/shard_map/ppermute | solution.py:189
  29.3 5.5 %collective-permute-start.7 = (f32[2,4,8]{2,1,0:T(4,128)S(1)}, f32[2,4,8]{2,1,0:T(4,128)S(1)}, u32[]{:S(2)}, u32[]{:S(2)}) collective-permute-start(f32[2,4,8]{2,1,0:T(4,128)S(1)} %constant_dynamic-update-slice_fusion), channel_id=1, source_target_pairs={{0,4},{4,8},{8,12},{12,0},{1,5},{5,9},{9,13},{13,1},{2,6},{6,10},{... | collective-permute-start | bytes 776 | tf_op jit(solution)/shard_map/ppermute | solution.py:189

commit v2 on v1

--- a/solution.py
+++ b/solution.py
@@ -37,15 +37,16 @@
 
 
 def slot_weights(group_sizes, scale_rows, slots):
-    group_ends = jnp.cumsum(group_sizes, axis=1)
-    group_starts = group_ends - group_sizes
+    groups = group_sizes.shape[1]
+    before = jnp.arange(groups)[:, None] < jnp.arange(groups)[None, :]
+    group_starts = jnp.sum(jnp.where(before[None], group_sizes[:, :, None], 0), axis=1)
+    group_ends = group_starts + group_sizes
     slot_index = jnp.arange(slots, dtype=jnp.int32)
-    membership = (
-        (slot_index[None, :, None] >= group_starts[:, None, :])
-        & (slot_index[None, :, None] < group_ends[:, None, :])
-    ).astype(jnp.float32)
-    gain_rows = jnp.sum(membership * scale_rows[:, None, :], axis=2)
-    live_mask = jnp.sum(membership, axis=2)
+    membership = (slot_index[None, :, None] >= group_starts[:, None, :]) & (
+        slot_index[None, :, None] < group_ends[:, None, :]
+    )
+    gain_rows = jnp.sum(jnp.where(membership, scale_rows[:, None, :], 0.0), axis=2)
+    live_mask = jnp.sum(membership.astype(jnp.float32), axis=2)
     return (gain_rows.reshape(-1), live_mask.reshape(-1))
 
 
@@ -103,6 +104,26 @@
     return (high, middle, rest - middle)
 
 
+def pack_rows(particles, group_counts, group_scale, defocus_bin):
+    slots = particles.shape[0]
+    slot_index = jnp.arange(slots, dtype=jnp.int32)
+    start = jnp.int32(0)
+    gain = jnp.zeros((slots,), jnp.float32)
+    live = jnp.zeros((slots,), jnp.float32)
+    for group in range(group_counts.shape[0]):
+        size = group_counts[group]
+        inside = (slot_index >= start) & (slot_index < start + size)
+        gain = jnp.where(inside, group_scale[group], gain)
+        live = jnp.where(inside, 1.0, live)
+        start = start + size
+    fields = (*split_exact(gain), live, defocus_bin.astype(jnp.float32))
+    column = jnp.arange(META, dtype=jnp.int32)[None, :]
+    meta = jnp.zeros((slots, META), jnp.float32)
+    for index, field in enumerate(fields):
+        meta = jnp.where(column == index, field[:, None], meta)
+    return jnp.concatenate([particles, meta.astype(jnp.bfloat16)], axis=1)
+
+
 def shift_gather(value, axis, size):
     pieces = [value] + [
         lax.ppermute(value, axis, [(i, (i + k) % size) for i in range(size)])
@@ -154,11 +175,7 @@
 
     small = n_blk <= 4
     if small:
-        meta = jnp.stack(
-            [*split_exact(gain_rows), live_mask, defocus_bin.astype(jnp.float32)], axis=1
-        )
-        meta = jnp.pad(meta, ((0, 0), (0, META - meta.shape[1]))).astype(jnp.bfloat16)
-        packed = jnp.concatenate([particles, meta], axis=1)
+        packed = pack_rows(particles, group_counts, group_scale, defocus_bin)
         everyone = shift_gather(packed, "blk", n_blk)
         images = everyone[:, :width]
         meta_all = everyone[:, width : width + 5].astype(jnp.float32)

time: 41.2 us -> 47.6 us (1.16)
  local copies, waits for them, and re-layouts: 2.66 us -> 5.46 us
  between operations: 0.82 us -> 3.35 us
  other arithmetic: 8.55 us -> 9.78 us
    slice x0 -> x2, local copies, waits for them, and re-layouts: none -> 2.93 us  [the longest x1 1.47 us: pack_rows(): gain = jnp.where(inside, group_scale[group], gain)]
    sub x1, other arithmetic: 0.66 us -> 3.18 us  [split_exact(): return (high, middle, rest - middle)]
    another operation x5 -> x1, other arithmetic: 3.09 us -> 1.55 us
    convert_element_type x0 -> x2, other arithmetic: none -> 0.78 us  [the longest x1 0.7 us: pack_rows(): fields = (*split_exact(gain), live, defocus_bin.astype(jnp.float32))]
    reduce_sum x1 -> x2, other arithmetic: 0.74 us -> 0.17 us  [the longest x1 0.09 us: slot_weights(): live_mask = jnp.sum(membership.astype(jnp.float32), axis=2)]
    unnamed x13 -> x14, local copies, waits for them, and re-layouts: 1.87 us -> 1.77 us
where the time goes in v2:
time: 47.6 us; the launch traced here: 47.3 us
  starting transfers between devices  12.5 us (26%)
  other arithmetic  9.78 us (21%)
  waiting for transfers between devices  9.47 us (20%)
  matrix products  6.73 us (14%)
  local copies, waits for them, and re-layouts  5.46 us (11%)
  between operations  3.35 us (7%)
    ppermute x3, starting transfers between devices, shift_gather(): lax.ppermute(value, axis, [(i, (i + k) % size) for i in range(size)])  6.06 us
    ppermute x3, starting transfers between devices, per_device(): lax.ppermute(stats, 'blk', [(i, (i + k) % n_blk) for i in range(n_blk)])  3.79 us
    ppermute x4, waiting for transfers between devices, xor_butterfly(): lax.ppermute(part, axis, [(i, i ^ step) for i in range(size)])  3.73 us
    ppermute x3, waiting for transfers between devices, per_device(): lax.ppermute(stats, 'blk', [(i, (i + k) % n_blk) for i in range(n_blk)])  3.49 us
    sub x1, other arithmetic, split_exact(): return (high, middle, rest - middle)  3.18 us
    ppermute x4, starting transfers between devices, xor_butterfly(): lax.ppermute(part, axis, [(i, i ^ step) for i in range(size)])  2.61 us
    dot_general x1, matrix products, accumulate(): lax.dot_general(scaled, shifted, (((0,), (0,)), ((), ())), preferred_elem...  2.57 us
    ppermute x3, waiting for transfers between devices, shift_gather(): lax.ppermute(value, axis, [(i, (i + k) % size) for i in range(size)])  2.26 us
  transfers between devices with their start and end apart: 10, of which 7 were waited for; matrix products, arithmetic and copies ran while one was open for 8% of the time, Pallas kernels for 0%

profile of v2, /device:TPU:0, one launch (start us, length us, event | category | flops | bytes accessed | tf_op | source)
XLA Modules:
  0.0 47.3 jit_solution(7353366346158703064)
XLA Ops:
  0.6 0.0 copy-start.5
  0.6 0.0 copy-start.1
  0.7 0.0 copy-start.2
  0.7 0.7 %convert_element_type.62 = bf16[8]{0:T(256)(128)(2,1)S(1)} convert(s32[8]{0:T(128)} %param.11) | non-fusion elementwise | flops 8 | bytes 48 | tf_op jit(solution)/shard_map/convert_element_type | solution.py:119
  1.4 1.5 %fusion.48 = (f32[1]{0:T(128)}, f32[1]{0:T(128)}, f32[1]{0:T(128)}, f32[1]{0:T(128)}) fusion(f32[4]{0:T(128)} %param.13), kind=kLoop, calls=%fused_computation.110 | loop fusion | bytes 32 | tf_op jit(solution)/shard_map/slice | solution.py:116
  2.9 1.5 %fusion.47 = (s32[1]{0:T(128)}, s32[1]{0:T(128)}, s32[1]{0:T(128)}, s32[1]{0:T(128)}) fusion(s32[4]{0:T(128)} %param.12), kind=kLoop, calls=%fused_computation.109 | loop fusion | bytes 32 | tf_op jit(solution)/shard_map/slice | solution.py:114
  6.8 3.2 %reduce-precision_subtract_fusion = (bf16[8]{0:T(256)(128)(2,1)S(1)}, f32[8]{0:T(128)S(1)}, bf16[8]{0:T(256)(128)(2,1)S(1)}) fusion(f32[]{:T(128)} %bitcast.7, f32[]{:T(128)} %bitcast.6, s32[]{:T(128)} %bitcast, f32[]{:T(128)} %bitcast.5, s32[]{:T(128)S(6)} %add.114, f32[]{:T(128)} %bitcast.4, s32[]{:T(128)S(6)} %add.116, s32[]{:T(128)S(6)} %add.115), kind=kLoop, calls=%fused_computation.102 | loop fusion | flops 184 | bytes 96 | tf_op jit(solution)/shard_map/sub | solution.py:104
  10.0 0.1 select_convert_fusion
  10.1 0.8 %pad_maximum_fusion.11 = bf16[8,4224]{1,0:T(8,128)(2,1)S(1)} fusion(bf16[8,128]{1,0:T(8,128)(2,1)S(1)} %select_convert_fusion, bf16[8,4096]{1,0:T(8,128)(2,1)} %param.7), kind=kLoop, calls=%fused_computation.33 | loop fusion | flops 135168 | bytes 135168 | tf_op jit(solution)/shard_map/concatenate | solution.py:124
  11.0 5.0 %collective-permute-start.2 = (bf16[8,4224]{1,0:T(8,128)(2,1)S(1)}, bf16[8,4224]{1,0:T(8,128)(2,1)S(1)}, u32[]{:S(2)}, u32[]{:S(2)}) collective-permute-start(bf16[8,4224]{1,0:T(8,128)(2,1)S(1)} %pad_maximum_fusion.11), channel_id=1, source_target_pairs={{0,12},{4,0},{8,4},{12,8},{1,13},{5,1},{9,5},{13,9},{2,14},{6,2},{... | collective-permute-start | bytes 202760 | tf_op jit(solution)/shard_map/ppermute | solution.py:129
  16.0 0.0 collective-permute-start.1
  16.0 1.0 %collective-permute-start = (bf16[8,4224]{1,0:T(8,128)(2,1)S(1)}, bf16[8,4224]{1,0:T(8,128)(2,1)S(1)}, u32[]{:S(2)}, u32[]{:S(2)}) collective-permute-start(bf16[8,4224]{1,0:T(8,128)(2,1)S(1)} %pad_maximum_fusion.11), channel_id=1, source_target_pairs={{0,4},{4,8},{8,12},{12,0},{1,5},{5,9},{9,13},{13,1},{2,6},{6,10},{... | collective-permute-start | bytes 202760 | tf_op jit(solution)/shard_map/ppermute | solution.py:129
  17.0 0.1 broadcast_in_dim.152
  17.1 0.1 mul.268
  17.2 0.1 mul.264
  17.3 1.1 %bitcast_convert_fusion = f32[50,4096]{1,0:T(8,128)S(1)} fusion(bf16[1,50,4096]{2,1,0:T(8,128)(2,1)} %param.8), kind=kLoop, calls=%fused_computation.16 | loop fusion | flops 204800 | bytes 1228800 | tf_op jit(solution)/shard_map/convert_element_type | solution.py:66
  18.4 1.4 %fusion.6 = f32[16,50]{1,0:T(8,128)S(1)} fusion(f32[50,4096]{1,0:T(8,128)S(1)} %bitcast_convert_fusion, f32[16,2048]{1,0:T(8,128)} %param.9), kind=kOutput, calls=%fused_computation.13 | convolution fusion | flops 20000768 | bytes 953472 | tf_op jit(solution)/shard_map/dot_general | solution.py:71
  19.7 0.6 %fusion.11 = (f32[16,2048]{1,0:T(8,128)S(1)}, f32[16,2048]{1,0:T(8,128)S(1)}) fusion(f32[2048]{0:T(1024)S(1)} %get-tuple-element.44, f32[16]{0:T(128)S(1)} %mul.268, f32[2048]{0:T(1024)S(1)} %get-tuple-element.43, f32[16]{0:T(128)S(1)} %mul.264), kind=kLoop, calls=%fused_computation.28 | loop fusion | flops 131072 | bytes 278656 | tf_op jit(solution)/shard_map/cos | solution.py:32
  20.3 0.0 copy-done.5
  20.3 0.1 select_reduce_fusion
  20.4 0.0 collective-permute-done.2
  20.4 2.2 %collective-permute-done.1 = bf16[8,4224]{1,0:T(8,128)(2,1)S(1)} collective-permute-done((bf16[8,4224]{1,0:T(8,128)(2,1)S(1)}, bf16[8,4224]{1,0:T(8,128)(2,1)S(1)}, u32[]{:S(2)}, u32[]{:S(2)}) %collective-permute-start.1) | collective-permute-done | bytes 67616 | tf_op jit(solution)/shard_map/ppermute | solution.py:129
  22.6 0.0 collective-permute-done
  22.7 0.0 copy-done.1
  22.7 0.2 multiply_reduce_fusion
  22.9 0.0 copy-done.2
  22.9 0.3 fusion.18
  23.2 0.2 convolution_multiply_fusion
  23.5 0.0 copy-start.3
  23.5 1.5 %multiply_convert_fusion.1 = (bf16[32,16,2048]{2,1,0:T(8,128)(2,1)S(1)}, bf16[32,16,2048]{2,1,0:T(8,128)(2,1)S(1)}) fusion(f32[32,2048]{1,0:T(8,128)S(1)} %fusion.18, f32[16,2048]{1,0:T(8,128)S(1)} %get-tuple-element.23, f32[32,2048]{1,0:T(8,128)S(1)} %get-tuple-element.21, f32[16,2048]{1,0:T(8,128)S(1)} %get-tuple-element.22, ...), kind=kLoop, calls=%fused_computation.5 | loop fusion | flops 10485760 | bytes 5242880 | tf_op jit(solution)/shard_map/convert
  25.0 0.0 copy-start
  25.0 0.0 copy-done.3
  25.1 0.0 copy-start.4
  25.1 1.4 %fusion.49 = (f32[32]{0:T(128)S(1)}, f32[32,16,50]{2,1,0:T(8,128)S(1)}) fusion(f32[32,50]{1,0:T(8,128)S(1)} %convolution_multiply_fusion, bf16[1,50,4096]{2,1,0:T(8,128)(2,1)S(1)} %copy-done.3, bf16[32,16,2048]{2,1,0:T(8,128)(2,1)S(1)} %get-tuple-element.19, bf16[32,16,2048]{2,1,0:T(8,128)(2,1)S(1)} %get-tuple-element.18, f32[32]{0:T(128)S(1)} %get-tuple-element.9), kind=kOutput, calls=%fused_computation.111 | convolution fusion | flops 218180576 | bytes 4712960 | tf_op jit(solution)/shard_map/dot_general | solution.py:76
  26.5 0.0 copy-done
  26.5 0.5 %exponential_reduce_fusion = f32[32]{0:T(128)S(1)} fusion(f32[32,16,50]{2,1,0:T(8,128)S(1)} %get-tuple-element.37, f32[32]{0:T(128)S(1)} %get-tuple-element.36), kind=kLoop, calls=%fused_computation.19 | loop fusion | flops 51168 | bytes 102656 | tf_op jit(solution)/shard_map/reduce_sum | solution.py:200
  27.0 0.1 collective-permute-start.5
  27.1 0.5 %collective-permute-start.3 = (f32[32]{0:T(128)S(1)}, f32[32]{0:T(128)S(1)}, u32[]{:S(2)}, u32[]{:S(2)}) collective-permute-start(f32[32]{0:T(128)S(1)} %get-tuple-element.36), channel_id=1, source_target_pairs={{0,1},{1,0},{2,3},{3,2},{4,5},{5,4},{6,7},{7,6},{8,9},{9,8},{10,11... | collective-permute-start | bytes 392 | tf_op jit(solution)/shard_map/ppermute | solution.py:139
  27.6 0.6 %collective-permute-done.5 = f32[32]{0:T(128)S(1)} collective-permute-done((f32[32]{0:T(128)S(1)}, f32[32]{0:T(128)S(1)}, u32[]{:S(2)}, u32[]{:S(2)}) %collective-permute-start.5) | collective-permute-done | bytes 160 | tf_op jit(solution)/shard_map/ppermute | solution.py:139
  28.2 0.2 collective-permute-done.3
  28.4 1.5 %collective-permute-start.6 = (f32[32]{0:T(128)S(1)}, f32[32]{0:T(128)S(1)}, u32[]{:S(2)}, u32[]{:S(2)}) collective-permute-start(f32[32]{0:T(128)S(1)} %get-tuple-element.14), channel_id=1, source_target_pairs={{0,2},{1,3},{2,0},{3,1},{4,6},{5,7},{6,4},{7,5},{8,10},{9,11},{10,... | collective-permute-start | bytes 392 | tf_op jit(solution)/shard_map/ppermute | solution.py:139
  29.9 0.5 %collective-permute-start.4 = (f32[32]{0:T(128)S(1)}, f32[32]{0:T(128)S(1)}, u32[]{:S(2)}, u32[]{:S(2)}) collective-permute-start(f32[32]{0:T(128)S(1)} %get-tuple-element.15), channel_id=1, source_target_pairs={{0,2},{1,3},{2,0},{3,1},{4,6},{5,7},{6,4},{7,5},{8,10},{9,11},{10,... | collective-permute-start | bytes 392 | tf_op jit(solution)/shard_map/ppermute | solution.py:139
  30.5 0.1 convert_reduce_fusion
  30.5 1.4 %collective-permute-done.6 = f32[32]{0:T(128)S(1)} collective-permute-done((f32[32]{0:T(128)S(1)}, f32[32]{0:T(128)S(1)}, u32[]{:S(2)}, u32[]{:S(2)}) %collective-permute-start.6) | collective-permute-done | bytes 160 | tf_op jit(solution)/shard_map/ppermute | solution.py:139
  32.0 1.5 %collective-permute-done.4 = f32[32]{0:T(128)S(1)} collective-permute-done((f32[32]{0:T(128)S(1)}, f32[32]{0:T(128)S(1)}, u32[]{:S(2)}, u32[]{:S(2)}) %collective-permute-start.4) | collective-permute-done | bytes 160 | tf_op jit(solution)/shard_map/ppermute | solution.py:139
  33.5 0.1 stack.31
  33.6 0.1 stack.30
  33.7 1.9 %collective-permute-start.9 = (f32[2,4,8]{2,1,0:T(4,128)S(1)}, f32[2,4,8]{2,1,0:T(4,128)S(1)}, u32[]{:S(2)}, u32[]{:S(2)}) collective-permute-start(f32[2,4,8]{2,1,0:T(4,128)S(1)} %constant_dynamic-update-slice_fusion), channel_id=1, source_target_pairs={{0,12},{4,0},{8,4},{12,8},{1,13},{5,1},{9,5},{13,9},{2,14},{6,2},{... | collective-permute-start | bytes 776 | tf_op jit(solution)/shard_map/ppermute | solution.py:206
  35.5 0.0 copy-done.4
  35.5 0.1 stack.28
  35.6 0.1 stack.27
  35.7 0.0 collective-permute-start.8
  35.7 1.9 %collective-permute-start.7 = (f32[2,4,8]{2,1,0:T(4,128)S(1)}, f32[2,4,8]{2,1,0:T(4,128)S(1)}, u32[]{:S(2)}, u32[]{:S(2)}) collective-permute-start(f32[2,4,8]{2,1,0:T(4,128)S(1)} %constant_dynamic-update-slice_fusion), channel_id=1, source_target_pairs={{0,4},{4,8},{8,12},{12,0},{1,5},{5,9},{9,13},{13,1},{2,6},{6,10},{... | collective-permute-start | bytes 776 | tf_op jit(solution)/shard_map/ppermute | solution.py:206
  37.6 0.0 collective-permute-done.9
  37.6 2.5 %collective-permute-done.8 = f32[2,4,8]{2,1,0:T(4,128)S(1)} collective-permute-done((f32[2,4,8]{2,1,0:T(4,128)S(1)}, f32[2,4,8]{2,1,0:T(4,128)S(1)}, u32[]{:S(2)}, u32[]{:S(2)}) %collective-permute-start.8) | collective-permute-done | bytes 288 | tf_op jit(solution)/shard_map/ppermute | solution.py:206
  40.2 0.9 %collective-permute-done.7 = f32[2,4,8]{2,1,0:T(4,128)S(1)} collective-permute-done((f32[2,4,8]{2,1,0:T(4,128)S(1)}, f32[2,4,8]{2,1,0:T(4,128)S(1)}, u32[]{:S(2)}, u32[]{:S(2)}) %collective-permute-start.7) | collective-permute-done | bytes 288 | tf_op jit(solution)/shard_map/ppermute | solution.py:206
  41.2 0.1 sub.112
  41.3 0.1 div.29
  41.4 0.5 %compare_select_fusion = f32[8]{0:T(128)} fusion(f32[8]{0:T(128)S(1)} %convert_reduce_fusion, f32[4,8]{1,0:T(4,128)S(1)} %fusion.24, f32[4,8]{1,0:T(4,128)S(1)} %slice_reduce_fusion.2), kind=kLoop, calls=%fused_computation.81 | loop fusion | flops 24 | bytes 128 | tf_op jit(solution)/shard_map/jit(_where)/select_n | solution.py:228
  41.9 0.2 fusion.44
  42.1 0.3 fusion.16
  42.4 0.6 %fusion.13 = f32[50,2048]{1,0:T(8,128)S(1)} fusion(f32[50,16]{0,1:T(8,128)S(1)} %fusion.16, f32[16,2048]{1,0:T(8,128)S(1)} %copy-done.2), kind=kOutput, calls=%fused_computation.30 | convolution fusion | flops 19693568 | bytes 543872 | tf_op jit(solution)/shard_map/dot_general | solution.py:229
  42.9 2.6 %fusion.1 = f32[1,50,4096]{2,1,0:T(8,128)S(1)} fusion(bf16[32,16,2048]{2,1,0:T(8,128)(2,1)} %copy-done, bf16[32,16,2048]{2,1,0:T(8,128)(2,1)S(1)} %get-tuple-element.18, f32[50,2048]{1,0:T(8,128)S(1)} %fusion.13, f32[4096]{0:T(1024)S(1)} %pad_maximum_fusion.13, f32[32]{0:T(128)S(1)} %get-tuple-element.9, f32[32,16,50]{2,1,0:T(8,128)S(1)} %get-tuple-element.37, ...), kind=kOutput, calls=%fused_computation.2 | convolution fusion | flops 218846208 | bytes 5542400 | tf_op jit(solution)/shard_map/dot_general | solution.py:153
  45.5 1.7 %copy.15 = f32[1,50,4096]{2,0,1:T(1,128)} copy(f32[1,50,4096]{2,1,0:T(8,128)S(1)} %fusion.1) | data formatting | bytes 1638400
  (26 shorter events, 0.2 us)
Async XLA Ops:
  0.6 19.7 %copy-start.5 = (s32[4]{0:T(128)S(1)}, s32[4]{0:T(128)}, u32[]{:S(2)}) copy-start(s32[4]{0:T(128)} %param.12) | copy-start | bytes 52
  0.6 22.0 %copy-start.1 = (bf16[8,4096]{1,0:T(8,128)(2,1)S(1)}, bf16[8,4096]{1,0:T(8,128)(2,1)}, u32[]{:S(2)}) copy-start(bf16[8,4096]{1,0:T(8,128)(2,1)} %param.7) | copy-start | bytes 196612
  0.7 22.2 %copy-start.2 = (f32[16,2048]{1,0:T(8,128)S(1)}, f32[16,2048]{1,0:T(8,128)}, u32[]{:S(2)}) copy-start(f32[16,2048]{1,0:T(8,128)} %param.9) | copy-start | bytes 393220
  11.0 9.4 %collective-permute-start.2 = (bf16[8,4224]{1,0:T(8,128)(2,1)S(1)}, bf16[8,4224]{1,0:T(8,128)(2,1)S(1)}, u32[]{:S(2)}, u32[]{:S(2)}) collective-permute-start(bf16[8,4224]{1,0:T(8,128)(2,1)S(1)} %pad_maximum_fusion.11), channel_id=1, source_target_pairs={{0,12},{4,0},{8,4},{12,8},{1,13},{5,1},{9,5},{13,9},{2,14},{6,2},{... | collective-permute-start | bytes 202760 | tf_op jit(solution)/shard_map/ppermute | solution.py:129
  16.0 6.6 %collective-permute-start.1 = (bf16[8,4224]{1,0:T(8,128)(2,1)S(1)}, bf16[8,4224]{1,0:T(8,128)(2,1)S(1)}, u32[]{:S(2)}, u32[]{:S(2)}) collective-permute-start(bf16[8,4224]{1,0:T(8,128)(2,1)S(1)} %pad_maximum_fusion.11), channel_id=1, source_target_pairs={{0,8},{4,12},{8,0},{12,4},{1,9},{5,13},{9,1},{13,5},{2,10},{6,14},... | collective-permute-start | bytes 202760 | tf_op jit(solution)/shard_map/ppermute | solution.py:129
  16.0 6.6 %collective-permute-start = (bf16[8,4224]{1,0:T(8,128)(2,1)S(1)}, bf16[8,4224]{1,0:T(8,128)(2,1)S(1)}, u32[]{:S(2)}, u32[]{:S(2)}) collective-permute-start(bf16[8,4224]{1,0:T(8,128)(2,1)S(1)} %pad_maximum_fusion.11), channel_id=1, source_target_pairs={{0,4},{4,8},{8,12},{12,0},{1,5},{5,9},{9,13},{13,1},{2,6},{6,10},{... | collective-permute-start | bytes 202760 | tf_op jit(solution)/shard_map/ppermute | solution.py:129
  23.5 1.6 %copy-start.3 = (bf16[1,50,4096]{2,1,0:T(8,128)(2,1)S(1)}, bf16[1,50,4096]{2,1,0:T(8,128)(2,1)}, u32[]{:S(2)}) copy-start(bf16[1,50,4096]{2,1,0:T(8,128)(2,1)} %param.8) | copy-start | bytes 1228804
  25.0 1.5 %copy-start = (bf16[32,16,2048]{2,1,0:T(8,128)(2,1)}, bf16[32,16,2048]{2,1,0:T(8,128)(2,1)S(1)}, u32[]{:S(2)}) copy-start(bf16[32,16,2048]{2,1,0:T(8,128)(2,1)S(1)} %get-tuple-element.19) | copy-start | bytes 6291460
  25.1 10.5 %copy-start.4 = (f32[2048]{0:T(1024)S(1)}, f32[2048]{0:T(1024)}, u32[]{:S(2)}) copy-start(f32[2048]{0:T(1024)} %param.10) | copy-start | bytes 24580
  27.0 1.2 %collective-permute-start.5 = (f32[32]{0:T(128)S(1)}, f32[32]{0:T(128)S(1)}, u32[]{:S(2)}, u32[]{:S(2)}) collective-permute-start(f32[32]{0:T(128)S(1)} %exponential_reduce_fusion), channel_id=1, source_target_pairs={{0,1},{1,0},{2,3},{3,2},{4,5},{5,4},{6,7},{7,6},{8,9},{9,8},{10,11... | collective-permute-start | bytes 392 | tf_op jit(solution)/shard_map/ppermute | solution.py:139
  27.1 1.3 %collective-permute-start.3 = (f32[32]{0:T(128)S(1)}, f32[32]{0:T(128)S(1)}, u32[]{:S(2)}, u32[]{:S(2)}) collective-permute-start(f32[32]{0:T(128)S(1)} %get-tuple-element.36), channel_id=1, source_target_pairs={{0,1},{1,0},{2,3},{3,2},{4,5},{5,4},{6,7},{7,6},{8,9},{9,8},{10,11... | collective-permute-start | bytes 392 | tf_op jit(solution)/shard_map/ppermute | solution.py:139
  28.4 3.6 %collective-permute-start.6 = (f32[32]{0:T(128)S(1)}, f32[32]{0:T(128)S(1)}, u32[]{:S(2)}, u32[]{:S(2)}) collective-permute-start(f32[32]{0:T(128)S(1)} %get-tuple-element.14), channel_id=1, source_target_pairs={{0,2},{1,3},{2,0},{3,1},{4,6},{5,7},{6,4},{7,5},{8,10},{9,11},{10,... | collective-permute-start | bytes 392 | tf_op jit(solution)/shard_map/ppermute | solution.py:139
  29.9 3.5 %collective-permute-start.4 = (f32[32]{0:T(128)S(1)}, f32[32]{0:T(128)S(1)}, u32[]{:S(2)}, u32[]{:S(2)}) collective-permute-start(f32[32]{0:T(128)S(1)} %get-tuple-element.15), channel_id=1, source_target_pairs={{0,2},{1,3},{2,0},{3,1},{4,6},{5,7},{6,4},{7,5},{8,10},{9,11},{10,... | collective-permute-start | bytes 392 | tf_op jit(solution)/shard_map/ppermute | solution.py:139
  33.7 4.0 %collective-permute-start.9 = (f32[2,4,8]{2,1,0:T(4,128)S(1)}, f32[2,4,8]{2,1,0:T(4,128)S(1)}, u32[]{:S(2)}, u32[]{:S(2)}) collective-permute-start(f32[2,4,8]{2,1,0:T(4,128)S(1)} %constant_dynamic-update-slice_fusion), channel_id=1, source_target_pairs={{0,12},{4,0},{8,4},{12,8},{1,13},{5,1},{9,5},{13,9},{2,14},{6,2},{... | collective-permute-start | bytes 776 | tf_op jit(solution)/shard_map/ppermute | solution.py:206
  35.7 4.5 %collective-permute-start.8 = (f32[2,4,8]{2,1,0:T(4,128)S(1)}, f32[2,4,8]{2,1,0:T(4,128)S(1)}, u32[]{:S(2)}, u32[]{:S(2)}) collective-permute-start(f32[2,4,8]{2,1,0:T(4,128)S(1)} %constant_dynamic-update-slice_fusion), channel_id=1, source_target_pairs={{0,8},{4,12},{8,0},{12,4},{1,9},{5,13},{9,1},{13,5},{2,10},{6,14},... | collective-permute-start | bytes 776 | tf_op jit(solution)/shard_map/ppermute | solution.py:206
  35.7 5.5 %collective-permute-start.7 = (f32[2,4,8]{2,1,0:T(4,128)S(1)}, f32[2,4,8]{2,1,0:T(4,128)S(1)}, u32[]{:S(2)}, u32[]{:S(2)}) collective-permute-start(f32[2,4,8]{2,1,0:T(4,128)S(1)} %constant_dynamic-update-slice_fusion), channel_id=1, source_target_pairs={{0,4},{4,8},{8,12},{12,0},{1,5},{5,9},{9,13},{13,1},{2,6},{6,10},{... | collective-permute-start | bytes 776 | tf_op jit(solution)/shard_map/ppermute | solution.py:206

commit v3 on v1

--- a/solution.py
+++ b/solution.py
@@ -3,6 +3,8 @@
 import jax
 import jax.numpy as jnp
 from jax import lax
+from jax.experimental import pallas as pl
+from jax.experimental.pallas import tpu as pltpu
 from jax.sharding import PartitionSpec as P
 
 KX = 32
@@ -103,6 +105,45 @@
     return (high, middle, rest - middle)
 
 
+def pack_kernel(sizes_ref, scales_ref, bins_ref, images_ref, out_ref):
+    slots, width = images_ref.shape
+    row = lax.broadcasted_iota(jnp.int32, (slots, META), 0)
+    column = lax.broadcasted_iota(jnp.int32, (slots, META), 1)
+    start = jnp.int32(0)
+    gain = jnp.zeros((slots, META), jnp.float32)
+    live = jnp.zeros((slots, META), jnp.float32)
+    for group in range(sizes_ref.shape[0]):
+        size = sizes_ref[group]
+        inside = (row >= start) & (row < start + size)
+        gain = jnp.where(inside, scales_ref[group], gain)
+        live = jnp.where(inside, 1.0, live)
+        start = start + size
+    bins = jnp.zeros((slots, META), jnp.float32)
+    for slot in range(slots):
+        bins = jnp.where(row == slot, bins_ref[slot].astype(jnp.float32), bins)
+    high = gain.astype(jnp.bfloat16).astype(jnp.float32)
+    rest = gain - high
+    middle = rest.astype(jnp.bfloat16).astype(jnp.float32)
+    fields = (high, middle, rest - middle, live, bins)
+    meta = jnp.zeros((slots, META), jnp.float32)
+    for index, field in enumerate(fields):
+        meta = jnp.where(column == index, field, meta)
+    out_ref[:, :width] = images_ref[...]
+    out_ref[:, width:] = meta.astype(out_ref.dtype)
+
+
+def pack_rows(particles, group_counts, group_scale, defocus_bin):
+    slots, width = particles.shape
+    scalar = pl.BlockSpec(memory_space=pltpu.SMEM)
+    whole = pl.BlockSpec(memory_space=pltpu.VMEM)
+    return pl.pallas_call(
+        pack_kernel,
+        out_shape=jax.ShapeDtypeStruct((slots, width + META), particles.dtype),
+        in_specs=[scalar, scalar, scalar, whole],
+        out_specs=whole,
+    )(group_counts, group_scale, defocus_bin, particles)
+
+
 def shift_gather(value, axis, size):
     pieces = [value] + [
         lax.ppermute(value, axis, [(i, (i + k) % size) for i in range(size)])
@@ -144,9 +185,6 @@
     cosine_table, sine_table = phase_tables()
     ctf_square = ctf_table * ctf_table
     batch_size, width = particles.shape
-    gain_rows, live_mask = slot_weights(
-        group_counts.reshape(1, -1), group_scale.reshape(1, -1), batch_size
-    )
     ref_tile = references[0]
     own_norms = tile_norms(ref_tile, ctf_square)
     classes_here = ref_tile.shape[0]
@@ -154,18 +192,18 @@
 
     small = n_blk <= 4
     if small:
-        meta = jnp.stack(
-            [*split_exact(gain_rows), live_mask, defocus_bin.astype(jnp.float32)], axis=1
-        )
-        meta = jnp.pad(meta, ((0, 0), (0, META - meta.shape[1]))).astype(jnp.bfloat16)
-        packed = jnp.concatenate([particles, meta], axis=1)
+        packed = pack_rows(particles, group_counts, group_scale, defocus_bin)
         everyone = shift_gather(packed, "blk", n_blk)
         images = everyone[:, :width]
         meta_all = everyone[:, width : width + 5].astype(jnp.float32)
         gain_all = (meta_all[:, 0] + meta_all[:, 1]) + meta_all[:, 2]
         live_all = meta_all[:, 3]
         bins_all = meta_all[:, 4]
+        live_mask = live_all[:batch_size]
     else:
+        gain_rows, live_mask = slot_weights(
+            group_counts.reshape(1, -1), group_scale.reshape(1, -1), batch_size
+        )
         images = lax.all_gather(particles, "blk", axis=0, tiled=True)
         gain_all, bins_all, live_all = (
             lax.all_gather(gain_rows, "blk", axis=0, tiled=True),

time: 41.2 us -> 39 us (0.947)
  other arithmetic: 8.55 us -> 4.94 us
  Pallas kernels: 0 us -> 1.53 us
    another operation x5 -> x1, other arithmetic: 3.09 us -> 1.53 us
    pallas_call x0 -> x1, Pallas kernels: none -> 1.53 us  [pack_rows(): pl.pallas_call(pack_kernel, out_shape=jax.ShapeDtypeStruct((slots, width...]
    concatenate x1 -> x0, other arithmetic: 0.84 us -> none  [per_device(): packed = jnp.concatenate([particles, meta], axis=1)]
    reduce_sum x1 -> x0, other arithmetic: 0.74 us -> none  [slot_weights(): live_mask = jnp.sum(membership, axis=2)]
    sub x1 -> x0, other arithmetic: 0.66 us -> none  [slot_weights(): group_starts = group_ends - group_sizes]
    unnamed x13 -> x12, local copies, waits for them, and re-layouts: 1.87 us -> 1.77 us
  transfers between devices with their start and end apart: 10 -> 10, of which waited for: 7 -> 7; matrix products, arithmetic and copies ran while one was open for 8% -> 9% of each run, Pallas kernels for 0% -> 0%
where the time goes in v3:
time: 39 us; the launch traced here: 38.8 us
  starting transfers between devices  12.5 us (32%)
  waiting for transfers between devices  9.87 us (25%)
  matrix products  6.68 us (17%)
  other arithmetic  4.94 us (13%)
  local copies, waits for them, and re-layouts  2.52 us (6%)
  Pallas kernels  1.53 us (4%)
  between operations  0.81 us (2%)
    ppermute x3, starting transfers between devices, shift_gather(): lax.ppermute(value, axis, [(i, (i + k) % size) for i in range(size)])  6.06 us
    ppermute x4, waiting for transfers between devices, xor_butterfly(): lax.ppermute(part, axis, [(i, i ^ step) for i in range(size)])  3.82 us
    ppermute x3, starting transfers between devices, per_device(): lax.ppermute(stats, 'blk', [(i, (i + k) % n_blk) for i in range(n_blk)])  3.79 us
    ppermute x3, waiting for transfers between devices, per_device(): lax.ppermute(stats, 'blk', [(i, (i + k) % n_blk) for i in range(n_blk)])  3.48 us
    ppermute x4, starting transfers between devices, xor_butterfly(): lax.ppermute(part, axis, [(i, i ^ step) for i in range(size)])  2.61 us
    dot_general x1, matrix products, accumulate(): lax.dot_general(scaled, shifted, (((0,), (0,)), ((), ())), preferred_elem...  2.57 us
    ppermute x3, waiting for transfers between devices, shift_gather(): lax.ppermute(value, axis, [(i, (i + k) % size) for i in range(size)])  2.57 us
    unnamed x12, local copies, waits for them, and re-layouts  1.77 us
  transfers between devices with their start and end apart: 10, of which 7 were waited for; matrix products, arithmetic and copies ran while one was open for 9% of the time, Pallas kernels for 0%

profile of v3, /device:TPU:0, one launch (start us, length us, event | category | flops | bytes accessed | tf_op | source)
XLA Modules:
  0.0 38.8 jit_solution(10265602750721330629)
XLA Ops:
  0.6 0.0 copy-start.2
  0.6 1.5 %shard_map.86 = bf16[8,4224]{1,0:T(8,128)(2,1)} custom-call(s32[4]{0:T(128)} %sizes_ref.1, f32[4]{0:T(128)} %scales_ref.1, s32[8]{0:T(128)} %bins_ref.1, bf16[8,4096]{1,0:T(8,128)(2,1)} %images_ref.1), custom_call_target="tpu_custom_call" | custom-call | tf_op jit(solution)/shard_map/pallas_call | solution.py:139
  2.2 0.0 copy-start.1
  2.2 5.0 %collective-permute-start.2 = (bf16[8,4224]{1,0:T(8,128)(2,1)}, bf16[8,4224]{1,0:T(8,128)(2,1)S(1)}, u32[]{:S(2)}, u32[]{:S(2)}) collective-permute-start(bf16[8,4224]{1,0:T(8,128)(2,1)} %shard_map.86), channel_id=1, source_target_pairs={{0,12},{4,0},{8,4},{12,8},{1,13},{5,1},{9,5},{13,9},{2,14},{6,2},{... | collective-permute-start | bytes 202760 | tf_op jit(solution)/shard_map/ppermute | solution.py:149
  7.2 0.0 collective-permute-start.1
  7.2 1.0 %collective-permute-start = (bf16[8,4224]{1,0:T(8,128)(2,1)}, bf16[8,4224]{1,0:T(8,128)(2,1)S(1)}, u32[]{:S(2)}, u32[]{:S(2)}) collective-permute-start(bf16[8,4224]{1,0:T(8,128)(2,1)} %shard_map.86), channel_id=1, source_target_pairs={{0,4},{4,8},{8,12},{12,0},{1,5},{5,9},{9,13},{13,1},{2,6},{6,10},{... | collective-permute-start | bytes 202760 | tf_op jit(solution)/shard_map/ppermute | solution.py:149
  8.3 0.1 broadcast_in_dim.13
  8.3 0.1 mul.268
  8.4 0.1 mul.264
  8.5 1.1 %bitcast_convert_fusion = f32[50,4096]{1,0:T(8,128)S(1)} fusion(bf16[1,50,4096]{2,1,0:T(8,128)(2,1)} %param.8), kind=kLoop, calls=%fused_computation.16 | loop fusion | flops 204800 | bytes 1228800 | tf_op jit(solution)/shard_map/convert_element_type | solution.py:67
  9.6 0.5 %fusion.11 = (f32[16,2048]{1,0:T(8,128)S(1)}, f32[16,2048]{1,0:T(8,128)S(1)}) fusion(f32[2048]{0:T(1024)S(1)} %get-tuple-element.25, f32[16]{0:T(128)S(1)} %mul.268, f32[2048]{0:T(1024)S(1)} %get-tuple-element.24, f32[16]{0:T(128)S(1)} %mul.264), kind=kLoop, calls=%fused_computation.27 | loop fusion | flops 131072 | bytes 278656 | tf_op jit(solution)/shard_map/cos | solution.py:34
  10.1 1.4 %fusion.6 = f32[16,50]{1,0:T(8,128)S(1)} fusion(f32[50,4096]{1,0:T(8,128)S(1)} %bitcast_convert_fusion, f32[16,2048]{1,0:T(8,128)} %param.9), kind=kOutput, calls=%fused_computation.13 | convolution fusion | flops 20000768 | bytes 953472 | tf_op jit(solution)/shard_map/dot_general | solution.py:72
  11.5 0.0 collective-permute-done.2
  11.5 2.6 %collective-permute-done.1 = bf16[8,4224]{1,0:T(8,128)(2,1)S(1)} collective-permute-done((bf16[8,4224]{1,0:T(8,128)(2,1)}, bf16[8,4224]{1,0:T(8,128)(2,1)S(1)}, u32[]{:S(2)}, u32[]{:S(2)}) %collective-permute-start.1) | collective-permute-done | bytes 67616 | tf_op jit(solution)/shard_map/ppermute | solution.py:149
  14.1 0.0 collective-permute-done
  14.1 0.0 copy-done.1
  14.1 0.2 multiply_reduce_fusion
  14.3 0.0 copy-done.2
  14.3 0.3 fusion.18
  14.7 0.2 convolution_multiply_fusion
  14.9 0.0 copy-start.3
  14.9 1.5 %multiply_convert_fusion.1 = (bf16[32,16,2048]{2,1,0:T(8,128)(2,1)S(1)}, bf16[32,16,2048]{2,1,0:T(8,128)(2,1)S(1)}) fusion(f32[32,2048]{1,0:T(8,128)S(1)} %fusion.18, f32[16,2048]{1,0:T(8,128)S(1)} %get-tuple-element.19, f32[32,2048]{1,0:T(8,128)S(1)} %get-tuple-element.17, f32[16,2048]{1,0:T(8,128)S(1)} %get-tuple-element.18, ...), kind=kLoop, calls=%fused_computation.5 | loop fusion | flops 10485760 | bytes 5242880 | tf_op jit(solution)/shard_map/convert
  16.5 0.0 copy-start
  16.5 0.0 copy-done.3
  16.5 0.0 copy-start.4
  16.5 1.4 %fusion.40 = (f32[32]{0:T(128)S(1)}, f32[32,16,50]{2,1,0:T(8,128)S(1)}) fusion(f32[32,50]{1,0:T(8,128)S(1)} %convolution_multiply_fusion, bf16[1,50,4096]{2,1,0:T(8,128)(2,1)S(1)} %copy-done.3, bf16[32,16,2048]{2,1,0:T(8,128)(2,1)S(1)} %get-tuple-element.15, bf16[32,16,2048]{2,1,0:T(8,128)(2,1)S(1)} %get-tuple-element.14, f32[32]{0:T(128)S(1)} %get-tuple-element.8), kind=kOutput, calls=%fused_computation.84 | convolution fusion | flops 218180576 | bytes 4712960 | tf_op jit(solution)/shard_map/dot_general | solution.py:77
  17.9 0.0 copy-done
  17.9 0.5 %exponential_reduce_fusion = f32[32]{0:T(128)S(1)} fusion(f32[32,16,50]{2,1,0:T(8,128)S(1)} %get-tuple-element.23, f32[32]{0:T(128)S(1)} %get-tuple-element.22), kind=kLoop, calls=%fused_computation.19 | loop fusion | flops 51168 | bytes 102656 | tf_op jit(solution)/shard_map/reduce_sum | solution.py:221
  18.4 0.1 collective-permute-start.5
  18.5 0.5 %collective-permute-start.3 = (f32[32]{0:T(128)S(1)}, f32[32]{0:T(128)S(1)}, u32[]{:S(2)}, u32[]{:S(2)}) collective-permute-start(f32[32]{0:T(128)S(1)} %get-tuple-element.22), channel_id=1, source_target_pairs={{0,1},{1,0},{2,3},{3,2},{4,5},{5,4},{6,7},{7,6},{8,9},{9,8},{10,11... | collective-permute-start | bytes 392 | tf_op jit(solution)/shard_map/ppermute | solution.py:159
  19.0 0.6 %collective-permute-done.5 = f32[32]{0:T(128)S(1)} collective-permute-done((f32[32]{0:T(128)S(1)}, f32[32]{0:T(128)S(1)}, u32[]{:S(2)}, u32[]{:S(2)}) %collective-permute-start.5) | collective-permute-done | bytes 160 | tf_op jit(solution)/shard_map/ppermute | solution.py:159
  19.6 0.2 collective-permute-done.3
  19.8 1.5 %collective-permute-start.6 = (f32[32]{0:T(128)S(1)}, f32[32]{0:T(128)S(1)}, u32[]{:S(2)}, u32[]{:S(2)}) collective-permute-start(f32[32]{0:T(128)S(1)} %get-tuple-element.12), channel_id=1, source_target_pairs={{0,2},{1,3},{2,0},{3,1},{4,6},{5,7},{6,4},{7,5},{8,10},{9,11},{10,... | collective-permute-start | bytes 392 | tf_op jit(solution)/shard_map/ppermute | solution.py:159
  21.3 0.5 %collective-permute-start.4 = (f32[32]{0:T(128)S(1)}, f32[32]{0:T(128)S(1)}, u32[]{:S(2)}, u32[]{:S(2)}) collective-permute-start(f32[32]{0:T(128)S(1)} %get-tuple-element.13), channel_id=1, source_target_pairs={{0,2},{1,3},{2,0},{3,1},{4,6},{5,7},{6,4},{7,5},{8,10},{9,11},{10,... | collective-permute-start | bytes 392 | tf_op jit(solution)/shard_map/ppermute | solution.py:159
  21.9 0.0 copy-done.4
  21.9 1.5 %collective-permute-done.6 = f32[32]{0:T(128)S(1)} collective-permute-done((f32[32]{0:T(128)S(1)}, f32[32]{0:T(128)S(1)}, u32[]{:S(2)}, u32[]{:S(2)}) %collective-permute-start.6) | collective-permute-done | bytes 160 | tf_op jit(solution)/shard_map/ppermute | solution.py:159
  23.4 1.5 %collective-permute-done.4 = f32[32]{0:T(128)S(1)} collective-permute-done((f32[32]{0:T(128)S(1)}, f32[32]{0:T(128)S(1)}, u32[]{:S(2)}, u32[]{:S(2)}) %collective-permute-start.4) | collective-permute-done | bytes 160 | tf_op jit(solution)/shard_map/ppermute | solution.py:159
  24.9 0.1 stack.31
  25.0 0.1 stack.30
  25.1 1.9 %collective-permute-start.9 = (f32[2,4,8]{2,1,0:T(4,128)S(1)}, f32[2,4,8]{2,1,0:T(4,128)S(1)}, u32[]{:S(2)}, u32[]{:S(2)}) collective-permute-start(f32[2,4,8]{2,1,0:T(4,128)S(1)} %constant_dynamic-update-slice_fusion), channel_id=1, source_target_pairs={{0,12},{4,0},{8,4},{12,8},{1,13},{5,1},{9,5},{13,9},{2,14},{6,2},{... | collective-permute-start | bytes 776 | tf_op jit(solution)/shard_map/ppermute | solution.py:227
  26.9 0.2 fusion.34
  27.1 0.1 stack.28
  27.2 0.1 stack.27
  27.3 0.0 collective-permute-start.8
  27.3 1.9 %collective-permute-start.7 = (f32[2,4,8]{2,1,0:T(4,128)S(1)}, f32[2,4,8]{2,1,0:T(4,128)S(1)}, u32[]{:S(2)}, u32[]{:S(2)}) collective-permute-start(f32[2,4,8]{2,1,0:T(4,128)S(1)} %constant_dynamic-update-slice_fusion), channel_id=1, source_target_pairs={{0,4},{4,8},{8,12},{12,0},{1,5},{5,9},{9,13},{13,1},{2,6},{6,10},{... | collective-permute-start | bytes 776 | tf_op jit(solution)/shard_map/ppermute | solution.py:227
  29.2 0.0 collective-permute-done.9
  29.2 2.5 %collective-permute-done.8 = f32[2,4,8]{2,1,0:T(4,128)S(1)} collective-permute-done((f32[2,4,8]{2,1,0:T(4,128)S(1)}, f32[2,4,8]{2,1,0:T(4,128)S(1)}, u32[]{:S(2)}, u32[]{:S(2)}) %collective-permute-start.8) | collective-permute-done | bytes 288 | tf_op jit(solution)/shard_map/ppermute | solution.py:227
  31.8 0.9 %collective-permute-done.7 = f32[2,4,8]{2,1,0:T(4,128)S(1)} collective-permute-done((f32[2,4,8]{2,1,0:T(4,128)S(1)}, f32[2,4,8]{2,1,0:T(4,128)S(1)}, u32[]{:S(2)}, u32[]{:S(2)}) %collective-permute-start.7) | collective-permute-done | bytes 288 | tf_op jit(solution)/shard_map/ppermute | solution.py:227
  32.8 0.1 sub.93
  32.9 0.1 div.29
  33.0 0.5 %bitcast_select_fusion = f32[8]{0:T(128)} fusion(pred[8]{0:T(512)(128)(4,1)S(1)} %fusion.34, f32[4,8]{1,0:T(4,128)S(1)} %fusion.24, f32[4,8]{1,0:T(4,128)S(1)} %slice_reduce_fusion.2), kind=kLoop, calls=%fused_computation.74 | loop fusion | flops 16 | bytes 104 | tf_op jit(solution)/shard_map/jit(_where)/select_n | solution.py:249
  33.5 0.2 fusion.38
  33.7 0.3 fusion.16
  34.0 0.5 %fusion.13 = f32[50,2048]{1,0:T(8,128)S(1)} fusion(f32[50,16]{1,0:T(8,128)S(1)} %fusion.16, f32[16,2048]{1,0:T(8,128)S(1)} %copy-done.2), kind=kOutput, calls=%fused_computation.29 | convolution fusion | flops 19693568 | bytes 543872 | tf_op jit(solution)/shard_map/dot_general | solution.py:250
  34.5 2.6 %fusion.1 = f32[1,50,4096]{2,1,0:T(8,128)S(1)} fusion(bf16[32,16,2048]{2,1,0:T(8,128)(2,1)} %copy-done, bf16[32,16,2048]{2,1,0:T(8,128)(2,1)S(1)} %get-tuple-element.14, f32[50,2048]{1,0:T(8,128)S(1)} %fusion.13, f32[4096]{0:T(1024)S(1)} %pad_maximum_fusion.11, f32[32]{0:T(128)S(1)} %get-tuple-element.8, f32[32,16,50]{2,1,0:T(8,128)S(1)} %get-tuple-element.23, ...), kind=kOutput, calls=%fused_computation.2 | convolution fusion | flops 218846208 | bytes 5542400 | tf_op jit(solution)/shard_map/dot_general | solution.py:173
  37.1 1.7 %copy.14 = f32[1,50,4096]{2,0,1:T(1,128)} copy(f32[1,50,4096]{2,1,0:T(8,128)S(1)} %fusion.1) | data formatting | bytes 1638400
  (21 shorter events, 0.2 us)
Async XLA Ops:
  0.6 13.7 %copy-start.2 = (f32[16,2048]{1,0:T(8,128)S(1)}, f32[16,2048]{1,0:T(8,128)}, u32[]{:S(2)}) copy-start(f32[16,2048]{1,0:T(8,128)} %param.9) | copy-start | bytes 393220
  2.2 11.9 %copy-start.1 = (bf16[8,4224]{1,0:T(8,128)(2,1)S(1)}, bf16[8,4224]{1,0:T(8,128)(2,1)}, u32[]{:S(2)}) copy-start(bf16[8,4224]{1,0:T(8,128)(2,1)} %shard_map.86) | copy-start | bytes 202756
  2.2 9.3 %collective-permute-start.2 = (bf16[8,4224]{1,0:T(8,128)(2,1)}, bf16[8,4224]{1,0:T(8,128)(2,1)S(1)}, u32[]{:S(2)}, u32[]{:S(2)}) collective-permute-start(bf16[8,4224]{1,0:T(8,128)(2,1)} %shard_map.86), channel_id=1, source_target_pairs={{0,12},{4,0},{8,4},{12,8},{1,13},{5,1},{9,5},{13,9},{2,14},{6,2},{... | collective-permute-start | bytes 202760 | tf_op jit(solution)/shard_map/ppermute | solution.py:149
  7.2 6.9 %collective-permute-start.1 = (bf16[8,4224]{1,0:T(8,128)(2,1)}, bf16[8,4224]{1,0:T(8,128)(2,1)S(1)}, u32[]{:S(2)}, u32[]{:S(2)}) collective-permute-start(bf16[8,4224]{1,0:T(8,128)(2,1)} %shard_map.86), channel_id=1, source_target_pairs={{0,8},{4,12},{8,0},{12,4},{1,9},{5,13},{9,1},{13,5},{2,10},{6,14},... | collective-permute-start | bytes 202760 | tf_op jit(solution)/shard_map/ppermute | solution.py:149
  7.2 6.9 %collective-permute-start = (bf16[8,4224]{1,0:T(8,128)(2,1)}, bf16[8,4224]{1,0:T(8,128)(2,1)S(1)}, u32[]{:S(2)}, u32[]{:S(2)}) collective-permute-start(bf16[8,4224]{1,0:T(8,128)(2,1)} %shard_map.86), channel_id=1, source_target_pairs={{0,4},{4,8},{8,12},{12,0},{1,5},{5,9},{9,13},{13,1},{2,6},{6,10},{... | collective-permute-start | bytes 202760 | tf_op jit(solution)/shard_map/ppermute | solution.py:149
  14.9 1.6 %copy-start.3 = (bf16[1,50,4096]{2,1,0:T(8,128)(2,1)S(1)}, bf16[1,50,4096]{2,1,0:T(8,128)(2,1)}, u32[]{:S(2)}) copy-start(bf16[1,50,4096]{2,1,0:T(8,128)(2,1)} %param.8) | copy-start | bytes 1228804
  16.5 1.5 %copy-start = (bf16[32,16,2048]{2,1,0:T(8,128)(2,1)}, bf16[32,16,2048]{2,1,0:T(8,128)(2,1)S(1)}, u32[]{:S(2)}) copy-start(bf16[32,16,2048]{2,1,0:T(8,128)(2,1)S(1)} %get-tuple-element.15) | copy-start | bytes 6291460
  16.5 5.4 %copy-start.4 = (f32[2048]{0:T(1024)S(1)}, f32[2048]{0:T(1024)}, u32[]{:S(2)}) copy-start(f32[2048]{0:T(1024)} %param.10) | copy-start | bytes 24580
  18.4 1.2 %collective-permute-start.5 = (f32[32]{0:T(128)S(1)}, f32[32]{0:T(128)S(1)}, u32[]{:S(2)}, u32[]{:S(2)}) collective-permute-start(f32[32]{0:T(128)S(1)} %exponential_reduce_fusion), channel_id=1, source_target_pairs={{0,1},{1,0},{2,3},{3,2},{4,5},{5,4},{6,7},{7,6},{8,9},{9,8},{10,11... | collective-permute-start | bytes 392 | tf_op jit(solution)/shard_map/ppermute | solution.py:159
  18.5 1.3 %collective-permute-start.3 = (f32[32]{0:T(128)S(1)}, f32[32]{0:T(128)S(1)}, u32[]{:S(2)}, u32[]{:S(2)}) collective-permute-start(f32[32]{0:T(128)S(1)} %get-tuple-element.22), channel_id=1, source_target_pairs={{0,1},{1,0},{2,3},{3,2},{4,5},{5,4},{6,7},{7,6},{8,9},{9,8},{10,11... | collective-permute-start | bytes 392 | tf_op jit(solution)/shard_map/ppermute | solution.py:159
  19.8 3.6 %collective-permute-start.6 = (f32[32]{0:T(128)S(1)}, f32[32]{0:T(128)S(1)}, u32[]{:S(2)}, u32[]{:S(2)}) collective-permute-start(f32[32]{0:T(128)S(1)} %get-tuple-element.12), channel_id=1, source_target_pairs={{0,2},{1,3},{2,0},{3,1},{4,6},{5,7},{6,4},{7,5},{8,10},{9,11},{10,... | collective-permute-start | bytes 392 | tf_op jit(solution)/shard_map/ppermute | solution.py:159
  21.3 3.5 %collective-permute-start.4 = (f32[32]{0:T(128)S(1)}, f32[32]{0:T(128)S(1)}, u32[]{:S(2)}, u32[]{:S(2)}) collective-permute-start(f32[32]{0:T(128)S(1)} %get-tuple-element.13), channel_id=1, source_target_pairs={{0,2},{1,3},{2,0},{3,1},{4,6},{5,7},{6,4},{7,5},{8,10},{9,11},{10,... | collective-permute-start | bytes 392 | tf_op jit(solution)/shard_map/ppermute | solution.py:159
  25.1 4.1 %collective-permute-start.9 = (f32[2,4,8]{2,1,0:T(4,128)S(1)}, f32[2,4,8]{2,1,0:T(4,128)S(1)}, u32[]{:S(2)}, u32[]{:S(2)}) collective-permute-start(f32[2,4,8]{2,1,0:T(4,128)S(1)} %constant_dynamic-update-slice_fusion), channel_id=1, source_target_pairs={{0,12},{4,0},{8,4},{12,8},{1,13},{5,1},{9,5},{13,9},{2,14},{6,2},{... | collective-permute-start | bytes 776 | tf_op jit(solution)/shard_map/ppermute | solution.py:227
  27.3 4.5 %collective-permute-start.8 = (f32[2,4,8]{2,1,0:T(4,128)S(1)}, f32[2,4,8]{2,1,0:T(4,128)S(1)}, u32[]{:S(2)}, u32[]{:S(2)}) collective-permute-start(f32[2,4,8]{2,1,0:T(4,128)S(1)} %constant_dynamic-update-slice_fusion), channel_id=1, source_target_pairs={{0,8},{4,12},{8,0},{12,4},{1,9},{5,13},{9,1},{13,5},{2,10},{6,14},... | collective-permute-start | bytes 776 | tf_op jit(solution)/shard_map/ppermute | solution.py:227
  27.3 5.5 %collective-permute-start.7 = (f32[2,4,8]{2,1,0:T(4,128)S(1)}, f32[2,4,8]{2,1,0:T(4,128)S(1)}, u32[]{:S(2)}, u32[]{:S(2)}) collective-permute-start(f32[2,4,8]{2,1,0:T(4,128)S(1)} %constant_dynamic-update-slice_fusion), channel_id=1, source_target_pairs={{0,4},{4,8},{8,12},{12,0},{1,5},{5,9},{9,13},{13,1},{2,6},{6,10},{... | collective-permute-start | bytes 776 | tf_op jit(solution)/shard_map/ppermute | solution.py:227

commit v4 on v3

--- a/solution.py
+++ b/solution.py
@@ -155,15 +155,13 @@
 def xor_butterfly(stats, axis, size):
     step = 1
     while step < size:
-        other = jax.tree.map(
-            lambda part: lax.ppermute(part, axis, [(i, i ^ step) for i in range(size)]), stats
-        )
-        stats = combine_stats(stats, other)
+        other = lax.ppermute(stats, axis, [(i, i ^ step) for i in range(size)])
+        stats = jnp.stack(combine_stats(stats, other))
         step *= 2
     return stats
 
 
-def accumulate(shifted, scores, gain_rows, bin_rows, live_mask, peak_score, totals):
+def accumulate(shifted, scores, gain_rows, ctf_rows, live_mask, peak_score, totals):
     weights = (
         jnp.exp(scores - peak_score[:, None, None])
         / totals[:, None, None]
@@ -174,8 +172,10 @@
         scaled, shifted, (((0,), (0,)), ((), ())), preferred_element_type=jnp.float32
     )
     summed = jnp.sum(weights, axis=1) * (gain_rows * gain_rows)[:, None]
-    bin_weight = lax.dot_general(summed, bin_rows, (((0,), (0,)), ((), ())), precision=HIGHEST)
-    return (numerator, bin_weight)
+    denominator = lax.dot_general(
+        summed, ctf_rows * ctf_rows, (((0,), (0,)), ((), ())), precision=HIGHEST
+    )
+    return (numerator, denominator)
 
 
 def per_device(
@@ -221,8 +221,8 @@
     totals_all = jnp.sum(jnp.exp(flattened - peak_all[:, None]), axis=1)
 
     if small and n_cls & (n_cls - 1) == 0:
-        peak_all, totals_all = xor_butterfly((peak_all, totals_all), "cls", n_cls)
-        stats = jnp.stack([peak_all, totals_all]).reshape(2, n_blk, batch_size)
+        stats = xor_butterfly(jnp.stack([peak_all, totals_all]), "cls", n_cls)
+        stats = stats.reshape(2, n_blk, batch_size)
         parts = [stats] + [
             jnp.roll(lax.ppermute(stats, "blk", [(i, (i + k) % n_blk) for i in range(n_blk)]), k, axis=1)
             for k in range(1, n_blk)
@@ -243,11 +243,10 @@
         peak_score = lax.dynamic_slice_in_dim(peak_all, own_offset, batch_size)
         totals = lax.dynamic_slice_in_dim(totals_all, own_offset, batch_size)
 
-    numerator, bin_weight = accumulate(
-        shifted, all_scores, gain_all, bin_rows, live_all, peak_all, totals_all
+    numerator, denominator = accumulate(
+        shifted, all_scores, gain_all, ctf_rows, live_all, peak_all, totals_all
     )
     log_evidence = jnp.where(live_mask > 0.5, peak_score + jnp.log(totals), 0.0)
-    denominator = jnp.dot(bin_weight, ctf_square, precision=HIGHEST)
     denominator = (
         jnp.concatenate([denominator, denominator], axis=1)
         + jnp.concatenate([spectral_reg, spectral_reg])[None, :]

time: 39 us -> 38.1 us (0.977)
  waiting for transfers between devices: 9.87 us -> 8.84 us
  starting transfers between devices: 12.5 us -> 11.5 us
  other arithmetic: 4.94 us -> 5.61 us
  local copies, waits for them, and re-layouts: 2.52 us -> 3.03 us
    ppermute x4 -> x2, starting transfers between devices: 2.61 us -> 1.63 us  [xor_butterfly(): other = lax.ppermute(stats, axis, [(i, i ^ step) for i in range(size)])]
    ppermute x4 -> x2, waiting for transfers between devices: 3.82 us -> 3 us  [xor_butterfly(): other = lax.ppermute(stats, axis, [(i, i ^ step) for i in range(size)])]
    max x0 -> x1, other arithmetic: none -> 0.68 us  [combine_stats(): new_peak = jnp.maximum(former[0], latter[0])]
    add x0 -> x1, local copies, waits for them, and re-layouts: none -> 0.51 us  [combine_stats(): former[1] * jnp.exp(former[0] - new_peak)]
    dot_general x2 -> x1, matrix products: 0.79 us -> 0.64 us  [accumulate(): lax.dot_general(summed, ctf_rows * ctf_rows, (((0,), (0,)), ((), ())), pr...]
    another operation x1 -> x3, other arithmetic: 1.53 us -> 1.54 us
  transfers between devices with their start and end apart: 10 -> 8, of which waited for: 7 -> 5; matrix products, arithmetic and copies ran while one was open for 9% -> 10% of each run, Pallas kernels for 0% -> 0%
where the time goes in v4:
time: 38.1 us; the launch traced here: 37.8 us
  starting transfers between devices  11.5 us (30%)
  waiting for transfers between devices  8.84 us (23%)
  matrix products  6.53 us (17%)
  other arithmetic  5.61 us (15%)
  local copies, waits for them, and re-layouts  3.03 us (8%)
  Pallas kernels  1.53 us (4%)
  between operations  0.83 us (2%)
    ppermute x3, starting transfers between devices, shift_gather(): lax.ppermute(value, axis, [(i, (i + k) % size) for i in range(size)])  6.06 us
    ppermute x3, starting transfers between devices, per_device(): lax.ppermute(stats, 'blk', [(i, (i + k) % n_blk) for i in range(n_blk)])  3.77 us
    ppermute x3, waiting for transfers between devices, per_device(): lax.ppermute(stats, 'blk', [(i, (i + k) % n_blk) for i in range(n_blk)])  3.28 us
    ppermute x2, waiting for transfers between devices, xor_butterfly(): other = lax.ppermute(stats, axis, [(i, i ^ step) for i in range(size)])  3 us
    dot_general x1, matrix products, accumulate(): lax.dot_general(scaled, shifted, (((0,), (0,)), ((), ())), preferred_elem...  2.57 us
    ppermute x3, waiting for transfers between devices, shift_gather(): lax.ppermute(value, axis, [(i, (i + k) % size) for i in range(size)])  2.57 us
    unnamed x12, local copies, waits for them, and re-layouts  1.77 us
    ppermute x2, starting transfers between devices, xor_butterfly(): other = lax.ppermute(stats, axis, [(i, i ^ step) for i in range(size)])  1.63 us
  transfers between devices with their start and end apart: 8, of which 5 were waited for; matrix products, arithmetic and copies ran while one was open for 10% of the time, Pallas kernels for 0%

profile of v4, /device:TPU:0, one launch (start us, length us, event | category | flops | bytes accessed | tf_op | source)
XLA Modules:
  0.0 37.8 jit_solution(6311573441162852992)
XLA Ops:
  0.6 0.0 copy-start.3
  0.6 1.5 %shard_map.86 = bf16[8,4224]{1,0:T(8,128)(2,1)} custom-call(s32[4]{0:T(128)} %sizes_ref.1, f32[4]{0:T(128)} %scales_ref.1, s32[8]{0:T(128)} %bins_ref.1, bf16[8,4096]{1,0:T(8,128)(2,1)} %images_ref.1), custom_call_target="tpu_custom_call" | custom-call | tf_op jit(solution)/shard_map/pallas_call | solution.py:139
  2.2 0.0 copy-start.1
  2.2 5.0 %collective-permute-start.2 = (bf16[8,4224]{1,0:T(8,128)(2,1)}, bf16[8,4224]{1,0:T(8,128)(2,1)S(1)}, u32[]{:S(2)}, u32[]{:S(2)}) collective-permute-start(bf16[8,4224]{1,0:T(8,128)(2,1)} %shard_map.86), channel_id=1, source_target_pairs={{0,12},{4,0},{8,4},{12,8},{1,13},{5,1},{9,5},{13,9},{2,14},{6,2},{... | collective-permute-start | bytes 202760 | tf_op jit(solution)/shard_map/ppermute | solution.py:149
  7.2 0.0 collective-permute-start.1
  7.2 1.0 %collective-permute-start = (bf16[8,4224]{1,0:T(8,128)(2,1)}, bf16[8,4224]{1,0:T(8,128)(2,1)S(1)}, u32[]{:S(2)}, u32[]{:S(2)}) collective-permute-start(bf16[8,4224]{1,0:T(8,128)(2,1)} %shard_map.86), channel_id=1, source_target_pairs={{0,4},{4,8},{8,12},{12,0},{1,5},{5,9},{9,13},{13,1},{2,6},{6,10},{... | collective-permute-start | bytes 202760 | tf_op jit(solution)/shard_map/ppermute | solution.py:149
  8.3 0.1 broadcast_in_dim.13
  8.3 0.1 mul.277
  8.4 0.1 mul.273
  8.5 1.1 %bitcast_convert_fusion = f32[50,4096]{1,0:T(8,128)S(1)} fusion(bf16[1,50,4096]{2,1,0:T(8,128)(2,1)} %param.8), kind=kLoop, calls=%fused_computation.16 | loop fusion | flops 204800 | bytes 1228800 | tf_op jit(solution)/shard_map/convert_element_type | solution.py:67
  9.6 0.5 %fusion.14 = (f32[16,2048]{1,0:T(8,128)S(1)}, f32[16,2048]{1,0:T(8,128)S(1)}) fusion(f32[2048]{0:T(1024)S(1)} %get-tuple-element.29, f32[16]{0:T(128)S(1)} %mul.277, f32[2048]{0:T(1024)S(1)} %get-tuple-element.28, f32[16]{0:T(128)S(1)} %mul.273), kind=kLoop, calls=%fused_computation.30 | loop fusion | flops 131072 | bytes 278656 | tf_op jit(solution)/shard_map/cos | solution.py:34
  10.1 1.4 %fusion.6 = f32[16,50]{1,0:T(8,128)S(1)} fusion(f32[50,4096]{1,0:T(8,128)S(1)} %bitcast_convert_fusion, f32[16,2048]{1,0:T(8,128)} %param.9), kind=kOutput, calls=%fused_computation.13 | convolution fusion | flops 20000768 | bytes 953472 | tf_op jit(solution)/shard_map/dot_general | solution.py:72
  11.5 0.0 collective-permute-done.2
  11.5 2.6 %collective-permute-done.1 = bf16[8,4224]{1,0:T(8,128)(2,1)S(1)} collective-permute-done((bf16[8,4224]{1,0:T(8,128)(2,1)}, bf16[8,4224]{1,0:T(8,128)(2,1)S(1)}, u32[]{:S(2)}, u32[]{:S(2)}) %collective-permute-start.1) | collective-permute-done | bytes 67616 | tf_op jit(solution)/shard_map/ppermute | solution.py:149
  14.1 0.0 collective-permute-done
  14.1 0.0 copy-done.1
  14.1 0.2 multiply_reduce_fusion
  14.3 0.0 copy-done.3
  14.3 0.3 fusion.17
  14.7 0.2 convolution_multiply_fusion
  14.9 0.0 copy-start.2
  14.9 1.5 %multiply_convert_fusion.1 = (bf16[32,16,2048]{2,1,0:T(8,128)(2,1)S(1)}, bf16[32,16,2048]{2,1,0:T(8,128)(2,1)S(1)}) fusion(f32[32,2048]{1,0:T(8,128)S(1)} %fusion.17, f32[16,2048]{1,0:T(8,128)S(1)} %get-tuple-element.19, f32[32,2048]{1,0:T(8,128)S(1)} %get-tuple-element.17, f32[16,2048]{1,0:T(8,128)S(1)} %get-tuple-element.18, ...), kind=kLoop, calls=%fused_computation.5 | loop fusion | flops 10485760 | bytes 5242880 | tf_op jit(solution)/shard_map/convert
  16.4 0.0 copy-start
  16.5 0.0 copy-done.2
  16.5 0.0 copy-start.4
  16.5 1.4 %fusion.41 = (f32[32]{0:T(128)S(1)}, f32[32,16,50]{2,1,0:T(8,128)S(1)}) fusion(f32[32,50]{1,0:T(8,128)S(1)} %convolution_multiply_fusion, bf16[1,50,4096]{2,1,0:T(8,128)(2,1)S(1)} %copy-done.2, bf16[32,16,2048]{2,1,0:T(8,128)(2,1)S(1)} %get-tuple-element.15, bf16[32,16,2048]{2,1,0:T(8,128)(2,1)S(1)} %get-tuple-element.14, f32[32]{0:T(128)S(1)} %get-tuple-element.8), kind=kOutput, calls=%fused_computation.89 | convolution fusion | flops 218180576 | bytes 4712960 | tf_op jit(solution)/shard_map/dot_general | solution.py:77
  17.9 0.0 copy-done
  17.9 0.5 %exponential_reduce_fusion = f32[32]{0:T(128)S(1)} fusion(f32[32,16,50]{2,1,0:T(8,128)S(1)} %get-tuple-element.27, f32[32]{0:T(128)S(1)} %get-tuple-element.26), kind=kLoop, calls=%fused_computation.21 | loop fusion | flops 51168 | bytes 102656 | tf_op jit(solution)/shard_map/reduce_sum | solution.py:221
  18.4 0.1 collective-permute-start.3
  18.5 0.0 copy-done.4
  18.5 1.1 %collective-permute-done.3 = f32[2,32]{1,0:T(2,128)S(1)} collective-permute-done((f32[2,32]{1,0:T(2,128)S(1)}, f32[2,32]{1,0:T(2,128)S(1)}, u32[]{:S(2)}, u32[]{:S(2)}) %collective-permute-start.3) | collective-permute-done | bytes 288 | tf_op jit(solution)/shard_map/ppermute | solution.py:158
  19.7 1.6 %collective-permute-start.4 = (f32[2,32]{1,0:T(2,128)S(1)}, f32[2,32]{1,0:T(2,128)S(1)}, u32[]{:S(2)}, u32[]{:S(2)}) collective-permute-start(f32[2,32]{1,0:T(2,128)S(1)} %pad_maximum_fusion.13), channel_id=1, source_target_pairs={{0,2},{1,3},{2,0},{3,1},{4,6},{5,7},{6,4},{7,5},{8,10},{9,11},{10,... | collective-permute-start | bytes 776 | tf_op jit(solution)/shard_map/ppermute | solution.py:158
  21.2 0.2 fusion.32
  21.4 1.9 %collective-permute-done.4 = f32[2,32]{1,0:T(2,128)S(1)} collective-permute-done((f32[2,32]{1,0:T(2,128)S(1)}, f32[2,32]{1,0:T(2,128)S(1)}, u32[]{:S(2)}, u32[]{:S(2)}) %collective-permute-start.4) | collective-permute-done | bytes 288 | tf_op jit(solution)/shard_map/ppermute | solution.py:158
  23.3 0.5 %broadcast.180 = f32[]{:T(128)} broadcast(f32[]{:T(128)} %constant.49), dimensions={} | broadcast | bytes 8 | tf_op jit(solution)/shard_map/add | solution.py:92
  23.8 0.7 %fusion.35 = (f32[32]{0:T(128)S(1)}, f32[32]{0:T(128)S(1)}, f32[32]{0:T(128)S(1)}, f32[1,32]{1,0:T(1,128)S(1)}) fusion(f32[1,32]{1,0:T(1,128)S(1)} %get-tuple-element.13, f32[2,32]{1,0:T(2,128)S(1)} %collective-permute-done.4, f32[]{:T(128)} %broadcast.180, f32[1,32]{1,0:T(1,128)S(1)} %get-tuple-element.12), kind=kLoop, calls=%fused_computation.83 | loop fusion | flops 192 | bytes 1028 | tf_op jit(solution)/shard_map/max | solution.py:89
  24.5 0.1 stack.45
  24.6 0.1 stack.46
  24.7 1.8 %collective-permute-start.7 = (f32[2,4,8]{2,1,0:T(4,128)S(1)}, f32[2,4,8]{2,1,0:T(4,128)S(1)}, u32[]{:S(2)}, u32[]{:S(2)}) collective-permute-start(f32[2,4,8]{2,1,0:T(4,128)S(1)} %constant_dynamic-update-slice_fusion), channel_id=1, source_target_pairs={{0,12},{4,0},{8,4},{12,8},{1,13},{5,1},{9,5},{13,9},{2,14},{6,2},{... | collective-permute-start | bytes 776 | tf_op jit(solution)/shard_map/ppermute | solution.py:227
  26.5 0.0 collective-permute-start.6
  26.5 1.9 %collective-permute-start.5 = (f32[2,4,8]{2,1,0:T(4,128)S(1)}, f32[2,4,8]{2,1,0:T(4,128)S(1)}, u32[]{:S(2)}, u32[]{:S(2)}) collective-permute-start(f32[2,4,8]{2,1,0:T(4,128)S(1)} %constant_dynamic-update-slice_fusion), channel_id=1, source_target_pairs={{0,4},{4,8},{8,12},{12,0},{1,5},{5,9},{9,13},{13,1},{2,6},{6,10},{... | collective-permute-start | bytes 776 | tf_op jit(solution)/shard_map/ppermute | solution.py:227
  28.4 0.1 stack.42
  28.5 0.1 stack.43
  28.6 0.0 collective-permute-done.7
  28.6 2.4 %collective-permute-done.6 = f32[2,4,8]{2,1,0:T(4,128)S(1)} collective-permute-done((f32[2,4,8]{2,1,0:T(4,128)S(1)}, f32[2,4,8]{2,1,0:T(4,128)S(1)}, u32[]{:S(2)}, u32[]{:S(2)}) %collective-permute-start.6) | collective-permute-done | bytes 288 | tf_op jit(solution)/shard_map/ppermute | solution.py:227
  31.0 0.9 %collective-permute-done.5 = f32[2,4,8]{2,1,0:T(4,128)S(1)} collective-permute-done((f32[2,4,8]{2,1,0:T(4,128)S(1)}, f32[2,4,8]{2,1,0:T(4,128)S(1)}, u32[]{:S(2)}, u32[]{:S(2)}) %collective-permute-start.5) | collective-permute-done | bytes 288 | tf_op jit(solution)/shard_map/ppermute | solution.py:227
  32.0 0.1 sub.99
  32.1 0.1 div.29
  32.2 0.5 %bitcast_select_fusion = f32[8]{0:T(128)} fusion(pred[8]{0:T(512)(128)(4,1)S(1)} %fusion.32, f32[4,8]{1,0:T(4,128)S(1)} %fusion.23, f32[4,8]{1,0:T(4,128)S(1)} %slice_reduce_fusion.2), kind=kLoop, calls=%fused_computation.74 | loop fusion | flops 16 | bytes 104 | tf_op jit(solution)/shard_map/jit(_where)/select_n | solution.py:249
  32.7 0.2 fusion.38
  32.9 0.6 %fusion.9 = f32[50,2048]{1,0:T(8,128)S(1)} fusion(f32[32,2048]{1,0:T(8,128)S(1)} %fusion.17, f32[32,50]{1,0:T(8,128)S(1)} %fusion.38, f32[32]{0:T(128)S(1)} %get-tuple-element.6), kind=kOutput, calls=%fused_computation.17 | convolution fusion | flops 39388736 | bytes 678272 | tf_op jit(solution)/shard_map/dot_general | solution.py:175
  33.5 2.6 %fusion.1 = f32[1,50,4096]{2,1,0:T(8,128)S(1)} fusion(bf16[32,16,2048]{2,1,0:T(8,128)(2,1)} %copy-done, bf16[32,16,2048]{2,1,0:T(8,128)(2,1)S(1)} %get-tuple-element.14, f32[50,2048]{1,0:T(8,128)S(1)} %fusion.9, f32[4096]{0:T(1024)S(1)} %pad_maximum_fusion.11, f32[32]{0:T(128)S(1)} %get-tuple-element.8, f32[32,16,50]{2,1,0:T(8,128)S(1)} %get-tuple-element.27, ...), kind=kOutput, calls=%fused_computation.2 | convolution fusion | flops 218846208 | bytes 5542400 | tf_op jit(solution)/shard_map/dot_general | solution.py:171
  36.1 1.7 %copy.14 = f32[1,50,4096]{2,0,1:T(1,128)} copy(f32[1,50,4096]{2,1,0:T(8,128)S(1)} %fusion.1) | data formatting | bytes 1638400
  (22 shorter events, 0.2 us)
Async XLA Ops:
  0.6 13.7 %copy-start.3 = (f32[16,2048]{1,0:T(8,128)S(1)}, f32[16,2048]{1,0:T(8,128)}, u32[]{:S(2)}) copy-start(f32[16,2048]{1,0:T(8,128)} %param.9) | copy-start | bytes 393220
  2.2 11.9 %copy-start.1 = (bf16[8,4224]{1,0:T(8,128)(2,1)S(1)}, bf16[8,4224]{1,0:T(8,128)(2,1)}, u32[]{:S(2)}) copy-start(bf16[8,4224]{1,0:T(8,128)(2,1)} %shard_map.86) | copy-start | bytes 202756
  2.2 9.3 %collective-permute-start.2 = (bf16[8,4224]{1,0:T(8,128)(2,1)}, bf16[8,4224]{1,0:T(8,128)(2,1)S(1)}, u32[]{:S(2)}, u32[]{:S(2)}) collective-permute-start(bf16[8,4224]{1,0:T(8,128)(2,1)} %shard_map.86), channel_id=1, source_target_pairs={{0,12},{4,0},{8,4},{12,8},{1,13},{5,1},{9,5},{13,9},{2,14},{6,2},{... | collective-permute-start | bytes 202760 | tf_op jit(solution)/shard_map/ppermute | solution.py:149
  7.2 6.9 %collective-permute-start.1 = (bf16[8,4224]{1,0:T(8,128)(2,1)}, bf16[8,4224]{1,0:T(8,128)(2,1)S(1)}, u32[]{:S(2)}, u32[]{:S(2)}) collective-permute-start(bf16[8,4224]{1,0:T(8,128)(2,1)} %shard_map.86), channel_id=1, source_target_pairs={{0,8},{4,12},{8,0},{12,4},{1,9},{5,13},{9,1},{13,5},{2,10},{6,14},... | collective-permute-start | bytes 202760 | tf_op jit(solution)/shard_map/ppermute | solution.py:149
  7.2 6.9 %collective-permute-start = (bf16[8,4224]{1,0:T(8,128)(2,1)}, bf16[8,4224]{1,0:T(8,128)(2,1)S(1)}, u32[]{:S(2)}, u32[]{:S(2)}) collective-permute-start(bf16[8,4224]{1,0:T(8,128)(2,1)} %shard_map.86), channel_id=1, source_target_pairs={{0,4},{4,8},{8,12},{12,0},{1,5},{5,9},{9,13},{13,1},{2,6},{6,10},{... | collective-permute-start | bytes 202760 | tf_op jit(solution)/shard_map/ppermute | solution.py:149
  14.9 1.6 %copy-start.2 = (bf16[1,50,4096]{2,1,0:T(8,128)(2,1)S(1)}, bf16[1,50,4096]{2,1,0:T(8,128)(2,1)}, u32[]{:S(2)}) copy-start(bf16[1,50,4096]{2,1,0:T(8,128)(2,1)} %param.8) | copy-start | bytes 1228804
  16.4 1.5 %copy-start = (bf16[32,16,2048]{2,1,0:T(8,128)(2,1)}, bf16[32,16,2048]{2,1,0:T(8,128)(2,1)S(1)}, u32[]{:S(2)}) copy-start(bf16[32,16,2048]{2,1,0:T(8,128)(2,1)S(1)} %get-tuple-element.15) | copy-start | bytes 6291460
  16.5 2.0 %copy-start.4 = (f32[2048]{0:T(1024)S(1)}, f32[2048]{0:T(1024)}, u32[]{:S(2)}) copy-start(f32[2048]{0:T(1024)} %param.10) | copy-start | bytes 24580
  18.4 1.2 %collective-permute-start.3 = (f32[2,32]{1,0:T(2,128)S(1)}, f32[2,32]{1,0:T(2,128)S(1)}, u32[]{:S(2)}, u32[]{:S(2)}) collective-permute-start(f32[2,32]{1,0:T(2,128)S(1)} %pad_maximum_fusion.12), channel_id=1, source_target_pairs={{0,1},{1,0},{2,3},{3,2},{4,5},{5,4},{6,7},{7,6},{8,9},{9,8},{10,11... | collective-permute-start | bytes 776 | tf_op jit(solution)/shard_map/ppermute | solution.py:158
  19.7 3.6 %collective-permute-start.4 = (f32[2,32]{1,0:T(2,128)S(1)}, f32[2,32]{1,0:T(2,128)S(1)}, u32[]{:S(2)}, u32[]{:S(2)}) collective-permute-start(f32[2,32]{1,0:T(2,128)S(1)} %pad_maximum_fusion.13), channel_id=1, source_target_pairs={{0,2},{1,3},{2,0},{3,1},{4,6},{5,7},{6,4},{7,5},{8,10},{9,11},{10,... | collective-permute-start | bytes 776 | tf_op jit(solution)/shard_map/ppermute | solution.py:158
  24.7 3.9 %collective-permute-start.7 = (f32[2,4,8]{2,1,0:T(4,128)S(1)}, f32[2,4,8]{2,1,0:T(4,128)S(1)}, u32[]{:S(2)}, u32[]{:S(2)}) collective-permute-start(f32[2,4,8]{2,1,0:T(4,128)S(1)} %constant_dynamic-update-slice_fusion), channel_id=1, source_target_pairs={{0,12},{4,0},{8,4},{12,8},{1,13},{5,1},{9,5},{13,9},{2,14},{6,2},{... | collective-permute-start | bytes 776 | tf_op jit(solution)/shard_map/ppermute | solution.py:227
  26.5 4.5 %collective-permute-start.6 = (f32[2,4,8]{2,1,0:T(4,128)S(1)}, f32[2,4,8]{2,1,0:T(4,128)S(1)}, u32[]{:S(2)}, u32[]{:S(2)}) collective-permute-start(f32[2,4,8]{2,1,0:T(4,128)S(1)} %constant_dynamic-update-slice_fusion), channel_id=1, source_target_pairs={{0,8},{4,12},{8,0},{12,4},{1,9},{5,13},{9,1},{13,5},{2,10},{6,14},... | collective-permute-start | bytes 776 | tf_op jit(solution)/shard_map/ppermute | solution.py:227
  26.5 5.4 %collective-permute-start.5 = (f32[2,4,8]{2,1,0:T(4,128)S(1)}, f32[2,4,8]{2,1,0:T(4,128)S(1)}, u32[]{:S(2)}, u32[]{:S(2)}) collective-permute-start(f32[2,4,8]{2,1,0:T(4,128)S(1)} %constant_dynamic-update-slice_fusion), channel_id=1, source_target_pairs={{0,4},{4,8},{8,12},{12,0},{1,5},{5,9},{9,13},{13,1},{2,6},{6,10},{... | collective-permute-start | bytes 776 | tf_op jit(solution)/shard_map/ppermute | solution.py:227

commit v5 on v4

--- a/solution.py
+++ b/solution.py
@@ -1,6 +1,7 @@
 import math
 
 import jax
+import numpy as np
 import jax.numpy as jnp
 from jax import lax
 from jax.experimental import pallas as pl
@@ -19,19 +20,16 @@
 
 
 def phase_tables():
-    column = jnp.arange(KX * KY, dtype=jnp.int32)
-    freq_x = (column % KX).astype(jnp.float32)
-    freq_y = (column // KX - KY // 2).astype(jnp.float32)
-    offsets = jnp.arange(SIDE, dtype=jnp.float32) - (SIDE - 1) / 2.0
-    shift_x = jnp.tile(offsets, SIDE)
-    shift_y = jnp.repeat(offsets, SIDE)
-    phases = (
-        2.0
-        * math.pi
-        / IMG
-        * (shift_x[:, None] * freq_x[None, :] + shift_y[:, None] * freq_y[None, :])
-    )
-    return (jnp.cos(phases), jnp.sin(phases))
+    column = np.arange(KX * KY, dtype=np.int32)
+    freq_x = (column % KX).astype(np.float32)
+    freq_y = (column // KX - KY // 2).astype(np.float32)
+    offsets = np.arange(SIDE, dtype=np.float32) - np.float32((SIDE - 1) / 2.0)
+    shift_x = np.tile(offsets, SIDE)
+    shift_y = np.repeat(offsets, SIDE)
+    phases = np.float32(2.0 * math.pi / IMG) * (
+        shift_x[:, None] * freq_x[None, :] + shift_y[:, None] * freq_y[None, :]
+    )
+    return (jnp.asarray(np.cos(phases)), jnp.asarray(np.sin(phases)))
 
 
 def bin_matrix(bin_values):
@@ -161,21 +159,38 @@
     return stats
 
 
-def accumulate(shifted, scores, gain_rows, ctf_rows, live_mask, peak_score, totals):
+def accumulate(pieces, scores, gain_rows, ctf_rows, live_mask, peak_score, totals):
     weights = (
         jnp.exp(scores - peak_score[:, None, None])
         / totals[:, None, None]
         * live_mask[:, None, None]
     )
-    scaled = (weights * gain_rows[:, None, None]).astype(jnp.bfloat16).reshape(shifted.shape[0], -1)
-    numerator = lax.dot_general(
-        scaled, shifted, (((0,), (0,)), ((), ())), preferred_element_type=jnp.float32
-    )
+    scaled = (weights * gain_rows[:, None, None]).astype(jnp.bfloat16)
+    numerator = None
+    start = 0
+    for shifted in pieces:
+        count = shifted.shape[0] // scaled.shape[1]
+        part = lax.dot_general(
+            scaled[start : start + count].reshape(shifted.shape[0], -1),
+            shifted,
+            (((0,), (0,)), ((), ())),
+            preferred_element_type=jnp.float32,
+        )
+        numerator = part if numerator is None else numerator + part
+        start += count
     summed = jnp.sum(weights, axis=1) * (gain_rows * gain_rows)[:, None]
     denominator = lax.dot_general(
         summed, ctf_rows * ctf_rows, (((0,), (0,)), ((), ())), precision=HIGHEST
     )
     return (numerator, denominator)
+
+
+def block_rows(images, gains, bins, norms, ref_tile, ctf_table, cosine_table, sine_table):
+    bin_rows = bin_matrix(bins)
+    ctf_rows = jnp.dot(bin_rows, ctf_table, precision=HIGHEST)
+    shifted = shifted_rows(images, ctf_rows, cosine_table, sine_table)
+    scores = tile_scores(shifted, ref_tile, norms, gains, bin_rows)
+    return (shifted, scores, ctf_rows)
 
 
 def per_device(
@@ -191,31 +206,33 @@
     shifts_count = cosine_table.shape[0]
 
     small = n_blk <= 4
+    tables = (ref_tile, ctf_table, cosine_table, sine_table)
     if small:
         packed = pack_rows(particles, group_counts, group_scale, defocus_bin)
-        everyone = shift_gather(packed, "blk", n_blk)
-        images = everyone[:, :width]
-        meta_all = everyone[:, width : width + 5].astype(jnp.float32)
-        gain_all = (meta_all[:, 0] + meta_all[:, 1]) + meta_all[:, 2]
-        live_all = meta_all[:, 3]
-        bins_all = meta_all[:, 4]
-        live_mask = live_all[:batch_size]
+        others = shift_gather(packed, "blk", n_blk)[batch_size:]
+        groups = []
+        for rows in (packed, others):
+            meta = rows[:, width : width + 5].astype(jnp.float32)
+            gains = (meta[:, 0] + meta[:, 1]) + meta[:, 2]
+            groups.append((rows[:, :width], gains, meta[:, 3], meta[:, 4]))
+        live_mask = groups[0][2]
     else:
         gain_rows, live_mask = slot_weights(
             group_counts.reshape(1, -1), group_scale.reshape(1, -1), batch_size
         )
-        images = lax.all_gather(particles, "blk", axis=0, tiled=True)
-        gain_all, bins_all, live_all = (
+        groups = [(
+            lax.all_gather(particles, "blk", axis=0, tiled=True),
             lax.all_gather(gain_rows, "blk", axis=0, tiled=True),
+            lax.all_gather(live_mask, "blk", axis=0, tiled=True),
             lax.all_gather(defocus_bin.astype(jnp.float32), "blk", axis=0, tiled=True),
-            lax.all_gather(live_mask, "blk", axis=0, tiled=True),
-        )
-    whole_count = images.shape[0]
-
-    bin_rows = bin_matrix(bins_all)
-    ctf_rows = jnp.dot(bin_rows, ctf_table, precision=HIGHEST)
-    shifted = shifted_rows(images, ctf_rows, cosine_table, sine_table)
-    all_scores = tile_scores(shifted, ref_tile, own_norms, gain_all, bin_rows)
+        )]
+    results = [block_rows(images, gains, bins, own_norms, *tables) for images, gains, _, bins in groups]
+    pieces = [shifted for shifted, _, _ in results]
+    all_scores = jnp.concatenate([scores for _, scores, _ in results], axis=0)
+    ctf_rows = jnp.concatenate([rows for _, _, rows in results], axis=0)
+    gain_all = jnp.concatenate([group[1] for group in groups])
+    live_all = jnp.concatenate([group[2] for group in groups])
+    whole_count = all_scores.shape[0]
     flattened = all_scores.reshape(whole_count, -1)
     peak_all = jnp.max(flattened, axis=1)
     totals_all = jnp.sum(jnp.exp(flattened - peak_all[:, None]), axis=1)
@@ -244,7 +261,7 @@
         totals = lax.dynamic_slice_in_dim(totals_all, own_offset, batch_size)
 
     numerator, denominator = accumulate(
-        shifted, all_scores, gain_all, ctf_rows, live_all, peak_all, totals_all
+        pieces, all_scores, gain_all, ctf_rows, live_all, peak_all, totals_all
     )
     log_evidence = jnp.where(live_mask > 0.5, peak_score + jnp.log(totals), 0.0)
     denominator = (

time: 38.1 us -> 36.5 us (0.958)
  matrix products: 6.53 us -> 4.56 us
  other arithmetic: 5.61 us -> 6.92 us
  waiting for transfers between devices: 8.84 us -> 7.78 us
    ppermute x3, waiting for transfers between devices: 2.57 us -> 0.01 us  [shift_gather(): lax.ppermute(value, axis, [(i, (i + k) % size) for i in range(size)])]
    ppermute x3, waiting for transfers between devices: 3.28 us -> 4.67 us  [per_device(): lax.ppermute(stats, 'blk', [(i, (i + k) % n_blk) for i in range(n_blk)])]
    dot_general x2 -> x4, matrix products: 2.88 us -> 1.69 us  [the longest x2 1.19 us: accumulate(): lax.dot_general(scaled[start:start + count].reshape(shifted.shape[0], -1)...]
    ppermute x3, starting transfers between devices: 3.77 us -> 2.71 us  [per_device(): lax.ppermute(stats, 'blk', [(i, (i + k) % n_blk) for i in range(n_blk)])]
    dot_general x1, matrix products: 1.38 us -> 0.47 us  [tile_norms(): lax.dot_general(ctf_square, power_sum, (((1,), (1,)), ((), ())), precisio...]
    ppermute x3, starting transfers between devices: 6.06 us -> 6.96 us  [shift_gather(): lax.ppermute(value, axis, [(i, (i + k) % size) for i in range(size)])]
    convert_element_type x1 -> x2, other arithmetic: 0.04 us -> 0.81 us  [shifted_rows(): real_part = images[:, :half_width].astype(jnp.float32)[:, None, :]]
    convert_element_type x2, other arithmetic: 0.01 us -> 0.72 us  [per_device(): meta = rows[:, width:width + 5].astype(jnp.float32)]
  transfers between devices with their start and end apart: 8 -> 8, of which waited for: 5 -> 5; matrix products, arithmetic and copies ran while one was open for 10% -> 13% of each run, Pallas kernels for 0% -> 0%
where the time goes in v5:
time: 36.5 us; the launch traced here: 36.2 us
  starting transfers between devices  11.3 us (31%)
  waiting for transfers between devices  7.78 us (21%)
  other arithmetic  6.92 us (19%)
  matrix products  4.56 us (12%)
  local copies, waits for them, and re-layouts  3.15 us (9%)
  Pallas kernels  1.57 us (4%)
  between operations  0.9 us (2%)
    ppermute x3, starting transfers between devices, shift_gather(): lax.ppermute(value, axis, [(i, (i + k) % size) for i in range(size)])  6.96 us
    ppermute x3, waiting for transfers between devices, per_device(): lax.ppermute(stats, 'blk', [(i, (i + k) % n_blk) for i in range(n_blk)])  4.67 us
    ppermute x2, waiting for transfers between devices, xor_butterfly(): other = lax.ppermute(stats, axis, [(i, i ^ step) for i in range(size)])  3.1 us
    ppermute x3, starting transfers between devices, per_device(): lax.ppermute(stats, 'blk', [(i, (i + k) % n_blk) for i in range(n_blk)])  2.71 us
    unnamed x18, local copies, waits for them, and re-layouts  2.12 us
    ppermute x2, starting transfers between devices, xor_butterfly(): other = lax.ppermute(stats, axis, [(i, i ^ step) for i in range(size)])  1.63 us
    pallas_call x1, Pallas kernels, pack_rows(): pl.pallas_call(pack_kernel, out_shape=jax.ShapeDtypeStruct((slots, width...  1.57 us
    another operation x2, other arithmetic  1.4 us
  transfers between devices with their start and end apart: 8, of which 5 were waited for; matrix products, arithmetic and copies ran while one was open for 13% of the time, Pallas kernels for 0%

profile of v5, /device:TPU:0, one launch (start us, length us, event | category | flops | bytes accessed | tf_op | source)
XLA Modules:
  0.0 36.2 jit_solution(4979101073298147220)
XLA Ops:
  0.6 0.0 copy-start.2
  0.6 0.0 copy-start.3
  0.7 0.0 copy-start.4
  0.7 1.6 %shard_map.104 = bf16[8,4224]{1,0:T(8,128)(2,1)} custom-call(s32[4]{0:T(128)} %sizes_ref.1, f32[4]{0:T(128)} %scales_ref.1, s32[8]{0:T(128)} %bins_ref.1, bf16[8,4096]{1,0:T(8,128)(2,1)} %images_ref.1), custom_call_target="tpu_custom_call" | custom-call | tf_op jit(solution)/shard_map/pallas_call | solution.py:137
  2.2 3.0 %collective-permute-start = (bf16[8,4224]{1,0:T(8,128)(2,1)}, bf16[8,4224]{1,0:T(8,128)(2,1)S(1)}, u32[]{:S(2)}, u32[]{:S(2)}) collective-permute-start(bf16[8,4224]{1,0:T(8,128)(2,1)} %shard_map.104), channel_id=1, source_target_pairs={{0,4},{4,8},{8,12},{12,0},{1,5},{5,9},{9,13},{13,1},{2,6},{6,10},{... | collective-permute-start | bytes 202760 | tf_op jit(solution)/shard_map/ppermute | solution.py:147
  5.3 2.6 %collective-permute-start.1 = (bf16[8,4224]{1,0:T(8,128)(2,1)}, bf16[8,4224]{1,0:T(8,128)(2,1)S(1)}, u32[]{:S(2)}, u32[]{:S(2)}) collective-permute-start(bf16[8,4224]{1,0:T(8,128)(2,1)} %shard_map.104), channel_id=1, source_target_pairs={{0,8},{4,12},{8,0},{12,4},{1,9},{5,13},{9,1},{13,5},{2,10},{6,14},... | collective-permute-start | bytes 202760 | tf_op jit(solution)/shard_map/ppermute | solution.py:147
  7.8 1.3 %collective-permute-start.2 = (bf16[8,4224]{1,0:T(8,128)(2,1)}, bf16[8,4224]{1,0:T(8,128)(2,1)S(1)}, u32[]{:S(2)}, u32[]{:S(2)}) collective-permute-start(bf16[8,4224]{1,0:T(8,128)(2,1)} %shard_map.104), channel_id=1, source_target_pairs={{0,12},{4,0},{8,4},{12,8},{1,13},{5,1},{9,5},{13,9},{2,14},{6,2},{... | collective-permute-start | bytes 202760 | tf_op jit(solution)/shard_map/ppermute | solution.py:147
  9.2 0.7 %slice_convert_fusion.5 = f32[8,5]{1,0:T(8,128)S(1)} fusion(bf16[8,4224]{1,0:T(8,128)(2,1)} %shard_map.104), kind=kLoop, calls=%fused_computation.73 | loop fusion | flops 40 | bytes 240 | tf_op jit(solution)/shard_map/convert_element_type | solution.py:215
  9.9 0.8 %slice_convert_fusion.3 = (f32[8,2048]{1,0:T(8,128)S(1)}, f32[8,2048]{1,0:T(8,128)S(1)}) fusion(bf16[8,4224]{1,0:T(8,128)(2,1)} %shard_map.104), kind=kLoop, calls=%fused_computation.39 | loop fusion | flops 32768 | bytes 196608 | tf_op jit(solution)/shard_map/convert_element_type | solution.py:54
  10.7 0.2 slice_reduce_fusion.3
  10.9 0.0 copy-start.5
  10.9 1.2 %bitcast_convert_fusion = f32[50,4096]{1,0:T(8,128)S(1)} fusion(bf16[1,50,4096]{2,1,0:T(8,128)(2,1)} %param.10), kind=kLoop, calls=%fused_computation.25 | loop fusion | flops 204800 | bytes 1228800 | tf_op jit(solution)/shard_map/convert_element_type | solution.py:65
  12.1 0.0 copy-done.4
  12.1 0.2 fusion.26
  12.3 0.5 %fusion.8 = f32[16,50]{1,0:T(8,128)S(1)} fusion(f32[50,4096]{1,0:T(8,128)S(1)} %bitcast_convert_fusion, f32[16,2048]{1,0:T(8,128)S(1)} %copy-done.4), kind=kOutput, calls=%fused_computation.21 | convolution fusion | flops 20000768 | bytes 953472 | tf_op jit(solution)/shard_map/dot_general | solution.py:70
  12.8 0.2 convolution_multiply_fusion.2
  13.0 0.0 copy-done.2
  13.0 0.0 copy-done.3
  13.0 0.3 multiply_convert_fusion.3
  13.3 0.0 copy-done.5
  13.3 0.4 %fusion.6 = f32[8,16,50]{2,1,0:T(8,128)S(1)} fusion(bf16[8,16,2048]{2,1,0:T(8,128)(2,1)S(1)} %get-tuple-element.21, bf16[8,16,2048]{2,1,0:T(8,128)(2,1)S(1)} %get-tuple-element.20, bf16[1,50,4096]{2,1,0:T(8,128)(2,1)S(1)} %copy-done.5, f32[8,50]{1,0:T(8,128)S(1)} %convolution_multiply_fusion.2, f32[8]{0:T(128)S(1)} %get-tuple-element.10), kind=kOutput, calls=%fused_computation.12 | convolution fusion | flops 54538752 | bytes 1485408 | tf_op jit(solution)/shard_map/dot_general | solution.py:75
  13.8 0.0 collective-permute-done
  13.8 0.0 collective-permute-done.1
  13.8 0.0 collective-permute-done.2
  13.9 0.2 slice_reduce_fusion
  14.1 0.3 fusion.19
  14.4 0.2 convolution_multiply_fusion.1
  14.6 1.1 %multiply_convert_fusion.1 = (bf16[24,16,2048]{2,1,0:T(8,128)(2,1)S(1)}, bf16[24,16,2048]{2,1,0:T(8,128)(2,1)S(1)}) fusion(f32[24,2048]{1,0:T(8,128)S(1)} %fusion.19, f32[16,2048]{1,0:T(8,128)S(1)} %copy-done.2, f32[24,2048]{1,0:T(8,128)S(1)} %get-tuple-element.23, f32[16,2048]{1,0:T(8,128)S(1)} %copy-done.3, f32[24,2048]{1,0:T(8,128)S(1)} %get-tuple-element.22), kind=kLoop, calls=%fused_computation.7 | loop fusion | flops 7864320 | bytes 3997696 | tf_op jit(solution)/shard_map/convert
  15.7 0.0 copy-start
  15.7 0.0 copy-start.6
  15.7 1.0 %fusion.5 = f32[24,16,50]{2,1,0:T(8,128)S(1)} fusion(bf16[24,16,2048]{2,1,0:T(8,128)(2,1)S(1)} %get-tuple-element.19, bf16[24,16,2048]{2,1,0:T(8,128)(2,1)S(1)} %get-tuple-element.18, bf16[1,50,4096]{2,1,0:T(8,128)(2,1)S(1)} %copy-done.5, f32[24,50]{1,0:T(8,128)S(1)} %convolution_multiply_fusion.1, f32[24]{0:T(128)S(1)} %get-tuple-element.7), kind=kOutput, calls=%fused_computation.10 | convolution fusion | flops 163616256 | bytes 3637024 | tf_op jit(solution)/shard_map/dot_general | solution.py:75
  16.7 0.2 copy-done
  16.8 0.3 fusion.15
  17.2 0.5 %exponential_reduce_fusion = f32[32]{0:T(128)S(1)} fusion(f32[24,16,50]{2,1,0:T(8,128)S(1)} %fusion.5, f32[8,16,50]{2,1,0:T(8,128)S(1)} %fusion.6, f32[32]{0:T(128)S(1)} %fusion.15), kind=kLoop, calls=%fused_computation.33 | loop fusion | flops 76768 | bytes 102656 | tf_op jit(solution)/shard_map/reduce_sum | solution.py:238
  17.7 0.1 collective-permute-start.3
  17.8 0.0 copy-done.6
  17.8 1.1 %collective-permute-done.3 = f32[2,32]{1,0:T(2,128)S(1)} collective-permute-done((f32[2,32]{1,0:T(2,128)S(1)}, f32[2,32]{1,0:T(2,128)S(1)}, u32[]{:S(2)}, u32[]{:S(2)}) %collective-permute-start.3) | collective-permute-done | bytes 288 | tf_op jit(solution)/shard_map/ppermute | solution.py:156
  18.9 1.6 %collective-permute-start.4 = (f32[2,32]{1,0:T(2,128)S(1)}, f32[2,32]{1,0:T(2,128)S(1)}, u32[]{:S(2)}, u32[]{:S(2)}) collective-permute-start(f32[2,32]{1,0:T(2,128)S(1)} %pad_maximum_fusion.14), channel_id=1, source_target_pairs={{0,2},{1,3},{2,0},{3,1},{4,6},{5,7},{6,4},{7,5},{8,10},{9,11},{10,... | collective-permute-start | bytes 776 | tf_op jit(solution)/shard_map/ppermute | solution.py:156
  20.5 0.1 fusion.37
  20.5 2.0 %collective-permute-done.4 = f32[2,32]{1,0:T(2,128)S(1)} collective-permute-done((f32[2,32]{1,0:T(2,128)S(1)}, f32[2,32]{1,0:T(2,128)S(1)}, u32[]{:S(2)}, u32[]{:S(2)}) %collective-permute-start.4) | collective-permute-done | bytes 288 | tf_op jit(solution)/shard_map/ppermute | solution.py:156
  22.5 0.5 %broadcast.61 = f32[]{:T(128)} broadcast(f32[]{:T(128)} %constant.17), dimensions={} | broadcast | bytes 8 | tf_op jit(solution)/shard_map/add | solution.py:90
  23.1 0.7 %fusion.34 = (f32[32]{0:T(128)S(1)}, f32[32]{0:T(128)S(1)}, f32[32]{0:T(128)S(1)}, f32[1,32]{1,0:T(1,128)S(1)}) fusion(f32[1,32]{1,0:T(1,128)S(1)} %get-tuple-element.17, f32[2,32]{1,0:T(2,128)S(1)} %collective-permute-done.4, f32[]{:T(128)} %broadcast.61, f32[1,32]{1,0:T(1,128)S(1)} %get-tuple-element.16), kind=kLoop, calls=%fused_computation.92 | loop fusion | flops 192 | bytes 1028 | tf_op jit(solution)/shard_map/max | solution.py:87
  23.7 0.1 stack.45
  23.8 0.1 stack.46
  23.9 2.1 %collective-permute-start.7 = (f32[2,4,8]{2,1,0:T(4,128)S(1)}, f32[2,4,8]{2,1,0:T(4,128)S(1)}, u32[]{:S(2)}, u32[]{:S(2)}) collective-permute-start(f32[2,4,8]{2,1,0:T(4,128)S(1)} %constant_dynamic-update-slice_fusion.3), channel_id=1, source_target_pairs={{0,12},{4,0},{8,4},{12,8},{1,13},{5,1},{9,5},{13,9},{2,14},{6,2},{... | collective-permute-start | bytes 776 | tf_op jit(solution)/shard_map/ppermute | solution.py:244
  26.0 0.1 collective-permute-start.6
  26.1 0.5 %collective-permute-start.5 = (f32[2,4,8]{2,1,0:T(4,128)S(1)}, f32[2,4,8]{2,1,0:T(4,128)S(1)}, u32[]{:S(2)}, u32[]{:S(2)}) collective-permute-start(f32[2,4,8]{2,1,0:T(4,128)S(1)} %constant_dynamic-update-slice_fusion.3), channel_id=1, source_target_pairs={{0,4},{4,8},{8,12},{12,0},{1,5},{5,9},{9,13},{13,1},{2,6},{6,10},{... | collective-permute-start | bytes 776 | tf_op jit(solution)/shard_map/ppermute | solution.py:244
  26.6 0.1 stack.43
  26.7 0.1 stack.42
  26.8 0.7 %collective-permute-done.7 = f32[2,4,8]{2,1,0:T(4,128)S(1)} collective-permute-done((f32[2,4,8]{2,1,0:T(4,128)S(1)}, f32[2,4,8]{2,1,0:T(4,128)S(1)}, u32[]{:S(2)}, u32[]{:S(2)}) %collective-permute-start.7) | collective-permute-done | bytes 288 | tf_op jit(solution)/shard_map/ppermute | solution.py:244
  27.5 3.0 %collective-permute-done.6 = f32[2,4,8]{2,1,0:T(4,128)S(1)} collective-permute-done((f32[2,4,8]{2,1,0:T(4,128)S(1)}, f32[2,4,8]{2,1,0:T(4,128)S(1)}, u32[]{:S(2)}, u32[]{:S(2)}) %collective-permute-start.6) | collective-permute-done | bytes 288 | tf_op jit(solution)/shard_map/ppermute | solution.py:244
  30.5 1.0 %collective-permute-done.5 = f32[2,4,8]{2,1,0:T(4,128)S(1)} collective-permute-done((f32[2,4,8]{2,1,0:T(4,128)S(1)}, f32[2,4,8]{2,1,0:T(4,128)S(1)}, u32[]{:S(2)}, u32[]{:S(2)}) %collective-permute-start.5) | collective-permute-done | bytes 288 | tf_op jit(solution)/shard_map/ppermute | solution.py:244
  31.6 0.1 sub.79
  31.6 0.1 div.13
  31.7 0.5 %compare_select_fusion = f32[8]{0:T(128)} fusion(f32[8]{0:T(128)S(1)} %get-tuple-element.9, f32[4,8]{1,0:T(4,128)S(1)} %fusion.21, f32[4,8]{1,0:T(4,128)S(1)} %slice_reduce_fusion.2), kind=kLoop, calls=%fused_computation.76 | loop fusion | flops 24 | bytes 128 | tf_op jit(solution)/shard_map/jit(_where)/select_n | solution.py:266
  32.3 0.0 copy-start.1
  32.3 0.2 fusion.36
  32.4 0.4 %convolution_bitcast_fusion.1 = f32[50,4096]{1,0:T(8,128)S(1)} fusion(bf16[8,16,2048]{2,1,0:T(8,128)(2,1)S(1)} %get-tuple-element.21, bf16[8,16,2048]{2,1,0:T(8,128)(2,1)S(1)} %get-tuple-element.20, f32[32]{0:T(128)S(1)} %get-tuple-element.13, f32[24,16,50]{2,1,0:T(8,128)S(1)} %fusion.5, f32[8,16,50]{2,1,0:T(8,128)S(1)} %fusion.6, ...), kind=kOutput, calls=%fused_computation.4 | convolution fusion | flops 54679552 | bytes 1970688 | tf_op jit(solution)/shard_map/dot_general | solution.py:173
  32.9 0.6 %fusion.12 = f32[50,2048]{1,0:T(8,128)S(1)} fusion(f32[24,2048]{1,0:T(8,128)S(1)} %fusion.19, f32[8,2048]{1,0:T(8,128)S(1)} %fusion.26, f32[32,50]{1,0:T(8,128)S(1)} %fusion.36, f32[32]{0:T(128)S(1)} %get-tuple-element.12), kind=kOutput, calls=%fused_computation.28 | convolution fusion | flops 39454272 | bytes 678272 | tf_op jit(solution)/shard_map/dot_general | solution.py:182
  33.5 0.2 copy-done.1
  33.7 0.8 %fusion.2 = f32[1,50,4096]{2,1,0:T(8,128)S(1)} fusion(f32[50,4096]{1,0:T(8,128)S(1)} %convolution_bitcast_fusion.1, bf16[24,16,2048]{2,1,0:T(8,128)(2,1)S(1)} %copy-done.1, bf16[24,16,2048]{2,1,0:T(8,128)(2,1)S(1)} %get-tuple-element.18, f32[50,2048]{1,0:T(8,128)S(1)} %fusion.12, f32[4096]{0:T(1024)S(1)} %pad_maximum_fusion.12, ...), kind=kOutput, calls=%fused_computation.3 | convolution fusion | flops 164550656 | bytes 5313024 | tf_op jit(solution)/shard_map/dot_general | solution.py:173
  34.5 1.7 %copy.16 = f32[1,50,4096]{2,0,1:T(1,128)} copy(f32[1,50,4096]{2,1,0:T(8,128)S(1)} %fusion.2) | data formatting | bytes 1638400
  (23 shorter events, 0.2 us)
Async XLA Ops:
  0.6 12.4 %copy-start.2 = (f32[16,2048]{1,0:T(8,128)S(1)}, f32[16,2048]{1,0:T(8,128)}, u32[]{:S(2)}) copy-start(f32[16,2048]{1,0:T(8,128)} %constant.4.clone) | copy-start | bytes 393220
  0.6 12.3 %copy-start.3 = (f32[16,2048]{1,0:T(8,128)S(1)}, f32[16,2048]{1,0:T(8,128)}, u32[]{:S(2)}) copy-start(f32[16,2048]{1,0:T(8,128)} %constant.3.clone) | copy-start | bytes 393220
  0.7 11.4 %copy-start.4 = (f32[16,2048]{1,0:T(8,128)S(1)}, f32[16,2048]{1,0:T(8,128)}, u32[]{:S(2)}) copy-start(f32[16,2048]{1,0:T(8,128)} %param.11) | copy-start | bytes 393220
  2.2 11.5 %collective-permute-start = (bf16[8,4224]{1,0:T(8,128)(2,1)}, bf16[8,4224]{1,0:T(8,128)(2,1)S(1)}, u32[]{:S(2)}, u32[]{:S(2)}) collective-permute-start(bf16[8,4224]{1,0:T(8,128)(2,1)} %shard_map.104), channel_id=1, source_target_pairs={{0,4},{4,8},{8,12},{12,0},{1,5},{5,9},{9,13},{13,1},{2,6},{6,10},{... | collective-permute-start | bytes 202760 | tf_op jit(solution)/shard_map/ppermute | solution.py:147
  5.3 8.5 %collective-permute-start.1 = (bf16[8,4224]{1,0:T(8,128)(2,1)}, bf16[8,4224]{1,0:T(8,128)(2,1)S(1)}, u32[]{:S(2)}, u32[]{:S(2)}) collective-permute-start(bf16[8,4224]{1,0:T(8,128)(2,1)} %shard_map.104), channel_id=1, source_target_pairs={{0,8},{4,12},{8,0},{12,4},{1,9},{5,13},{9,1},{13,5},{2,10},{6,14},... | collective-permute-start | bytes 202760 | tf_op jit(solution)/shard_map/ppermute | solution.py:147
  7.8 6.0 %collective-permute-start.2 = (bf16[8,4224]{1,0:T(8,128)(2,1)}, bf16[8,4224]{1,0:T(8,128)(2,1)S(1)}, u32[]{:S(2)}, u32[]{:S(2)}) collective-permute-start(bf16[8,4224]{1,0:T(8,128)(2,1)} %shard_map.104), channel_id=1, source_target_pairs={{0,12},{4,0},{8,4},{12,8},{1,13},{5,1},{9,5},{13,9},{2,14},{6,2},{... | collective-permute-start | bytes 202760 | tf_op jit(solution)/shard_map/ppermute | solution.py:147
  10.9 2.4 %copy-start.5 = (bf16[1,50,4096]{2,1,0:T(8,128)(2,1)S(1)}, bf16[1,50,4096]{2,1,0:T(8,128)(2,1)}, u32[]{:S(2)}) copy-start(bf16[1,50,4096]{2,1,0:T(8,128)(2,1)} %param.10) | copy-start | bytes 1228804
  15.7 1.2 %copy-start = (bf16[24,16,2048]{2,1,0:T(8,128)(2,1)}, bf16[24,16,2048]{2,1,0:T(8,128)(2,1)S(1)}, u32[]{:S(2)}) copy-start(bf16[24,16,2048]{2,1,0:T(8,128)(2,1)S(1)} %get-tuple-element.19) | copy-start | bytes 4718596
  15.7 2.1 %copy-start.6 = (f32[2048]{0:T(1024)S(1)}, f32[2048]{0:T(1024)}, u32[]{:S(2)}) copy-start(f32[2048]{0:T(1024)} %param.12) | copy-start | bytes 24580
  17.7 1.2 %collective-permute-start.3 = (f32[2,32]{1,0:T(2,128)S(1)}, f32[2,32]{1,0:T(2,128)S(1)}, u32[]{:S(2)}, u32[]{:S(2)}) collective-permute-start(f32[2,32]{1,0:T(2,128)S(1)} %pad_maximum_fusion.13), channel_id=1, source_target_pairs={{0,1},{1,0},{2,3},{3,2},{4,5},{5,4},{6,7},{7,6},{8,9},{9,8},{10,11... | collective-permute-start | bytes 776 | tf_op jit(solution)/shard_map/ppermute | solution.py:156
  18.9 3.6 %collective-permute-start.4 = (f32[2,32]{1,0:T(2,128)S(1)}, f32[2,32]{1,0:T(2,128)S(1)}, u32[]{:S(2)}, u32[]{:S(2)}) collective-permute-start(f32[2,32]{1,0:T(2,128)S(1)} %pad_maximum_fusion.14), channel_id=1, source_target_pairs={{0,2},{1,3},{2,0},{3,1},{4,6},{5,7},{6,4},{7,5},{8,10},{9,11},{10,... | collective-permute-start | bytes 776 | tf_op jit(solution)/shard_map/ppermute | solution.py:156
  23.9 3.6 %collective-permute-start.7 = (f32[2,4,8]{2,1,0:T(4,128)S(1)}, f32[2,4,8]{2,1,0:T(4,128)S(1)}, u32[]{:S(2)}, u32[]{:S(2)}) collective-permute-start(f32[2,4,8]{2,1,0:T(4,128)S(1)} %constant_dynamic-update-slice_fusion.3), channel_id=1, source_target_pairs={{0,12},{4,0},{8,4},{12,8},{1,13},{5,1},{9,5},{13,9},{2,14},{6,2},{... | collective-permute-start | bytes 776 | tf_op jit(solution)/shard_map/ppermute | solution.py:244
  26.0 4.5 %collective-permute-start.6 = (f32[2,4,8]{2,1,0:T(4,128)S(1)}, f32[2,4,8]{2,1,0:T(4,128)S(1)}, u32[]{:S(2)}, u32[]{:S(2)}) collective-permute-start(f32[2,4,8]{2,1,0:T(4,128)S(1)} %constant_dynamic-update-slice_fusion.3), channel_id=1, source_target_pairs={{0,8},{4,12},{8,0},{12,4},{1,9},{5,13},{9,1},{13,5},{2,10},{6,14},... | collective-permute-start | bytes 776 | tf_op jit(solution)/shard_map/ppermute | solution.py:244
  26.1 5.4 %collective-permute-start.5 = (f32[2,4,8]{2,1,0:T(4,128)S(1)}, f32[2,4,8]{2,1,0:T(4,128)S(1)}, u32[]{:S(2)}, u32[]{:S(2)}) collective-permute-start(f32[2,4,8]{2,1,0:T(4,128)S(1)} %constant_dynamic-update-slice_fusion.3), channel_id=1, source_target_pairs={{0,4},{4,8},{8,12},{12,0},{1,5},{5,9},{9,13},{13,1},{2,6},{6,10},{... | collective-permute-start | bytes 776 | tf_op jit(solution)/shard_map/ppermute | solution.py:244
  32.3 1.4 %copy-start.1 = (bf16[24,16,2048]{2,1,0:T(8,128)(2,1)S(1)}, bf16[24,16,2048]{2,1,0:T(8,128)(2,1)}, u32[]{:S(2)}) copy-start(bf16[24,16,2048]{2,1,0:T(8,128)(2,1)} %copy-done) | copy-start | bytes 4718596

commit v6 on v5

--- a/solution.py
+++ b/solution.py
@@ -62,11 +62,9 @@
 
 def tile_norms(ref_rows, ctf_square):
     half_width = ctf_square.shape[1]
-    values = ref_rows.astype(jnp.float32)
-    power_sum = (
-        values[:, :half_width] * values[:, :half_width]
-        + values[:, half_width:] * values[:, half_width:]
-    )
+    real_part = ref_rows[:, :half_width].astype(jnp.float32)
+    imag_part = ref_rows[:, half_width:].astype(jnp.float32)
+    power_sum = real_part * real_part + imag_part * imag_part
     return lax.dot_general(ctf_square, power_sum, (((1,), (1,)), ((), ())), precision=HIGHEST)
 
 
@@ -238,8 +236,8 @@
     totals_all = jnp.sum(jnp.exp(flattened - peak_all[:, None]), axis=1)
 
     if small and n_cls & (n_cls - 1) == 0:
-        stats = xor_butterfly(jnp.stack([peak_all, totals_all]), "cls", n_cls)
-        stats = stats.reshape(2, n_blk, batch_size)
+        stats = jnp.stack([peak_all, totals_all]).reshape(2, n_blk, batch_size)
+        stats = xor_butterfly(stats, "cls", n_cls)
         parts = [stats] + [
             jnp.roll(lax.ppermute(stats, "blk", [(i, (i + k) % n_blk) for i in range(n_blk)]), k, axis=1)
             for k in range(1, n_blk)

time: 36.5 us -> 37.4 us (1.025)
  matrix products: 4.56 us -> 6.59 us
  waiting for transfers between devices: 7.78 us -> 8.63 us
  other arithmetic: 6.92 us -> 6.07 us
  starting transfers between devices: 11.3 us -> 10.7 us
  local copies, waits for them, and re-layouts: 3.15 us -> 2.56 us
    convert_element_type x1 -> x0, other arithmetic: 1.15 us -> none  [tile_norms(): values = ref_rows.astype(jnp.float32)]
    dot_general x1, matrix products: 0.47 us -> 1.6 us  [tile_norms(): lax.dot_general(ctf_square, power_sum, (((1,), (1,)), ((), ())), precisio...]
    another operation x3, other arithmetic: 1.41 us -> 2.38 us
    dot_general x2, matrix products: 0.5 us -> 1.4 us  [block_rows(): ctf_rows = jnp.dot(bin_rows, ctf_table, precision=HIGHEST)]
    ppermute x3, waiting for transfers between devices: 4.67 us -> 5.37 us  [per_device(): lax.ppermute(stats, 'blk', [(i, (i + k) % n_blk) for i in range(n_blk)])]
    max x1, other arithmetic: 0.68 us -> 0.01 us  [combine_stats(): new_peak = jnp.maximum(former[0], latter[0])]
    ppermute x3, starting transfers between devices: 2.71 us -> 2.19 us  [per_device(): lax.ppermute(stats, 'blk', [(i, (i + k) % n_blk) for i in range(n_blk)])]
    add x1 -> x0, local copies, waits for them, and re-layouts: 0.51 us -> none  [combine_stats(): former[1] * jnp.exp(former[0] - new_peak)]
  transfers between devices with their start and end apart: 8 -> 8, of which waited for: 5 -> 5; matrix products, arithmetic and copies ran while one was open for 13% -> 18% of each run, Pallas kernels for 0% -> 0%
where the time goes in v6:
time: 37.4 us; the launch traced here: 37 us
  starting transfers between devices  10.7 us (29%)
  waiting for transfers between devices  8.63 us (23%)
  matrix products  6.59 us (18%)
  other arithmetic  6.07 us (16%)
  local copies, waits for them, and re-layouts  2.56 us (7%)
  Pallas kernels  1.55 us (4%)
  between operations  0.89 us (2%)
    ppermute x3, starting transfers between devices, shift_gather(): lax.ppermute(value, axis, [(i, (i + k) % size) for i in range(size)])  6.96 us
    ppermute x3, waiting for transfers between devices, per_device(): lax.ppermute(stats, 'blk', [(i, (i + k) % n_blk) for i in range(n_blk)])  5.37 us
    ppermute x2, waiting for transfers between devices, xor_butterfly(): other = lax.ppermute(stats, axis, [(i, i ^ step) for i in range(size)])  3.26 us
    another operation x2, other arithmetic  2.37 us
    unnamed x19, local copies, waits for them, and re-layouts  2.2 us
    ppermute x3, starting transfers between devices, per_device(): lax.ppermute(stats, 'blk', [(i, (i + k) % n_blk) for i in range(n_blk)])  2.19 us
    dot_general x1, matrix products, tile_norms(): lax.dot_general(ctf_square, power_sum, (((1,), (1,)), ((), ())), precisio...  1.6 us
    ppermute x2, starting transfers between devices, xor_butterfly(): other = lax.ppermute(stats, axis, [(i, i ^ step) for i in range(size)])  1.58 us
  transfers between devices with their start and end apart: 8, of which 5 were waited for; matrix products, arithmetic and copies ran while one was open for 18% of the time, Pallas kernels for 0%

profile of v6, /device:TPU:0, one launch (start us, length us, event | category | flops | bytes accessed | tf_op | source)
XLA Modules:
  0.0 37.0 jit_solution(949758314897991065)
XLA Ops:
  0.6 0.0 copy-start.6
  0.6 1.6 %shard_map.104 = bf16[8,4224]{1,0:T(8,128)(2,1)} custom-call(s32[4]{0:T(128)} %sizes_ref.1, f32[4]{0:T(128)} %scales_ref.1, s32[8]{0:T(128)} %bins_ref.1, bf16[8,4096]{1,0:T(8,128)(2,1)} %images_ref.1), custom_call_target="tpu_custom_call" | custom-call | tf_op jit(solution)/shard_map/pallas_call | solution.py:135
  2.2 3.0 %collective-permute-start = (bf16[8,4224]{1,0:T(8,128)(2,1)}, bf16[8,4224]{1,0:T(8,128)(2,1)S(1)}, u32[]{:S(2)}, u32[]{:S(2)}) collective-permute-start(bf16[8,4224]{1,0:T(8,128)(2,1)} %shard_map.104), channel_id=1, source_target_pairs={{0,4},{4,8},{8,12},{12,0},{1,5},{5,9},{9,13},{13,1},{2,6},{6,10},{... | collective-permute-start | bytes 202760 | tf_op jit(solution)/shard_map/ppermute | solution.py:145
  5.2 2.6 %collective-permute-start.1 = (bf16[8,4224]{1,0:T(8,128)(2,1)}, bf16[8,4224]{1,0:T(8,128)(2,1)S(1)}, u32[]{:S(2)}, u32[]{:S(2)}) collective-permute-start(bf16[8,4224]{1,0:T(8,128)(2,1)} %shard_map.104), channel_id=1, source_target_pairs={{0,8},{4,12},{8,0},{12,4},{1,9},{5,13},{9,1},{13,5},{2,10},{6,14},... | collective-permute-start | bytes 202760 | tf_op jit(solution)/shard_map/ppermute | solution.py:145
  7.8 1.3 %collective-permute-start.2 = (bf16[8,4224]{1,0:T(8,128)(2,1)}, bf16[8,4224]{1,0:T(8,128)(2,1)S(1)}, u32[]{:S(2)}, u32[]{:S(2)}) collective-permute-start(bf16[8,4224]{1,0:T(8,128)(2,1)} %shard_map.104), channel_id=1, source_target_pairs={{0,12},{4,0},{8,4},{12,8},{1,13},{5,1},{9,5},{13,9},{2,14},{6,2},{... | collective-permute-start | bytes 202760 | tf_op jit(solution)/shard_map/ppermute | solution.py:145
  9.2 0.7 %slice_convert_fusion.5 = f32[8,5]{1,0:T(8,128)S(1)} fusion(bf16[8,4224]{1,0:T(8,128)(2,1)} %shard_map.104), kind=kLoop, calls=%fused_computation.81 | loop fusion | flops 40 | bytes 240 | tf_op jit(solution)/shard_map/convert_element_type | solution.py:213
  9.9 0.8 %slice_convert_fusion.3 = (f32[8,2048]{1,0:T(8,128)S(1)}, f32[8,2048]{1,0:T(8,128)S(1)}) fusion(bf16[8,4224]{1,0:T(8,128)(2,1)} %shard_map.104), kind=kLoop, calls=%fused_computation.42 | loop fusion | flops 32768 | bytes 196608 | tf_op jit(solution)/shard_map/convert_element_type | solution.py:54
  10.7 0.2 slice_reduce_fusion.3
  10.9 1.1 %fusion.31 = f32[8,2048]{1,0:T(8,128)S(1)} fusion(f32[16,2048]{1,0:T(8,128)} %param.11, f32[8]{0:T(128)S(1)} %get-tuple-element.11), kind=kOutput, calls=%fused_computation.74 | convolution fusion | flops 3145856 | bytes 196640 | tf_op jit(solution)/shard_map/dot_general | solution.py:188
  12.0 1.6 %fusion.9 = f32[16,50]{1,0:T(8,128)S(1)} fusion(bf16[50,4096]{1,0:T(8,128)(2,1)} %bitcast.46, f32[16,2048]{1,0:T(8,128)} %param.11), kind=kOutput, calls=%fused_computation.21 | convolution fusion | flops 20205568 | bytes 543872 | tf_op jit(solution)/shard_map/dot_general | solution.py:68
  13.6 0.2 convolution_multiply_fusion.2
  13.8 1.3 %multiply_convert_fusion.3 = (bf16[8,16,2048]{2,1,0:T(8,128)(2,1)S(1)}, bf16[8,16,2048]{2,1,0:T(8,128)(2,1)S(1)}) fusion(f32[8,2048]{1,0:T(8,128)S(1)} %fusion.31, f32[16,2048]{1,0:T(8,128)} %constant.4.clone, f32[8,2048]{1,0:T(8,128)S(1)} %get-tuple-element.23, f32[16,2048]{1,0:T(8,128)} %constant.3.clone, f32[8,2048]{1,0:T(8,128)S(1)} %get-tuple-element.22), kind=kLoop, calls=%fused_computation.17 | loop fusion | flops 2621440 | bytes 1507328 | tf_op jit(solution)/shard_map/convert.2
  15.1 0.0 copy-done.6
  15.1 0.0 copy-start.4
  15.1 0.0 copy-start.2
  15.1 0.0 copy-start.3
  15.2 0.4 %fusion.6 = f32[8,16,50]{2,1,0:T(8,128)S(1)} fusion(bf16[8,16,2048]{2,1,0:T(8,128)(2,1)S(1)} %get-tuple-element.19, bf16[8,16,2048]{2,1,0:T(8,128)(2,1)S(1)} %get-tuple-element.18, bf16[1,50,4096]{2,1,0:T(8,128)(2,1)S(1)} %copy-done.6, f32[8,50]{1,0:T(8,128)S(1)} %convolution_multiply_fusion.2, f32[8]{0:T(128)S(1)} %get-tuple-element.10), kind=kOutput, calls=%fused_computation.12 | convolution fusion | flops 54538752 | bytes 1485408 | tf_op jit(solution)/shard_map/dot_general | solution.py:73
  15.6 0.0 collective-permute-done
  15.6 0.0 collective-permute-done.1
  15.6 0.0 collective-permute-done.2
  15.7 0.2 slice_reduce_fusion
  15.9 0.1 copy-done.4
  16.0 0.3 fusion.24
  16.3 0.2 convolution_multiply_fusion.1
  16.5 0.0 copy-done.2
  16.5 0.0 copy-done.3
  16.5 0.0 copy-start.7
  16.5 1.1 %multiply_convert_fusion.1 = (bf16[24,16,2048]{2,1,0:T(8,128)(2,1)S(1)}, bf16[24,16,2048]{2,1,0:T(8,128)(2,1)S(1)}) fusion(f32[24,2048]{1,0:T(8,128)S(1)} %fusion.24, f32[16,2048]{1,0:T(8,128)S(1)} %copy-done.2, f32[24,2048]{1,0:T(8,128)S(1)} %get-tuple-element.21, f32[16,2048]{1,0:T(8,128)S(1)} %copy-done.3, f32[24,2048]{1,0:T(8,128)S(1)} %get-tuple-element.20), kind=kLoop, calls=%fused_computation.7 | loop fusion | flops 7864320 | bytes 3997696 | tf_op jit(solution)/shard_map/convert
  17.6 0.0 copy-start
  17.6 0.0 copy-done.7
  17.7 0.0 copy-start.5
  17.7 1.0 %fusion.5 = f32[24,16,50]{2,1,0:T(8,128)S(1)} fusion(bf16[24,16,2048]{2,1,0:T(8,128)(2,1)S(1)} %get-tuple-element.17, bf16[24,16,2048]{2,1,0:T(8,128)(2,1)S(1)} %get-tuple-element.16, bf16[1,50,4096]{2,1,0:T(8,128)(2,1)S(1)} %copy-done.7, f32[24,50]{1,0:T(8,128)S(1)} %convolution_multiply_fusion.1, f32[24]{0:T(128)S(1)} %get-tuple-element.7), kind=kOutput, calls=%fused_computation.10 | convolution fusion | flops 163616256 | bytes 3637024 | tf_op jit(solution)/shard_map/dot_general | solution.py:73
  18.6 0.2 copy-done
  18.8 0.3 fusion.20
  19.1 0.5 %exponential_reduce_fusion = f32[32]{0:T(128)S(1)} fusion(f32[24,16,50]{2,1,0:T(8,128)S(1)} %fusion.5, f32[8,16,50]{2,1,0:T(8,128)S(1)} %fusion.6, f32[32]{0:T(128)S(1)} %fusion.20), kind=kLoop, calls=%fused_computation.34 | loop fusion | flops 76768 | bytes 102656 | tf_op jit(solution)/shard_map/reduce_sum | solution.py:236
  19.6 0.1 squeeze.13
  19.7 0.1 stack.32
  19.8 0.0 collective-permute-start.3
  19.8 1.2 %collective-permute-done.3 = f32[2,4,8]{2,1,0:T(4,128)S(1)} collective-permute-done((f32[2,4,8]{2,1,0:T(4,128)S(1)}, f32[2,4,8]{2,1,0:T(4,128)S(1)}, u32[]{:S(2)}, u32[]{:S(2)}) %collective-permute-start.3) | collective-permute-done | bytes 288 | tf_op jit(solution)/shard_map/ppermute | solution.py:154
  21.0 1.6 %collective-permute-start.4 = (f32[2,4,8]{2,1,0:T(4,128)S(1)}, f32[2,4,8]{2,1,0:T(4,128)S(1)}, u32[]{:S(2)}, u32[]{:S(2)}) collective-permute-start(f32[2,4,8]{2,1,0:T(4,128)S(1)} %pad_maximum_fusion.14), channel_id=1, source_target_pairs={{0,2},{1,3},{2,0},{3,1},{4,6},{5,7},{6,4},{7,5},{8,10},{9,11},{10,... | collective-permute-start | bytes 776 | tf_op jit(solution)/shard_map/ppermute | solution.py:154
  22.5 0.0 copy-done.5
  22.5 2.1 %collective-permute-done.4 = f32[2,4,8]{2,1,0:T(4,128)S(1)} collective-permute-done((f32[2,4,8]{2,1,0:T(4,128)S(1)}, f32[2,4,8]{2,1,0:T(4,128)S(1)}, u32[]{:S(2)}, u32[]{:S(2)}) %collective-permute-start.4) | collective-permute-done | bytes 288 | tf_op jit(solution)/shard_map/ppermute | solution.py:154
  24.7 0.5 %collective-permute-start.7 = (f32[2,4,8]{2,1,0:T(4,128)S(1)}, f32[2,4,8]{2,1,0:T(4,128)S(1)}, u32[]{:S(2)}, u32[]{:S(2)}) collective-permute-start(f32[2,4,8]{2,1,0:T(4,128)S(1)} %get-tuple-element.27), channel_id=1, source_target_pairs={{0,12},{4,0},{8,4},{12,8},{1,13},{5,1},{9,5},{13,9},{2,14},{6,2},{... | collective-permute-start | bytes 776 | tf_op jit(solution)/shard_map/ppermute | solution.py:242
  25.2 0.1 fusion.43
  25.3 1.7 %collective-permute-start.6 = (f32[2,4,8]{2,1,0:T(4,128)S(1)}, f32[2,4,8]{2,1,0:T(4,128)S(1)}, u32[]{:S(2)}, u32[]{:S(2)}) collective-permute-start(f32[2,4,8]{2,1,0:T(4,128)S(1)} %get-tuple-element.27), channel_id=1, source_target_pairs={{0,8},{4,12},{8,0},{12,4},{1,9},{5,13},{9,1},{13,5},{2,10},{6,14},... | collective-permute-start | bytes 776 | tf_op jit(solution)/shard_map/ppermute | solution.py:242
  26.9 0.0 collective-permute-start.5
  26.9 1.4 %collective-permute-done.7 = f32[2,4,8]{2,1,0:T(4,128)S(1)} collective-permute-done((f32[2,4,8]{2,1,0:T(4,128)S(1)}, f32[2,4,8]{2,1,0:T(4,128)S(1)}, u32[]{:S(2)}, u32[]{:S(2)}) %collective-permute-start.7) | collective-permute-done | bytes 288 | tf_op jit(solution)/shard_map/ppermute | solution.py:242
  28.3 1.4 %collective-permute-done.6 = f32[2,4,8]{2,1,0:T(4,128)S(1)} collective-permute-done((f32[2,4,8]{2,1,0:T(4,128)S(1)}, f32[2,4,8]{2,1,0:T(4,128)S(1)}, u32[]{:S(2)}, u32[]{:S(2)}) %collective-permute-start.6) | collective-permute-done | bytes 288 | tf_op jit(solution)/shard_map/ppermute | solution.py:242
  29.8 2.6 %collective-permute-done.5 = f32[2,4,8]{2,1,0:T(4,128)S(1)} collective-permute-done((f32[2,4,8]{2,1,0:T(4,128)S(1)}, f32[2,4,8]{2,1,0:T(4,128)S(1)}, u32[]{:S(2)}, u32[]{:S(2)}) %collective-permute-start.5) | collective-permute-done | bytes 288 | tf_op jit(solution)/shard_map/ppermute | solution.py:242
  32.4 0.1 sub.79
  32.5 0.1 div.13
  32.6 0.5 %compare_select_fusion = f32[8]{0:T(128)} fusion(f32[8]{0:T(128)S(1)} %get-tuple-element.9, f32[4,8]{1,0:T(4,128)S(1)} %fusion.26, f32[4,8]{1,0:T(4,128)S(1)} %slice_reduce_fusion.2), kind=kLoop, calls=%fused_computation.84 | loop fusion | flops 24 | bytes 128 | tf_op jit(solution)/shard_map/jit(_where)/select_n | solution.py:264
  33.1 0.0 copy-start.1
  33.1 0.2 fusion.42
  33.3 0.4 %convolution_bitcast_fusion.1 = f32[50,4096]{1,0:T(8,128)S(1)} fusion(bf16[8,16,2048]{2,1,0:T(8,128)(2,1)S(1)} %get-tuple-element.19, bf16[8,16,2048]{2,1,0:T(8,128)(2,1)S(1)} %get-tuple-element.18, f32[32]{0:T(128)S(1)} %get-tuple-element.13, f32[24,16,50]{2,1,0:T(8,128)S(1)} %fusion.5, f32[8,16,50]{2,1,0:T(8,128)S(1)} %fusion.6, ...), kind=kOutput, calls=%fused_computation.4 | convolution fusion | flops 54679552 | bytes 1970688 | tf_op jit(solution)/shard_map/dot_general | solution.py:171
  33.7 0.6 %fusion.15 = f32[50,2048]{1,0:T(8,128)S(1)} fusion(f32[24,2048]{1,0:T(8,128)S(1)} %fusion.24, f32[8,2048]{1,0:T(8,128)S(1)} %fusion.31, f32[32,50]{1,0:T(8,128)S(1)} %fusion.42, f32[32]{0:T(128)S(1)} %get-tuple-element.12), kind=kOutput, calls=%fused_computation.29 | convolution fusion | flops 39454272 | bytes 678272 | tf_op jit(solution)/shard_map/dot_general | solution.py:180
  34.3 0.2 copy-done.1
  34.5 0.8 %fusion.2 = f32[1,50,4096]{2,1,0:T(8,128)S(1)} fusion(f32[50,4096]{1,0:T(8,128)S(1)} %convolution_bitcast_fusion.1, bf16[24,16,2048]{2,1,0:T(8,128)(2,1)S(1)} %copy-done.1, bf16[24,16,2048]{2,1,0:T(8,128)(2,1)S(1)} %get-tuple-element.16, f32[50,2048]{1,0:T(8,128)S(1)} %fusion.15, f32[4096]{0:T(1024)S(1)} %pad_maximum_fusion.12, ...), kind=kOutput, calls=%fused_computation.3 | convolution fusion | flops 164550656 | bytes 5313024 | tf_op jit(solution)/shard_map/dot_general | solution.py:171
  35.3 1.7 %copy.16 = f32[1,50,4096]{2,0,1:T(1,128)} copy(f32[1,50,4096]{2,1,0:T(8,128)S(1)} %fusion.2) | data formatting | bytes 1638400
  (23 shorter events, 0.2 us)
Async XLA Ops:
  0.6 14.5 %copy-start.6 = (bf16[1,50,4096]{2,1,0:T(8,128)(2,1)S(1)}, bf16[1,50,4096]{2,1,0:T(8,128)(2,1)}, u32[]{:S(2)}) copy-start(bf16[1,50,4096]{2,1,0:T(8,128)(2,1)} %param.10) | copy-start | bytes 1228804
  2.2 13.4 %collective-permute-start = (bf16[8,4224]{1,0:T(8,128)(2,1)}, bf16[8,4224]{1,0:T(8,128)(2,1)S(1)}, u32[]{:S(2)}, u32[]{:S(2)}) collective-permute-start(bf16[8,4224]{1,0:T(8,128)(2,1)} %shard_map.104), channel_id=1, source_target_pairs={{0,4},{4,8},{8,12},{12,0},{1,5},{5,9},{9,13},{13,1},{2,6},{6,10},{... | collective-permute-start | bytes 202760 | tf_op jit(solution)/shard_map/ppermute | solution.py:145
  5.2 10.4 %collective-permute-start.1 = (bf16[8,4224]{1,0:T(8,128)(2,1)}, bf16[8,4224]{1,0:T(8,128)(2,1)S(1)}, u32[]{:S(2)}, u32[]{:S(2)}) collective-permute-start(bf16[8,4224]{1,0:T(8,128)(2,1)} %shard_map.104), channel_id=1, source_target_pairs={{0,8},{4,12},{8,0},{12,4},{1,9},{5,13},{9,1},{13,5},{2,10},{6,14},... | collective-permute-start | bytes 202760 | tf_op jit(solution)/shard_map/ppermute | solution.py:145
  7.8 7.8 %collective-permute-start.2 = (bf16[8,4224]{1,0:T(8,128)(2,1)}, bf16[8,4224]{1,0:T(8,128)(2,1)S(1)}, u32[]{:S(2)}, u32[]{:S(2)}) collective-permute-start(bf16[8,4224]{1,0:T(8,128)(2,1)} %shard_map.104), channel_id=1, source_target_pairs={{0,12},{4,0},{8,4},{12,8},{1,13},{5,1},{9,5},{13,9},{2,14},{6,2},{... | collective-permute-start | bytes 202760 | tf_op jit(solution)/shard_map/ppermute | solution.py:145
  15.1 0.9 %copy-start.4 = (f32[16,2048]{1,0:T(8,128)S(1)}, f32[16,2048]{1,0:T(8,128)}, u32[]{:S(2)}) copy-start(f32[16,2048]{1,0:T(8,128)} %param.11) | copy-start | bytes 393220
  15.1 1.4 %copy-start.2 = (f32[16,2048]{1,0:T(8,128)S(1)}, f32[16,2048]{1,0:T(8,128)}, u32[]{:S(2)}) copy-start(f32[16,2048]{1,0:T(8,128)} %constant.4.clone) | copy-start | bytes 393220
  15.1 1.4 %copy-start.3 = (f32[16,2048]{1,0:T(8,128)S(1)}, f32[16,2048]{1,0:T(8,128)}, u32[]{:S(2)}) copy-start(f32[16,2048]{1,0:T(8,128)} %constant.3.clone) | copy-start | bytes 393220
  16.5 1.1 %copy-start.7 = (bf16[1,50,4096]{2,1,0:T(8,128)(2,1)S(1)}, bf16[1,50,4096]{2,1,0:T(8,128)(2,1)}, u32[]{:S(2)}) copy-start(bf16[1,50,4096]{2,1,0:T(8,128)(2,1)} %param.10) | copy-start | bytes 1228804
  17.6 1.2 %copy-start = (bf16[24,16,2048]{2,1,0:T(8,128)(2,1)}, bf16[24,16,2048]{2,1,0:T(8,128)(2,1)S(1)}, u32[]{:S(2)}) copy-start(bf16[24,16,2048]{2,1,0:T(8,128)(2,1)S(1)} %get-tuple-element.17) | copy-start | bytes 4718596
  17.7 4.9 %copy-start.5 = (f32[2048]{0:T(1024)S(1)}, f32[2048]{0:T(1024)}, u32[]{:S(2)}) copy-start(f32[2048]{0:T(1024)} %param.12) | copy-start | bytes 24580
  19.8 1.2 %collective-permute-start.3 = (f32[2,4,8]{2,1,0:T(4,128)S(1)}, f32[2,4,8]{2,1,0:T(4,128)S(1)}, u32[]{:S(2)}, u32[]{:S(2)}) collective-permute-start(f32[2,4,8]{2,1,0:T(4,128)S(1)} %pad_maximum_fusion.13), channel_id=1, source_target_pairs={{0,1},{1,0},{2,3},{3,2},{4,5},{5,4},{6,7},{7,6},{8,9},{9,8},{10,11... | collective-permute-start | bytes 776 | tf_op jit(solution)/shard_map/ppermute | solution.py:154
  21.0 3.7 %collective-permute-start.4 = (f32[2,4,8]{2,1,0:T(4,128)S(1)}, f32[2,4,8]{2,1,0:T(4,128)S(1)}, u32[]{:S(2)}, u32[]{:S(2)}) collective-permute-start(f32[2,4,8]{2,1,0:T(4,128)S(1)} %pad_maximum_fusion.14), channel_id=1, source_target_pairs={{0,2},{1,3},{2,0},{3,1},{4,6},{5,7},{6,4},{7,5},{8,10},{9,11},{10,... | collective-permute-start | bytes 776 | tf_op jit(solution)/shard_map/ppermute | solution.py:154
  24.7 3.7 %collective-permute-start.7 = (f32[2,4,8]{2,1,0:T(4,128)S(1)}, f32[2,4,8]{2,1,0:T(4,128)S(1)}, u32[]{:S(2)}, u32[]{:S(2)}) collective-permute-start(f32[2,4,8]{2,1,0:T(4,128)S(1)} %get-tuple-element.27), channel_id=1, source_target_pairs={{0,12},{4,0},{8,4},{12,8},{1,13},{5,1},{9,5},{13,9},{2,14},{6,2},{... | collective-permute-start | bytes 776 | tf_op jit(solution)/shard_map/ppermute | solution.py:242
  25.3 4.5 %collective-permute-start.6 = (f32[2,4,8]{2,1,0:T(4,128)S(1)}, f32[2,4,8]{2,1,0:T(4,128)S(1)}, u32[]{:S(2)}, u32[]{:S(2)}) collective-permute-start(f32[2,4,8]{2,1,0:T(4,128)S(1)} %get-tuple-element.27), channel_id=1, source_target_pairs={{0,8},{4,12},{8,0},{12,4},{1,9},{5,13},{9,1},{13,5},{2,10},{6,14},... | collective-permute-start | bytes 776 | tf_op jit(solution)/shard_map/ppermute | solution.py:242
  26.9 5.4 %collective-permute-start.5 = (f32[2,4,8]{2,1,0:T(4,128)S(1)}, f32[2,4,8]{2,1,0:T(4,128)S(1)}, u32[]{:S(2)}, u32[]{:S(2)}) collective-permute-start(f32[2,4,8]{2,1,0:T(4,128)S(1)} %get-tuple-element.27), channel_id=1, source_target_pairs={{0,4},{4,8},{8,12},{12,0},{1,5},{5,9},{9,13},{13,1},{2,6},{6,10},{... | collective-permute-start | bytes 776 | tf_op jit(solution)/shard_map/ppermute | solution.py:242
  33.1 1.4 %copy-start.1 = (bf16[24,16,2048]{2,1,0:T(8,128)(2,1)S(1)}, bf16[24,16,2048]{2,1,0:T(8,128)(2,1)}, u32[]{:S(2)}) copy-start(bf16[24,16,2048]{2,1,0:T(8,128)(2,1)} %copy-done) | copy-start | bytes 4718596

commit v7 on v5

--- a/solution.py
+++ b/solution.py
@@ -238,8 +238,8 @@
     totals_all = jnp.sum(jnp.exp(flattened - peak_all[:, None]), axis=1)
 
     if small and n_cls & (n_cls - 1) == 0:
-        stats = xor_butterfly(jnp.stack([peak_all, totals_all]), "cls", n_cls)
-        stats = stats.reshape(2, n_blk, batch_size)
+        stats = jnp.stack([peak_all, totals_all]).reshape(2, n_blk, batch_size)
+        stats = xor_butterfly(stats, "cls", n_cls)
         parts = [stats] + [
             jnp.roll(lax.ppermute(stats, "blk", [(i, (i + k) % n_blk) for i in range(n_blk)]), k, axis=1)
             for k in range(1, n_blk)

time: 36.5 us -> 35.4 us (0.970)
  local copies, waits for them, and re-layouts: 3.15 us -> 2.46 us
  other arithmetic: 6.92 us -> 6.25 us
    max x1, other arithmetic: 0.68 us -> 0.01 us  [combine_stats(): new_peak = jnp.maximum(former[0], latter[0])]
    add x1 -> x0, local copies, waits for them, and re-layouts: 0.51 us -> none  [combine_stats(): former[1] * jnp.exp(former[0] - new_peak)]
    unnamed x18 -> x17, local copies, waits for them, and re-layouts: 2.12 us -> 2.1 us
where the time goes in v7:
time: 35.4 us; the launch traced here: 35.1 us
  starting transfers between devices  11.3 us (32%)
  waiting for transfers between devices  8.14 us (23%)
  other arithmetic  6.25 us (18%)
  matrix products  4.56 us (13%)
  local copies, waits for them, and re-layouts  2.46 us (7%)
  Pallas kernels  1.57 us (4%)
  between operations  0.88 us (2%)
    ppermute x3, starting transfers between devices, shift_gather(): lax.ppermute(value, axis, [(i, (i + k) % size) for i in range(size)])  6.96 us
    ppermute x3, waiting for transfers between devices, per_device(): lax.ppermute(stats, 'blk', [(i, (i + k) % n_blk) for i in range(n_blk)])  4.87 us
    ppermute x2, waiting for transfers between devices, xor_butterfly(): other = lax.ppermute(stats, axis, [(i, i ^ step) for i in range(size)])  3.26 us
    ppermute x3, starting transfers between devices, per_device(): lax.ppermute(stats, 'blk', [(i, (i + k) % n_blk) for i in range(n_blk)])  2.73 us
    unnamed x17, local copies, waits for them, and re-layouts  2.1 us
    ppermute x2, starting transfers between devices, xor_butterfly(): other = lax.ppermute(stats, axis, [(i, i ^ step) for i in range(size)])  1.58 us
    pallas_call x1, Pallas kernels, pack_rows(): pl.pallas_call(pack_kernel, out_shape=jax.ShapeDtypeStruct((slots, width...  1.57 us
    another operation x2, other arithmetic  1.4 us
  transfers between devices with their start and end apart: 8, of which 5 were waited for; matrix products, arithmetic and copies ran while one was open for 13% of the time, Pallas kernels for 0%

profile of v7, /device:TPU:0, one launch (start us, length us, event | category | flops | bytes accessed | tf_op | source)
XLA Modules:
  0.0 35.1 jit_solution(7309413660304980972)
XLA Ops:
  0.6 0.0 copy-start.2
  0.6 0.0 copy-start.3
  0.7 0.0 copy-start.4
  0.7 1.6 %shard_map.104 = bf16[8,4224]{1,0:T(8,128)(2,1)} custom-call(s32[4]{0:T(128)} %sizes_ref.1, f32[4]{0:T(128)} %scales_ref.1, s32[8]{0:T(128)} %bins_ref.1, bf16[8,4096]{1,0:T(8,128)(2,1)} %images_ref.1), custom_call_target="tpu_custom_call" | custom-call | tf_op jit(solution)/shard_map/pallas_call | solution.py:137
  2.2 3.0 %collective-permute-start = (bf16[8,4224]{1,0:T(8,128)(2,1)}, bf16[8,4224]{1,0:T(8,128)(2,1)S(1)}, u32[]{:S(2)}, u32[]{:S(2)}) collective-permute-start(bf16[8,4224]{1,0:T(8,128)(2,1)} %shard_map.104), channel_id=1, source_target_pairs={{0,4},{4,8},{8,12},{12,0},{1,5},{5,9},{9,13},{13,1},{2,6},{6,10},{... | collective-permute-start | bytes 202760 | tf_op jit(solution)/shard_map/ppermute | solution.py:147
  5.3 2.6 %collective-permute-start.1 = (bf16[8,4224]{1,0:T(8,128)(2,1)}, bf16[8,4224]{1,0:T(8,128)(2,1)S(1)}, u32[]{:S(2)}, u32[]{:S(2)}) collective-permute-start(bf16[8,4224]{1,0:T(8,128)(2,1)} %shard_map.104), channel_id=1, source_target_pairs={{0,8},{4,12},{8,0},{12,4},{1,9},{5,13},{9,1},{13,5},{2,10},{6,14},... | collective-permute-start | bytes 202760 | tf_op jit(solution)/shard_map/ppermute | solution.py:147
  7.8 1.3 %collective-permute-start.2 = (bf16[8,4224]{1,0:T(8,128)(2,1)}, bf16[8,4224]{1,0:T(8,128)(2,1)S(1)}, u32[]{:S(2)}, u32[]{:S(2)}) collective-permute-start(bf16[8,4224]{1,0:T(8,128)(2,1)} %shard_map.104), channel_id=1, source_target_pairs={{0,12},{4,0},{8,4},{12,8},{1,13},{5,1},{9,5},{13,9},{2,14},{6,2},{... | collective-permute-start | bytes 202760 | tf_op jit(solution)/shard_map/ppermute | solution.py:147
  9.2 0.7 %slice_convert_fusion.5 = f32[8,5]{1,0:T(8,128)S(1)} fusion(bf16[8,4224]{1,0:T(8,128)(2,1)} %shard_map.104), kind=kLoop, calls=%fused_computation.78 | loop fusion | flops 40 | bytes 240 | tf_op jit(solution)/shard_map/convert_element_type | solution.py:215
  9.9 0.8 %slice_convert_fusion.3 = (f32[8,2048]{1,0:T(8,128)S(1)}, f32[8,2048]{1,0:T(8,128)S(1)}) fusion(bf16[8,4224]{1,0:T(8,128)(2,1)} %shard_map.104), kind=kLoop, calls=%fused_computation.39 | loop fusion | flops 32768 | bytes 196608 | tf_op jit(solution)/shard_map/convert_element_type | solution.py:54
  10.7 0.2 slice_reduce_fusion.3
  10.9 0.0 copy-start.5
  10.9 1.2 %bitcast_convert_fusion = f32[50,4096]{1,0:T(8,128)S(1)} fusion(bf16[1,50,4096]{2,1,0:T(8,128)(2,1)} %param.10), kind=kLoop, calls=%fused_computation.25 | loop fusion | flops 204800 | bytes 1228800 | tf_op jit(solution)/shard_map/convert_element_type | solution.py:65
  12.1 0.0 copy-done.4
  12.1 0.2 fusion.26
  12.3 0.5 %fusion.8 = f32[16,50]{1,0:T(8,128)S(1)} fusion(f32[50,4096]{1,0:T(8,128)S(1)} %bitcast_convert_fusion, f32[16,2048]{1,0:T(8,128)S(1)} %copy-done.4), kind=kOutput, calls=%fused_computation.21 | convolution fusion | flops 20000768 | bytes 953472 | tf_op jit(solution)/shard_map/dot_general | solution.py:70
  12.8 0.2 convolution_multiply_fusion.2
  13.0 0.0 copy-done.2
  13.0 0.0 copy-done.3
  13.0 0.3 multiply_convert_fusion.3
  13.3 0.0 copy-done.5
  13.3 0.4 %fusion.6 = f32[8,16,50]{2,1,0:T(8,128)S(1)} fusion(bf16[8,16,2048]{2,1,0:T(8,128)(2,1)S(1)} %get-tuple-element.19, bf16[8,16,2048]{2,1,0:T(8,128)(2,1)S(1)} %get-tuple-element.18, bf16[1,50,4096]{2,1,0:T(8,128)(2,1)S(1)} %copy-done.5, f32[8,50]{1,0:T(8,128)S(1)} %convolution_multiply_fusion.2, f32[8]{0:T(128)S(1)} %get-tuple-element.10), kind=kOutput, calls=%fused_computation.12 | convolution fusion | flops 54538752 | bytes 1485408 | tf_op jit(solution)/shard_map/dot_general | solution.py:75
  13.8 0.0 collective-permute-done
  13.8 0.0 collective-permute-done.1
  13.8 0.0 collective-permute-done.2
  13.9 0.2 slice_reduce_fusion
  14.1 0.3 fusion.19
  14.4 0.2 convolution_multiply_fusion.1
  14.6 1.1 %multiply_convert_fusion.1 = (bf16[24,16,2048]{2,1,0:T(8,128)(2,1)S(1)}, bf16[24,16,2048]{2,1,0:T(8,128)(2,1)S(1)}) fusion(f32[24,2048]{1,0:T(8,128)S(1)} %fusion.19, f32[16,2048]{1,0:T(8,128)S(1)} %copy-done.2, f32[24,2048]{1,0:T(8,128)S(1)} %get-tuple-element.21, f32[16,2048]{1,0:T(8,128)S(1)} %copy-done.3, f32[24,2048]{1,0:T(8,128)S(1)} %get-tuple-element.20), kind=kLoop, calls=%fused_computation.7 | loop fusion | flops 7864320 | bytes 3997696 | tf_op jit(solution)/shard_map/convert
  15.7 0.0 copy-start
  15.7 0.0 copy-start.6
  15.7 1.0 %fusion.5 = f32[24,16,50]{2,1,0:T(8,128)S(1)} fusion(bf16[24,16,2048]{2,1,0:T(8,128)(2,1)S(1)} %get-tuple-element.17, bf16[24,16,2048]{2,1,0:T(8,128)(2,1)S(1)} %get-tuple-element.16, bf16[1,50,4096]{2,1,0:T(8,128)(2,1)S(1)} %copy-done.5, f32[24,50]{1,0:T(8,128)S(1)} %convolution_multiply_fusion.1, f32[24]{0:T(128)S(1)} %get-tuple-element.7), kind=kOutput, calls=%fused_computation.10 | convolution fusion | flops 163616256 | bytes 3637024 | tf_op jit(solution)/shard_map/dot_general | solution.py:75
  16.7 0.2 copy-done
  16.8 0.3 fusion.15
  17.2 0.5 %exponential_reduce_fusion = f32[32]{0:T(128)S(1)} fusion(f32[24,16,50]{2,1,0:T(8,128)S(1)} %fusion.5, f32[8,16,50]{2,1,0:T(8,128)S(1)} %fusion.6, f32[32]{0:T(128)S(1)} %fusion.15), kind=kLoop, calls=%fused_computation.33 | loop fusion | flops 76768 | bytes 102656 | tf_op jit(solution)/shard_map/reduce_sum | solution.py:238
  17.7 0.1 squeeze.13
  17.7 0.1 stack.32
  17.8 0.0 collective-permute-start.3
  17.9 1.2 %collective-permute-done.3 = f32[2,4,8]{2,1,0:T(4,128)S(1)} collective-permute-done((f32[2,4,8]{2,1,0:T(4,128)S(1)}, f32[2,4,8]{2,1,0:T(4,128)S(1)}, u32[]{:S(2)}, u32[]{:S(2)}) %collective-permute-start.3) | collective-permute-done | bytes 288 | tf_op jit(solution)/shard_map/ppermute | solution.py:156
  19.0 1.6 %collective-permute-start.4 = (f32[2,4,8]{2,1,0:T(4,128)S(1)}, f32[2,4,8]{2,1,0:T(4,128)S(1)}, u32[]{:S(2)}, u32[]{:S(2)}) collective-permute-start(f32[2,4,8]{2,1,0:T(4,128)S(1)} %pad_maximum_fusion.14), channel_id=1, source_target_pairs={{0,2},{1,3},{2,0},{3,1},{4,6},{5,7},{6,4},{7,5},{8,10},{9,11},{10,... | collective-permute-start | bytes 776 | tf_op jit(solution)/shard_map/ppermute | solution.py:156
  20.6 0.0 copy-done.6
  20.6 2.1 %collective-permute-done.4 = f32[2,4,8]{2,1,0:T(4,128)S(1)} collective-permute-done((f32[2,4,8]{2,1,0:T(4,128)S(1)}, f32[2,4,8]{2,1,0:T(4,128)S(1)}, u32[]{:S(2)}, u32[]{:S(2)}) %collective-permute-start.4) | collective-permute-done | bytes 288 | tf_op jit(solution)/shard_map/ppermute | solution.py:156
  22.7 2.1 %collective-permute-start.7 = (f32[2,4,8]{2,1,0:T(4,128)S(1)}, f32[2,4,8]{2,1,0:T(4,128)S(1)}, u32[]{:S(2)}, u32[]{:S(2)}) collective-permute-start(f32[2,4,8]{2,1,0:T(4,128)S(1)} %get-tuple-element.27), channel_id=1, source_target_pairs={{0,12},{4,0},{8,4},{12,8},{1,13},{5,1},{9,5},{13,9},{2,14},{6,2},{... | collective-permute-start | bytes 776 | tf_op jit(solution)/shard_map/ppermute | solution.py:244
  24.9 0.1 fusion.38
  24.9 0.1 collective-permute-start.6
  25.0 0.5 %collective-permute-start.5 = (f32[2,4,8]{2,1,0:T(4,128)S(1)}, f32[2,4,8]{2,1,0:T(4,128)S(1)}, u32[]{:S(2)}, u32[]{:S(2)}) collective-permute-start(f32[2,4,8]{2,1,0:T(4,128)S(1)} %get-tuple-element.27), channel_id=1, source_target_pairs={{0,4},{4,8},{8,12},{12,0},{1,5},{5,9},{9,13},{13,1},{2,6},{6,10},{... | collective-permute-start | bytes 776 | tf_op jit(solution)/shard_map/ppermute | solution.py:244
  25.5 0.9 %collective-permute-done.7 = f32[2,4,8]{2,1,0:T(4,128)S(1)} collective-permute-done((f32[2,4,8]{2,1,0:T(4,128)S(1)}, f32[2,4,8]{2,1,0:T(4,128)S(1)}, u32[]{:S(2)}, u32[]{:S(2)}) %collective-permute-start.7) | collective-permute-done | bytes 288 | tf_op jit(solution)/shard_map/ppermute | solution.py:244
  26.4 3.0 %collective-permute-done.6 = f32[2,4,8]{2,1,0:T(4,128)S(1)} collective-permute-done((f32[2,4,8]{2,1,0:T(4,128)S(1)}, f32[2,4,8]{2,1,0:T(4,128)S(1)}, u32[]{:S(2)}, u32[]{:S(2)}) %collective-permute-start.6) | collective-permute-done | bytes 288 | tf_op jit(solution)/shard_map/ppermute | solution.py:244
  29.5 1.0 %collective-permute-done.5 = f32[2,4,8]{2,1,0:T(4,128)S(1)} collective-permute-done((f32[2,4,8]{2,1,0:T(4,128)S(1)}, f32[2,4,8]{2,1,0:T(4,128)S(1)}, u32[]{:S(2)}, u32[]{:S(2)}) %collective-permute-start.5) | collective-permute-done | bytes 288 | tf_op jit(solution)/shard_map/ppermute | solution.py:244
  30.5 0.1 sub.79
  30.6 0.1 div.13
  30.7 0.5 %compare_select_fusion = f32[8]{0:T(128)} fusion(f32[8]{0:T(128)S(1)} %get-tuple-element.9, f32[4,8]{1,0:T(4,128)S(1)} %fusion.21, f32[4,8]{1,0:T(4,128)S(1)} %slice_reduce_fusion.2), kind=kLoop, calls=%fused_computation.81 | loop fusion | flops 24 | bytes 128 | tf_op jit(solution)/shard_map/jit(_where)/select_n | solution.py:266
  31.2 0.0 copy-start.1
  31.2 0.2 fusion.37
  31.4 0.4 %convolution_bitcast_fusion.1 = f32[50,4096]{1,0:T(8,128)S(1)} fusion(bf16[8,16,2048]{2,1,0:T(8,128)(2,1)S(1)} %get-tuple-element.19, bf16[8,16,2048]{2,1,0:T(8,128)(2,1)S(1)} %get-tuple-element.18, f32[32]{0:T(128)S(1)} %get-tuple-element.13, f32[24,16,50]{2,1,0:T(8,128)S(1)} %fusion.5, f32[8,16,50]{2,1,0:T(8,128)S(1)} %fusion.6, ...), kind=kOutput, calls=%fused_computation.4 | convolution fusion | flops 54679552 | bytes 1970688 | tf_op jit(solution)/shard_map/dot_general | solution.py:173
  31.8 0.6 %fusion.12 = f32[50,2048]{1,0:T(8,128)S(1)} fusion(f32[24,2048]{1,0:T(8,128)S(1)} %fusion.19, f32[8,2048]{1,0:T(8,128)S(1)} %fusion.26, f32[32,50]{1,0:T(8,128)S(1)} %fusion.37, f32[32]{0:T(128)S(1)} %get-tuple-element.12), kind=kOutput, calls=%fused_computation.28 | convolution fusion | flops 39454272 | bytes 678272 | tf_op jit(solution)/shard_map/dot_general | solution.py:182
  32.5 0.2 copy-done.1
  32.6 0.8 %fusion.2 = f32[1,50,4096]{2,1,0:T(8,128)S(1)} fusion(f32[50,4096]{1,0:T(8,128)S(1)} %convolution_bitcast_fusion.1, bf16[24,16,2048]{2,1,0:T(8,128)(2,1)S(1)} %copy-done.1, bf16[24,16,2048]{2,1,0:T(8,128)(2,1)S(1)} %get-tuple-element.16, f32[50,2048]{1,0:T(8,128)S(1)} %fusion.12, f32[4096]{0:T(1024)S(1)} %pad_maximum_fusion.12, ...), kind=kOutput, calls=%fused_computation.3 | convolution fusion | flops 164550656 | bytes 5313024 | tf_op jit(solution)/shard_map/dot_general | solution.py:173
  33.4 1.7 %copy.16 = f32[1,50,4096]{2,0,1:T(1,128)} copy(f32[1,50,4096]{2,1,0:T(8,128)S(1)} %fusion.2) | data formatting | bytes 1638400
  (23 shorter events, 0.2 us)
Async XLA Ops:
  0.6 12.4 %copy-start.2 = (f32[16,2048]{1,0:T(8,128)S(1)}, f32[16,2048]{1,0:T(8,128)}, u32[]{:S(2)}) copy-start(f32[16,2048]{1,0:T(8,128)} %constant.4.clone) | copy-start | bytes 393220
  0.6 12.3 %copy-start.3 = (f32[16,2048]{1,0:T(8,128)S(1)}, f32[16,2048]{1,0:T(8,128)}, u32[]{:S(2)}) copy-start(f32[16,2048]{1,0:T(8,128)} %constant.3.clone) | copy-start | bytes 393220
  0.7 11.4 %copy-start.4 = (f32[16,2048]{1,0:T(8,128)S(1)}, f32[16,2048]{1,0:T(8,128)}, u32[]{:S(2)}) copy-start(f32[16,2048]{1,0:T(8,128)} %param.11) | copy-start | bytes 393220
  2.2 11.5 %collective-permute-start = (bf16[8,4224]{1,0:T(8,128)(2,1)}, bf16[8,4224]{1,0:T(8,128)(2,1)S(1)}, u32[]{:S(2)}, u32[]{:S(2)}) collective-permute-start(bf16[8,4224]{1,0:T(8,128)(2,1)} %shard_map.104), channel_id=1, source_target_pairs={{0,4},{4,8},{8,12},{12,0},{1,5},{5,9},{9,13},{13,1},{2,6},{6,10},{... | collective-permute-start | bytes 202760 | tf_op jit(solution)/shard_map/ppermute | solution.py:147
  5.3 8.5 %collective-permute-start.1 = (bf16[8,4224]{1,0:T(8,128)(2,1)}, bf16[8,4224]{1,0:T(8,128)(2,1)S(1)}, u32[]{:S(2)}, u32[]{:S(2)}) collective-permute-start(bf16[8,4224]{1,0:T(8,128)(2,1)} %shard_map.104), channel_id=1, source_target_pairs={{0,8},{4,12},{8,0},{12,4},{1,9},{5,13},{9,1},{13,5},{2,10},{6,14},... | collective-permute-start | bytes 202760 | tf_op jit(solution)/shard_map/ppermute | solution.py:147
  7.8 6.0 %collective-permute-start.2 = (bf16[8,4224]{1,0:T(8,128)(2,1)}, bf16[8,4224]{1,0:T(8,128)(2,1)S(1)}, u32[]{:S(2)}, u32[]{:S(2)}) collective-permute-start(bf16[8,4224]{1,0:T(8,128)(2,1)} %shard_map.104), channel_id=1, source_target_pairs={{0,12},{4,0},{8,4},{12,8},{1,13},{5,1},{9,5},{13,9},{2,14},{6,2},{... | collective-permute-start | bytes 202760 | tf_op jit(solution)/shard_map/ppermute | solution.py:147
  10.9 2.4 %copy-start.5 = (bf16[1,50,4096]{2,1,0:T(8,128)(2,1)S(1)}, bf16[1,50,4096]{2,1,0:T(8,128)(2,1)}, u32[]{:S(2)}) copy-start(bf16[1,50,4096]{2,1,0:T(8,128)(2,1)} %param.10) | copy-start | bytes 1228804
  15.7 1.2 %copy-start = (bf16[24,16,2048]{2,1,0:T(8,128)(2,1)}, bf16[24,16,2048]{2,1,0:T(8,128)(2,1)S(1)}, u32[]{:S(2)}) copy-start(bf16[24,16,2048]{2,1,0:T(8,128)(2,1)S(1)} %get-tuple-element.17) | copy-start | bytes 4718596
  15.7 4.9 %copy-start.6 = (f32[2048]{0:T(1024)S(1)}, f32[2048]{0:T(1024)}, u32[]{:S(2)}) copy-start(f32[2048]{0:T(1024)} %param.12) | copy-start | bytes 24580
  17.8 1.2 %collective-permute-start.3 = (f32[2,4,8]{2,1,0:T(4,128)S(1)}, f32[2,4,8]{2,1,0:T(4,128)S(1)}, u32[]{:S(2)}, u32[]{:S(2)}) collective-permute-start(f32[2,4,8]{2,1,0:T(4,128)S(1)} %pad_maximum_fusion.13), channel_id=1, source_target_pairs={{0,1},{1,0},{2,3},{3,2},{4,5},{5,4},{6,7},{7,6},{8,9},{9,8},{10,11... | collective-permute-start | bytes 776 | tf_op jit(solution)/shard_map/ppermute | solution.py:156
  19.0 3.7 %collective-permute-start.4 = (f32[2,4,8]{2,1,0:T(4,128)S(1)}, f32[2,4,8]{2,1,0:T(4,128)S(1)}, u32[]{:S(2)}, u32[]{:S(2)}) collective-permute-start(f32[2,4,8]{2,1,0:T(4,128)S(1)} %pad_maximum_fusion.14), channel_id=1, source_target_pairs={{0,2},{1,3},{2,0},{3,1},{4,6},{5,7},{6,4},{7,5},{8,10},{9,11},{10,... | collective-permute-start | bytes 776 | tf_op jit(solution)/shard_map/ppermute | solution.py:156
  22.7 3.7 %collective-permute-start.7 = (f32[2,4,8]{2,1,0:T(4,128)S(1)}, f32[2,4,8]{2,1,0:T(4,128)S(1)}, u32[]{:S(2)}, u32[]{:S(2)}) collective-permute-start(f32[2,4,8]{2,1,0:T(4,128)S(1)} %get-tuple-element.27), channel_id=1, source_target_pairs={{0,12},{4,0},{8,4},{12,8},{1,13},{5,1},{9,5},{13,9},{2,14},{6,2},{... | collective-permute-start | bytes 776 | tf_op jit(solution)/shard_map/ppermute | solution.py:244
  24.9 4.5 %collective-permute-start.6 = (f32[2,4,8]{2,1,0:T(4,128)S(1)}, f32[2,4,8]{2,1,0:T(4,128)S(1)}, u32[]{:S(2)}, u32[]{:S(2)}) collective-permute-start(f32[2,4,8]{2,1,0:T(4,128)S(1)} %get-tuple-element.27), channel_id=1, source_target_pairs={{0,8},{4,12},{8,0},{12,4},{1,9},{5,13},{9,1},{13,5},{2,10},{6,14},... | collective-permute-start | bytes 776 | tf_op jit(solution)/shard_map/ppermute | solution.py:244
  25.0 5.4 %collective-permute-start.5 = (f32[2,4,8]{2,1,0:T(4,128)S(1)}, f32[2,4,8]{2,1,0:T(4,128)S(1)}, u32[]{:S(2)}, u32[]{:S(2)}) collective-permute-start(f32[2,4,8]{2,1,0:T(4,128)S(1)} %get-tuple-element.27), channel_id=1, source_target_pairs={{0,4},{4,8},{8,12},{12,0},{1,5},{5,9},{9,13},{13,1},{2,6},{6,10},{... | collective-permute-start | bytes 776 | tf_op jit(solution)/shard_map/ppermute | solution.py:244
  31.2 1.4 %copy-start.1 = (bf16[24,16,2048]{2,1,0:T(8,128)(2,1)S(1)}, bf16[24,16,2048]{2,1,0:T(8,128)(2,1)}, u32[]{:S(2)}) copy-start(bf16[24,16,2048]{2,1,0:T(8,128)(2,1)} %copy-done) | copy-start | bytes 4718596

commit v8 on v7

--- a/solution.py
+++ b/solution.py
@@ -142,12 +142,18 @@
     )(group_counts, group_scale, defocus_bin, particles)
 
 
-def shift_gather(value, axis, size):
+def xor_gather(value, axis, size):
     pieces = [value] + [
-        lax.ppermute(value, axis, [(i, (i + k) % size) for i in range(size)])
-        for k in range(1, size)
+        lax.ppermute(value, axis, [(i, i ^ k) for i in range(size)]) for k in range(1, size)
     ]
     return jnp.concatenate(pieces, axis=0)
+
+
+def xor_reorder(value, step, axis):
+    return jnp.concatenate(
+        [lax.slice_in_dim(value, j ^ step, (j ^ step) + 1, axis=axis) for j in range(value.shape[axis])],
+        axis=axis,
+    )
 
 
 def xor_butterfly(stats, axis, size):
@@ -205,11 +211,11 @@
     classes_here = ref_tile.shape[0]
     shifts_count = cosine_table.shape[0]
 
-    small = n_blk <= 4
+    small = n_blk <= 4 and n_blk & (n_blk - 1) == 0 and n_cls & (n_cls - 1) == 0
     tables = (ref_tile, ctf_table, cosine_table, sine_table)
     if small:
         packed = pack_rows(particles, group_counts, group_scale, defocus_bin)
-        others = shift_gather(packed, "blk", n_blk)[batch_size:]
+        others = xor_gather(packed, "blk", n_blk)[batch_size:]
         groups = []
         for rows in (packed, others):
             meta = rows[:, width : width + 5].astype(jnp.float32)
@@ -237,11 +243,11 @@
     peak_all = jnp.max(flattened, axis=1)
     totals_all = jnp.sum(jnp.exp(flattened - peak_all[:, None]), axis=1)
 
-    if small and n_cls & (n_cls - 1) == 0:
+    if small:
         stats = jnp.stack([peak_all, totals_all]).reshape(2, n_blk, batch_size)
         stats = xor_butterfly(stats, "cls", n_cls)
         parts = [stats] + [
-            jnp.roll(lax.ppermute(stats, "blk", [(i, (i + k) % n_blk) for i in range(n_blk)]), k, axis=1)
+            xor_reorder(lax.ppermute(stats, "blk", [(i, i ^ k) for i in range(n_blk)]), k, 1)
             for k in range(1, n_blk)
         ]
         parts = jnp.stack(parts)
@@ -253,10 +259,7 @@
     else:
         gathered = lax.all_gather(jnp.stack([peak_all, totals_all]), ("blk", "cls"))
         peak_all, totals_all = combine_many(gathered[:, 0], gathered[:, 1])
-        if small:
-            own_offset = 0
-        else:
-            own_offset = lax.axis_index("blk") * batch_size
+        own_offset = lax.axis_index("blk") * batch_size
         peak_score = lax.dynamic_slice_in_dim(peak_all, own_offset, batch_size)
         totals = lax.dynamic_slice_in_dim(totals_all, own_offset, batch_size)
 

time: 35.4 us -> 35 us (0.989)
  waiting for transfers between devices: 8.14 us -> 7.34 us
    ppermute x6, waiting for transfers between devices: 4.88 us -> 4.07 us  [the longest x3 2.3 us: per_device(): lax.ppermute(stats, 'blk', [(i, i ^ k) for i in range(n_blk)])]
    ppermute x6, starting transfers between devices: 9.69 us -> 10.1 us  [the longest x3 5.62 us: xor_gather(): lax.ppermute(value, axis, [(i, i ^ k) for i in range(size)])]
  transfers between devices with their start and end apart: 8 -> 8, of which waited for: 5 -> 7; matrix products, arithmetic and copies ran while one was open for 13% -> 13% of each run, Pallas kernels for 0% -> 0%
where the time goes in v8:
time: 35 us; the launch traced here: 34.7 us
  starting transfers between devices  11.6 us (33%)
  waiting for transfers between devices  7.34 us (21%)
  other arithmetic  6.28 us (18%)
  matrix products  4.56 us (13%)
  local copies, waits for them, and re-layouts  2.46 us (7%)
  Pallas kernels  1.57 us (4%)
  between operations  0.86 us (2%)
    ppermute x3, starting transfers between devices, xor_gather(): lax.ppermute(value, axis, [(i, i ^ k) for i in range(size)])  5.62 us
    ppermute x3, starting transfers between devices, per_device(): lax.ppermute(stats, 'blk', [(i, i ^ k) for i in range(n_blk)])  4.45 us
    ppermute x2, waiting for transfers between devices, xor_butterfly(): other = lax.ppermute(stats, axis, [(i, i ^ step) for i in range(size)])  3.26 us
    ppermute x3, waiting for transfers between devices, per_device(): lax.ppermute(stats, 'blk', [(i, i ^ k) for i in range(n_blk)])  2.3 us
    unnamed x17, local copies, waits for them, and re-layouts  2.11 us
    ppermute x3, waiting for transfers between devices, xor_gather(): lax.ppermute(value, axis, [(i, i ^ k) for i in range(size)])  1.77 us
    ppermute x2, starting transfers between devices, xor_butterfly(): other = lax.ppermute(stats, axis, [(i, i ^ step) for i in range(size)])  1.58 us
    pallas_call x1, Pallas kernels, pack_rows(): pl.pallas_call(pack_kernel, out_shape=jax.ShapeDtypeStruct((slots, width...  1.57 us
  transfers between devices with their start and end apart: 8, of which 7 were waited for; matrix products, arithmetic and copies ran while one was open for 13% of the time, Pallas kernels for 0%

profile of v8, /device:TPU:0, one launch (start us, length us, event | category | flops | bytes accessed | tf_op | source)
XLA Modules:
  0.0 34.7 jit_solution(11805641153627161268)
XLA Ops:
  0.6 0.0 copy-start.2
  0.6 0.0 copy-start.3
  0.7 0.0 copy-start.4
  0.7 1.6 %shard_map.104 = bf16[8,4224]{1,0:T(8,128)(2,1)} custom-call(s32[4]{0:T(128)} %sizes_ref.1, f32[4]{0:T(128)} %scales_ref.1, s32[8]{0:T(128)} %bins_ref.1, bf16[8,4096]{1,0:T(8,128)(2,1)} %images_ref.1), custom_call_target="tpu_custom_call" | custom-call | tf_op jit(solution)/shard_map/pallas_call | solution.py:137
  2.2 3.0 %collective-permute-start = (bf16[8,4224]{1,0:T(8,128)(2,1)}, bf16[8,4224]{1,0:T(8,128)(2,1)S(1)}, u32[]{:S(2)}, u32[]{:S(2)}) collective-permute-start(bf16[8,4224]{1,0:T(8,128)(2,1)} %shard_map.104), channel_id=1, source_target_pairs={{0,4},{4,0},{8,12},{12,8},{1,5},{5,1},{9,13},{13,9},{2,6},{6,2},{1... | collective-permute-start | bytes 202760 | tf_op jit(solution)/shard_map/ppermute | solution.py:147
  5.3 2.6 %collective-permute-start.1 = (bf16[8,4224]{1,0:T(8,128)(2,1)}, bf16[8,4224]{1,0:T(8,128)(2,1)S(1)}, u32[]{:S(2)}, u32[]{:S(2)}) collective-permute-start(bf16[8,4224]{1,0:T(8,128)(2,1)} %shard_map.104), channel_id=1, source_target_pairs={{0,8},{4,12},{8,0},{12,4},{1,9},{5,13},{9,1},{13,5},{2,10},{6,14},... | collective-permute-start | bytes 202760 | tf_op jit(solution)/shard_map/ppermute | solution.py:147
  7.8 0.0 collective-permute-start.2
  7.8 0.7 %slice_convert_fusion.5 = f32[8,5]{1,0:T(8,128)S(1)} fusion(bf16[8,4224]{1,0:T(8,128)(2,1)} %shard_map.104), kind=kLoop, calls=%fused_computation.78 | loop fusion | flops 40 | bytes 240 | tf_op jit(solution)/shard_map/convert_element_type | solution.py:221
  8.6 0.8 %slice_convert_fusion.3 = (f32[8,2048]{1,0:T(8,128)S(1)}, f32[8,2048]{1,0:T(8,128)S(1)}) fusion(bf16[8,4224]{1,0:T(8,128)(2,1)} %shard_map.104), kind=kLoop, calls=%fused_computation.39 | loop fusion | flops 32768 | bytes 196608 | tf_op jit(solution)/shard_map/convert_element_type | solution.py:54
  9.4 0.2 slice_reduce_fusion.3
  9.6 0.0 copy-start.5
  9.6 1.2 %bitcast_convert_fusion = f32[50,4096]{1,0:T(8,128)S(1)} fusion(bf16[1,50,4096]{2,1,0:T(8,128)(2,1)} %param.10), kind=kLoop, calls=%fused_computation.25 | loop fusion | flops 204800 | bytes 1228800 | tf_op jit(solution)/shard_map/convert_element_type | solution.py:65
  10.8 0.0 copy-done.4
  10.8 0.2 fusion.26
  11.0 0.5 %fusion.8 = f32[16,50]{1,0:T(8,128)S(1)} fusion(f32[50,4096]{1,0:T(8,128)S(1)} %bitcast_convert_fusion, f32[16,2048]{1,0:T(8,128)S(1)} %copy-done.4), kind=kOutput, calls=%fused_computation.21 | convolution fusion | flops 20000768 | bytes 953472 | tf_op jit(solution)/shard_map/dot_general | solution.py:70
  11.5 0.2 convolution_multiply_fusion.2
  11.7 0.0 copy-done.2
  11.7 0.0 copy-done.3
  11.7 0.3 multiply_convert_fusion.3
  12.0 0.0 copy-done.5
  12.0 0.4 %fusion.6 = f32[8,16,50]{2,1,0:T(8,128)S(1)} fusion(bf16[8,16,2048]{2,1,0:T(8,128)(2,1)S(1)} %get-tuple-element.19, bf16[8,16,2048]{2,1,0:T(8,128)(2,1)S(1)} %get-tuple-element.18, bf16[1,50,4096]{2,1,0:T(8,128)(2,1)S(1)} %copy-done.5, f32[8,50]{1,0:T(8,128)S(1)} %convolution_multiply_fusion.2, f32[8]{0:T(128)S(1)} %get-tuple-element.10), kind=kOutput, calls=%fused_computation.12 | convolution fusion | flops 54538752 | bytes 1485408 | tf_op jit(solution)/shard_map/dot_general | solution.py:75
  12.4 0.0 collective-permute-done
  12.5 0.4 %collective-permute-done.1 = bf16[8,4224]{1,0:T(8,128)(2,1)S(1)} collective-permute-done((bf16[8,4224]{1,0:T(8,128)(2,1)}, bf16[8,4224]{1,0:T(8,128)(2,1)S(1)}, u32[]{:S(2)}, u32[]{:S(2)}) %collective-permute-start.1) | collective-permute-done | bytes 67616 | tf_op jit(solution)/shard_map/ppermute | solution.py:147
  12.9 1.4 %collective-permute-done.2 = bf16[8,4224]{1,0:T(8,128)(2,1)S(1)} collective-permute-done((bf16[8,4224]{1,0:T(8,128)(2,1)}, bf16[8,4224]{1,0:T(8,128)(2,1)S(1)}, u32[]{:S(2)}, u32[]{:S(2)}) %collective-permute-start.2) | collective-permute-done | bytes 67616 | tf_op jit(solution)/shard_map/ppermute | solution.py:147
  14.3 0.2 slice_reduce_fusion
  14.5 0.3 fusion.19
  14.8 0.2 convolution_multiply_fusion.1
  15.0 1.1 %multiply_convert_fusion.1 = (bf16[24,16,2048]{2,1,0:T(8,128)(2,1)S(1)}, bf16[24,16,2048]{2,1,0:T(8,128)(2,1)S(1)}) fusion(f32[24,2048]{1,0:T(8,128)S(1)} %fusion.19, f32[16,2048]{1,0:T(8,128)S(1)} %copy-done.2, f32[24,2048]{1,0:T(8,128)S(1)} %get-tuple-element.21, f32[16,2048]{1,0:T(8,128)S(1)} %copy-done.3, f32[24,2048]{1,0:T(8,128)S(1)} %get-tuple-element.20), kind=kLoop, calls=%fused_computation.7 | loop fusion | flops 7864320 | bytes 3997696 | tf_op jit(solution)/shard_map/convert
  16.1 0.0 copy-start
  16.1 0.0 copy-start.6
  16.1 1.0 %fusion.5 = f32[24,16,50]{2,1,0:T(8,128)S(1)} fusion(bf16[24,16,2048]{2,1,0:T(8,128)(2,1)S(1)} %get-tuple-element.17, bf16[24,16,2048]{2,1,0:T(8,128)(2,1)S(1)} %get-tuple-element.16, bf16[1,50,4096]{2,1,0:T(8,128)(2,1)S(1)} %copy-done.5, f32[24,50]{1,0:T(8,128)S(1)} %convolution_multiply_fusion.1, f32[24]{0:T(128)S(1)} %get-tuple-element.7), kind=kOutput, calls=%fused_computation.10 | convolution fusion | flops 163616256 | bytes 3637024 | tf_op jit(solution)/shard_map/dot_general | solution.py:75
  17.1 0.2 copy-done
  17.3 0.3 fusion.15
  17.6 0.5 %exponential_reduce_fusion = f32[32]{0:T(128)S(1)} fusion(f32[24,16,50]{2,1,0:T(8,128)S(1)} %fusion.5, f32[8,16,50]{2,1,0:T(8,128)S(1)} %fusion.6, f32[32]{0:T(128)S(1)} %fusion.15), kind=kLoop, calls=%fused_computation.33 | loop fusion | flops 76768 | bytes 102656 | tf_op jit(solution)/shard_map/reduce_sum | solution.py:244
  18.1 0.1 squeeze.13
  18.2 0.1 stack.32
  18.3 0.0 collective-permute-start.3
  18.3 1.2 %collective-permute-done.3 = f32[2,4,8]{2,1,0:T(4,128)S(1)} collective-permute-done((f32[2,4,8]{2,1,0:T(4,128)S(1)}, f32[2,4,8]{2,1,0:T(4,128)S(1)}, u32[]{:S(2)}, u32[]{:S(2)}) %collective-permute-start.3) | collective-permute-done | bytes 288 | tf_op jit(solution)/shard_map/ppermute | solution.py:162
  19.5 1.6 %collective-permute-start.4 = (f32[2,4,8]{2,1,0:T(4,128)S(1)}, f32[2,4,8]{2,1,0:T(4,128)S(1)}, u32[]{:S(2)}, u32[]{:S(2)}) collective-permute-start(f32[2,4,8]{2,1,0:T(4,128)S(1)} %pad_maximum_fusion.14), channel_id=1, source_target_pairs={{0,2},{1,3},{2,0},{3,1},{4,6},{5,7},{6,4},{7,5},{8,10},{9,11},{10,... | collective-permute-start | bytes 776 | tf_op jit(solution)/shard_map/ppermute | solution.py:162
  21.0 0.0 copy-done.6
  21.0 2.1 %collective-permute-done.4 = f32[2,4,8]{2,1,0:T(4,128)S(1)} collective-permute-done((f32[2,4,8]{2,1,0:T(4,128)S(1)}, f32[2,4,8]{2,1,0:T(4,128)S(1)}, u32[]{:S(2)}, u32[]{:S(2)}) %collective-permute-start.4) | collective-permute-done | bytes 288 | tf_op jit(solution)/shard_map/ppermute | solution.py:162
  23.1 2.1 %collective-permute-start.7 = (f32[2,4,8]{2,1,0:T(4,128)S(1)}, f32[2,4,8]{2,1,0:T(4,128)S(1)}, u32[]{:S(2)}, u32[]{:S(2)}) collective-permute-start(f32[2,4,8]{2,1,0:T(4,128)S(1)} %get-tuple-element.27), channel_id=1, source_target_pairs={{0,12},{4,8},{8,4},{12,0},{1,13},{5,9},{9,5},{13,1},{2,14},{6,10},... | collective-permute-start | bytes 776 | tf_op jit(solution)/shard_map/ppermute | solution.py:250
  25.3 0.1 fusion.38
  25.3 0.2 collective-permute-start.5
  25.5 2.2 %collective-permute-start.6 = (f32[2,4,8]{2,1,0:T(4,128)S(1)}, f32[2,4,8]{2,1,0:T(4,128)S(1)}, u32[]{:S(2)}, u32[]{:S(2)}) collective-permute-start(f32[2,4,8]{2,1,0:T(4,128)S(1)} %get-tuple-element.27), channel_id=1, source_target_pairs={{0,8},{4,12},{8,0},{12,4},{1,9},{5,13},{9,1},{13,5},{2,10},{6,14},... | collective-permute-start | bytes 776 | tf_op jit(solution)/shard_map/ppermute | solution.py:250
  27.7 0.9 %collective-permute-done.7 = f32[2,4,8]{2,1,0:T(4,128)S(1)} collective-permute-done((f32[2,4,8]{2,1,0:T(4,128)S(1)}, f32[2,4,8]{2,1,0:T(4,128)S(1)}, u32[]{:S(2)}, u32[]{:S(2)}) %collective-permute-start.7) | collective-permute-done | bytes 288 | tf_op jit(solution)/shard_map/ppermute | solution.py:250
  28.6 0.3 collective-permute-done.5
  29.0 1.0 %collective-permute-done.6 = f32[2,4,8]{2,1,0:T(4,128)S(1)} collective-permute-done((f32[2,4,8]{2,1,0:T(4,128)S(1)}, f32[2,4,8]{2,1,0:T(4,128)S(1)}, u32[]{:S(2)}, u32[]{:S(2)}) %collective-permute-start.6) | collective-permute-done | bytes 288 | tf_op jit(solution)/shard_map/ppermute | solution.py:250
  30.1 0.1 sub.79
  30.2 0.1 div.13
  30.2 0.5 %compare_select_fusion = f32[8]{0:T(128)} fusion(f32[8]{0:T(128)S(1)} %get-tuple-element.9, f32[4,8]{1,0:T(4,128)S(1)} %fusion.21, f32[4,8]{1,0:T(4,128)S(1)} %slice_reduce_fusion.2), kind=kLoop, calls=%fused_computation.81 | loop fusion | flops 24 | bytes 128 | tf_op jit(solution)/shard_map/jit(_where)/select_n | solution.py:269
  30.8 0.0 copy-start.1
  30.8 0.2 fusion.37
  31.0 0.4 %convolution_bitcast_fusion.1 = f32[50,4096]{1,0:T(8,128)S(1)} fusion(bf16[8,16,2048]{2,1,0:T(8,128)(2,1)S(1)} %get-tuple-element.19, bf16[8,16,2048]{2,1,0:T(8,128)(2,1)S(1)} %get-tuple-element.18, f32[32]{0:T(128)S(1)} %get-tuple-element.13, f32[24,16,50]{2,1,0:T(8,128)S(1)} %fusion.5, f32[8,16,50]{2,1,0:T(8,128)S(1)} %fusion.6, ...), kind=kOutput, calls=%fused_computation.4 | convolution fusion | flops 54679552 | bytes 1970688 | tf_op jit(solution)/shard_map/dot_general | solution.py:179
  31.4 0.6 %fusion.12 = f32[50,2048]{1,0:T(8,128)S(1)} fusion(f32[24,2048]{1,0:T(8,128)S(1)} %fusion.19, f32[8,2048]{1,0:T(8,128)S(1)} %fusion.26, f32[32,50]{1,0:T(8,128)S(1)} %fusion.37, f32[32]{0:T(128)S(1)} %get-tuple-element.12), kind=kOutput, calls=%fused_computation.28 | convolution fusion | flops 39454272 | bytes 678272 | tf_op jit(solution)/shard_map/dot_general | solution.py:188
  32.0 0.2 copy-done.1
  32.2 0.8 %fusion.2 = f32[1,50,4096]{2,1,0:T(8,128)S(1)} fusion(f32[50,4096]{1,0:T(8,128)S(1)} %convolution_bitcast_fusion.1, bf16[24,16,2048]{2,1,0:T(8,128)(2,1)S(1)} %copy-done.1, bf16[24,16,2048]{2,1,0:T(8,128)(2,1)S(1)} %get-tuple-element.16, f32[50,2048]{1,0:T(8,128)S(1)} %fusion.12, f32[4096]{0:T(1024)S(1)} %pad_maximum_fusion.12, ...), kind=kOutput, calls=%fused_computation.3 | convolution fusion | flops 164550656 | bytes 5313024 | tf_op jit(solution)/shard_map/dot_general | solution.py:179
  33.0 1.7 %copy.16 = f32[1,50,4096]{2,0,1:T(1,128)} copy(f32[1,50,4096]{2,1,0:T(8,128)S(1)} %fusion.2) | data formatting | bytes 1638400
  (21 shorter events, 0.2 us)
Async XLA Ops:
  0.6 11.0 %copy-start.2 = (f32[16,2048]{1,0:T(8,128)S(1)}, f32[16,2048]{1,0:T(8,128)}, u32[]{:S(2)}) copy-start(f32[16,2048]{1,0:T(8,128)} %constant.4.clone) | copy-start | bytes 393220
  0.6 11.0 %copy-start.3 = (f32[16,2048]{1,0:T(8,128)S(1)}, f32[16,2048]{1,0:T(8,128)}, u32[]{:S(2)}) copy-start(f32[16,2048]{1,0:T(8,128)} %constant.3.clone) | copy-start | bytes 393220
  0.7 10.1 %copy-start.4 = (f32[16,2048]{1,0:T(8,128)S(1)}, f32[16,2048]{1,0:T(8,128)}, u32[]{:S(2)}) copy-start(f32[16,2048]{1,0:T(8,128)} %param.11) | copy-start | bytes 393220
  2.2 10.2 %collective-permute-start = (bf16[8,4224]{1,0:T(8,128)(2,1)}, bf16[8,4224]{1,0:T(8,128)(2,1)S(1)}, u32[]{:S(2)}, u32[]{:S(2)}) collective-permute-start(bf16[8,4224]{1,0:T(8,128)(2,1)} %shard_map.104), channel_id=1, source_target_pairs={{0,4},{4,0},{8,12},{12,8},{1,5},{5,1},{9,13},{13,9},{2,6},{6,2},{1... | collective-permute-start | bytes 202760 | tf_op jit(solution)/shard_map/ppermute | solution.py:147
  5.3 7.6 %collective-permute-start.1 = (bf16[8,4224]{1,0:T(8,128)(2,1)}, bf16[8,4224]{1,0:T(8,128)(2,1)S(1)}, u32[]{:S(2)}, u32[]{:S(2)}) collective-permute-start(bf16[8,4224]{1,0:T(8,128)(2,1)} %shard_map.104), channel_id=1, source_target_pairs={{0,8},{4,12},{8,0},{12,4},{1,9},{5,13},{9,1},{13,5},{2,10},{6,14},... | collective-permute-start | bytes 202760 | tf_op jit(solution)/shard_map/ppermute | solution.py:147
  7.8 6.4 %collective-permute-start.2 = (bf16[8,4224]{1,0:T(8,128)(2,1)}, bf16[8,4224]{1,0:T(8,128)(2,1)S(1)}, u32[]{:S(2)}, u32[]{:S(2)}) collective-permute-start(bf16[8,4224]{1,0:T(8,128)(2,1)} %shard_map.104), channel_id=1, source_target_pairs={{0,12},{4,8},{8,4},{12,0},{1,13},{5,9},{9,5},{13,1},{2,14},{6,10},... | collective-permute-start | bytes 202760 | tf_op jit(solution)/shard_map/ppermute | solution.py:147
  9.6 2.4 %copy-start.5 = (bf16[1,50,4096]{2,1,0:T(8,128)(2,1)S(1)}, bf16[1,50,4096]{2,1,0:T(8,128)(2,1)}, u32[]{:S(2)}) copy-start(bf16[1,50,4096]{2,1,0:T(8,128)(2,1)} %param.10) | copy-start | bytes 1228804
  16.1 1.2 %copy-start = (bf16[24,16,2048]{2,1,0:T(8,128)(2,1)}, bf16[24,16,2048]{2,1,0:T(8,128)(2,1)S(1)}, u32[]{:S(2)}) copy-start(bf16[24,16,2048]{2,1,0:T(8,128)(2,1)S(1)} %get-tuple-element.17) | copy-start | bytes 4718596
  16.1 4.9 %copy-start.6 = (f32[2048]{0:T(1024)S(1)}, f32[2048]{0:T(1024)}, u32[]{:S(2)}) copy-start(f32[2048]{0:T(1024)} %param.12) | copy-start | bytes 24580
  18.3 1.2 %collective-permute-start.3 = (f32[2,4,8]{2,1,0:T(4,128)S(1)}, f32[2,4,8]{2,1,0:T(4,128)S(1)}, u32[]{:S(2)}, u32[]{:S(2)}) collective-permute-start(f32[2,4,8]{2,1,0:T(4,128)S(1)} %pad_maximum_fusion.13), channel_id=1, source_target_pairs={{0,1},{1,0},{2,3},{3,2},{4,5},{5,4},{6,7},{7,6},{8,9},{9,8},{10,11... | collective-permute-start | bytes 776 | tf_op jit(solution)/shard_map/ppermute | solution.py:162
  19.5 3.7 %collective-permute-start.4 = (f32[2,4,8]{2,1,0:T(4,128)S(1)}, f32[2,4,8]{2,1,0:T(4,128)S(1)}, u32[]{:S(2)}, u32[]{:S(2)}) collective-permute-start(f32[2,4,8]{2,1,0:T(4,128)S(1)} %pad_maximum_fusion.14), channel_id=1, source_target_pairs={{0,2},{1,3},{2,0},{3,1},{4,6},{5,7},{6,4},{7,5},{8,10},{9,11},{10,... | collective-permute-start | bytes 776 | tf_op jit(solution)/shard_map/ppermute | solution.py:162
  23.1 5.5 %collective-permute-start.7 = (f32[2,4,8]{2,1,0:T(4,128)S(1)}, f32[2,4,8]{2,1,0:T(4,128)S(1)}, u32[]{:S(2)}, u32[]{:S(2)}) collective-permute-start(f32[2,4,8]{2,1,0:T(4,128)S(1)} %get-tuple-element.27), channel_id=1, source_target_pairs={{0,12},{4,8},{8,4},{12,0},{1,13},{5,9},{9,5},{13,1},{2,14},{6,10},... | collective-permute-start | bytes 776 | tf_op jit(solution)/shard_map/ppermute | solution.py:250
  25.3 3.6 %collective-permute-start.5 = (f32[2,4,8]{2,1,0:T(4,128)S(1)}, f32[2,4,8]{2,1,0:T(4,128)S(1)}, u32[]{:S(2)}, u32[]{:S(2)}) collective-permute-start(f32[2,4,8]{2,1,0:T(4,128)S(1)} %get-tuple-element.27), channel_id=1, source_target_pairs={{0,4},{4,0},{8,12},{12,8},{1,5},{5,1},{9,13},{13,9},{2,6},{6,2},{1... | collective-permute-start | bytes 776 | tf_op jit(solution)/shard_map/ppermute | solution.py:250
  25.5 4.5 %collective-permute-start.6 = (f32[2,4,8]{2,1,0:T(4,128)S(1)}, f32[2,4,8]{2,1,0:T(4,128)S(1)}, u32[]{:S(2)}, u32[]{:S(2)}) collective-permute-start(f32[2,4,8]{2,1,0:T(4,128)S(1)} %get-tuple-element.27), channel_id=1, source_target_pairs={{0,8},{4,12},{8,0},{12,4},{1,9},{5,13},{9,1},{13,5},{2,10},{6,14},... | collective-permute-start | bytes 776 | tf_op jit(solution)/shard_map/ppermute | solution.py:250
  30.8 1.4 %copy-start.1 = (bf16[24,16,2048]{2,1,0:T(8,128)(2,1)S(1)}, bf16[24,16,2048]{2,1,0:T(8,128)(2,1)}, u32[]{:S(2)}) copy-start(bf16[24,16,2048]{2,1,0:T(8,128)(2,1)} %copy-done) | copy-start | bytes 4718596

commit v9 on v8

--- a/solution.py
+++ b/solution.py
@@ -103,8 +103,10 @@
     return (high, middle, rest - middle)
 
 
-def pack_kernel(sizes_ref, scales_ref, bins_ref, images_ref, out_ref):
-    slots, width = images_ref.shape
+def pack_kernel(sizes_ref, scales_ref, bins_ref, images_hbm, out_hbm, meta_vmem, copy_sems):
+    slots, width = images_hbm.shape
+    image_copy = pltpu.make_async_copy(images_hbm, out_hbm.at[:, pl.ds(0, width)], copy_sems.at[0])
+    image_copy.start()
     row = lax.broadcasted_iota(jnp.int32, (slots, META), 0)
     column = lax.broadcasted_iota(jnp.int32, (slots, META), 1)
     start = jnp.int32(0)
@@ -126,19 +128,23 @@
     meta = jnp.zeros((slots, META), jnp.float32)
     for index, field in enumerate(fields):
         meta = jnp.where(column == index, field, meta)
-    out_ref[:, :width] = images_ref[...]
-    out_ref[:, width:] = meta.astype(out_ref.dtype)
+    meta_vmem[...] = meta.astype(meta_vmem.dtype)
+    meta_copy = pltpu.make_async_copy(meta_vmem, out_hbm.at[:, pl.ds(width, META)], copy_sems.at[1])
+    meta_copy.start()
+    image_copy.wait()
+    meta_copy.wait()
 
 
 def pack_rows(particles, group_counts, group_scale, defocus_bin):
     slots, width = particles.shape
     scalar = pl.BlockSpec(memory_space=pltpu.SMEM)
-    whole = pl.BlockSpec(memory_space=pltpu.VMEM)
+    anywhere = pl.BlockSpec(memory_space=pl.ANY)
     return pl.pallas_call(
         pack_kernel,
         out_shape=jax.ShapeDtypeStruct((slots, width + META), particles.dtype),
-        in_specs=[scalar, scalar, scalar, whole],
-        out_specs=whole,
+        in_specs=[scalar, scalar, scalar, anywhere],
+        out_specs=anywhere,
+        scratch_shapes=[pltpu.VMEM((slots, META), particles.dtype), pltpu.SemaphoreType.DMA((2,))],
     )(group_counts, group_scale, defocus_bin, particles)
 
 

time: 35 us -> 37.4 us (1.069)
  Pallas kernels: 1.57 us -> 3.92 us
    pallas_call x1, Pallas kernels: 1.57 us -> 3.92 us  [pack_rows(): pl.pallas_call(pack_kernel, out_shape=jax.ShapeDtypeStruct((slots, width...]
  transfers between devices with their start and end apart: 8 -> 8, of which waited for: 7 -> 7; matrix products, arithmetic and copies ran while one was open for 13% -> 12% of each run, Pallas kernels for 0% -> 0%
where the time goes in v9:
time: 37.4 us; the launch traced here: 37.1 us
  starting transfers between devices  11.7 us (31%)
  waiting for transfers between devices  7.33 us (20%)
  other arithmetic  6.28 us (17%)
  matrix products  4.57 us (12%)
  Pallas kernels  3.92 us (10%)
  local copies, waits for them, and re-layouts  2.46 us (7%)
  between operations  0.87 us (2%)
    ppermute x3, starting transfers between devices, xor_gather(): lax.ppermute(value, axis, [(i, i ^ k) for i in range(size)])  5.68 us
    ppermute x3, starting transfers between devices, per_device(): lax.ppermute(stats, 'blk', [(i, i ^ k) for i in range(n_blk)])  4.45 us
    pallas_call x1, Pallas kernels, pack_rows(): pl.pallas_call(pack_kernel, out_shape=jax.ShapeDtypeStruct((slots, width...  3.92 us
    ppermute x2, waiting for transfers between devices, xor_butterfly(): other = lax.ppermute(stats, axis, [(i, i ^ step) for i in range(size)])  3.27 us
    ppermute x3, waiting for transfers between devices, per_device(): lax.ppermute(stats, 'blk', [(i, i ^ k) for i in range(n_blk)])  2.28 us
    unnamed x17, local copies, waits for them, and re-layouts  2.1 us
    ppermute x3, waiting for transfers between devices, xor_gather(): lax.ppermute(value, axis, [(i, i ^ k) for i in range(size)])  1.77 us
    ppermute x2, starting transfers between devices, xor_butterfly(): other = lax.ppermute(stats, axis, [(i, i ^ step) for i in range(size)])  1.57 us
  transfers between devices with their start and end apart: 8, of which 7 were waited for; matrix products, arithmetic and copies ran while one was open for 12% of the time, Pallas kernels for 0%

profile of v9, /device:TPU:0, one launch (start us, length us, event | category | flops | bytes accessed | tf_op | source)
XLA Modules:
  0.0 37.1 jit_solution(5198544249877725004)
XLA Ops:
  0.6 0.0 copy-start.2
  0.6 0.0 copy-start.3
  0.7 0.0 copy-start.4
  0.7 3.9 %shard_map.104 = bf16[8,4224]{1,0:T(8,128)(2,1)} custom-call(s32[4]{0:T(128)} %sizes_ref.1, f32[4]{0:T(128)} %scales_ref.1, s32[8]{0:T(128)} %bins_ref.1, bf16[8,4096]{1,0:T(8,128)(2,1)} %images_hbm.1), custom_call_target="tpu_custom_call" | custom-call | tf_op jit(solution)/shard_map/pallas_call | solution.py:142
  4.6 3.1 %collective-permute-start = (bf16[8,4224]{1,0:T(8,128)(2,1)}, bf16[8,4224]{1,0:T(8,128)(2,1)S(1)}, u32[]{:S(2)}, u32[]{:S(2)}) collective-permute-start(bf16[8,4224]{1,0:T(8,128)(2,1)} %shard_map.104), channel_id=1, source_target_pairs={{0,4},{4,0},{8,12},{12,8},{1,5},{5,1},{9,13},{13,9},{2,6},{6,2},{1... | collective-permute-start | bytes 202760 | tf_op jit(solution)/shard_map/ppermute | solution.py:153
  7.7 2.6 %collective-permute-start.1 = (bf16[8,4224]{1,0:T(8,128)(2,1)}, bf16[8,4224]{1,0:T(8,128)(2,1)S(1)}, u32[]{:S(2)}, u32[]{:S(2)}) collective-permute-start(bf16[8,4224]{1,0:T(8,128)(2,1)} %shard_map.104), channel_id=1, source_target_pairs={{0,8},{4,12},{8,0},{12,4},{1,9},{5,13},{9,1},{13,5},{2,10},{6,14},... | collective-permute-start | bytes 202760 | tf_op jit(solution)/shard_map/ppermute | solution.py:153
  10.3 0.0 collective-permute-start.2
  10.3 0.7 %slice_convert_fusion.5 = f32[8,5]{1,0:T(8,128)S(1)} fusion(bf16[8,4224]{1,0:T(8,128)(2,1)} %shard_map.104), kind=kLoop, calls=%fused_computation.78 | loop fusion | flops 40 | bytes 240 | tf_op jit(solution)/shard_map/convert_element_type | solution.py:227
  11.0 0.8 %slice_convert_fusion.3 = (f32[8,2048]{1,0:T(8,128)S(1)}, f32[8,2048]{1,0:T(8,128)S(1)}) fusion(bf16[8,4224]{1,0:T(8,128)(2,1)} %shard_map.104), kind=kLoop, calls=%fused_computation.39 | loop fusion | flops 32768 | bytes 196608 | tf_op jit(solution)/shard_map/convert_element_type | solution.py:54
  11.8 0.2 slice_reduce_fusion.3
  12.0 0.0 copy-start.5
  12.0 1.2 %bitcast_convert_fusion = f32[50,4096]{1,0:T(8,128)S(1)} fusion(bf16[1,50,4096]{2,1,0:T(8,128)(2,1)} %param.10), kind=kLoop, calls=%fused_computation.25 | loop fusion | flops 204800 | bytes 1228800 | tf_op jit(solution)/shard_map/convert_element_type | solution.py:65
  13.2 0.0 copy-done.4
  13.2 0.2 fusion.26
  13.4 0.5 %fusion.8 = f32[16,50]{1,0:T(8,128)S(1)} fusion(f32[50,4096]{1,0:T(8,128)S(1)} %bitcast_convert_fusion, f32[16,2048]{1,0:T(8,128)S(1)} %copy-done.4), kind=kOutput, calls=%fused_computation.21 | convolution fusion | flops 20000768 | bytes 953472 | tf_op jit(solution)/shard_map/dot_general | solution.py:70
  13.9 0.2 convolution_multiply_fusion.2
  14.1 0.0 copy-done.2
  14.1 0.0 copy-done.3
  14.1 0.3 multiply_convert_fusion.3
  14.4 0.0 copy-done.5
  14.4 0.4 %fusion.6 = f32[8,16,50]{2,1,0:T(8,128)S(1)} fusion(bf16[8,16,2048]{2,1,0:T(8,128)(2,1)S(1)} %get-tuple-element.19, bf16[8,16,2048]{2,1,0:T(8,128)(2,1)S(1)} %get-tuple-element.18, bf16[1,50,4096]{2,1,0:T(8,128)(2,1)S(1)} %copy-done.5, f32[8,50]{1,0:T(8,128)S(1)} %convolution_multiply_fusion.2, f32[8]{0:T(128)S(1)} %get-tuple-element.10), kind=kOutput, calls=%fused_computation.12 | convolution fusion | flops 54538752 | bytes 1485408 | tf_op jit(solution)/shard_map/dot_general | solution.py:75
  14.9 0.0 collective-permute-done
  14.9 0.4 %collective-permute-done.1 = bf16[8,4224]{1,0:T(8,128)(2,1)S(1)} collective-permute-done((bf16[8,4224]{1,0:T(8,128)(2,1)}, bf16[8,4224]{1,0:T(8,128)(2,1)S(1)}, u32[]{:S(2)}, u32[]{:S(2)}) %collective-permute-start.1) | collective-permute-done | bytes 67616 | tf_op jit(solution)/shard_map/ppermute | solution.py:153
  15.3 1.4 %collective-permute-done.2 = bf16[8,4224]{1,0:T(8,128)(2,1)S(1)} collective-permute-done((bf16[8,4224]{1,0:T(8,128)(2,1)}, bf16[8,4224]{1,0:T(8,128)(2,1)S(1)}, u32[]{:S(2)}, u32[]{:S(2)}) %collective-permute-start.2) | collective-permute-done | bytes 67616 | tf_op jit(solution)/shard_map/ppermute | solution.py:153
  16.7 0.2 slice_reduce_fusion
  16.9 0.3 fusion.19
  17.3 0.2 convolution_multiply_fusion.1
  17.5 1.1 %multiply_convert_fusion.1 = (bf16[24,16,2048]{2,1,0:T(8,128)(2,1)S(1)}, bf16[24,16,2048]{2,1,0:T(8,128)(2,1)S(1)}) fusion(f32[24,2048]{1,0:T(8,128)S(1)} %fusion.19, f32[16,2048]{1,0:T(8,128)S(1)} %copy-done.2, f32[24,2048]{1,0:T(8,128)S(1)} %get-tuple-element.21, f32[16,2048]{1,0:T(8,128)S(1)} %copy-done.3, f32[24,2048]{1,0:T(8,128)S(1)} %get-tuple-element.20), kind=kLoop, calls=%fused_computation.7 | loop fusion | flops 7864320 | bytes 3997696 | tf_op jit(solution)/shard_map/convert
  18.5 0.0 copy-start
  18.6 0.0 copy-start.6
  18.6 1.0 %fusion.5 = f32[24,16,50]{2,1,0:T(8,128)S(1)} fusion(bf16[24,16,2048]{2,1,0:T(8,128)(2,1)S(1)} %get-tuple-element.17, bf16[24,16,2048]{2,1,0:T(8,128)(2,1)S(1)} %get-tuple-element.16, bf16[1,50,4096]{2,1,0:T(8,128)(2,1)S(1)} %copy-done.5, f32[24,50]{1,0:T(8,128)S(1)} %convolution_multiply_fusion.1, f32[24]{0:T(128)S(1)} %get-tuple-element.7), kind=kOutput, calls=%fused_computation.10 | convolution fusion | flops 163616256 | bytes 3637024 | tf_op jit(solution)/shard_map/dot_general | solution.py:75
  19.5 0.2 copy-done
  19.7 0.3 fusion.15
  20.0 0.5 %exponential_reduce_fusion = f32[32]{0:T(128)S(1)} fusion(f32[24,16,50]{2,1,0:T(8,128)S(1)} %fusion.5, f32[8,16,50]{2,1,0:T(8,128)S(1)} %fusion.6, f32[32]{0:T(128)S(1)} %fusion.15), kind=kLoop, calls=%fused_computation.33 | loop fusion | flops 76768 | bytes 102656 | tf_op jit(solution)/shard_map/reduce_sum | solution.py:250
  20.5 0.1 squeeze.13
  20.6 0.1 stack.32
  20.7 0.0 collective-permute-start.3
  20.7 1.2 %collective-permute-done.3 = f32[2,4,8]{2,1,0:T(4,128)S(1)} collective-permute-done((f32[2,4,8]{2,1,0:T(4,128)S(1)}, f32[2,4,8]{2,1,0:T(4,128)S(1)}, u32[]{:S(2)}, u32[]{:S(2)}) %collective-permute-start.3) | collective-permute-done | bytes 288 | tf_op jit(solution)/shard_map/ppermute | solution.py:168
  21.9 1.5 %collective-permute-start.4 = (f32[2,4,8]{2,1,0:T(4,128)S(1)}, f32[2,4,8]{2,1,0:T(4,128)S(1)}, u32[]{:S(2)}, u32[]{:S(2)}) collective-permute-start(f32[2,4,8]{2,1,0:T(4,128)S(1)} %pad_maximum_fusion.14), channel_id=1, source_target_pairs={{0,2},{1,3},{2,0},{3,1},{4,6},{5,7},{6,4},{7,5},{8,10},{9,11},{10,... | collective-permute-start | bytes 776 | tf_op jit(solution)/shard_map/ppermute | solution.py:168
  23.4 0.0 copy-done.6
  23.4 2.1 %collective-permute-done.4 = f32[2,4,8]{2,1,0:T(4,128)S(1)} collective-permute-done((f32[2,4,8]{2,1,0:T(4,128)S(1)}, f32[2,4,8]{2,1,0:T(4,128)S(1)}, u32[]{:S(2)}, u32[]{:S(2)}) %collective-permute-start.4) | collective-permute-done | bytes 288 | tf_op jit(solution)/shard_map/ppermute | solution.py:168
  25.6 2.1 %collective-permute-start.7 = (f32[2,4,8]{2,1,0:T(4,128)S(1)}, f32[2,4,8]{2,1,0:T(4,128)S(1)}, u32[]{:S(2)}, u32[]{:S(2)}) collective-permute-start(f32[2,4,8]{2,1,0:T(4,128)S(1)} %get-tuple-element.27), channel_id=1, source_target_pairs={{0,12},{4,8},{8,4},{12,0},{1,13},{5,9},{9,5},{13,1},{2,14},{6,10},... | collective-permute-start | bytes 776 | tf_op jit(solution)/shard_map/ppermute | solution.py:256
  27.7 0.1 fusion.38
  27.8 0.1 collective-permute-start.5
  27.9 2.2 %collective-permute-start.6 = (f32[2,4,8]{2,1,0:T(4,128)S(1)}, f32[2,4,8]{2,1,0:T(4,128)S(1)}, u32[]{:S(2)}, u32[]{:S(2)}) collective-permute-start(f32[2,4,8]{2,1,0:T(4,128)S(1)} %get-tuple-element.27), channel_id=1, source_target_pairs={{0,8},{4,12},{8,0},{12,4},{1,9},{5,13},{9,1},{13,5},{2,10},{6,14},... | collective-permute-start | bytes 776 | tf_op jit(solution)/shard_map/ppermute | solution.py:256
  30.1 0.9 %collective-permute-done.7 = f32[2,4,8]{2,1,0:T(4,128)S(1)} collective-permute-done((f32[2,4,8]{2,1,0:T(4,128)S(1)}, f32[2,4,8]{2,1,0:T(4,128)S(1)}, u32[]{:S(2)}, u32[]{:S(2)}) %collective-permute-start.7) | collective-permute-done | bytes 288 | tf_op jit(solution)/shard_map/ppermute | solution.py:256
  31.1 0.3 collective-permute-done.5
  31.4 1.0 %collective-permute-done.6 = f32[2,4,8]{2,1,0:T(4,128)S(1)} collective-permute-done((f32[2,4,8]{2,1,0:T(4,128)S(1)}, f32[2,4,8]{2,1,0:T(4,128)S(1)}, u32[]{:S(2)}, u32[]{:S(2)}) %collective-permute-start.6) | collective-permute-done | bytes 288 | tf_op jit(solution)/shard_map/ppermute | solution.py:256
  32.5 0.1 sub.79
  32.6 0.1 div.13
  32.7 0.5 %compare_select_fusion = f32[8]{0:T(128)} fusion(f32[8]{0:T(128)S(1)} %get-tuple-element.9, f32[4,8]{1,0:T(4,128)S(1)} %fusion.21, f32[4,8]{1,0:T(4,128)S(1)} %slice_reduce_fusion.2), kind=kLoop, calls=%fused_computation.81 | loop fusion | flops 24 | bytes 128 | tf_op jit(solution)/shard_map/jit(_where)/select_n | solution.py:275
  33.2 0.0 copy-start.1
  33.2 0.2 fusion.37
  33.4 0.4 %convolution_bitcast_fusion.1 = f32[50,4096]{1,0:T(8,128)S(1)} fusion(bf16[8,16,2048]{2,1,0:T(8,128)(2,1)S(1)} %get-tuple-element.19, bf16[8,16,2048]{2,1,0:T(8,128)(2,1)S(1)} %get-tuple-element.18, f32[32]{0:T(128)S(1)} %get-tuple-element.13, f32[24,16,50]{2,1,0:T(8,128)S(1)} %fusion.5, f32[8,16,50]{2,1,0:T(8,128)S(1)} %fusion.6, ...), kind=kOutput, calls=%fused_computation.4 | convolution fusion | flops 54679552 | bytes 1970688 | tf_op jit(solution)/shard_map/dot_general | solution.py:185
  33.8 0.6 %fusion.12 = f32[50,2048]{1,0:T(8,128)S(1)} fusion(f32[24,2048]{1,0:T(8,128)S(1)} %fusion.19, f32[8,2048]{1,0:T(8,128)S(1)} %fusion.26, f32[32,50]{1,0:T(8,128)S(1)} %fusion.37, f32[32]{0:T(128)S(1)} %get-tuple-element.12), kind=kOutput, calls=%fused_computation.28 | convolution fusion | flops 39454272 | bytes 678272 | tf_op jit(solution)/shard_map/dot_general | solution.py:194
  34.4 0.2 copy-done.1
  34.6 0.8 %fusion.2 = f32[1,50,4096]{2,1,0:T(8,128)S(1)} fusion(f32[50,4096]{1,0:T(8,128)S(1)} %convolution_bitcast_fusion.1, bf16[24,16,2048]{2,1,0:T(8,128)(2,1)S(1)} %copy-done.1, bf16[24,16,2048]{2,1,0:T(8,128)(2,1)S(1)} %get-tuple-element.16, f32[50,2048]{1,0:T(8,128)S(1)} %fusion.12, f32[4096]{0:T(1024)S(1)} %pad_maximum_fusion.12, ...), kind=kOutput, calls=%fused_computation.3 | convolution fusion | flops 164550656 | bytes 5313024 | tf_op jit(solution)/shard_map/dot_general | solution.py:185
  35.4 1.7 %copy.16 = f32[1,50,4096]{2,0,1:T(1,128)} copy(f32[1,50,4096]{2,1,0:T(8,128)S(1)} %fusion.2) | data formatting | bytes 1638400
  (21 shorter events, 0.2 us)
Async XLA Ops:
  0.6 13.5 %copy-start.2 = (f32[16,2048]{1,0:T(8,128)S(1)}, f32[16,2048]{1,0:T(8,128)}, u32[]{:S(2)}) copy-start(f32[16,2048]{1,0:T(8,128)} %constant.4.clone) | copy-start | bytes 393220
  0.6 13.5 %copy-start.3 = (f32[16,2048]{1,0:T(8,128)S(1)}, f32[16,2048]{1,0:T(8,128)}, u32[]{:S(2)}) copy-start(f32[16,2048]{1,0:T(8,128)} %constant.3.clone) | copy-start | bytes 393220
  0.7 12.5 %copy-start.4 = (f32[16,2048]{1,0:T(8,128)S(1)}, f32[16,2048]{1,0:T(8,128)}, u32[]{:S(2)}) copy-start(f32[16,2048]{1,0:T(8,128)} %param.11) | copy-start | bytes 393220
  4.6 10.3 %collective-permute-start = (bf16[8,4224]{1,0:T(8,128)(2,1)}, bf16[8,4224]{1,0:T(8,128)(2,1)S(1)}, u32[]{:S(2)}, u32[]{:S(2)}) collective-permute-start(bf16[8,4224]{1,0:T(8,128)(2,1)} %shard_map.104), channel_id=1, source_target_pairs={{0,4},{4,0},{8,12},{12,8},{1,5},{5,1},{9,13},{13,9},{2,6},{6,2},{1... | collective-permute-start | bytes 202760 | tf_op jit(solution)/shard_map/ppermute | solution.py:153
  7.7 7.6 %collective-permute-start.1 = (bf16[8,4224]{1,0:T(8,128)(2,1)}, bf16[8,4224]{1,0:T(8,128)(2,1)S(1)}, u32[]{:S(2)}, u32[]{:S(2)}) collective-permute-start(bf16[8,4224]{1,0:T(8,128)(2,1)} %shard_map.104), channel_id=1, source_target_pairs={{0,8},{4,12},{8,0},{12,4},{1,9},{5,13},{9,1},{13,5},{2,10},{6,14},... | collective-permute-start | bytes 202760 | tf_op jit(solution)/shard_map/ppermute | solution.py:153
  10.3 6.4 %collective-permute-start.2 = (bf16[8,4224]{1,0:T(8,128)(2,1)}, bf16[8,4224]{1,0:T(8,128)(2,1)S(1)}, u32[]{:S(2)}, u32[]{:S(2)}) collective-permute-start(bf16[8,4224]{1,0:T(8,128)(2,1)} %shard_map.104), channel_id=1, source_target_pairs={{0,12},{4,8},{8,4},{12,0},{1,13},{5,9},{9,5},{13,1},{2,14},{6,10},... | collective-permute-start | bytes 202760 | tf_op jit(solution)/shard_map/ppermute | solution.py:153
  12.0 2.4 %copy-start.5 = (bf16[1,50,4096]{2,1,0:T(8,128)(2,1)S(1)}, bf16[1,50,4096]{2,1,0:T(8,128)(2,1)}, u32[]{:S(2)}) copy-start(bf16[1,50,4096]{2,1,0:T(8,128)(2,1)} %param.10) | copy-start | bytes 1228804
  18.5 1.2 %copy-start = (bf16[24,16,2048]{2,1,0:T(8,128)(2,1)}, bf16[24,16,2048]{2,1,0:T(8,128)(2,1)S(1)}, u32[]{:S(2)}) copy-start(bf16[24,16,2048]{2,1,0:T(8,128)(2,1)S(1)} %get-tuple-element.17) | copy-start | bytes 4718596
  18.6 4.9 %copy-start.6 = (f32[2048]{0:T(1024)S(1)}, f32[2048]{0:T(1024)}, u32[]{:S(2)}) copy-start(f32[2048]{0:T(1024)} %param.12) | copy-start | bytes 24580
  20.7 1.2 %collective-permute-start.3 = (f32[2,4,8]{2,1,0:T(4,128)S(1)}, f32[2,4,8]{2,1,0:T(4,128)S(1)}, u32[]{:S(2)}, u32[]{:S(2)}) collective-permute-start(f32[2,4,8]{2,1,0:T(4,128)S(1)} %pad_maximum_fusion.13), channel_id=1, source_target_pairs={{0,1},{1,0},{2,3},{3,2},{4,5},{5,4},{6,7},{7,6},{8,9},{9,8},{10,11... | collective-permute-start | bytes 776 | tf_op jit(solution)/shard_map/ppermute | solution.py:168
  21.9 3.7 %collective-permute-start.4 = (f32[2,4,8]{2,1,0:T(4,128)S(1)}, f32[2,4,8]{2,1,0:T(4,128)S(1)}, u32[]{:S(2)}, u32[]{:S(2)}) collective-permute-start(f32[2,4,8]{2,1,0:T(4,128)S(1)} %pad_maximum_fusion.14), channel_id=1, source_target_pairs={{0,2},{1,3},{2,0},{3,1},{4,6},{5,7},{6,4},{7,5},{8,10},{9,11},{10,... | collective-permute-start | bytes 776 | tf_op jit(solution)/shard_map/ppermute | solution.py:168
  25.6 5.5 %collective-permute-start.7 = (f32[2,4,8]{2,1,0:T(4,128)S(1)}, f32[2,4,8]{2,1,0:T(4,128)S(1)}, u32[]{:S(2)}, u32[]{:S(2)}) collective-permute-start(f32[2,4,8]{2,1,0:T(4,128)S(1)} %get-tuple-element.27), channel_id=1, source_target_pairs={{0,12},{4,8},{8,4},{12,0},{1,13},{5,9},{9,5},{13,1},{2,14},{6,10},... | collective-permute-start | bytes 776 | tf_op jit(solution)/shard_map/ppermute | solution.py:256
  27.8 3.6 %collective-permute-start.5 = (f32[2,4,8]{2,1,0:T(4,128)S(1)}, f32[2,4,8]{2,1,0:T(4,128)S(1)}, u32[]{:S(2)}, u32[]{:S(2)}) collective-permute-start(f32[2,4,8]{2,1,0:T(4,128)S(1)} %get-tuple-element.27), channel_id=1, source_target_pairs={{0,4},{4,0},{8,12},{12,8},{1,5},{5,1},{9,13},{13,9},{2,6},{6,2},{1... | collective-permute-start | bytes 776 | tf_op jit(solution)/shard_map/ppermute | solution.py:256
  27.9 4.5 %collective-permute-start.6 = (f32[2,4,8]{2,1,0:T(4,128)S(1)}, f32[2,4,8]{2,1,0:T(4,128)S(1)}, u32[]{:S(2)}, u32[]{:S(2)}) collective-permute-start(f32[2,4,8]{2,1,0:T(4,128)S(1)} %get-tuple-element.27), channel_id=1, source_target_pairs={{0,8},{4,12},{8,0},{12,4},{1,9},{5,13},{9,1},{13,5},{2,10},{6,14},... | collective-permute-start | bytes 776 | tf_op jit(solution)/shard_map/ppermute | solution.py:256
  33.2 1.4 %copy-start.1 = (bf16[24,16,2048]{2,1,0:T(8,128)(2,1)S(1)}, bf16[24,16,2048]{2,1,0:T(8,128)(2,1)}, u32[]{:S(2)}) copy-start(bf16[24,16,2048]{2,1,0:T(8,128)(2,1)} %copy-done) | copy-start | bytes 4718596

commit v10 on v8

--- a/solution.py
+++ b/solution.py
@@ -216,8 +216,9 @@
     if small:
         packed = pack_rows(particles, group_counts, group_scale, defocus_bin)
         others = xor_gather(packed, "blk", n_blk)[batch_size:]
+        own_rows = lax.optimization_barrier(packed.astype(jnp.float32))
         groups = []
-        for rows in (packed, others):
+        for rows in (own_rows, others):
             meta = rows[:, width : width + 5].astype(jnp.float32)
             gains = (meta[:, 0] + meta[:, 1]) + meta[:, 2]
             groups.append((rows[:, :width], gains, meta[:, 3], meta[:, 4]))

time: 35 us -> 34.9 us (level)
  other arithmetic: 6.28 us -> 5.69 us
  waiting for transfers between devices: 7.34 us -> 7.9 us
    convert_element_type x0 -> x1, other arithmetic: none -> 0.96 us  [per_device(): own_rows = lax.optimization_barrier(packed.astype(jnp.float32))]
    convert_element_type x2 -> x1, other arithmetic: 0.81 us -> 0.03 us  [shifted_rows(): real_part = images[:, :half_width].astype(jnp.float32)[:, None, :]]
    convert_element_type x2 -> x1, other arithmetic: 0.76 us -> 0.01 us  [per_device(): meta = rows[:, width:width + 5].astype(jnp.float32)]
    ppermute x3, waiting for transfers between devices: 1.77 us -> 2.33 us  [xor_gather(): lax.ppermute(value, axis, [(i, i ^ k) for i in range(size)])]
  transfers between devices with their start and end apart: 8 -> 8, of which waited for: 7 -> 7; matrix products, arithmetic and copies ran while one was open for 13% -> 12% of each run, Pallas kernels for 0% -> 0%
where the time goes in v10:
time: 34.9 us; the launch traced here: 34.7 us
  starting transfers between devices  11.6 us (33%)
  waiting for transfers between devices  7.9 us (23%)
  other arithmetic  5.69 us (16%)
  matrix products  4.56 us (13%)
  local copies, waits for them, and re-layouts  2.47 us (7%)
  Pallas kernels  1.57 us (4%)
  between operations  0.87 us (2%)
    ppermute x3, starting transfers between devices, xor_gather(): lax.ppermute(value, axis, [(i, i ^ k) for i in range(size)])  5.62 us
    ppermute x3, starting transfers between devices, per_device(): lax.ppermute(stats, 'blk', [(i, i ^ k) for i in range(n_blk)])  4.45 us
    ppermute x2, waiting for transfers between devices, xor_butterfly(): other = lax.ppermute(stats, axis, [(i, i ^ step) for i in range(size)])  3.26 us
    ppermute x3, waiting for transfers between devices, xor_gather(): lax.ppermute(value, axis, [(i, i ^ k) for i in range(size)])  2.33 us
    ppermute x3, waiting for transfers between devices, per_device(): lax.ppermute(stats, 'blk', [(i, i ^ k) for i in range(n_blk)])  2.3 us
    unnamed x17, local copies, waits for them, and re-layouts  2.11 us
    ppermute x2, starting transfers between devices, xor_butterfly(): other = lax.ppermute(stats, axis, [(i, i ^ step) for i in range(size)])  1.58 us
    pallas_call x1, Pallas kernels, pack_rows(): pl.pallas_call(pack_kernel, out_shape=jax.ShapeDtypeStruct((slots, width...  1.57 us
  transfers between devices with their start and end apart: 8, of which 7 were waited for; matrix products, arithmetic and copies ran while one was open for 12% of the time, Pallas kernels for 0%

profile of v10, /device:TPU:0, one launch (start us, length us, event | category | flops | bytes accessed | tf_op | source)
XLA Modules:
  0.0 34.7 jit_solution(17713856253834064535)
XLA Ops:
  0.6 0.0 copy-start.2
  0.6 0.0 copy-start.3
  0.7 0.0 copy-start.4
  0.7 1.6 %shard_map.104 = bf16[8,4224]{1,0:T(8,128)(2,1)} custom-call(s32[4]{0:T(128)} %sizes_ref.1, f32[4]{0:T(128)} %scales_ref.1, s32[8]{0:T(128)} %bins_ref.1, bf16[8,4096]{1,0:T(8,128)(2,1)} %images_ref.1), custom_call_target="tpu_custom_call" | custom-call | tf_op jit(solution)/shard_map/pallas_call | solution.py:137
  2.2 3.0 %collective-permute-start = (bf16[8,4224]{1,0:T(8,128)(2,1)}, bf16[8,4224]{1,0:T(8,128)(2,1)S(1)}, u32[]{:S(2)}, u32[]{:S(2)}) collective-permute-start(bf16[8,4224]{1,0:T(8,128)(2,1)} %shard_map.104), channel_id=1, source_target_pairs={{0,4},{4,0},{8,12},{12,8},{1,5},{5,1},{9,13},{13,9},{2,6},{6,2},{1... | collective-permute-start | bytes 202760 | tf_op jit(solution)/shard_map/ppermute | solution.py:147
  5.3 2.6 %collective-permute-start.1 = (bf16[8,4224]{1,0:T(8,128)(2,1)}, bf16[8,4224]{1,0:T(8,128)(2,1)S(1)}, u32[]{:S(2)}, u32[]{:S(2)}) collective-permute-start(bf16[8,4224]{1,0:T(8,128)(2,1)} %shard_map.104), channel_id=1, source_target_pairs={{0,8},{4,12},{8,0},{12,4},{1,9},{5,13},{9,1},{13,5},{2,10},{6,14},... | collective-permute-start | bytes 202760 | tf_op jit(solution)/shard_map/ppermute | solution.py:147
  7.8 0.0 collective-permute-start.2
  7.8 1.0 %convert_element_type.26 = f32[8,4224]{1,0:T(8,128)S(1)} convert(bf16[8,4224]{1,0:T(8,128)(2,1)} %shard_map.104) | non-fusion elementwise | flops 33792 | bytes 202752 | tf_op jit(solution)/shard_map/convert_element_type | solution.py:219
  8.8 0.2 slice_reduce_fusion.3
  9.0 0.0 copy-start.5
  9.1 1.1 %bitcast_convert_fusion = f32[50,4096]{1,0:T(8,128)S(1)} fusion(bf16[1,50,4096]{2,1,0:T(8,128)(2,1)} %param.10), kind=kLoop, calls=%fused_computation.25 | loop fusion | flops 204800 | bytes 1228800 | tf_op jit(solution)/shard_map/convert_element_type | solution.py:65
  10.2 0.0 copy-done.4
  10.2 0.2 fusion.27
  10.4 0.5 %fusion.8 = f32[16,50]{1,0:T(8,128)S(1)} fusion(f32[50,4096]{1,0:T(8,128)S(1)} %bitcast_convert_fusion, f32[16,2048]{1,0:T(8,128)S(1)} %copy-done.4), kind=kOutput, calls=%fused_computation.21 | convolution fusion | flops 20000768 | bytes 953472 | tf_op jit(solution)/shard_map/dot_general | solution.py:70
  10.9 0.2 convolution_multiply_fusion.2
  11.1 0.0 copy-done.2
  11.1 0.0 copy-done.3
  11.1 0.3 multiply_convert_fusion.3
  11.4 0.0 copy-done.5
  11.5 0.4 %fusion.6 = f32[8,16,50]{2,1,0:T(8,128)S(1)} fusion(bf16[8,16,2048]{2,1,0:T(8,128)(2,1)S(1)} %get-tuple-element.19, bf16[8,16,2048]{2,1,0:T(8,128)(2,1)S(1)} %get-tuple-element.18, bf16[1,50,4096]{2,1,0:T(8,128)(2,1)S(1)} %copy-done.5, f32[8,50]{1,0:T(8,128)S(1)} %convolution_multiply_fusion.2, f32[8]{0:T(128)S(1)} %get-tuple-element.7), kind=kOutput, calls=%fused_computation.12 | convolution fusion | flops 54538752 | bytes 1485408 | tf_op jit(solution)/shard_map/dot_general | solution.py:75
  11.9 0.0 collective-permute-done
  11.9 1.0 %collective-permute-done.1 = bf16[8,4224]{1,0:T(8,128)(2,1)S(1)} collective-permute-done((bf16[8,4224]{1,0:T(8,128)(2,1)}, bf16[8,4224]{1,0:T(8,128)(2,1)S(1)}, u32[]{:S(2)}, u32[]{:S(2)}) %collective-permute-start.1) | collective-permute-done | bytes 67616 | tf_op jit(solution)/shard_map/ppermute | solution.py:147
  12.9 1.4 %collective-permute-done.2 = bf16[8,4224]{1,0:T(8,128)(2,1)S(1)} collective-permute-done((bf16[8,4224]{1,0:T(8,128)(2,1)}, bf16[8,4224]{1,0:T(8,128)(2,1)S(1)}, u32[]{:S(2)}, u32[]{:S(2)}) %collective-permute-start.2) | collective-permute-done | bytes 67616 | tf_op jit(solution)/shard_map/ppermute | solution.py:147
  14.3 0.2 slice_reduce_fusion
  14.5 0.3 fusion.19
  14.8 0.2 convolution_multiply_fusion.1
  15.0 1.1 %multiply_convert_fusion.1 = (bf16[24,16,2048]{2,1,0:T(8,128)(2,1)S(1)}, bf16[24,16,2048]{2,1,0:T(8,128)(2,1)S(1)}) fusion(f32[24,2048]{1,0:T(8,128)S(1)} %fusion.19, f32[16,2048]{1,0:T(8,128)S(1)} %copy-done.2, f32[24,2048]{1,0:T(8,128)S(1)} %get-tuple-element.21, f32[16,2048]{1,0:T(8,128)S(1)} %copy-done.3, f32[24,2048]{1,0:T(8,128)S(1)} %get-tuple-element.20), kind=kLoop, calls=%fused_computation.7 | loop fusion | flops 7864320 | bytes 3997696 | tf_op jit(solution)/shard_map/convert
  16.1 0.0 copy-start
  16.1 0.0 copy-start.6
  16.1 1.0 %fusion.5 = f32[24,16,50]{2,1,0:T(8,128)S(1)} fusion(bf16[24,16,2048]{2,1,0:T(8,128)(2,1)S(1)} %get-tuple-element.17, bf16[24,16,2048]{2,1,0:T(8,128)(2,1)S(1)} %get-tuple-element.16, bf16[1,50,4096]{2,1,0:T(8,128)(2,1)S(1)} %copy-done.5, f32[24,50]{1,0:T(8,128)S(1)} %convolution_multiply_fusion.1, f32[24]{0:T(128)S(1)} %get-tuple-element.10), kind=kOutput, calls=%fused_computation.10 | convolution fusion | flops 163616256 | bytes 3637024 | tf_op jit(solution)/shard_map/dot_general | solution.py:75
  17.1 0.2 copy-done
  17.3 0.3 fusion.15
  17.6 0.5 %exponential_reduce_fusion = f32[32]{0:T(128)S(1)} fusion(f32[24,16,50]{2,1,0:T(8,128)S(1)} %fusion.5, f32[8,16,50]{2,1,0:T(8,128)S(1)} %fusion.6, f32[32]{0:T(128)S(1)} %fusion.15), kind=kLoop, calls=%fused_computation.33 | loop fusion | flops 76768 | bytes 102656 | tf_op jit(solution)/shard_map/reduce_sum | solution.py:245
  18.1 0.1 squeeze.13
  18.2 0.1 stack.32
  18.3 0.0 collective-permute-start.3
  18.3 1.2 %collective-permute-done.3 = f32[2,4,8]{2,1,0:T(4,128)S(1)} collective-permute-done((f32[2,4,8]{2,1,0:T(4,128)S(1)}, f32[2,4,8]{2,1,0:T(4,128)S(1)}, u32[]{:S(2)}, u32[]{:S(2)}) %collective-permute-start.3) | collective-permute-done | bytes 288 | tf_op jit(solution)/shard_map/ppermute | solution.py:162
  19.5 1.6 %collective-permute-start.4 = (f32[2,4,8]{2,1,0:T(4,128)S(1)}, f32[2,4,8]{2,1,0:T(4,128)S(1)}, u32[]{:S(2)}, u32[]{:S(2)}) collective-permute-start(f32[2,4,8]{2,1,0:T(4,128)S(1)} %pad_maximum_fusion.14), channel_id=1, source_target_pairs={{0,2},{1,3},{2,0},{3,1},{4,6},{5,7},{6,4},{7,5},{8,10},{9,11},{10,... | collective-permute-start | bytes 776 | tf_op jit(solution)/shard_map/ppermute | solution.py:162
  21.0 0.0 copy-done.6
  21.0 2.1 %collective-permute-done.4 = f32[2,4,8]{2,1,0:T(4,128)S(1)} collective-permute-done((f32[2,4,8]{2,1,0:T(4,128)S(1)}, f32[2,4,8]{2,1,0:T(4,128)S(1)}, u32[]{:S(2)}, u32[]{:S(2)}) %collective-permute-start.4) | collective-permute-done | bytes 288 | tf_op jit(solution)/shard_map/ppermute | solution.py:162
  23.1 1.9 %collective-permute-start.7 = (f32[2,4,8]{2,1,0:T(4,128)S(1)}, f32[2,4,8]{2,1,0:T(4,128)S(1)}, u32[]{:S(2)}, u32[]{:S(2)}) collective-permute-start(f32[2,4,8]{2,1,0:T(4,128)S(1)} %get-tuple-element.27), channel_id=1, source_target_pairs={{0,12},{4,8},{8,4},{12,0},{1,13},{5,9},{9,5},{13,1},{2,14},{6,10},... | collective-permute-start | bytes 776 | tf_op jit(solution)/shard_map/ppermute | solution.py:251
  25.0 0.1 fusion.39
  25.1 0.4 %collective-permute-start.5 = (f32[2,4,8]{2,1,0:T(4,128)S(1)}, f32[2,4,8]{2,1,0:T(4,128)S(1)}, u32[]{:S(2)}, u32[]{:S(2)}) collective-permute-start(f32[2,4,8]{2,1,0:T(4,128)S(1)} %get-tuple-element.27), channel_id=1, source_target_pairs={{0,4},{4,0},{8,12},{12,8},{1,5},{5,1},{9,13},{13,9},{2,6},{6,2},{1... | collective-permute-start | bytes 776 | tf_op jit(solution)/shard_map/ppermute | solution.py:251
  25.5 2.2 %collective-permute-start.6 = (f32[2,4,8]{2,1,0:T(4,128)S(1)}, f32[2,4,8]{2,1,0:T(4,128)S(1)}, u32[]{:S(2)}, u32[]{:S(2)}) collective-permute-start(f32[2,4,8]{2,1,0:T(4,128)S(1)} %get-tuple-element.27), channel_id=1, source_target_pairs={{0,8},{4,12},{8,0},{12,4},{1,9},{5,13},{9,1},{13,5},{2,10},{6,14},... | collective-permute-start | bytes 776 | tf_op jit(solution)/shard_map/ppermute | solution.py:251
  27.7 0.9 %collective-permute-done.7 = f32[2,4,8]{2,1,0:T(4,128)S(1)} collective-permute-done((f32[2,4,8]{2,1,0:T(4,128)S(1)}, f32[2,4,8]{2,1,0:T(4,128)S(1)}, u32[]{:S(2)}, u32[]{:S(2)}) %collective-permute-start.7) | collective-permute-done | bytes 288 | tf_op jit(solution)/shard_map/ppermute | solution.py:251
  28.6 0.1 collective-permute-done.5
  28.8 1.3 %collective-permute-done.6 = f32[2,4,8]{2,1,0:T(4,128)S(1)} collective-permute-done((f32[2,4,8]{2,1,0:T(4,128)S(1)}, f32[2,4,8]{2,1,0:T(4,128)S(1)}, u32[]{:S(2)}, u32[]{:S(2)}) %collective-permute-start.6) | collective-permute-done | bytes 288 | tf_op jit(solution)/shard_map/ppermute | solution.py:251
  30.1 0.1 sub.79
  30.2 0.1 div.13
  30.2 0.5 %compare_select_fusion = f32[8]{0:T(128)} fusion(f32[8]{0:T(128)S(1)} %get-tuple-element.6, f32[4,8]{1,0:T(4,128)S(1)} %fusion.21, f32[4,8]{1,0:T(4,128)S(1)} %slice_reduce_fusion.2), kind=kLoop, calls=%fused_computation.80 | loop fusion | flops 24 | bytes 128 | tf_op jit(solution)/shard_map/jit(_where)/select_n | solution.py:270
  30.8 0.0 copy-start.1
  30.8 0.2 fusion.38
  31.0 0.4 %convolution_bitcast_fusion.1 = f32[50,4096]{1,0:T(8,128)S(1)} fusion(bf16[8,16,2048]{2,1,0:T(8,128)(2,1)S(1)} %get-tuple-element.19, bf16[8,16,2048]{2,1,0:T(8,128)(2,1)S(1)} %get-tuple-element.18, f32[32]{0:T(128)S(1)} %get-tuple-element.13, f32[24,16,50]{2,1,0:T(8,128)S(1)} %fusion.5, f32[8,16,50]{2,1,0:T(8,128)S(1)} %fusion.6, ...), kind=kOutput, calls=%fused_computation.4 | convolution fusion | flops 54679552 | bytes 1970688 | tf_op jit(solution)/shard_map/dot_general | solution.py:179
  31.4 0.6 %fusion.12 = f32[50,2048]{1,0:T(8,128)S(1)} fusion(f32[24,2048]{1,0:T(8,128)S(1)} %fusion.19, f32[8,2048]{1,0:T(8,128)S(1)} %fusion.27, f32[32,50]{1,0:T(8,128)S(1)} %fusion.38, f32[32]{0:T(128)S(1)} %get-tuple-element.12), kind=kOutput, calls=%fused_computation.28 | convolution fusion | flops 39454272 | bytes 678272 | tf_op jit(solution)/shard_map/dot_general | solution.py:188
  32.0 0.2 copy-done.1
  32.2 0.8 %fusion.2 = f32[1,50,4096]{2,1,0:T(8,128)S(1)} fusion(f32[50,4096]{1,0:T(8,128)S(1)} %convolution_bitcast_fusion.1, bf16[24,16,2048]{2,1,0:T(8,128)(2,1)S(1)} %copy-done.1, bf16[24,16,2048]{2,1,0:T(8,128)(2,1)S(1)} %get-tuple-element.16, f32[50,2048]{1,0:T(8,128)S(1)} %fusion.12, f32[4096]{0:T(1024)S(1)} %pad_maximum_fusion.12, ...), kind=kOutput, calls=%fused_computation.3 | convolution fusion | flops 164550656 | bytes 5313024 | tf_op jit(solution)/shard_map/dot_general | solution.py:179
  33.0 1.7 %copy.16 = f32[1,50,4096]{2,0,1:T(1,128)} copy(f32[1,50,4096]{2,1,0:T(8,128)S(1)} %fusion.2) | data formatting | bytes 1638400
  (22 shorter events, 0.2 us)
Async XLA Ops:
  0.6 10.5 %copy-start.2 = (f32[16,2048]{1,0:T(8,128)S(1)}, f32[16,2048]{1,0:T(8,128)}, u32[]{:S(2)}) copy-start(f32[16,2048]{1,0:T(8,128)} %constant.4.clone) | copy-start | bytes 393220
  0.6 10.5 %copy-start.3 = (f32[16,2048]{1,0:T(8,128)S(1)}, f32[16,2048]{1,0:T(8,128)}, u32[]{:S(2)}) copy-start(f32[16,2048]{1,0:T(8,128)} %constant.3.clone) | copy-start | bytes 393220
  0.7 9.6 %copy-start.4 = (f32[16,2048]{1,0:T(8,128)S(1)}, f32[16,2048]{1,0:T(8,128)}, u32[]{:S(2)}) copy-start(f32[16,2048]{1,0:T(8,128)} %param.11) | copy-start | bytes 393220
  2.2 9.6 %collective-permute-start = (bf16[8,4224]{1,0:T(8,128)(2,1)}, bf16[8,4224]{1,0:T(8,128)(2,1)S(1)}, u32[]{:S(2)}, u32[]{:S(2)}) collective-permute-start(bf16[8,4224]{1,0:T(8,128)(2,1)} %shard_map.104), channel_id=1, source_target_pairs={{0,4},{4,0},{8,12},{12,8},{1,5},{5,1},{9,13},{13,9},{2,6},{6,2},{1... | collective-permute-start | bytes 202760 | tf_op jit(solution)/shard_map/ppermute | solution.py:147
  5.3 7.6 %collective-permute-start.1 = (bf16[8,4224]{1,0:T(8,128)(2,1)}, bf16[8,4224]{1,0:T(8,128)(2,1)S(1)}, u32[]{:S(2)}, u32[]{:S(2)}) collective-permute-start(bf16[8,4224]{1,0:T(8,128)(2,1)} %shard_map.104), channel_id=1, source_target_pairs={{0,8},{4,12},{8,0},{12,4},{1,9},{5,13},{9,1},{13,5},{2,10},{6,14},... | collective-permute-start | bytes 202760 | tf_op jit(solution)/shard_map/ppermute | solution.py:147
  7.8 6.4 %collective-permute-start.2 = (bf16[8,4224]{1,0:T(8,128)(2,1)}, bf16[8,4224]{1,0:T(8,128)(2,1)S(1)}, u32[]{:S(2)}, u32[]{:S(2)}) collective-permute-start(bf16[8,4224]{1,0:T(8,128)(2,1)} %shard_map.104), channel_id=1, source_target_pairs={{0,12},{4,8},{8,4},{12,0},{1,13},{5,9},{9,5},{13,1},{2,14},{6,10},... | collective-permute-start | bytes 202760 | tf_op jit(solution)/shard_map/ppermute | solution.py:147
  9.0 2.4 %copy-start.5 = (bf16[1,50,4096]{2,1,0:T(8,128)(2,1)S(1)}, bf16[1,50,4096]{2,1,0:T(8,128)(2,1)}, u32[]{:S(2)}) copy-start(bf16[1,50,4096]{2,1,0:T(8,128)(2,1)} %param.10) | copy-start | bytes 1228804
  16.1 1.2 %copy-start = (bf16[24,16,2048]{2,1,0:T(8,128)(2,1)}, bf16[24,16,2048]{2,1,0:T(8,128)(2,1)S(1)}, u32[]{:S(2)}) copy-start(bf16[24,16,2048]{2,1,0:T(8,128)(2,1)S(1)} %get-tuple-element.17) | copy-start | bytes 4718596
  16.1 4.9 %copy-start.6 = (f32[2048]{0:T(1024)S(1)}, f32[2048]{0:T(1024)}, u32[]{:S(2)}) copy-start(f32[2048]{0:T(1024)} %param.12) | copy-start | bytes 24580
  18.3 1.2 %collective-permute-start.3 = (f32[2,4,8]{2,1,0:T(4,128)S(1)}, f32[2,4,8]{2,1,0:T(4,128)S(1)}, u32[]{:S(2)}, u32[]{:S(2)}) collective-permute-start(f32[2,4,8]{2,1,0:T(4,128)S(1)} %pad_maximum_fusion.13), channel_id=1, source_target_pairs={{0,1},{1,0},{2,3},{3,2},{4,5},{5,4},{6,7},{7,6},{8,9},{9,8},{10,11... | collective-permute-start | bytes 776 | tf_op jit(solution)/shard_map/ppermute | solution.py:162
  19.5 3.7 %collective-permute-start.4 = (f32[2,4,8]{2,1,0:T(4,128)S(1)}, f32[2,4,8]{2,1,0:T(4,128)S(1)}, u32[]{:S(2)}, u32[]{:S(2)}) collective-permute-start(f32[2,4,8]{2,1,0:T(4,128)S(1)} %pad_maximum_fusion.14), channel_id=1, source_target_pairs={{0,2},{1,3},{2,0},{3,1},{4,6},{5,7},{6,4},{7,5},{8,10},{9,11},{10,... | collective-permute-start | bytes 776 | tf_op jit(solution)/shard_map/ppermute | solution.py:162
  23.1 5.5 %collective-permute-start.7 = (f32[2,4,8]{2,1,0:T(4,128)S(1)}, f32[2,4,8]{2,1,0:T(4,128)S(1)}, u32[]{:S(2)}, u32[]{:S(2)}) collective-permute-start(f32[2,4,8]{2,1,0:T(4,128)S(1)} %get-tuple-element.27), channel_id=1, source_target_pairs={{0,12},{4,8},{8,4},{12,0},{1,13},{5,9},{9,5},{13,1},{2,14},{6,10},... | collective-permute-start | bytes 776 | tf_op jit(solution)/shard_map/ppermute | solution.py:251
  25.1 3.6 %collective-permute-start.5 = (f32[2,4,8]{2,1,0:T(4,128)S(1)}, f32[2,4,8]{2,1,0:T(4,128)S(1)}, u32[]{:S(2)}, u32[]{:S(2)}) collective-permute-start(f32[2,4,8]{2,1,0:T(4,128)S(1)} %get-tuple-element.27), channel_id=1, source_target_pairs={{0,4},{4,0},{8,12},{12,8},{1,5},{5,1},{9,13},{13,9},{2,6},{6,2},{1... | collective-permute-start | bytes 776 | tf_op jit(solution)/shard_map/ppermute | solution.py:251
  25.5 4.5 %collective-permute-start.6 = (f32[2,4,8]{2,1,0:T(4,128)S(1)}, f32[2,4,8]{2,1,0:T(4,128)S(1)}, u32[]{:S(2)}, u32[]{:S(2)}) collective-permute-start(f32[2,4,8]{2,1,0:T(4,128)S(1)} %get-tuple-element.27), channel_id=1, source_target_pairs={{0,8},{4,12},{8,0},{12,4},{1,9},{5,13},{9,1},{13,5},{2,10},{6,14},... | collective-permute-start | bytes 776 | tf_op jit(solution)/shard_map/ppermute | solution.py:251
  30.8 1.4 %copy-start.1 = (bf16[24,16,2048]{2,1,0:T(8,128)(2,1)S(1)}, bf16[24,16,2048]{2,1,0:T(8,128)(2,1)}, u32[]{:S(2)}) copy-start(bf16[24,16,2048]{2,1,0:T(8,128)(2,1)} %copy-done) | copy-start | bytes 4718596

commit v11 on v10

--- a/solution.py
+++ b/solution.py
@@ -142,11 +142,10 @@
     )(group_counts, group_scale, defocus_bin, particles)
 
 
-def xor_gather(value, axis, size):
-    pieces = [value] + [
+def xor_gather_pieces(value, axis, size):
+    return [value] + [
         lax.ppermute(value, axis, [(i, i ^ k) for i in range(size)]) for k in range(1, size)
     ]
-    return jnp.concatenate(pieces, axis=0)
 
 
 def xor_reorder(value, step, axis):
@@ -215,25 +214,34 @@
     tables = (ref_tile, ctf_table, cosine_table, sine_table)
     if small:
         packed = pack_rows(particles, group_counts, group_scale, defocus_bin)
-        others = xor_gather(packed, "blk", n_blk)[batch_size:]
+        pieces = xor_gather_pieces(packed, "blk", n_blk)
+        others = [pieces[1]] + ([jnp.concatenate(pieces[2:], axis=0)] if n_blk > 2 else [])
         own_rows = lax.optimization_barrier(packed.astype(jnp.float32))
-        groups = []
-        for rows in (own_rows, others):
-            meta = rows[:, width : width + 5].astype(jnp.float32)
-            gains = (meta[:, 0] + meta[:, 1]) + meta[:, 2]
-            groups.append((rows[:, :width], gains, meta[:, 3], meta[:, 4]))
-        live_mask = groups[0][2]
+        raw_groups = [own_rows, *others]
     else:
         gain_rows, live_mask = slot_weights(
             group_counts.reshape(1, -1), group_scale.reshape(1, -1), batch_size
         )
+        raw_groups = []
         groups = [(
             lax.all_gather(particles, "blk", axis=0, tiled=True),
             lax.all_gather(gain_rows, "blk", axis=0, tiled=True),
             lax.all_gather(live_mask, "blk", axis=0, tiled=True),
             lax.all_gather(defocus_bin.astype(jnp.float32), "blk", axis=0, tiled=True),
         )]
-    results = [block_rows(images, gains, bins, own_norms, *tables) for images, gains, _, bins in groups]
+    results = []
+    if small:
+        groups = []
+        for rows in raw_groups:
+            if results:
+                rows, _ = lax.optimization_barrier((rows, results[-1][1]))
+            meta = rows[:, width : width + 5].astype(jnp.float32)
+            gains = (meta[:, 0] + meta[:, 1]) + meta[:, 2]
+            groups.append((rows[:, :width], gains, meta[:, 3], meta[:, 4]))
+            results.append(block_rows(rows[:, :width], gains, meta[:, 4], own_norms, *tables))
+        live_mask = groups[0][2]
+    else:
+        results = [block_rows(images, gains, bins, own_norms, *tables) for images, gains, _, bins in groups]
     pieces = [shifted for shifted, _, _ in results]
     all_scores = jnp.concatenate([scores for _, scores, _ in results], axis=0)
     ctf_rows = jnp.concatenate([rows for _, _, rows in results], axis=0)

time: 34.9 us -> 41.5 us (1.19)
  other arithmetic: 5.69 us -> 10.7 us
  local copies, waits for them, and re-layouts: 2.47 us -> 4.65 us
  waiting for transfers between devices: 7.9 us -> 6.35 us
  matrix products: 4.56 us -> 5.08 us
    ppermute x3, waiting for transfers between devices: 2.33 us -> 0.01 us  [xor_gather_pieces(): lax.ppermute(value, axis, [(i, i ^ k) for i in range(size)])]
    ppermute x3, waiting for transfers between devices: 2.3 us -> 3.9 us  [per_device(): lax.ppermute(stats, 'blk', [(i, i ^ k) for i in range(n_blk)])]
    mul x1, other arithmetic: 0.08 us -> 1.32 us  [accumulate(): summed = jnp.sum(weights, axis=1) * (gain_rows * gain_rows)[:, None]]
    slice x2, other arithmetic: 0.44 us -> 1.52 us  [per_device(): groups.append((rows[:, :width], gains, meta[:, 3], meta[:, 4]))]
    reduce_sum x1, other arithmetic: 0.18 us -> 1.08 us  [accumulate(): summed = jnp.sum(weights, axis=1) * (gain_rows * gain_rows)[:, None]]
    ppermute x2, waiting for transfers between devices: 3.26 us -> 2.44 us  [xor_butterfly(): other = lax.ppermute(stats, axis, [(i, i ^ step) for i in range(size)])]
    add x0 -> x1, other arithmetic: none -> 0.7 us  [per_device(): gains = meta[:, 0] + meta[:, 1] + meta[:, 2]]
    concatenate x1, other arithmetic: 0.01 us -> 0.6 us  [per_device(): jnp.concatenate([spectral_reg, spectral_reg])[None, :]]
  transfers between devices with their start and end apart: 8 -> 8, of which waited for: 7 -> 4; matrix products, arithmetic and copies ran while one was open for 12% -> 20% of each run, Pallas kernels for 0% -> 0%
where the time goes in v11:
time: 41.5 us; the launch traced here: 41.2 us
  starting transfers between devices  11.9 us (29%)
  other arithmetic  10.7 us (26%)
  waiting for transfers between devices  6.35 us (15%)
  matrix products  5.08 us (12%)
  local copies, waits for them, and re-layouts  4.65 us (11%)
  Pallas kernels  1.54 us (4%)
  between operations  1.02 us (2%)
    ppermute x3, starting transfers between devices, xor_gather_pieces(): lax.ppermute(value, axis, [(i, i ^ k) for i in range(size)])  5.62 us
    ppermute x3, starting transfers between devices, per_device(): lax.ppermute(stats, 'blk', [(i, i ^ k) for i in range(n_blk)])  4.46 us
    ppermute x3, waiting for transfers between devices, per_device(): lax.ppermute(stats, 'blk', [(i, i ^ k) for i in range(n_blk)])  3.9 us
    unnamed x33, local copies, waits for them, and re-layouts  2.62 us
    ppermute x2, waiting for transfers between devices, xor_butterfly(): other = lax.ppermute(stats, axis, [(i, i ^ step) for i in range(size)])  2.44 us
    ppermute x2, starting transfers between devices, xor_butterfly(): other = lax.ppermute(stats, axis, [(i, i ^ step) for i in range(size)])  1.8 us
    dot_general x3, matrix products, tile_scores(): lax.dot_general(shifted, ref_rows, (((1,), (1,)), ((), ())), preferred_el...  1.55 us
    pallas_call x1, Pallas kernels, pack_rows(): pl.pallas_call(pack_kernel, out_shape=jax.ShapeDtypeStruct((slots, width...  1.54 us
  transfers between devices with their start and end apart: 8, of which 4 were waited for; matrix products, arithmetic and copies ran while one was open for 20% of the time, Pallas kernels for 0%

profile of v11, /device:TPU:0, one launch (start us, length us, event | category | flops | bytes accessed | tf_op | source)
XLA Modules:
  0.0 41.2 jit_solution(18332409356590793468)
XLA Ops:
  0.6 1.5 %shard_map.104 = bf16[8,4224]{1,0:T(8,128)(2,1)} custom-call(s32[4]{0:T(128)} %sizes_ref.1, f32[4]{0:T(128)} %scales_ref.1, s32[8]{0:T(128)} %bins_ref.1, bf16[8,4096]{1,0:T(8,128)(2,1)} %images_ref.1), custom_call_target="tpu_custom_call" | custom-call | tf_op jit(solution)/shard_map/pallas_call | solution.py:137
  2.2 5.0 %collective-permute-start.2 = (bf16[8,4224]{1,0:T(8,128)(2,1)}, bf16[8,4224]{1,0:T(8,128)(2,1)S(1)}, u32[]{:S(2)}, u32[]{:S(2)}) collective-permute-start(bf16[8,4224]{1,0:T(8,128)(2,1)} %shard_map.104), channel_id=1, source_target_pairs={{0,12},{4,8},{8,4},{12,0},{1,13},{5,9},{9,5},{13,1},{2,14},{6,10},... | collective-permute-start | bytes 202760 | tf_op jit(solution)/shard_map/ppermute | solution.py:147
  7.2 0.0 collective-permute-start.1
  7.2 0.6 %collective-permute-start = (bf16[8,4224]{1,0:T(8,128)(2,1)}, bf16[8,4224]{1,0:T(8,128)(2,1)S(1)}, u32[]{:S(2)}, u32[]{:S(2)}) collective-permute-start(bf16[8,4224]{1,0:T(8,128)(2,1)} %shard_map.104), channel_id=1, source_target_pairs={{0,4},{4,0},{8,12},{12,8},{1,5},{5,1},{9,13},{13,9},{2,6},{6,2},{1... | collective-permute-start | bytes 202760 | tf_op jit(solution)/shard_map/ppermute | solution.py:147
  7.8 0.9 %convert_element_type.39 = f32[8,4224]{1,0:T(8,128)S(1)} convert(bf16[8,4224]{1,0:T(8,128)(2,1)} %shard_map.104) | non-fusion elementwise | flops 33792 | bytes 202752 | tf_op jit(solution)/shard_map/convert_element_type | solution.py:219
  8.7 0.8 %slice_reduce_fusion.3 = (f32[8]{0:T(128)}, f32[8]{0:T(128)S(1)}, f32[8]{0:T(128)S(1)}) fusion(f32[8,4224]{1,0:T(8,128)S(1)} %convert_element_type.39), kind=kLoop, calls=%fused_computation.69 | loop fusion | flops 16 | bytes 256 | tf_op jit(solution)/shard_map/slice | solution.py:240
  9.5 0.0 copy-start.1
  9.5 0.0 copy-start.2
  9.5 1.1 %bitcast_convert_fusion = f32[50,4096]{1,0:T(8,128)S(1)} fusion(bf16[1,50,4096]{2,1,0:T(8,128)(2,1)} %param.10), kind=kLoop, calls=%fused_computation.34 | loop fusion | flops 204800 | bytes 1228800 | tf_op jit(solution)/shard_map/convert_element_type | solution.py:65
  10.7 0.2 fusion.33
  10.9 0.0 copy-start.9
  10.9 0.5 %fusion.10 = f32[16,50]{1,0:T(8,128)S(1)} fusion(f32[50,4096]{1,0:T(8,128)S(1)} %bitcast_convert_fusion, f32[16,2048]{1,0:T(8,128)S(1)} %copy-done), kind=kOutput, calls=%fused_computation.29 | convolution fusion | flops 20000768 | bytes 953472 | tf_op jit(solution)/shard_map/dot_general | solution.py:70
  11.4 0.2 convolution_multiply_fusion.4
  11.6 0.0 copy-done.1
  11.6 0.3 multiply_convert_fusion.5
  11.9 0.4 %fusion.8 = f32[8,16,50]{2,1,0:T(8,128)S(1)} fusion(bf16[8,16,2048]{2,1,0:T(8,128)(2,1)S(1)} %get-tuple-element.30, bf16[8,16,2048]{2,1,0:T(8,128)(2,1)S(1)} %get-tuple-element.29, bf16[1,50,4096]{2,1,0:T(8,128)(2,1)S(1)} %copy-done.9, f32[8,50]{1,0:T(8,128)S(1)} %convolution_multiply_fusion.4, f32[8]{0:T(128)S(1)} %get-tuple-element.11), kind=kOutput, calls=%fused_computation.16 | convolution fusion | flops 54538752 | bytes 1485408 | tf_op jit(solution)/shard_map/dot_general | solution.py:75
  12.4 0.0 collective-permute-done
  12.4 0.8 %slice_reduce_fusion.5 = (f32[8]{0:T(128)}, f32[8]{0:T(128)S(1)}, f32[8]{0:T(128)S(1)}) fusion(f32[8,5]{1,0:T(8,128)S(1)} %slice_convert_fusion.5), kind=kLoop, calls=%fused_computation.80 | loop fusion | flops 16 | bytes 256 | tf_op jit(solution)/shard_map/slice | solution.py:240
  13.2 0.2 fusion.32
  13.4 0.2 convolution_multiply_fusion.3
  13.6 0.3 multiply_convert_fusion.3
  13.9 0.0 copy-start.7
  13.9 0.4 %fusion.7 = f32[8,16,50]{2,1,0:T(8,128)S(1)} fusion(bf16[8,16,2048]{2,1,0:T(8,128)(2,1)S(1)} %get-tuple-element.28, bf16[8,16,2048]{2,1,0:T(8,128)(2,1)S(1)} %get-tuple-element.27, bf16[1,50,4096]{2,1,0:T(8,128)(2,1)S(1)} %copy-done.9, f32[8,50]{1,0:T(8,128)S(1)} %convolution_multiply_fusion.3, f32[8]{0:T(128)S(1)} %get-tuple-element.17), kind=kOutput, calls=%fused_computation.14 | convolution fusion | flops 54538752 | bytes 1485408 | tf_op jit(solution)/shard_map/dot_general | solution.py:75
  14.4 0.3 copy-done.5
  14.7 0.2 copy-done.7
  14.9 0.0 collective-permute-done.2
  14.9 0.0 collective-permute-done.1
  14.9 0.7 %fusion.25 = (f32[16]{0:T(128)S(1)}, f32[16]{0:T(128)}, f32[16]{0:T(128)S(1)}) fusion(f32[16,5]{1,0:T(8,128)S(1)} %slice_convert_fusion.4), kind=kLoop, calls=%fused_computation.61 | loop fusion | flops 32 | bytes 512 | tf_op jit(solution)/shard_map/add | solution.py:239
  15.6 0.3 fusion.28
  15.9 0.2 convolution_multiply_fusion.2
  16.1 0.7 %multiply_convert_fusion.1 = (bf16[16,16,2048]{2,1,0:T(8,128)(2,1)S(1)}, bf16[16,16,2048]{2,1,0:T(8,128)(2,1)S(1)}) fusion(f32[16,2048]{1,0:T(8,128)S(1)} %fusion.28, f32[16,2048]{1,0:T(8,128)S(1)} %copy-done.1, f32[16,2048]{1,0:T(8,128)S(1)} %get-tuple-element.32, f32[16,2048]{1,0:T(8,128)S(1)} %copy-done.2, f32[16,2048]{1,0:T(8,128)S(1)} %get-tuple-element.31), kind=kLoop, calls=%fused_computation.9 | loop fusion | flops 5242880 | bytes 2752512 | tf_op jit(solution)/shard_map/convert
  16.8 0.0 copy-done.13
  16.8 0.0 copy-start.11
  16.8 0.7 %fusion.6 = f32[16,16,50]{2,1,0:T(8,128)S(1)} fusion(bf16[16,16,2048]{2,1,0:T(8,128)(2,1)S(1)} %get-tuple-element.26, bf16[16,16,2048]{2,1,0:T(8,128)(2,1)S(1)} %get-tuple-element.25, bf16[1,50,4096]{2,1,0:T(8,128)(2,1)S(1)} %copy-done.9, f32[16,50]{1,0:T(8,128)S(1)} %convolution_multiply_fusion.2, f32[16]{0:T(128)S(1)} %get-tuple-element.13), kind=kOutput, calls=%fused_computation.12 | convolution fusion | flops 109077504 | bytes 2561216 | tf_op jit(solution)/shard_map/dot_general | solution.py:75
  17.5 0.3 fusion.21
  17.9 0.0 copy-done.4
  17.9 1.0 %exponential_reduce_fusion = f32[32]{0:T(128)} fusion(f32[32]{0:T(128)S(1)} %fusion.21, f32[16,16,50]{2,1,0:T(8,128)S(1)} %fusion.6, f32[8,16,50]{2,1,0:T(8,128)S(1)} %fusion.7, f32[8,16,50]{2,1,0:T(8,128)S(1)} %fusion.8), kind=kLoop, calls=%fused_computation.44 | loop fusion | flops 102368 | bytes 102656 | tf_op jit(solution)/shard_map/reduce_sum | solution.py:253
  18.9 0.1 squeeze.15
  19.0 0.7 %stack.32 = f32[1,4,8]{2,1,0:T(4,128)S(1)} reshape(f32[32]{0:T(128)} %exponential_reduce_fusion) | data formatting | bytes 256 | tf_op jit(solution)/shard_map/stack | solution.py:256
  19.6 0.0 collective-permute-start.3
  19.7 1.2 %collective-permute-done.3 = f32[2,4,8]{2,1,0:T(4,128)S(1)} collective-permute-done((f32[2,4,8]{2,1,0:T(4,128)S(1)}, f32[2,4,8]{2,1,0:T(4,128)S(1)}, u32[]{:S(2)}, u32[]{:S(2)}) %collective-permute-start.3) | collective-permute-done | bytes 288 | tf_op jit(solution)/shard_map/ppermute | solution.py:161
  20.8 1.8 %collective-permute-start.4 = (f32[2,4,8]{2,1,0:T(4,128)S(1)}, f32[2,4,8]{2,1,0:T(4,128)S(1)}, u32[]{:S(2)}, u32[]{:S(2)}) collective-permute-start(f32[2,4,8]{2,1,0:T(4,128)S(1)} %pad_maximum_fusion.18), channel_id=1, source_target_pairs={{0,2},{1,3},{2,0},{3,1},{4,6},{5,7},{6,4},{7,5},{8,10},{9,11},{10,... | collective-permute-start | bytes 776 | tf_op jit(solution)/shard_map/ppermute | solution.py:161
  22.6 0.6 %pad_maximum_fusion.16 = f32[4096]{0:T(1024)} fusion(f32[2048]{0:T(1024)S(1)} %copy-done.11), kind=kLoop, calls=%fused_computation.53 | loop fusion | flops 4096 | bytes 24576 | tf_op jit(solution)/shard_map/concatenate | solution.py:281
  23.2 1.3 %collective-permute-done.4 = f32[2,4,8]{2,1,0:T(4,128)S(1)} collective-permute-done((f32[2,4,8]{2,1,0:T(4,128)S(1)}, f32[2,4,8]{2,1,0:T(4,128)S(1)}, u32[]{:S(2)}, u32[]{:S(2)}) %collective-permute-start.4) | collective-permute-done | bytes 288 | tf_op jit(solution)/shard_map/ppermute | solution.py:161
  24.5 3.9 %collective-permute-start.7 = (f32[2,4,8]{2,1,0:T(4,128)S(1)}, f32[2,4,8]{2,1,0:T(4,128)S(1)}, u32[]{:S(2)}, u32[]{:S(2)}) collective-permute-start(f32[2,4,8]{2,1,0:T(4,128)S(1)} %get-tuple-element.40), channel_id=1, source_target_pairs={{0,12},{4,8},{8,4},{12,0},{1,13},{5,9},{9,5},{13,1},{2,14},{6,10},... | collective-permute-start | bytes 776 | tf_op jit(solution)/shard_map/ppermute | solution.py:259
  28.4 1.3 %fusion.48 = (f32[32]{0:T(128)S(1)}, f32[32]{0:T(128)S(1)}, f32[32]{0:T(128)}) fusion(f32[16]{0:T(128)} %copy-done.13, f32[8]{0:T(128)} %copy-done.15, f32[8]{0:T(128)} %copy-done.14, f32[16]{0:T(128)} %get-tuple-element.14, f32[8]{0:T(128)} %get-tuple-element.16, f32[8]{0:T(128)} %get-tuple-element.10), kind=kLoop, calls=%fused_computation.115 | loop fusion | flops 160 | bytes 640 | tf_op jit(solution)/shard_map/mul | solution.py:186
  29.7 0.0 collective-permute-start.5
  29.7 0.6 %collective-permute-start.6 = (f32[2,4,8]{2,1,0:T(4,128)S(1)}, f32[2,4,8]{2,1,0:T(4,128)S(1)}, u32[]{:S(2)}, u32[]{:S(2)}) collective-permute-start(f32[2,4,8]{2,1,0:T(4,128)S(1)} %get-tuple-element.40), channel_id=1, source_target_pairs={{0,8},{4,12},{8,0},{12,4},{1,9},{5,13},{9,1},{13,5},{2,10},{6,14},... | collective-permute-start | bytes 776 | tf_op jit(solution)/shard_map/ppermute | solution.py:259
  30.3 0.0 collective-permute-done.7
  30.3 3.0 %collective-permute-done.5 = f32[2,4,8]{2,1,0:T(4,128)S(1)} collective-permute-done((f32[2,4,8]{2,1,0:T(4,128)S(1)}, f32[2,4,8]{2,1,0:T(4,128)S(1)}, u32[]{:S(2)}, u32[]{:S(2)}) %collective-permute-start.5) | collective-permute-done | bytes 288 | tf_op jit(solution)/shard_map/ppermute | solution.py:259
  33.4 0.9 %collective-permute-done.6 = f32[2,4,8]{2,1,0:T(4,128)S(1)} collective-permute-done((f32[2,4,8]{2,1,0:T(4,128)S(1)}, f32[2,4,8]{2,1,0:T(4,128)S(1)}, u32[]{:S(2)}, u32[]{:S(2)}) %collective-permute-start.6) | collective-permute-done | bytes 288 | tf_op jit(solution)/shard_map/ppermute | solution.py:259
  34.3 0.7 %sub.93 = f32[32]{0:T(128)} reshape(f32[4,8]{1,0:T(4,128)S(1)} %slice_reduce_fusion.2) | data formatting | bytes 256 | tf_op jit(solution)/shard_map/sub | solution.py:169
  35.0 0.6 %div.13 = f32[32]{0:T(128)} reshape(f32[4,8]{1,0:T(4,128)S(1)} %fusion.24) | data formatting | bytes 256 | tf_op jit(solution)/shard_map/div | solution.py:169
  35.6 1.1 %fusion.49 = (f32[32,50]{1,0:T(8,128)S(1)}, f32[32,16,50]{2,1,0:T(8,128)S(1)}) fusion(f32[32]{0:T(128)} %get-tuple-element.51, f32[32]{0:T(128)} %div.13, f32[32]{0:T(128)} %sub.93, f32[16,16,50]{2,1,0:T(8,128)S(1)} %fusion.6, f32[8,16,50]{2,1,0:T(8,128)} %copy-done.4, f32[8,16,50]{2,1,0:T(8,128)} %copy-done.3), kind=kLoop, calls=%fused_computation.116 | loop fusion | flops 152000 | bytes 211584 | tf_op jit(solution)/shard_map/reduce_sum | solution.py:186
  36.7 0.1 multiply_convert_fusion.6
  36.8 0.5 %convolution_bitcast_fusion.2 = f32[50,4096]{1,0:T(8,128)S(1)} fusion(bf16[32,16,50]{2,1,0:T(8,128)(2,1)S(1)} %multiply_convert_fusion.6, bf16[16,16,2048]{2,1,0:T(8,128)(2,1)S(1)} %get-tuple-element.26, bf16[16,16,2048]{2,1,0:T(8,128)(2,1)S(1)} %get-tuple-element.25), kind=kOutput, calls=%fused_computation.6 | convolution fusion | flops 109051904 | bytes 2967552 | tf_op jit(solution)/shard_map/dot_general | solution.py:178
  37.3 0.0 copy-start.8
  37.3 0.0 copy-start.10
  37.3 0.3 convolution_bitcast_fusion.1
  37.6 0.3 copy-done.12
  37.9 0.5 %compare_select_fusion = f32[8]{0:T(128)} fusion(f32[8]{0:T(128)S(1)} %copy-done.12, f32[4,8]{1,0:T(4,128)S(1)} %fusion.24, f32[4,8]{1,0:T(4,128)S(1)} %slice_reduce_fusion.2), kind=kLoop, calls=%fused_computation.99 | loop fusion | flops 24 | bytes 128 | tf_op jit(solution)/shard_map/jit(_where)/select_n | solution.py:278
  38.4 0.6 %fusion.15 = f32[50,2048]{1,0:T(8,128)S(1)} fusion(f32[16,2048]{1,0:T(8,128)S(1)} %fusion.28, f32[8,2048]{1,0:T(8,128)S(1)} %fusion.32, f32[8,2048]{1,0:T(8,128)S(1)} %fusion.33, f32[32,50]{1,0:T(8,128)S(1)} %get-tuple-element.21, f32[32]{0:T(128)S(1)} %get-tuple-element.19), kind=kOutput, calls=%fused_computation.37 | convolution fusion | flops 39519808 | bytes 678272 | tf_op jit(solution)/shard_map/dot_general | solution.py:187
  39.1 0.4 fusion.3
  39.5 1.7 %copy.12 = f32[1,50,4096]{2,0,1:T(1,128)} copy(f32[1,50,4096]{2,1,0:T(8,128)S(1)} %fusion.3) | data formatting | bytes 1638400
  (41 shorter events, 0.2 us)
Async XLA Ops:
  0.6 10.0 %copy-start = (f32[16,2048]{1,0:T(8,128)S(1)}, f32[16,2048]{1,0:T(8,128)}, u32[]{:S(2)}) copy-start(f32[16,2048]{1,0:T(8,128)} %param.11) | copy-start | bytes 393220
  2.2 12.7 %collective-permute-start.2 = (bf16[8,4224]{1,0:T(8,128)(2,1)}, bf16[8,4224]{1,0:T(8,128)(2,1)S(1)}, u32[]{:S(2)}, u32[]{:S(2)}) collective-permute-start(bf16[8,4224]{1,0:T(8,128)(2,1)} %shard_map.104), channel_id=1, source_target_pairs={{0,12},{4,8},{8,4},{12,0},{1,13},{5,9},{9,5},{13,1},{2,14},{6,10},... | collective-permute-start | bytes 202760 | tf_op jit(solution)/shard_map/ppermute | solution.py:147
  7.2 7.7 %collective-permute-start.1 = (bf16[8,4224]{1,0:T(8,128)(2,1)}, bf16[8,4224]{1,0:T(8,128)(2,1)S(1)}, u32[]{:S(2)}, u32[]{:S(2)}) collective-permute-start(bf16[8,4224]{1,0:T(8,128)(2,1)} %shard_map.104), channel_id=1, source_target_pairs={{0,8},{4,12},{8,0},{12,4},{1,9},{5,13},{9,1},{13,5},{2,10},{6,14},... | collective-permute-start | bytes 202760 | tf_op jit(solution)/shard_map/ppermute | solution.py:147
  7.2 5.1 %collective-permute-start = (bf16[8,4224]{1,0:T(8,128)(2,1)}, bf16[8,4224]{1,0:T(8,128)(2,1)S(1)}, u32[]{:S(2)}, u32[]{:S(2)}) collective-permute-start(bf16[8,4224]{1,0:T(8,128)(2,1)} %shard_map.104), channel_id=1, source_target_pairs={{0,4},{4,0},{8,12},{12,8},{1,5},{5,1},{9,13},{13,9},{2,6},{6,2},{1... | collective-permute-start | bytes 202760 | tf_op jit(solution)/shard_map/ppermute | solution.py:147
  9.5 2.4 %copy-start.14 = (f32[8]{0:T(128)}, f32[8]{0:T(128)S(1)}, u32[]{:S(2)}) copy-start(f32[8]{0:T(128)S(1)} %get-tuple-element.11) | copy-start | bytes 100
  9.5 2.1 %copy-start.1 = (f32[16,2048]{1,0:T(8,128)S(1)}, f32[16,2048]{1,0:T(8,128)}, u32[]{:S(2)}) copy-start(f32[16,2048]{1,0:T(8,128)} %constant.4.clone) | copy-start | bytes 393220
  9.5 2.1 %copy-start.2 = (f32[16,2048]{1,0:T(8,128)S(1)}, f32[16,2048]{1,0:T(8,128)}, u32[]{:S(2)}) copy-start(f32[16,2048]{1,0:T(8,128)} %constant.3.clone) | copy-start | bytes 393220
  10.9 1.0 %copy-start.9 = (bf16[1,50,4096]{2,1,0:T(8,128)(2,1)S(1)}, bf16[1,50,4096]{2,1,0:T(8,128)(2,1)}, u32[]{:S(2)}) copy-start(bf16[1,50,4096]{2,1,0:T(8,128)(2,1)} %param.10) | copy-start | bytes 1228804
  12.4 5.5 %copy-start.3 = (f32[8,16,50]{2,1,0:T(8,128)}, f32[8,16,50]{2,1,0:T(8,128)S(1)}, u32[]{:S(2)}) copy-start(f32[8,16,50]{2,1,0:T(8,128)S(1)} %fusion.8) | copy-start | bytes 76804
  13.2 1.2 %copy-start.15 = (f32[8]{0:T(128)}, f32[8]{0:T(128)S(1)}, u32[]{:S(2)}) copy-start(f32[8]{0:T(128)S(1)} %get-tuple-element.17) | copy-start | bytes 100
  13.9 0.8 %copy-start.5 = (bf16[8,16,2048]{2,1,0:T(8,128)(2,1)}, bf16[8,16,2048]{2,1,0:T(8,128)(2,1)S(1)}, u32[]{:S(2)}) copy-start(bf16[8,16,2048]{2,1,0:T(8,128)(2,1)S(1)} %get-tuple-element.27) | copy-start | bytes 1572868
  13.9 1.0 %copy-start.7 = (bf16[8,16,2048]{2,1,0:T(8,128)(2,1)}, bf16[8,16,2048]{2,1,0:T(8,128)(2,1)S(1)}, u32[]{:S(2)}) copy-start(bf16[8,16,2048]{2,1,0:T(8,128)(2,1)S(1)} %get-tuple-element.28) | copy-start | bytes 1572868
  14.9 3.0 %copy-start.4 = (f32[8,16,50]{2,1,0:T(8,128)}, f32[8,16,50]{2,1,0:T(8,128)S(1)}, u32[]{:S(2)}) copy-start(f32[8,16,50]{2,1,0:T(8,128)S(1)} %fusion.7) | copy-start | bytes 76804
  15.6 1.2 %copy-start.13 = (f32[16]{0:T(128)}, f32[16]{0:T(128)S(1)}, u32[]{:S(2)}) copy-start(f32[16]{0:T(128)S(1)} %get-tuple-element.13) | copy-start | bytes 196
  16.8 5.8 %copy-start.11 = (f32[2048]{0:T(1024)S(1)}, f32[2048]{0:T(1024)}, u32[]{:S(2)}) copy-start(f32[2048]{0:T(1024)} %param.12) | copy-start | bytes 24580
  19.6 1.2 %collective-permute-start.3 = (f32[2,4,8]{2,1,0:T(4,128)S(1)}, f32[2,4,8]{2,1,0:T(4,128)S(1)}, u32[]{:S(2)}, u32[]{:S(2)}) collective-permute-start(f32[2,4,8]{2,1,0:T(4,128)S(1)} %pad_maximum_fusion.17), channel_id=1, source_target_pairs={{0,1},{1,0},{2,3},{3,2},{4,5},{5,4},{6,7},{7,6},{8,9},{9,8},{10,11... | collective-permute-start | bytes 776 | tf_op jit(solution)/shard_map/ppermute | solution.py:161
  20.8 3.7 %collective-permute-start.4 = (f32[2,4,8]{2,1,0:T(4,128)S(1)}, f32[2,4,8]{2,1,0:T(4,128)S(1)}, u32[]{:S(2)}, u32[]{:S(2)}) collective-permute-start(f32[2,4,8]{2,1,0:T(4,128)S(1)} %pad_maximum_fusion.18), channel_id=1, source_target_pairs={{0,2},{1,3},{2,0},{3,1},{4,6},{5,7},{6,4},{7,5},{8,10},{9,11},{10,... | collective-permute-start | bytes 776 | tf_op jit(solution)/shard_map/ppermute | solution.py:161
  24.5 5.8 %collective-permute-start.7 = (f32[2,4,8]{2,1,0:T(4,128)S(1)}, f32[2,4,8]{2,1,0:T(4,128)S(1)}, u32[]{:S(2)}, u32[]{:S(2)}) collective-permute-start(f32[2,4,8]{2,1,0:T(4,128)S(1)} %get-tuple-element.40), channel_id=1, source_target_pairs={{0,12},{4,8},{8,4},{12,0},{1,13},{5,9},{9,5},{13,1},{2,14},{6,10},... | collective-permute-start | bytes 776 | tf_op jit(solution)/shard_map/ppermute | solution.py:259
  29.7 3.6 %collective-permute-start.5 = (f32[2,4,8]{2,1,0:T(4,128)S(1)}, f32[2,4,8]{2,1,0:T(4,128)S(1)}, u32[]{:S(2)}, u32[]{:S(2)}) collective-permute-start(f32[2,4,8]{2,1,0:T(4,128)S(1)} %get-tuple-element.40), channel_id=1, source_target_pairs={{0,4},{4,0},{8,12},{12,8},{1,5},{5,1},{9,13},{13,9},{2,6},{6,2},{1... | collective-permute-start | bytes 776 | tf_op jit(solution)/shard_map/ppermute | solution.py:259
  29.7 4.5 %collective-permute-start.6 = (f32[2,4,8]{2,1,0:T(4,128)S(1)}, f32[2,4,8]{2,1,0:T(4,128)S(1)}, u32[]{:S(2)}, u32[]{:S(2)}) collective-permute-start(f32[2,4,8]{2,1,0:T(4,128)S(1)} %get-tuple-element.40), channel_id=1, source_target_pairs={{0,8},{4,12},{8,0},{12,4},{1,9},{5,13},{9,1},{13,5},{2,10},{6,14},... | collective-permute-start | bytes 776 | tf_op jit(solution)/shard_map/ppermute | solution.py:259
  37.3 0.7 %copy-start.12 = (f32[8]{0:T(128)S(1)}, f32[8]{0:T(128)}, u32[]{:S(2)}) copy-start(f32[8]{0:T(128)} %get-tuple-element.10) | copy-start | bytes 100
  37.3 1.8 %copy-start.6 = (bf16[8,16,2048]{2,1,0:T(8,128)(2,1)S(1)}, bf16[8,16,2048]{2,1,0:T(8,128)(2,1)}, u32[]{:S(2)}) copy-start(bf16[8,16,2048]{2,1,0:T(8,128)(2,1)} %copy-done.5) | copy-start | bytes 1572868
  37.3 1.8 %copy-start.8 = (bf16[8,16,2048]{2,1,0:T(8,128)(2,1)S(1)}, bf16[8,16,2048]{2,1,0:T(8,128)(2,1)}, u32[]{:S(2)}) copy-start(bf16[8,16,2048]{2,1,0:T(8,128)(2,1)} %copy-done.7) | copy-start | bytes 1572868
  37.3 1.8 %copy-start.10 = (f32[4096]{0:T(1024)S(1)}, f32[4096]{0:T(1024)}, u32[]{:S(2)}) copy-start(f32[4096]{0:T(1024)} %pad_maximum_fusion.16) | copy-start | bytes 49156

commit v12 on v10

--- a/solution.py
+++ b/solution.py
@@ -247,12 +247,12 @@
     if small:
         stats = jnp.stack([peak_all, totals_all]).reshape(2, n_blk, batch_size)
         stats = xor_butterfly(stats, "cls", n_cls)
-        parts = [stats] + [
-            xor_reorder(lax.ppermute(stats, "blk", [(i, i ^ k) for i in range(n_blk)]), k, 1)
-            for k in range(1, n_blk)
-        ]
-        parts = jnp.stack(parts)
-        peak_all, totals_all = combine_many(parts[:, 0], parts[:, 1])
+        step = 1
+        while step < n_blk:
+            other = xor_reorder(lax.ppermute(stats, "blk", [(i, i ^ step) for i in range(n_blk)]), step, 1)
+            stats = jnp.stack(combine_stats(stats, other))
+            step *= 2
+        peak_all, totals_all = stats[0], stats[1]
         peak_all = peak_all.reshape(-1)
         totals_all = totals_all.reshape(-1)
         peak_score = peak_all[:batch_size]

time: 34.9 us -> 36.4 us (1.043)
  waiting for transfers between devices: 7.9 us -> 10.7 us
  starting transfers between devices: 11.6 us -> 9.61 us
  local copies, waits for them, and re-layouts: 2.47 us -> 3.12 us
    ppermute x3 -> x2, waiting for transfers between devices: 2.3 us -> 5.4 us  [per_device(): lax.ppermute(stats, 'blk', [(i, i ^ step) for i in range(n_blk)])]
    ppermute x3 -> x2, starting transfers between devices: 4.45 us -> 2.42 us  [per_device(): lax.ppermute(stats, 'blk', [(i, i ^ step) for i in range(n_blk)])]
    squeeze x0 -> x5, local copies, waits for them, and re-layouts: none -> 0.41 us  [the longest x4 0.33 us: combine_stats(): latter[1] * jnp.exp(latter[0] - new_peak)]
    another operation x6 -> x3, other arithmetic: 1.44 us -> 1.4 us
  transfers between devices with their start and end apart: 8 -> 7, of which waited for: 7 -> 6; matrix products, arithmetic and copies ran while one was open for 12% -> 13% of each run, Pallas kernels for 0% -> 0%
where the time goes in v12:
time: 36.4 us; the launch traced here: 36.1 us
  waiting for transfers between devices  10.7 us (29%)
  starting transfers between devices  9.61 us (26%)
  other arithmetic  5.71 us (16%)
  matrix products  4.56 us (13%)
  local copies, waits for them, and re-layouts  3.12 us (9%)
  Pallas kernels  1.57 us (4%)
  between operations  0.9 us (2%)
    ppermute x3, starting transfers between devices, xor_gather(): lax.ppermute(value, axis, [(i, i ^ k) for i in range(size)])  5.62 us
    ppermute x2, waiting for transfers between devices, per_device(): lax.ppermute(stats, 'blk', [(i, i ^ step) for i in range(n_blk)])  5.4 us
    ppermute x2, waiting for transfers between devices, xor_butterfly(): other = lax.ppermute(stats, axis, [(i, i ^ step) for i in range(size)])  2.92 us
    ppermute x2, starting transfers between devices, per_device(): lax.ppermute(stats, 'blk', [(i, i ^ step) for i in range(n_blk)])  2.42 us
    ppermute x3, waiting for transfers between devices, xor_gather(): lax.ppermute(value, axis, [(i, i ^ k) for i in range(size)])  2.33 us
    unnamed x17, local copies, waits for them, and re-layouts  2.11 us
    ppermute x2, starting transfers between devices, xor_butterfly(): other = lax.ppermute(stats, axis, [(i, i ^ step) for i in range(size)])  1.58 us
    pallas_call x1, Pallas kernels, pack_rows(): pl.pallas_call(pack_kernel, out_shape=jax.ShapeDtypeStruct((slots, width...  1.57 us
  transfers between devices with their start and end apart: 7, of which 6 were waited for; matrix products, arithmetic and copies ran while one was open for 13% of the time, Pallas kernels for 0%

profile of v12, /device:TPU:0, one launch (start us, length us, event | category | flops | bytes accessed | tf_op | source)
XLA Modules:
  0.0 36.1 jit_solution(17210292384457900591)
XLA Ops:
  0.6 0.0 copy-start.2
  0.6 0.0 copy-start.3
  0.7 0.0 copy-start.4
  0.7 1.6 %shard_map.104 = bf16[8,4224]{1,0:T(8,128)(2,1)} custom-call(s32[4]{0:T(128)} %sizes_ref.1, f32[4]{0:T(128)} %scales_ref.1, s32[8]{0:T(128)} %bins_ref.1, bf16[8,4096]{1,0:T(8,128)(2,1)} %images_ref.1), custom_call_target="tpu_custom_call" | custom-call | tf_op jit(solution)/shard_map/pallas_call | solution.py:137
  2.2 3.0 %collective-permute-start = (bf16[8,4224]{1,0:T(8,128)(2,1)}, bf16[8,4224]{1,0:T(8,128)(2,1)S(1)}, u32[]{:S(2)}, u32[]{:S(2)}) collective-permute-start(bf16[8,4224]{1,0:T(8,128)(2,1)} %shard_map.104), channel_id=1, source_target_pairs={{0,4},{4,0},{8,12},{12,8},{1,5},{5,1},{9,13},{13,9},{2,6},{6,2},{1... | collective-permute-start | bytes 202760 | tf_op jit(solution)/shard_map/ppermute | solution.py:147
  5.3 2.6 %collective-permute-start.1 = (bf16[8,4224]{1,0:T(8,128)(2,1)}, bf16[8,4224]{1,0:T(8,128)(2,1)S(1)}, u32[]{:S(2)}, u32[]{:S(2)}) collective-permute-start(bf16[8,4224]{1,0:T(8,128)(2,1)} %shard_map.104), channel_id=1, source_target_pairs={{0,8},{4,12},{8,0},{12,4},{1,9},{5,13},{9,1},{13,5},{2,10},{6,14},... | collective-permute-start | bytes 202760 | tf_op jit(solution)/shard_map/ppermute | solution.py:147
  7.8 0.0 collective-permute-start.2
  7.8 1.0 %convert_element_type.26 = f32[8,4224]{1,0:T(8,128)S(1)} convert(bf16[8,4224]{1,0:T(8,128)(2,1)} %shard_map.104) | non-fusion elementwise | flops 33792 | bytes 202752 | tf_op jit(solution)/shard_map/convert_element_type | solution.py:219
  8.8 0.2 slice_reduce_fusion.2
  9.0 0.0 copy-start.5
  9.1 1.1 %bitcast_convert_fusion = f32[50,4096]{1,0:T(8,128)S(1)} fusion(bf16[1,50,4096]{2,1,0:T(8,128)(2,1)} %param.10), kind=kLoop, calls=%fused_computation.25 | loop fusion | flops 204800 | bytes 1228800 | tf_op jit(solution)/shard_map/convert_element_type | solution.py:65
  10.2 0.0 copy-done.4
  10.2 0.2 fusion.24
  10.4 0.5 %fusion.8 = f32[16,50]{1,0:T(8,128)S(1)} fusion(f32[50,4096]{1,0:T(8,128)S(1)} %bitcast_convert_fusion, f32[16,2048]{1,0:T(8,128)S(1)} %copy-done.4), kind=kOutput, calls=%fused_computation.21 | convolution fusion | flops 20000768 | bytes 953472 | tf_op jit(solution)/shard_map/dot_general | solution.py:70
  10.9 0.2 convolution_multiply_fusion.2
  11.1 0.0 copy-done.2
  11.1 0.0 copy-done.3
  11.1 0.3 multiply_convert_fusion.3
  11.4 0.0 copy-done.5
  11.5 0.4 %fusion.6 = f32[8,16,50]{2,1,0:T(8,128)S(1)} fusion(bf16[8,16,2048]{2,1,0:T(8,128)(2,1)S(1)} %get-tuple-element.30, bf16[8,16,2048]{2,1,0:T(8,128)(2,1)S(1)} %get-tuple-element.29, bf16[1,50,4096]{2,1,0:T(8,128)(2,1)S(1)} %copy-done.5, f32[8,50]{1,0:T(8,128)S(1)} %convolution_multiply_fusion.2, f32[8]{0:T(128)S(1)} %get-tuple-element.7), kind=kOutput, calls=%fused_computation.12 | convolution fusion | flops 54538752 | bytes 1485408 | tf_op jit(solution)/shard_map/dot_general | solution.py:75
  11.9 0.0 collective-permute-done
  11.9 1.0 %collective-permute-done.1 = bf16[8,4224]{1,0:T(8,128)(2,1)S(1)} collective-permute-done((bf16[8,4224]{1,0:T(8,128)(2,1)}, bf16[8,4224]{1,0:T(8,128)(2,1)S(1)}, u32[]{:S(2)}, u32[]{:S(2)}) %collective-permute-start.1) | collective-permute-done | bytes 67616 | tf_op jit(solution)/shard_map/ppermute | solution.py:147
  12.9 1.4 %collective-permute-done.2 = bf16[8,4224]{1,0:T(8,128)(2,1)S(1)} collective-permute-done((bf16[8,4224]{1,0:T(8,128)(2,1)}, bf16[8,4224]{1,0:T(8,128)(2,1)S(1)}, u32[]{:S(2)}, u32[]{:S(2)}) %collective-permute-start.2) | collective-permute-done | bytes 67616 | tf_op jit(solution)/shard_map/ppermute | solution.py:147
  14.3 0.2 slice_reduce_fusion
  14.5 0.3 fusion.19
  14.8 0.2 convolution_multiply_fusion.1
  15.0 1.1 %multiply_convert_fusion.1 = (bf16[24,16,2048]{2,1,0:T(8,128)(2,1)S(1)}, bf16[24,16,2048]{2,1,0:T(8,128)(2,1)S(1)}) fusion(f32[24,2048]{1,0:T(8,128)S(1)} %fusion.19, f32[16,2048]{1,0:T(8,128)S(1)} %copy-done.2, f32[24,2048]{1,0:T(8,128)S(1)} %get-tuple-element.32, f32[16,2048]{1,0:T(8,128)S(1)} %copy-done.3, f32[24,2048]{1,0:T(8,128)S(1)} %get-tuple-element.31), kind=kLoop, calls=%fused_computation.7 | loop fusion | flops 7864320 | bytes 3997696 | tf_op jit(solution)/shard_map/convert
  16.1 0.0 copy-start
  16.1 0.0 copy-start.6
  16.1 1.0 %fusion.5 = f32[24,16,50]{2,1,0:T(8,128)S(1)} fusion(bf16[24,16,2048]{2,1,0:T(8,128)(2,1)S(1)} %get-tuple-element.28, bf16[24,16,2048]{2,1,0:T(8,128)(2,1)S(1)} %get-tuple-element.27, bf16[1,50,4096]{2,1,0:T(8,128)(2,1)S(1)} %copy-done.5, f32[24,50]{1,0:T(8,128)S(1)} %convolution_multiply_fusion.1, f32[24]{0:T(128)S(1)} %get-tuple-element.10), kind=kOutput, calls=%fused_computation.10 | convolution fusion | flops 163616256 | bytes 3637024 | tf_op jit(solution)/shard_map/dot_general | solution.py:75
  17.1 0.2 copy-done
  17.3 0.3 fusion.15
  17.6 0.5 %exponential_reduce_fusion = f32[32]{0:T(128)S(1)} fusion(f32[24,16,50]{2,1,0:T(8,128)S(1)} %fusion.5, f32[8,16,50]{2,1,0:T(8,128)S(1)} %fusion.6, f32[32]{0:T(128)S(1)} %fusion.15), kind=kLoop, calls=%fused_computation.33 | loop fusion | flops 76768 | bytes 102656 | tf_op jit(solution)/shard_map/reduce_sum | solution.py:245
  18.1 0.1 stack.24
  18.2 0.1 stack.25
  18.3 0.0 collective-permute-start.3
  18.3 0.0 copy-done.6
  18.3 1.1 %collective-permute-done.3 = f32[2,4,8]{2,1,0:T(4,128)S(1)} collective-permute-done((f32[2,4,8]{2,1,0:T(4,128)S(1)}, f32[2,4,8]{2,1,0:T(4,128)S(1)}, u32[]{:S(2)}, u32[]{:S(2)}) %collective-permute-start.3) | collective-permute-done | bytes 288 | tf_op jit(solution)/shard_map/ppermute | solution.py:162
  19.5 1.6 %collective-permute-start.4 = (f32[2,4,8]{2,1,0:T(4,128)S(1)}, f32[2,4,8]{2,1,0:T(4,128)S(1)}, u32[]{:S(2)}, u32[]{:S(2)}) collective-permute-start(f32[2,4,8]{2,1,0:T(4,128)S(1)} %pad_maximum_fusion.13), channel_id=1, source_target_pairs={{0,2},{1,3},{2,0},{3,1},{4,6},{5,7},{6,4},{7,5},{8,10},{9,11},{10,... | collective-permute-start | bytes 776 | tf_op jit(solution)/shard_map/ppermute | solution.py:162
  21.0 0.1 fusion.50
  21.1 0.1 squeeze.77
  21.2 0.1 squeeze.82
  21.3 0.1 squeeze.67
  21.3 1.8 %collective-permute-done.4 = f32[2,4,8]{2,1,0:T(4,128)S(1)} collective-permute-done((f32[2,4,8]{2,1,0:T(4,128)S(1)}, f32[2,4,8]{2,1,0:T(4,128)S(1)}, u32[]{:S(2)}, u32[]{:S(2)}) %collective-permute-start.4) | collective-permute-done | bytes 288 | tf_op jit(solution)/shard_map/ppermute | solution.py:162
  23.2 0.7 %collective-permute-start.5 = (f32[2,4,8]{2,1,0:T(4,128)S(1)}, f32[2,4,8]{2,1,0:T(4,128)S(1)}, u32[]{:S(2)}, u32[]{:S(2)}) collective-permute-start(f32[2,4,8]{2,1,0:T(4,128)S(1)} %pad_maximum_fusion.14), channel_id=1, source_target_pairs={{0,4},{4,0},{8,12},{12,8},{1,5},{5,1},{9,13},{13,9},{2,6},{6,2},{1... | collective-permute-start | bytes 776 | tf_op jit(solution)/shard_map/ppermute | solution.py:252
  23.9 0.1 squeeze.71
  24.0 0.1 squeeze.68
  24.0 0.1 squeeze.72
  24.1 2.7 %collective-permute-done.5 = f32[2,4,8]{2,1,0:T(4,128)S(1)} collective-permute-done((f32[2,4,8]{2,1,0:T(4,128)S(1)}, f32[2,4,8]{2,1,0:T(4,128)S(1)}, u32[]{:S(2)}, u32[]{:S(2)}) %collective-permute-start.5) | collective-permute-done | bytes 288 | tf_op jit(solution)/shard_map/ppermute | solution.py:252
  26.9 1.7 %collective-permute-start.6 = (f32[2,4,8]{2,1,0:T(4,128)S(1)}, f32[2,4,8]{2,1,0:T(4,128)S(1)}, u32[]{:S(2)}, u32[]{:S(2)}) collective-permute-start(f32[2,4,8]{2,1,0:T(4,128)S(1)} %pad_maximum_fusion.16), channel_id=1, source_target_pairs={{0,8},{4,12},{8,0},{12,4},{1,9},{5,13},{9,1},{13,5},{2,10},{6,14},... | collective-permute-start | bytes 776 | tf_op jit(solution)/shard_map/ppermute | solution.py:252
  28.6 0.1 squeeze.69
  28.7 0.1 squeeze.73
  28.8 2.7 %collective-permute-done.6 = f32[2,4,8]{2,1,0:T(4,128)S(1)} collective-permute-done((f32[2,4,8]{2,1,0:T(4,128)S(1)}, f32[2,4,8]{2,1,0:T(4,128)S(1)}, u32[]{:S(2)}, u32[]{:S(2)}) %collective-permute-start.6) | collective-permute-done | bytes 288 | tf_op jit(solution)/shard_map/ppermute | solution.py:252
  31.5 0.1 squeeze.70
  31.6 0.1 squeeze.74
  31.7 0.0 copy-start.1
  31.7 0.2 fusion.48
  31.9 0.4 %convolution_bitcast_fusion.1 = f32[50,4096]{1,0:T(8,128)S(1)} fusion(bf16[8,16,2048]{2,1,0:T(8,128)(2,1)S(1)} %get-tuple-element.30, bf16[8,16,2048]{2,1,0:T(8,128)(2,1)S(1)} %get-tuple-element.29, f32[32]{0:T(128)S(1)} %get-tuple-element.17, f32[24,16,50]{2,1,0:T(8,128)S(1)} %fusion.5, f32[8,16,50]{2,1,0:T(8,128)S(1)} %fusion.6, ...), kind=kOutput, calls=%fused_computation.4 | convolution fusion | flops 54679552 | bytes 1970688 | tf_op jit(solution)/shard_map/dot_general | solution.py:179
  32.3 0.6 %fusion.12 = f32[50,2048]{1,0:T(8,128)S(1)} fusion(f32[24,2048]{1,0:T(8,128)S(1)} %fusion.19, f32[8,2048]{1,0:T(8,128)S(1)} %fusion.24, f32[32,50]{1,0:T(8,128)S(1)} %fusion.48, f32[32]{0:T(128)S(1)} %get-tuple-element.16), kind=kOutput, calls=%fused_computation.28 | convolution fusion | flops 39454272 | bytes 678272 | tf_op jit(solution)/shard_map/dot_general | solution.py:188
  32.9 0.1 copy-done.1
  33.1 0.8 %fusion.2 = f32[1,50,4096]{2,1,0:T(8,128)S(1)} fusion(f32[50,4096]{1,0:T(8,128)S(1)} %convolution_bitcast_fusion.1, bf16[24,16,2048]{2,1,0:T(8,128)(2,1)S(1)} %copy-done.1, bf16[24,16,2048]{2,1,0:T(8,128)(2,1)S(1)} %get-tuple-element.27, f32[50,2048]{1,0:T(8,128)S(1)} %fusion.12, f32[4096]{0:T(1024)S(1)} %pad_maximum_fusion.11, ...), kind=kOutput, calls=%fused_computation.3 | convolution fusion | flops 164550656 | bytes 5313024 | tf_op jit(solution)/shard_map/dot_general | solution.py:179
  33.9 1.7 %copy.16 = f32[1,50,4096]{2,0,1:T(1,128)} copy(f32[1,50,4096]{2,1,0:T(8,128)S(1)} %fusion.2) | data formatting | bytes 1638400
  35.6 0.5 %compare_select_fusion = f32[8]{0:T(128)} fusion(f32[8]{0:T(128)S(1)} %get-tuple-element.6, f32[4,8]{1,0:T(4,128)S(1)} %get-tuple-element.14, f32[4,8]{1,0:T(4,128)S(1)} %get-tuple-element.12), kind=kLoop, calls=%fused_computation.102 | loop fusion | flops 24 | bytes 128 | tf_op jit(solution)/shard_map/jit(_where)/select_n | solution.py:270
  (23 shorter events, 0.2 us)
Async XLA Ops:
  0.6 10.5 %copy-start.2 = (f32[16,2048]{1,0:T(8,128)S(1)}, f32[16,2048]{1,0:T(8,128)}, u32[]{:S(2)}) copy-start(f32[16,2048]{1,0:T(8,128)} %constant.4.clone) | copy-start | bytes 393220
  0.6 10.5 %copy-start.3 = (f32[16,2048]{1,0:T(8,128)S(1)}, f32[16,2048]{1,0:T(8,128)}, u32[]{:S(2)}) copy-start(f32[16,2048]{1,0:T(8,128)} %constant.3.clone) | copy-start | bytes 393220
  0.7 9.6 %copy-start.4 = (f32[16,2048]{1,0:T(8,128)S(1)}, f32[16,2048]{1,0:T(8,128)}, u32[]{:S(2)}) copy-start(f32[16,2048]{1,0:T(8,128)} %param.11) | copy-start | bytes 393220
  2.2 9.7 %collective-permute-start = (bf16[8,4224]{1,0:T(8,128)(2,1)}, bf16[8,4224]{1,0:T(8,128)(2,1)S(1)}, u32[]{:S(2)}, u32[]{:S(2)}) collective-permute-start(bf16[8,4224]{1,0:T(8,128)(2,1)} %shard_map.104), channel_id=1, source_target_pairs={{0,4},{4,0},{8,12},{12,8},{1,5},{5,1},{9,13},{13,9},{2,6},{6,2},{1... | collective-permute-start | bytes 202760 | tf_op jit(solution)/shard_map/ppermute | solution.py:147
  5.3 7.6 %collective-permute-start.1 = (bf16[8,4224]{1,0:T(8,128)(2,1)}, bf16[8,4224]{1,0:T(8,128)(2,1)S(1)}, u32[]{:S(2)}, u32[]{:S(2)}) collective-permute-start(bf16[8,4224]{1,0:T(8,128)(2,1)} %shard_map.104), channel_id=1, source_target_pairs={{0,8},{4,12},{8,0},{12,4},{1,9},{5,13},{9,1},{13,5},{2,10},{6,14},... | collective-permute-start | bytes 202760 | tf_op jit(solution)/shard_map/ppermute | solution.py:147
  7.8 6.4 %collective-permute-start.2 = (bf16[8,4224]{1,0:T(8,128)(2,1)}, bf16[8,4224]{1,0:T(8,128)(2,1)S(1)}, u32[]{:S(2)}, u32[]{:S(2)}) collective-permute-start(bf16[8,4224]{1,0:T(8,128)(2,1)} %shard_map.104), channel_id=1, source_target_pairs={{0,12},{4,8},{8,4},{12,0},{1,13},{5,9},{9,5},{13,1},{2,14},{6,10},... | collective-permute-start | bytes 202760 | tf_op jit(solution)/shard_map/ppermute | solution.py:147
  9.0 2.4 %copy-start.5 = (bf16[1,50,4096]{2,1,0:T(8,128)(2,1)S(1)}, bf16[1,50,4096]{2,1,0:T(8,128)(2,1)}, u32[]{:S(2)}) copy-start(bf16[1,50,4096]{2,1,0:T(8,128)(2,1)} %param.10) | copy-start | bytes 1228804
  16.1 1.2 %copy-start = (bf16[24,16,2048]{2,1,0:T(8,128)(2,1)}, bf16[24,16,2048]{2,1,0:T(8,128)(2,1)S(1)}, u32[]{:S(2)}) copy-start(bf16[24,16,2048]{2,1,0:T(8,128)(2,1)S(1)} %get-tuple-element.28) | copy-start | bytes 4718596
  16.1 2.2 %copy-start.6 = (f32[2048]{0:T(1024)S(1)}, f32[2048]{0:T(1024)}, u32[]{:S(2)}) copy-start(f32[2048]{0:T(1024)} %param.12) | copy-start | bytes 24580
  18.3 1.2 %collective-permute-start.3 = (f32[2,4,8]{2,1,0:T(4,128)S(1)}, f32[2,4,8]{2,1,0:T(4,128)S(1)}, u32[]{:S(2)}, u32[]{:S(2)}) collective-permute-start(f32[2,4,8]{2,1,0:T(4,128)S(1)} %pad_maximum_fusion.12), channel_id=1, source_target_pairs={{0,1},{1,0},{2,3},{3,2},{4,5},{5,4},{6,7},{7,6},{8,9},{9,8},{10,11... | collective-permute-start | bytes 776 | tf_op jit(solution)/shard_map/ppermute | solution.py:162
  19.5 3.7 %collective-permute-start.4 = (f32[2,4,8]{2,1,0:T(4,128)S(1)}, f32[2,4,8]{2,1,0:T(4,128)S(1)}, u32[]{:S(2)}, u32[]{:S(2)}) collective-permute-start(f32[2,4,8]{2,1,0:T(4,128)S(1)} %pad_maximum_fusion.13), channel_id=1, source_target_pairs={{0,2},{1,3},{2,0},{3,1},{4,6},{5,7},{6,4},{7,5},{8,10},{9,11},{10,... | collective-permute-start | bytes 776 | tf_op jit(solution)/shard_map/ppermute | solution.py:162
  23.2 3.7 %collective-permute-start.5 = (f32[2,4,8]{2,1,0:T(4,128)S(1)}, f32[2,4,8]{2,1,0:T(4,128)S(1)}, u32[]{:S(2)}, u32[]{:S(2)}) collective-permute-start(f32[2,4,8]{2,1,0:T(4,128)S(1)} %pad_maximum_fusion.14), channel_id=1, source_target_pairs={{0,4},{4,0},{8,12},{12,8},{1,5},{5,1},{9,13},{13,9},{2,6},{6,2},{1... | collective-permute-start | bytes 776 | tf_op jit(solution)/shard_map/ppermute | solution.py:252
  26.9 4.6 %collective-permute-start.6 = (f32[2,4,8]{2,1,0:T(4,128)S(1)}, f32[2,4,8]{2,1,0:T(4,128)S(1)}, u32[]{:S(2)}, u32[]{:S(2)}) collective-permute-start(f32[2,4,8]{2,1,0:T(4,128)S(1)} %pad_maximum_fusion.16), channel_id=1, source_target_pairs={{0,8},{4,12},{8,0},{12,4},{1,9},{5,13},{9,1},{13,5},{2,10},{6,14},... | collective-permute-start | bytes 776 | tf_op jit(solution)/shard_map/ppermute | solution.py:252
  31.7 1.4 %copy-start.1 = (bf16[24,16,2048]{2,1,0:T(8,128)(2,1)S(1)}, bf16[24,16,2048]{2,1,0:T(8,128)(2,1)}, u32[]{:S(2)}) copy-start(bf16[24,16,2048]{2,1,0:T(8,128)(2,1)} %copy-done) | copy-start | bytes 4718596

commit v13 on v10

--- a/solution.py
+++ b/solution.py
@@ -197,6 +197,25 @@
     shifted = shifted_rows(images, ctf_rows, cosine_table, sine_table)
     scores = tile_scores(shifted, ref_tile, norms, gains, bin_rows)
     return (shifted, scores, ctf_rows)
+
+
+def divide_kernel(numerator_ref, denominator_ref, reg_ref, out_ref):
+    half = denominator_ref.shape[1]
+    denominator = denominator_ref[...] + reg_ref[...]
+    out_ref[:, :, :half] = (numerator_ref[:, :half] / denominator)[:, None, :]
+    out_ref[:, :, half:] = (numerator_ref[:, half:] / denominator)[:, None, :]
+
+
+def finish_average(numerator, denominator, spectral_reg):
+    rows, width = numerator.shape
+    whole = pl.BlockSpec(memory_space=pltpu.VMEM)
+    out = pl.pallas_call(
+        divide_kernel,
+        out_shape=jax.ShapeDtypeStruct((rows, 1, width), numerator.dtype),
+        in_specs=[whole, whole, whole],
+        out_specs=whole,
+    )(numerator, denominator, spectral_reg[None, :])
+    return out.transpose(1, 0, 2)
 
 
 def per_device(
@@ -268,11 +287,7 @@
         pieces, all_scores, gain_all, ctf_rows, live_all, peak_all, totals_all
     )
     log_evidence = jnp.where(live_mask > 0.5, peak_score + jnp.log(totals), 0.0)
-    denominator = (
-        jnp.concatenate([denominator, denominator], axis=1)
-        + jnp.concatenate([spectral_reg, spectral_reg])[None, :]
-    )
-    class_average = (numerator / denominator)[None]
+    class_average = finish_average(numerator, denominator, spectral_reg)
     return (class_average, log_evidence)
 
 

time: 34.9 us -> 38.9 us (1.11)
  Pallas kernels: 1.57 us -> 4 us
  matrix products: 4.56 us -> 6.25 us
  local copies, waits for them, and re-layouts: 2.47 us -> 1.39 us
  waiting for transfers between devices: 7.9 us -> 8.87 us
    pallas_call x0 -> x1, Pallas kernels: none -> 2.43 us  [finish_average(): pl.pallas_call(divide_kernel, out_shape=jax.ShapeDtypeStruct((rows, 1, wi...]
    ppermute x3, waiting for transfers between devices: 2.3 us -> 4.22 us  [per_device(): lax.ppermute(stats, 'blk', [(i, i ^ k) for i in range(n_blk)])]
    unnamed x17 -> x14, local copies, waits for them, and re-layouts: 2.11 us -> 1.03 us
    ppermute x3, waiting for transfers between devices: 2.33 us -> 1.39 us  [xor_gather(): lax.ppermute(value, axis, [(i, i ^ k) for i in range(size)])]
    dot_general x2, matrix products: 1.19 us -> 2.11 us  [accumulate(): lax.dot_general(scaled[start:start + count].reshape(shifted.shape[0], -1)...]
    dot_general x1, matrix products: 0.64 us -> 1.42 us  [accumulate(): lax.dot_general(summed, ctf_rows * ctf_rows, (((0,), (0,)), ((), ())), pr...]
  transfers between devices with their start and end apart: 8 -> 8, of which waited for: 7 -> 5; matrix products, arithmetic and copies ran while one was open for 12% -> 10% of each run, Pallas kernels for 0% -> 0%
where the time goes in v13:
time: 38.9 us; the launch traced here: 38.7 us
  starting transfers between devices  11.7 us (30%)
  waiting for transfers between devices  8.87 us (23%)
  matrix products  6.25 us (16%)
  other arithmetic  5.66 us (15%)
  Pallas kernels  4 us (10%)
  local copies, waits for them, and re-layouts  1.39 us (4%)
  between operations  0.86 us (2%)
    ppermute x3, starting transfers between devices, xor_gather(): lax.ppermute(value, axis, [(i, i ^ k) for i in range(size)])  5.62 us
    ppermute x3, starting transfers between devices, per_device(): lax.ppermute(stats, 'blk', [(i, i ^ k) for i in range(n_blk)])  4.45 us
    ppermute x3, waiting for transfers between devices, per_device(): lax.ppermute(stats, 'blk', [(i, i ^ k) for i in range(n_blk)])  4.22 us
    ppermute x2, waiting for transfers between devices, xor_butterfly(): other = lax.ppermute(stats, axis, [(i, i ^ step) for i in range(size)])  3.26 us
    pallas_call x1, Pallas kernels, finish_average(): pl.pallas_call(divide_kernel, out_shape=jax.ShapeDtypeStruct((rows, 1, wi...  2.43 us
    dot_general x2, matrix products, accumulate(): lax.dot_general(scaled[start:start + count].reshape(shifted.shape[0], -1)...  2.11 us
    ppermute x2, starting transfers between devices, xor_butterfly(): other = lax.ppermute(stats, axis, [(i, i ^ step) for i in range(size)])  1.59 us
    pallas_call x1, Pallas kernels, pack_rows(): pl.pallas_call(pack_kernel, out_shape=jax.ShapeDtypeStruct((slots, width...  1.57 us
  transfers between devices with their start and end apart: 8, of which 5 were waited for; matrix products, arithmetic and copies ran while one was open for 10% of the time, Pallas kernels for 0%

profile of v13, /device:TPU:0, one launch (start us, length us, event | category | flops | bytes accessed | tf_op | source)
XLA Modules:
  0.0 38.7 jit_solution(14655199592926105627)
XLA Ops:
  0.6 0.0 copy-start.2
  0.6 0.0 copy-start.3
  0.7 0.0 copy-start.4
  0.7 1.6 %shard_map.104 = bf16[8,4224]{1,0:T(8,128)(2,1)} custom-call(s32[4]{0:T(128)} %sizes_ref.1, f32[4]{0:T(128)} %scales_ref.1, s32[8]{0:T(128)} %bins_ref.1, bf16[8,4096]{1,0:T(8,128)(2,1)} %images_ref.1), custom_call_target="tpu_custom_call" | custom-call | tf_op jit(solution)/shard_map/pallas_call | solution.py:137
  2.2 5.0 %collective-permute-start.2 = (bf16[8,4224]{1,0:T(8,128)(2,1)}, bf16[8,4224]{1,0:T(8,128)(2,1)S(1)}, u32[]{:S(2)}, u32[]{:S(2)}) collective-permute-start(bf16[8,4224]{1,0:T(8,128)(2,1)} %shard_map.104), channel_id=1, source_target_pairs={{0,12},{4,8},{8,4},{12,0},{1,13},{5,9},{9,5},{13,1},{2,14},{6,10},... | collective-permute-start | bytes 202760 | tf_op jit(solution)/shard_map/ppermute | solution.py:147
  7.3 0.0 collective-permute-start.1
  7.3 0.6 %collective-permute-start = (bf16[8,4224]{1,0:T(8,128)(2,1)}, bf16[8,4224]{1,0:T(8,128)(2,1)S(1)}, u32[]{:S(2)}, u32[]{:S(2)}) collective-permute-start(bf16[8,4224]{1,0:T(8,128)(2,1)} %shard_map.104), channel_id=1, source_target_pairs={{0,4},{4,0},{8,12},{12,8},{1,5},{5,1},{9,13},{13,9},{2,6},{6,2},{1... | collective-permute-start | bytes 202760 | tf_op jit(solution)/shard_map/ppermute | solution.py:147
  7.8 0.9 %convert_element_type.26 = f32[8,4224]{1,0:T(8,128)S(1)} convert(bf16[8,4224]{1,0:T(8,128)(2,1)} %shard_map.104) | non-fusion elementwise | flops 33792 | bytes 202752 | tf_op jit(solution)/shard_map/convert_element_type | solution.py:238
  8.8 0.2 slice_reduce_fusion.3
  9.0 0.0 copy-start.5
  9.0 1.1 %bitcast_convert_fusion = f32[50,4096]{1,0:T(8,128)S(1)} fusion(bf16[1,50,4096]{2,1,0:T(8,128)(2,1)} %param.10), kind=kLoop, calls=%fused_computation.22 | loop fusion | flops 204800 | bytes 1228800 | tf_op jit(solution)/shard_map/convert_element_type | solution.py:65
  10.2 0.0 copy-done.4
  10.2 0.2 fusion.25
  10.4 0.5 %fusion.6 = f32[16,50]{1,0:T(8,128)S(1)} fusion(f32[50,4096]{1,0:T(8,128)S(1)} %bitcast_convert_fusion, f32[16,2048]{1,0:T(8,128)S(1)} %copy-done.4), kind=kOutput, calls=%fused_computation.18 | convolution fusion | flops 20000768 | bytes 953472 | tf_op jit(solution)/shard_map/dot_general | solution.py:70
  10.9 0.2 convolution_multiply_fusion.2
  11.1 0.0 copy-done.2
  11.1 0.0 copy-done.3
  11.1 0.3 multiply_convert_fusion.3
  11.4 0.0 copy-done.5
  11.4 0.4 %fusion.4 = f32[8,16,50]{2,1,0:T(8,128)S(1)} fusion(bf16[8,16,2048]{2,1,0:T(8,128)(2,1)S(1)} %get-tuple-element.15, bf16[8,16,2048]{2,1,0:T(8,128)(2,1)S(1)} %get-tuple-element.14, bf16[1,50,4096]{2,1,0:T(8,128)(2,1)S(1)} %copy-done.5, f32[8,50]{1,0:T(8,128)S(1)} %convolution_multiply_fusion.2, f32[8]{0:T(128)S(1)} %get-tuple-element.3), kind=kOutput, calls=%fused_computation.10 | convolution fusion | flops 54538752 | bytes 1485408 | tf_op jit(solution)/shard_map/dot_general | solution.py:75
  11.9 0.1 collective-permute-done
  11.9 1.3 %collective-permute-done.1 = bf16[8,4224]{1,0:T(8,128)(2,1)S(1)} collective-permute-done((bf16[8,4224]{1,0:T(8,128)(2,1)}, bf16[8,4224]{1,0:T(8,128)(2,1)S(1)}, u32[]{:S(2)}, u32[]{:S(2)}) %collective-permute-start.1) | collective-permute-done | bytes 67616 | tf_op jit(solution)/shard_map/ppermute | solution.py:147
  13.3 0.0 collective-permute-done.2
  13.3 0.2 slice_reduce_fusion
  13.6 0.3 fusion.17
  13.8 0.2 convolution_multiply_fusion.1
  14.0 1.1 %multiply_convert_fusion.1 = (bf16[24,16,2048]{2,1,0:T(8,128)(2,1)S(1)}, bf16[24,16,2048]{2,1,0:T(8,128)(2,1)S(1)}) fusion(f32[24,2048]{1,0:T(8,128)S(1)} %fusion.17, f32[16,2048]{1,0:T(8,128)S(1)} %copy-done.2, f32[24,2048]{1,0:T(8,128)S(1)} %get-tuple-element.17, f32[16,2048]{1,0:T(8,128)S(1)} %copy-done.3, f32[24,2048]{1,0:T(8,128)S(1)} %get-tuple-element.16), kind=kLoop, calls=%fused_computation.5 | loop fusion | flops 7864320 | bytes 3997696 | tf_op jit(solution)/shard_map/convert
  15.1 0.0 copy-start
  15.1 1.0 %fusion.3 = f32[24,16,50]{2,1,0:T(8,128)S(1)} fusion(bf16[24,16,2048]{2,1,0:T(8,128)(2,1)S(1)} %get-tuple-element.13, bf16[24,16,2048]{2,1,0:T(8,128)(2,1)S(1)} %get-tuple-element.12, bf16[1,50,4096]{2,1,0:T(8,128)(2,1)S(1)} %copy-done.5, f32[24,50]{1,0:T(8,128)S(1)} %convolution_multiply_fusion.1, f32[24]{0:T(128)S(1)} %get-tuple-element.6), kind=kOutput, calls=%fused_computation.8 | convolution fusion | flops 163616256 | bytes 3637024 | tf_op jit(solution)/shard_map/dot_general | solution.py:75
  16.1 0.2 copy-done
  16.3 0.3 fusion.13
  16.6 0.5 %exponential_reduce_fusion = f32[32]{0:T(128)S(1)} fusion(f32[24,16,50]{2,1,0:T(8,128)S(1)} %fusion.3, f32[8,16,50]{2,1,0:T(8,128)S(1)} %fusion.4, f32[32]{0:T(128)S(1)} %fusion.13), kind=kLoop, calls=%fused_computation.30 | loop fusion | flops 76768 | bytes 102656 | tf_op jit(solution)/shard_map/reduce_sum | solution.py:264
  17.1 0.1 squeeze.13
  17.2 0.1 stack.32
  17.3 0.0 collective-permute-start.3
  17.3 1.2 %collective-permute-done.3 = f32[2,4,8]{2,1,0:T(4,128)S(1)} collective-permute-done((f32[2,4,8]{2,1,0:T(4,128)S(1)}, f32[2,4,8]{2,1,0:T(4,128)S(1)}, u32[]{:S(2)}, u32[]{:S(2)}) %collective-permute-start.3) | collective-permute-done | bytes 288 | tf_op jit(solution)/shard_map/ppermute | solution.py:162
  18.5 1.6 %collective-permute-start.4 = (f32[2,4,8]{2,1,0:T(4,128)S(1)}, f32[2,4,8]{2,1,0:T(4,128)S(1)}, u32[]{:S(2)}, u32[]{:S(2)}) collective-permute-start(f32[2,4,8]{2,1,0:T(4,128)S(1)} %pad_maximum_fusion.13), channel_id=1, source_target_pairs={{0,2},{1,3},{2,0},{3,1},{4,6},{5,7},{6,4},{7,5},{8,10},{9,11},{10,... | collective-permute-start | bytes 776 | tf_op jit(solution)/shard_map/ppermute | solution.py:162
  20.0 2.1 %collective-permute-done.4 = f32[2,4,8]{2,1,0:T(4,128)S(1)} collective-permute-done((f32[2,4,8]{2,1,0:T(4,128)S(1)}, f32[2,4,8]{2,1,0:T(4,128)S(1)}, u32[]{:S(2)}, u32[]{:S(2)}) %collective-permute-start.4) | collective-permute-done | bytes 288 | tf_op jit(solution)/shard_map/ppermute | solution.py:162
  22.2 1.6 %collective-permute-start.6 = (f32[2,4,8]{2,1,0:T(4,128)S(1)}, f32[2,4,8]{2,1,0:T(4,128)S(1)}, u32[]{:S(2)}, u32[]{:S(2)}) collective-permute-start(f32[2,4,8]{2,1,0:T(4,128)S(1)} %get-tuple-element.23), channel_id=1, source_target_pairs={{0,8},{4,12},{8,0},{12,4},{1,9},{5,13},{9,1},{13,5},{2,10},{6,14},... | collective-permute-start | bytes 776 | tf_op jit(solution)/shard_map/ppermute | solution.py:270
  23.7 0.1 fusion.37
  23.8 1.7 %collective-permute-start.5 = (f32[2,4,8]{2,1,0:T(4,128)S(1)}, f32[2,4,8]{2,1,0:T(4,128)S(1)}, u32[]{:S(2)}, u32[]{:S(2)}) collective-permute-start(f32[2,4,8]{2,1,0:T(4,128)S(1)} %get-tuple-element.23), channel_id=1, source_target_pairs={{0,4},{4,0},{8,12},{12,8},{1,5},{5,1},{9,13},{13,9},{2,6},{6,2},{1... | collective-permute-start | bytes 776 | tf_op jit(solution)/shard_map/ppermute | solution.py:270
  25.5 1.2 %collective-permute-start.7 = (f32[2,4,8]{2,1,0:T(4,128)S(1)}, f32[2,4,8]{2,1,0:T(4,128)S(1)}, u32[]{:S(2)}, u32[]{:S(2)}) collective-permute-start(f32[2,4,8]{2,1,0:T(4,128)S(1)} %get-tuple-element.23), channel_id=1, source_target_pairs={{0,12},{4,8},{8,4},{12,0},{1,13},{5,9},{9,5},{13,1},{2,14},{6,10},... | collective-permute-start | bytes 776 | tf_op jit(solution)/shard_map/ppermute | solution.py:270
  26.7 0.0 collective-permute-done.6
  26.7 4.2 %collective-permute-done.7 = f32[2,4,8]{2,1,0:T(4,128)S(1)} collective-permute-done((f32[2,4,8]{2,1,0:T(4,128)S(1)}, f32[2,4,8]{2,1,0:T(4,128)S(1)}, u32[]{:S(2)}, u32[]{:S(2)}) %collective-permute-start.7) | collective-permute-done | bytes 288 | tf_op jit(solution)/shard_map/ppermute | solution.py:270
  30.9 0.0 collective-permute-done.5
  31.0 0.1 sub.79
  31.1 0.5 %compare_select_fusion = f32[8]{0:T(128)} fusion(f32[8]{0:T(128)S(1)} %get-tuple-element.2, f32[4,8]{1,0:T(4,128)S(1)} %fusion.19, f32[4,8]{1,0:T(4,128)S(1)} %slice_reduce_fusion.2), kind=kLoop, calls=%fused_computation.76 | loop fusion | flops 24 | bytes 128 | tf_op jit(solution)/shard_map/jit(_where)/select_n | solution.py:289
  31.6 0.1 div.10
  31.7 0.0 copy-start.1
  31.7 0.2 fusion.36
  31.9 0.4 %convolution_bitcast_fusion.1 = f32[50,4096]{1,0:T(8,128)S(1)} fusion(bf16[8,16,2048]{2,1,0:T(8,128)(2,1)S(1)} %get-tuple-element.15, bf16[8,16,2048]{2,1,0:T(8,128)(2,1)S(1)} %get-tuple-element.14, f32[32]{0:T(128)S(1)} %get-tuple-element.9, f32[24,16,50]{2,1,0:T(8,128)S(1)} %fusion.3, f32[8,16,50]{2,1,0:T(8,128)S(1)} %fusion.4, ...), kind=kOutput, calls=%fused_computation.2 | convolution fusion | flops 54679552 | bytes 1970688 | tf_op jit(solution)/shard_map/dot_general | solution.py:179
  32.3 0.8 %copy-done.1 = bf16[24,16,2048]{2,1,0:T(8,128)(2,1)S(1)} copy-done((bf16[24,16,2048]{2,1,0:T(8,128)(2,1)S(1)}, bf16[24,16,2048]{2,1,0:T(8,128)(2,1)}, u32[]{:S(2)}) %copy-start.1) | copy-done | bytes 1572888
  33.1 1.7 %fusion.numerator_ref = f32[50,4096]{1,0:T(8,128)} fusion(f32[50,4096]{1,0:T(8,128)S(1)} %convolution_bitcast_fusion.1, bf16[24,16,2048]{2,1,0:T(8,128)(2,1)S(1)} %copy-done.1, bf16[24,16,2048]{2,1,0:T(8,128)(2,1)S(1)} %get-tuple-element.12, f32[32]{0:T(128)S(1)} %get-tuple-element.9, f32[24,16,50]{2,1,0:T(8,128)S(1)} %fusion.3, ...), kind=kOutput, calls=%fused_computation.1 | convolution fusion | flops 163936256 | bytes 4887040 | tf_op jit(solution)/shard_map/dot_general | solution.py:179
  34.8 1.4 %fusion.10.denominator_ref = f32[50,2048]{1,0:T(8,128)} fusion(f32[24,2048]{1,0:T(8,128)S(1)} %fusion.17, f32[8,2048]{1,0:T(8,128)S(1)} %fusion.25, f32[32,50]{1,0:T(8,128)S(1)} %fusion.36, f32[32]{0:T(128)S(1)} %get-tuple-element.8), kind=kOutput, calls=%fused_computation.25 | convolution fusion | flops 39454272 | bytes 678272 | tf_op jit(solution)/shard_map/dot_general | solution.py:188
  36.2 2.4 %shard_map.105 = f32[50,1,4096]{2,1,0:T(1,128)} custom-call(f32[50,4096]{1,0:T(8,128)} %fusion.numerator_ref, f32[50,2048]{1,0:T(8,128)} %fusion.10.denominator_ref, f32[1,2048]{1,0:T(1,128)} %bitcast.42), custom_call_target="tpu_custom_call" | custom-call | tf_op jit(solution)/shard_map/pallas_call | solution.py:212
  (21 shorter events, 0.2 us)
Async XLA Ops:
  0.6 10.5 %copy-start.2 = (f32[16,2048]{1,0:T(8,128)S(1)}, f32[16,2048]{1,0:T(8,128)}, u32[]{:S(2)}) copy-start(f32[16,2048]{1,0:T(8,128)} %constant.4.clone) | copy-start | bytes 393220
  0.6 10.4 %copy-start.3 = (f32[16,2048]{1,0:T(8,128)S(1)}, f32[16,2048]{1,0:T(8,128)}, u32[]{:S(2)}) copy-start(f32[16,2048]{1,0:T(8,128)} %constant.3.clone) | copy-start | bytes 393220
  0.7 9.5 %copy-start.4 = (f32[16,2048]{1,0:T(8,128)S(1)}, f32[16,2048]{1,0:T(8,128)}, u32[]{:S(2)}) copy-start(f32[16,2048]{1,0:T(8,128)} %param.11) | copy-start | bytes 393220
  2.2 11.0 %collective-permute-start.2 = (bf16[8,4224]{1,0:T(8,128)(2,1)}, bf16[8,4224]{1,0:T(8,128)(2,1)S(1)}, u32[]{:S(2)}, u32[]{:S(2)}) collective-permute-start(bf16[8,4224]{1,0:T(8,128)(2,1)} %shard_map.104), channel_id=1, source_target_pairs={{0,12},{4,8},{8,4},{12,0},{1,13},{5,9},{9,5},{13,1},{2,14},{6,10},... | collective-permute-start | bytes 202760 | tf_op jit(solution)/shard_map/ppermute | solution.py:147
  7.3 6.0 %collective-permute-start.1 = (bf16[8,4224]{1,0:T(8,128)(2,1)}, bf16[8,4224]{1,0:T(8,128)(2,1)S(1)}, u32[]{:S(2)}, u32[]{:S(2)}) collective-permute-start(bf16[8,4224]{1,0:T(8,128)(2,1)} %shard_map.104), channel_id=1, source_target_pairs={{0,8},{4,12},{8,0},{12,4},{1,9},{5,13},{9,1},{13,5},{2,10},{6,14},... | collective-permute-start | bytes 202760 | tf_op jit(solution)/shard_map/ppermute | solution.py:147
  7.3 4.7 %collective-permute-start = (bf16[8,4224]{1,0:T(8,128)(2,1)}, bf16[8,4224]{1,0:T(8,128)(2,1)S(1)}, u32[]{:S(2)}, u32[]{:S(2)}) collective-permute-start(bf16[8,4224]{1,0:T(8,128)(2,1)} %shard_map.104), channel_id=1, source_target_pairs={{0,4},{4,0},{8,12},{12,8},{1,5},{5,1},{9,13},{13,9},{2,6},{6,2},{1... | collective-permute-start | bytes 202760 | tf_op jit(solution)/shard_map/ppermute | solution.py:147
  9.0 2.4 %copy-start.5 = (bf16[1,50,4096]{2,1,0:T(8,128)(2,1)S(1)}, bf16[1,50,4096]{2,1,0:T(8,128)(2,1)}, u32[]{:S(2)}) copy-start(bf16[1,50,4096]{2,1,0:T(8,128)(2,1)} %param.10) | copy-start | bytes 1228804
  15.1 1.2 %copy-start = (bf16[24,16,2048]{2,1,0:T(8,128)(2,1)}, bf16[24,16,2048]{2,1,0:T(8,128)(2,1)S(1)}, u32[]{:S(2)}) copy-start(bf16[24,16,2048]{2,1,0:T(8,128)(2,1)S(1)} %get-tuple-element.13) | copy-start | bytes 4718596
  17.3 1.2 %collective-permute-start.3 = (f32[2,4,8]{2,1,0:T(4,128)S(1)}, f32[2,4,8]{2,1,0:T(4,128)S(1)}, u32[]{:S(2)}, u32[]{:S(2)}) collective-permute-start(f32[2,4,8]{2,1,0:T(4,128)S(1)} %pad_maximum_fusion.12), channel_id=1, source_target_pairs={{0,1},{1,0},{2,3},{3,2},{4,5},{5,4},{6,7},{7,6},{8,9},{9,8},{10,11... | collective-permute-start | bytes 776 | tf_op jit(solution)/shard_map/ppermute | solution.py:162
  18.5 3.7 %collective-permute-start.4 = (f32[2,4,8]{2,1,0:T(4,128)S(1)}, f32[2,4,8]{2,1,0:T(4,128)S(1)}, u32[]{:S(2)}, u32[]{:S(2)}) collective-permute-start(f32[2,4,8]{2,1,0:T(4,128)S(1)} %pad_maximum_fusion.13), channel_id=1, source_target_pairs={{0,2},{1,3},{2,0},{3,1},{4,6},{5,7},{6,4},{7,5},{8,10},{9,11},{10,... | collective-permute-start | bytes 776 | tf_op jit(solution)/shard_map/ppermute | solution.py:162
  22.2 4.6 %collective-permute-start.6 = (f32[2,4,8]{2,1,0:T(4,128)S(1)}, f32[2,4,8]{2,1,0:T(4,128)S(1)}, u32[]{:S(2)}, u32[]{:S(2)}) collective-permute-start(f32[2,4,8]{2,1,0:T(4,128)S(1)} %get-tuple-element.23), channel_id=1, source_target_pairs={{0,8},{4,12},{8,0},{12,4},{1,9},{5,13},{9,1},{13,5},{2,10},{6,14},... | collective-permute-start | bytes 776 | tf_op jit(solution)/shard_map/ppermute | solution.py:270
  23.8 7.1 %collective-permute-start.5 = (f32[2,4,8]{2,1,0:T(4,128)S(1)}, f32[2,4,8]{2,1,0:T(4,128)S(1)}, u32[]{:S(2)}, u32[]{:S(2)}) collective-permute-start(f32[2,4,8]{2,1,0:T(4,128)S(1)} %get-tuple-element.23), channel_id=1, source_target_pairs={{0,4},{4,0},{8,12},{12,8},{1,5},{5,1},{9,13},{13,9},{2,6},{6,2},{1... | collective-permute-start | bytes 776 | tf_op jit(solution)/shard_map/ppermute | solution.py:270
  25.5 5.4 %collective-permute-start.7 = (f32[2,4,8]{2,1,0:T(4,128)S(1)}, f32[2,4,8]{2,1,0:T(4,128)S(1)}, u32[]{:S(2)}, u32[]{:S(2)}) collective-permute-start(f32[2,4,8]{2,1,0:T(4,128)S(1)} %get-tuple-element.23), channel_id=1, source_target_pairs={{0,12},{4,8},{8,4},{12,0},{1,13},{5,9},{9,5},{13,1},{2,14},{6,10},... | collective-permute-start | bytes 776 | tf_op jit(solution)/shard_map/ppermute | solution.py:270
  31.7 1.4 %copy-start.1 = (bf16[24,16,2048]{2,1,0:T(8,128)(2,1)S(1)}, bf16[24,16,2048]{2,1,0:T(8,128)(2,1)}, u32[]{:S(2)}) copy-start(bf16[24,16,2048]{2,1,0:T(8,128)(2,1)} %copy-done) | copy-start | bytes 4718596

commit v14 on v10

--- a/solution.py
+++ b/solution.py
@@ -94,6 +94,22 @@
 def combine_many(peaks, totals):
     new_peak = jnp.max(peaks, axis=0)
     return (new_peak, jnp.sum(totals * jnp.exp(peaks - new_peak[None]), axis=0))
+
+
+def merge_pair(former, latter):
+    new_peak = jnp.maximum(former[0], latter[0])
+    scale_former = jnp.where(former[0] == new_peak, 1.0, jnp.exp(former[0] - new_peak))
+    scale_latter = jnp.where(latter[0] == new_peak, 1.0, jnp.exp(latter[0] - new_peak))
+    return (new_peak, former[1] * scale_former + latter[1] * scale_latter)
+
+
+def local_stats(flattened):
+    return lax.reduce(
+        (flattened, jnp.ones_like(flattened)),
+        (jnp.float32(-jnp.inf), jnp.float32(0.0)),
+        merge_pair,
+        (1,),
+    )
 
 
 def split_exact(value):
@@ -241,8 +257,7 @@
     live_all = jnp.concatenate([group[2] for group in groups])
     whole_count = all_scores.shape[0]
     flattened = all_scores.reshape(whole_count, -1)
-    peak_all = jnp.max(flattened, axis=1)
-    totals_all = jnp.sum(jnp.exp(flattened - peak_all[:, None]), axis=1)
+    peak_all, totals_all = local_stats(flattened)
 
     if small:
         stats = jnp.stack([peak_all, totals_all]).reshape(2, n_blk, batch_size)

time: 34.9 us -> 34.5 us (0.989)
  other arithmetic: 5.69 us -> 5.08 us
    reduce_sum x1 -> x0, other arithmetic: 0.49 us -> none  [per_device(): totals_all = jnp.sum(jnp.exp(flattened - peak_all[:, None]), axis=1)]
    another operation x2 -> x3, other arithmetic: 1.4 us -> 1.57 us
where the time goes in v14:
time: 34.5 us; the launch traced here: 34.2 us
  starting transfers between devices  11.6 us (34%)
  waiting for transfers between devices  7.89 us (23%)
  other arithmetic  5.08 us (15%)
  matrix products  4.56 us (13%)
  local copies, waits for them, and re-layouts  2.62 us (8%)
  Pallas kernels  1.57 us (5%)
  between operations  0.87 us (3%)
    ppermute x3, starting transfers between devices, xor_gather(): lax.ppermute(value, axis, [(i, i ^ k) for i in range(size)])  5.62 us
    ppermute x3, starting transfers between devices, per_device(): lax.ppermute(stats, 'blk', [(i, i ^ k) for i in range(n_blk)])  4.45 us
    ppermute x2, waiting for transfers between devices, xor_butterfly(): other = lax.ppermute(stats, axis, [(i, i ^ step) for i in range(size)])  3.27 us
    ppermute x3, waiting for transfers between devices, xor_gather(): lax.ppermute(value, axis, [(i, i ^ k) for i in range(size)])  2.33 us
    ppermute x3, waiting for transfers between devices, per_device(): lax.ppermute(stats, 'blk', [(i, i ^ k) for i in range(n_blk)])  2.28 us
    unnamed x17, local copies, waits for them, and re-layouts  2.11 us
    pallas_call x1, Pallas kernels, pack_rows(): pl.pallas_call(pack_kernel, out_shape=jax.ShapeDtypeStruct((slots, width...  1.57 us
    ppermute x2, starting transfers between devices, xor_butterfly(): other = lax.ppermute(stats, axis, [(i, i ^ step) for i in range(size)])  1.56 us
  transfers between devices with their start and end apart: 8, of which 7 were waited for; matrix products, arithmetic and copies ran while one was open for 12% of the time, Pallas kernels for 0%

profile of v14, /device:TPU:0, one launch (start us, length us, event | category | flops | bytes accessed | tf_op | source)
XLA Modules:
  0.0 34.2 jit_solution(3839165788964596020)
XLA Ops:
  0.6 0.0 copy-start.2
  0.6 0.0 copy-start.3
  0.7 0.0 copy-start.4
  0.7 1.6 %shard_map.104 = bf16[8,4224]{1,0:T(8,128)(2,1)} custom-call(s32[4]{0:T(128)} %sizes_ref.1, f32[4]{0:T(128)} %scales_ref.1, s32[8]{0:T(128)} %bins_ref.1, bf16[8,4096]{1,0:T(8,128)(2,1)} %images_ref.1), custom_call_target="tpu_custom_call" | custom-call | tf_op jit(solution)/shard_map/pallas_call | solution.py:153
  2.2 3.0 %collective-permute-start = (bf16[8,4224]{1,0:T(8,128)(2,1)}, bf16[8,4224]{1,0:T(8,128)(2,1)S(1)}, u32[]{:S(2)}, u32[]{:S(2)}) collective-permute-start(bf16[8,4224]{1,0:T(8,128)(2,1)} %shard_map.104), channel_id=1, source_target_pairs={{0,4},{4,0},{8,12},{12,8},{1,5},{5,1},{9,13},{13,9},{2,6},{6,2},{1... | collective-permute-start | bytes 202760 | tf_op jit(solution)/shard_map/ppermute | solution.py:163
  5.3 2.6 %collective-permute-start.1 = (bf16[8,4224]{1,0:T(8,128)(2,1)}, bf16[8,4224]{1,0:T(8,128)(2,1)S(1)}, u32[]{:S(2)}, u32[]{:S(2)}) collective-permute-start(bf16[8,4224]{1,0:T(8,128)(2,1)} %shard_map.104), channel_id=1, source_target_pairs={{0,8},{4,12},{8,0},{12,4},{1,9},{5,13},{9,1},{13,5},{2,10},{6,14},... | collective-permute-start | bytes 202760 | tf_op jit(solution)/shard_map/ppermute | solution.py:163
  7.8 0.0 collective-permute-start.2
  7.8 1.0 %convert_element_type.26 = f32[8,4224]{1,0:T(8,128)S(1)} convert(bf16[8,4224]{1,0:T(8,128)(2,1)} %shard_map.104) | non-fusion elementwise | flops 33792 | bytes 202752 | tf_op jit(solution)/shard_map/convert_element_type | solution.py:235
  8.8 0.2 slice_reduce_fusion.3
  9.0 0.0 copy-start.5
  9.1 1.1 %bitcast_convert_fusion = f32[50,4096]{1,0:T(8,128)S(1)} fusion(bf16[1,50,4096]{2,1,0:T(8,128)(2,1)} %param.10), kind=kLoop, calls=%fused_computation.25 | loop fusion | flops 204800 | bytes 1228800 | tf_op jit(solution)/shard_map/convert_element_type | solution.py:65
  10.2 0.0 copy-done.4
  10.2 0.2 fusion.26
  10.4 0.5 %fusion.8 = f32[16,50]{1,0:T(8,128)S(1)} fusion(f32[50,4096]{1,0:T(8,128)S(1)} %bitcast_convert_fusion, f32[16,2048]{1,0:T(8,128)S(1)} %copy-done.4), kind=kOutput, calls=%fused_computation.21 | convolution fusion | flops 20000768 | bytes 953472 | tf_op jit(solution)/shard_map/dot_general | solution.py:70
  10.9 0.2 convolution_multiply_fusion.2
  11.1 0.0 copy-done.2
  11.1 0.0 copy-done.3
  11.1 0.3 multiply_convert_fusion.3
  11.4 0.0 copy-done.5
  11.5 0.4 %fusion.6 = f32[8,16,50]{2,1,0:T(8,128)S(1)} fusion(bf16[8,16,2048]{2,1,0:T(8,128)(2,1)S(1)} %get-tuple-element.23, bf16[8,16,2048]{2,1,0:T(8,128)(2,1)S(1)} %get-tuple-element.22, bf16[1,50,4096]{2,1,0:T(8,128)(2,1)S(1)} %copy-done.5, f32[8,50]{1,0:T(8,128)S(1)} %convolution_multiply_fusion.2, f32[8]{0:T(128)S(1)} %get-tuple-element.11), kind=kOutput, calls=%fused_computation.12 | convolution fusion | flops 54538752 | bytes 1485408 | tf_op jit(solution)/shard_map/dot_general | solution.py:75
  11.9 0.0 collective-permute-done
  11.9 1.0 %collective-permute-done.1 = bf16[8,4224]{1,0:T(8,128)(2,1)S(1)} collective-permute-done((bf16[8,4224]{1,0:T(8,128)(2,1)}, bf16[8,4224]{1,0:T(8,128)(2,1)S(1)}, u32[]{:S(2)}, u32[]{:S(2)}) %collective-permute-start.1) | collective-permute-done | bytes 67616 | tf_op jit(solution)/shard_map/ppermute | solution.py:163
  12.9 1.4 %collective-permute-done.2 = bf16[8,4224]{1,0:T(8,128)(2,1)S(1)} collective-permute-done((bf16[8,4224]{1,0:T(8,128)(2,1)}, bf16[8,4224]{1,0:T(8,128)(2,1)S(1)}, u32[]{:S(2)}, u32[]{:S(2)}) %collective-permute-start.2) | collective-permute-done | bytes 67616 | tf_op jit(solution)/shard_map/ppermute | solution.py:163
  14.3 0.2 slice_reduce_fusion.1
  14.5 0.3 fusion.18
  14.8 0.2 convolution_multiply_fusion.1
  15.0 1.1 %multiply_convert_fusion.1 = (bf16[24,16,2048]{2,1,0:T(8,128)(2,1)S(1)}, bf16[24,16,2048]{2,1,0:T(8,128)(2,1)S(1)}) fusion(f32[24,2048]{1,0:T(8,128)S(1)} %fusion.18, f32[16,2048]{1,0:T(8,128)S(1)} %copy-done.2, f32[24,2048]{1,0:T(8,128)S(1)} %get-tuple-element.25, f32[16,2048]{1,0:T(8,128)S(1)} %copy-done.3, f32[24,2048]{1,0:T(8,128)S(1)} %get-tuple-element.24), kind=kLoop, calls=%fused_computation.7 | loop fusion | flops 7864320 | bytes 3997696 | tf_op jit(solution)/shard_map/convert
  16.1 0.0 copy-start
  16.1 0.0 copy-start.6
  16.1 1.0 %fusion.5 = f32[24,16,50]{2,1,0:T(8,128)S(1)} fusion(bf16[24,16,2048]{2,1,0:T(8,128)(2,1)S(1)} %get-tuple-element.21, bf16[24,16,2048]{2,1,0:T(8,128)(2,1)S(1)} %get-tuple-element.20, bf16[1,50,4096]{2,1,0:T(8,128)(2,1)S(1)} %copy-done.5, f32[24,50]{1,0:T(8,128)S(1)} %convolution_multiply_fusion.1, f32[24]{0:T(128)S(1)} %get-tuple-element.14), kind=kOutput, calls=%fused_computation.10 | convolution fusion | flops 163616256 | bytes 3637024 | tf_op jit(solution)/shard_map/dot_general | solution.py:75
  17.1 0.2 copy-done
  17.3 0.1 reshape.142
  17.4 0.2 broadcast_reduce_fusion
  17.6 0.1 stack.32
  17.7 0.1 squeeze.13
  17.8 0.0 collective-permute-start.3
  17.8 1.2 %collective-permute-done.3 = f32[2,4,8]{2,1,0:T(4,128)S(1)} collective-permute-done((f32[2,4,8]{2,1,0:T(4,128)S(1)}, f32[2,4,8]{2,1,0:T(4,128)S(1)}, u32[]{:S(2)}, u32[]{:S(2)}) %collective-permute-start.3) | collective-permute-done | bytes 288 | tf_op jit(solution)/shard_map/ppermute | solution.py:178
  19.0 1.5 %collective-permute-start.4 = (f32[2,4,8]{2,1,0:T(4,128)S(1)}, f32[2,4,8]{2,1,0:T(4,128)S(1)}, u32[]{:S(2)}, u32[]{:S(2)}) collective-permute-start(f32[2,4,8]{2,1,0:T(4,128)S(1)} %pad_maximum_fusion.14), channel_id=1, source_target_pairs={{0,2},{1,3},{2,0},{3,1},{4,6},{5,7},{6,4},{7,5},{8,10},{9,11},{10,... | collective-permute-start | bytes 776 | tf_op jit(solution)/shard_map/ppermute | solution.py:178
  20.5 0.0 copy-done.6
  20.5 2.1 %collective-permute-done.4 = f32[2,4,8]{2,1,0:T(4,128)S(1)} collective-permute-done((f32[2,4,8]{2,1,0:T(4,128)S(1)}, f32[2,4,8]{2,1,0:T(4,128)S(1)}, u32[]{:S(2)}, u32[]{:S(2)}) %collective-permute-start.4) | collective-permute-done | bytes 288 | tf_op jit(solution)/shard_map/ppermute | solution.py:178
  22.7 1.9 %collective-permute-start.7 = (f32[2,4,8]{2,1,0:T(4,128)S(1)}, f32[2,4,8]{2,1,0:T(4,128)S(1)}, u32[]{:S(2)}, u32[]{:S(2)}) collective-permute-start(f32[2,4,8]{2,1,0:T(4,128)S(1)} %get-tuple-element.31), channel_id=1, source_target_pairs={{0,12},{4,8},{8,4},{12,0},{1,13},{5,9},{9,5},{13,1},{2,14},{6,10},... | collective-permute-start | bytes 776 | tf_op jit(solution)/shard_map/ppermute | solution.py:266
  24.6 0.1 fusion.38
  24.7 0.4 %collective-permute-start.5 = (f32[2,4,8]{2,1,0:T(4,128)S(1)}, f32[2,4,8]{2,1,0:T(4,128)S(1)}, u32[]{:S(2)}, u32[]{:S(2)}) collective-permute-start(f32[2,4,8]{2,1,0:T(4,128)S(1)} %get-tuple-element.31), channel_id=1, source_target_pairs={{0,4},{4,0},{8,12},{12,8},{1,5},{5,1},{9,13},{13,9},{2,6},{6,2},{1... | collective-permute-start | bytes 776 | tf_op jit(solution)/shard_map/ppermute | solution.py:266
  25.0 2.2 %collective-permute-start.6 = (f32[2,4,8]{2,1,0:T(4,128)S(1)}, f32[2,4,8]{2,1,0:T(4,128)S(1)}, u32[]{:S(2)}, u32[]{:S(2)}) collective-permute-start(f32[2,4,8]{2,1,0:T(4,128)S(1)} %get-tuple-element.31), channel_id=1, source_target_pairs={{0,8},{4,12},{8,0},{12,4},{1,9},{5,13},{9,1},{13,5},{2,10},{6,14},... | collective-permute-start | bytes 776 | tf_op jit(solution)/shard_map/ppermute | solution.py:266
  27.2 0.9 %collective-permute-done.7 = f32[2,4,8]{2,1,0:T(4,128)S(1)} collective-permute-done((f32[2,4,8]{2,1,0:T(4,128)S(1)}, f32[2,4,8]{2,1,0:T(4,128)S(1)}, u32[]{:S(2)}, u32[]{:S(2)}) %collective-permute-start.7) | collective-permute-done | bytes 288 | tf_op jit(solution)/shard_map/ppermute | solution.py:266
  28.2 0.1 collective-permute-done.5
  28.3 1.2 %collective-permute-done.6 = f32[2,4,8]{2,1,0:T(4,128)S(1)} collective-permute-done((f32[2,4,8]{2,1,0:T(4,128)S(1)}, f32[2,4,8]{2,1,0:T(4,128)S(1)}, u32[]{:S(2)}, u32[]{:S(2)}) %collective-permute-start.6) | collective-permute-done | bytes 288 | tf_op jit(solution)/shard_map/ppermute | solution.py:266
  29.6 0.1 sub.72
  29.7 0.1 div.13
  29.8 0.5 %compare_select_fusion = f32[8]{0:T(128)} fusion(f32[8]{0:T(128)S(1)} %get-tuple-element.10, f32[4,8]{1,0:T(4,128)S(1)} %fusion.20, f32[4,8]{1,0:T(4,128)S(1)} %slice_reduce_fusion.2), kind=kLoop, calls=%fused_computation.79 | loop fusion | flops 24 | bytes 128 | tf_op jit(solution)/shard_map/jit(_where)/select_n | solution.py:285
  30.3 0.0 copy-start.1
  30.3 0.2 fusion.37
  30.5 0.4 %convolution_bitcast_fusion.1 = f32[50,4096]{1,0:T(8,128)S(1)} fusion(bf16[8,16,2048]{2,1,0:T(8,128)(2,1)S(1)} %get-tuple-element.23, bf16[8,16,2048]{2,1,0:T(8,128)(2,1)S(1)} %get-tuple-element.22, f32[32]{0:T(128)S(1)} %get-tuple-element.17, f32[32]{0:T(128)S(1)} %get-tuple-element.42, f32[32]{0:T(128)S(1)} %div.13, f32[32]{0:T(128)S(1)} %sub.72, ...), kind=kOutput, calls=%fused_computation.4 | convolution fusion | flops 54679552 | bytes 1970688 | tf_op jit(solution)/shard_map/dot_general | solution.py:195
  30.9 0.6 %fusion.12 = f32[50,2048]{1,0:T(8,128)S(1)} fusion(f32[24,2048]{1,0:T(8,128)S(1)} %fusion.18, f32[8,2048]{1,0:T(8,128)S(1)} %fusion.26, f32[32,50]{1,0:T(8,128)S(1)} %fusion.37, f32[32]{0:T(128)S(1)} %get-tuple-element.16), kind=kOutput, calls=%fused_computation.28 | convolution fusion | flops 39454272 | bytes 678272 | tf_op jit(solution)/shard_map/dot_general | solution.py:204
  31.5 0.2 copy-done.1
  31.7 0.8 %fusion.2 = f32[1,50,4096]{2,1,0:T(8,128)S(1)} fusion(f32[50,4096]{1,0:T(8,128)S(1)} %convolution_bitcast_fusion.1, bf16[24,16,2048]{2,1,0:T(8,128)(2,1)S(1)} %copy-done.1, bf16[24,16,2048]{2,1,0:T(8,128)(2,1)S(1)} %get-tuple-element.20, f32[50,2048]{1,0:T(8,128)S(1)} %fusion.12, f32[4096]{0:T(1024)S(1)} %pad_maximum_fusion.12, ...), kind=kOutput, calls=%fused_computation.3 | convolution fusion | flops 164550656 | bytes 5313024 | tf_op jit(solution)/shard_map/dot_general | solution.py:195
  32.5 1.7 %copy.16 = f32[1,50,4096]{2,0,1:T(1,128)} copy(f32[1,50,4096]{2,1,0:T(8,128)S(1)} %fusion.2) | data formatting | bytes 1638400
  (23 shorter events, 0.2 us)
Async XLA Ops:
  0.6 10.5 %copy-start.2 = (f32[16,2048]{1,0:T(8,128)S(1)}, f32[16,2048]{1,0:T(8,128)}, u32[]{:S(2)}) copy-start(f32[16,2048]{1,0:T(8,128)} %constant.6.clone) | copy-start | bytes 393220
  0.6 10.5 %copy-start.3 = (f32[16,2048]{1,0:T(8,128)S(1)}, f32[16,2048]{1,0:T(8,128)}, u32[]{:S(2)}) copy-start(f32[16,2048]{1,0:T(8,128)} %constant.5.clone) | copy-start | bytes 393220
  0.7 9.6 %copy-start.4 = (f32[16,2048]{1,0:T(8,128)S(1)}, f32[16,2048]{1,0:T(8,128)}, u32[]{:S(2)}) copy-start(f32[16,2048]{1,0:T(8,128)} %param.11) | copy-start | bytes 393220
  2.2 9.6 %collective-permute-start = (bf16[8,4224]{1,0:T(8,128)(2,1)}, bf16[8,4224]{1,0:T(8,128)(2,1)S(1)}, u32[]{:S(2)}, u32[]{:S(2)}) collective-permute-start(bf16[8,4224]{1,0:T(8,128)(2,1)} %shard_map.104), channel_id=1, source_target_pairs={{0,4},{4,0},{8,12},{12,8},{1,5},{5,1},{9,13},{13,9},{2,6},{6,2},{1... | collective-permute-start | bytes 202760 | tf_op jit(solution)/shard_map/ppermute | solution.py:163
  5.3 7.6 %collective-permute-start.1 = (bf16[8,4224]{1,0:T(8,128)(2,1)}, bf16[8,4224]{1,0:T(8,128)(2,1)S(1)}, u32[]{:S(2)}, u32[]{:S(2)}) collective-permute-start(bf16[8,4224]{1,0:T(8,128)(2,1)} %shard_map.104), channel_id=1, source_target_pairs={{0,8},{4,12},{8,0},{12,4},{1,9},{5,13},{9,1},{13,5},{2,10},{6,14},... | collective-permute-start | bytes 202760 | tf_op jit(solution)/shard_map/ppermute | solution.py:163
  7.8 6.4 %collective-permute-start.2 = (bf16[8,4224]{1,0:T(8,128)(2,1)}, bf16[8,4224]{1,0:T(8,128)(2,1)S(1)}, u32[]{:S(2)}, u32[]{:S(2)}) collective-permute-start(bf16[8,4224]{1,0:T(8,128)(2,1)} %shard_map.104), channel_id=1, source_target_pairs={{0,12},{4,8},{8,4},{12,0},{1,13},{5,9},{9,5},{13,1},{2,14},{6,10},... | collective-permute-start | bytes 202760 | tf_op jit(solution)/shard_map/ppermute | solution.py:163
  9.0 2.4 %copy-start.5 = (bf16[1,50,4096]{2,1,0:T(8,128)(2,1)S(1)}, bf16[1,50,4096]{2,1,0:T(8,128)(2,1)}, u32[]{:S(2)}) copy-start(bf16[1,50,4096]{2,1,0:T(8,128)(2,1)} %param.10) | copy-start | bytes 1228804
  16.1 1.2 %copy-start = (bf16[24,16,2048]{2,1,0:T(8,128)(2,1)}, bf16[24,16,2048]{2,1,0:T(8,128)(2,1)S(1)}, u32[]{:S(2)}) copy-start(bf16[24,16,2048]{2,1,0:T(8,128)(2,1)S(1)} %get-tuple-element.21) | copy-start | bytes 4718596
  16.1 4.4 %copy-start.6 = (f32[2048]{0:T(1024)S(1)}, f32[2048]{0:T(1024)}, u32[]{:S(2)}) copy-start(f32[2048]{0:T(1024)} %param.12) | copy-start | bytes 24580
  17.8 1.2 %collective-permute-start.3 = (f32[2,4,8]{2,1,0:T(4,128)S(1)}, f32[2,4,8]{2,1,0:T(4,128)S(1)}, u32[]{:S(2)}, u32[]{:S(2)}) collective-permute-start(f32[2,4,8]{2,1,0:T(4,128)S(1)} %pad_maximum_fusion.13), channel_id=1, source_target_pairs={{0,1},{1,0},{2,3},{3,2},{4,5},{5,4},{6,7},{7,6},{8,9},{9,8},{10,11... | collective-permute-start | bytes 776 | tf_op jit(solution)/shard_map/ppermute | solution.py:178
  19.0 3.7 %collective-permute-start.4 = (f32[2,4,8]{2,1,0:T(4,128)S(1)}, f32[2,4,8]{2,1,0:T(4,128)S(1)}, u32[]{:S(2)}, u32[]{:S(2)}) collective-permute-start(f32[2,4,8]{2,1,0:T(4,128)S(1)} %pad_maximum_fusion.14), channel_id=1, source_target_pairs={{0,2},{1,3},{2,0},{3,1},{4,6},{5,7},{6,4},{7,5},{8,10},{9,11},{10,... | collective-permute-start | bytes 776 | tf_op jit(solution)/shard_map/ppermute | solution.py:178
  22.7 5.5 %collective-permute-start.7 = (f32[2,4,8]{2,1,0:T(4,128)S(1)}, f32[2,4,8]{2,1,0:T(4,128)S(1)}, u32[]{:S(2)}, u32[]{:S(2)}) collective-permute-start(f32[2,4,8]{2,1,0:T(4,128)S(1)} %get-tuple-element.31), channel_id=1, source_target_pairs={{0,12},{4,8},{8,4},{12,0},{1,13},{5,9},{9,5},{13,1},{2,14},{6,10},... | collective-permute-start | bytes 776 | tf_op jit(solution)/shard_map/ppermute | solution.py:266
  24.7 3.6 %collective-permute-start.5 = (f32[2,4,8]{2,1,0:T(4,128)S(1)}, f32[2,4,8]{2,1,0:T(4,128)S(1)}, u32[]{:S(2)}, u32[]{:S(2)}) collective-permute-start(f32[2,4,8]{2,1,0:T(4,128)S(1)} %get-tuple-element.31), channel_id=1, source_target_pairs={{0,4},{4,0},{8,12},{12,8},{1,5},{5,1},{9,13},{13,9},{2,6},{6,2},{1... | collective-permute-start | bytes 776 | tf_op jit(solution)/shard_map/ppermute | solution.py:266
  25.0 4.5 %collective-permute-start.6 = (f32[2,4,8]{2,1,0:T(4,128)S(1)}, f32[2,4,8]{2,1,0:T(4,128)S(1)}, u32[]{:S(2)}, u32[]{:S(2)}) collective-permute-start(f32[2,4,8]{2,1,0:T(4,128)S(1)} %get-tuple-element.31), channel_id=1, source_target_pairs={{0,8},{4,12},{8,0},{12,4},{1,9},{5,13},{9,1},{13,5},{2,10},{6,14},... | collective-permute-start | bytes 776 | tf_op jit(solution)/shard_map/ppermute | solution.py:266
  30.3 1.4 %copy-start.1 = (bf16[24,16,2048]{2,1,0:T(8,128)(2,1)S(1)}, bf16[24,16,2048]{2,1,0:T(8,128)(2,1)}, u32[]{:S(2)}) copy-start(bf16[24,16,2048]{2,1,0:T(8,128)(2,1)} %copy-done) | copy-start | bytes 4718596

commit v15 on v14

--- a/solution.py
+++ b/solution.py
@@ -70,13 +70,12 @@
     return lax.dot_general(ctf_square, power_sum, (((1,), (1,)), ((), ())), precision=HIGHEST)
 
 
-def tile_scores(shifted, ref_rows, norms, gain_rows, bin_rows):
+def tile_scores(shifted, ref_rows, norm_term, gain_rows):
     count_here = gain_rows.shape[0]
     products = lax.dot_general(
         shifted, ref_rows, (((1,), (1,)), ((), ())), preferred_element_type=jnp.float32
     )
     products = products.reshape(count_here, shifted.shape[0] // count_here, ref_rows.shape[0])
-    norm_term = jnp.dot(bin_rows, norms, precision=HIGHEST)
     return (
         gain_rows[:, None, None] * products
         - 0.5 * (gain_rows * gain_rows)[:, None, None] * norm_term[:, None, :]
@@ -207,11 +206,12 @@
     return (numerator, denominator)
 
 
-def block_rows(images, gains, bins, norms, ref_tile, ctf_table, cosine_table, sine_table):
-    bin_rows = bin_matrix(bins)
-    ctf_rows = jnp.dot(bin_rows, ctf_table, precision=HIGHEST)
+def block_rows(images, gains, bins, bin_table, ref_tile, cosine_table, sine_table):
+    half_width = images.shape[1] // 2
+    picked = jnp.dot(bin_matrix(bins), bin_table, precision=HIGHEST)
+    ctf_rows = picked[:, :half_width]
     shifted = shifted_rows(images, ctf_rows, cosine_table, sine_table)
-    scores = tile_scores(shifted, ref_tile, norms, gains, bin_rows)
+    scores = tile_scores(shifted, ref_tile, picked[:, half_width:], gains)
     return (shifted, scores, ctf_rows)
 
 
@@ -228,7 +228,7 @@
     shifts_count = cosine_table.shape[0]
 
     small = n_blk <= 4 and n_blk & (n_blk - 1) == 0 and n_cls & (n_cls - 1) == 0
-    tables = (ref_tile, ctf_table, cosine_table, sine_table)
+    tables = (jnp.concatenate([ctf_table, own_norms], axis=1), ref_tile, cosine_table, sine_table)
     if small:
         packed = pack_rows(particles, group_counts, group_scale, defocus_bin)
         others = xor_gather(packed, "blk", n_blk)[batch_size:]
@@ -249,7 +249,7 @@
             lax.all_gather(live_mask, "blk", axis=0, tiled=True),
             lax.all_gather(defocus_bin.astype(jnp.float32), "blk", axis=0, tiled=True),
         )]
-    results = [block_rows(images, gains, bins, own_norms, *tables) for images, gains, _, bins in groups]
+    results = [block_rows(images, gains, bins, *tables) for images, gains, _, bins in groups]
     pieces = [shifted for shifted, _, _ in results]
     all_scores = jnp.concatenate([scores for _, scores, _ in results], axis=0)
     ctf_rows = jnp.concatenate([rows for _, _, rows in results], axis=0)

time: 34.5 us -> 34.4 us (level)
  matrix products: 4.56 us -> 4.21 us
    dot_general x4 -> x2, matrix products: 0.88 us -> 0.53 us  [block_rows(): picked = jnp.dot(bin_matrix(bins), bin_table, precision=HIGHEST)]
  transfers between devices with their start and end apart: 8 -> 8, of which waited for: 7 -> 7; matrix products, arithmetic and copies ran while one was open for 12% -> 11% of each run, Pallas kernels for 0% -> 0%
where the time goes in v15:
time: 34.4 us; the launch traced here: 34.1 us
  starting transfers between devices  11.6 us (34%)
  waiting for transfers between devices  8.04 us (23%)
  other arithmetic  5.14 us (15%)
  matrix products  4.21 us (12%)
  local copies, waits for them, and re-layouts  2.65 us (8%)
  Pallas kernels  1.57 us (5%)
  between operations  0.88 us (3%)
    ppermute x3, starting transfers between devices, xor_gather(): lax.ppermute(value, axis, [(i, i ^ k) for i in range(size)])  5.62 us
    ppermute x3, starting transfers between devices, per_device(): lax.ppermute(stats, 'blk', [(i, i ^ k) for i in range(n_blk)])  4.45 us
    ppermute x2, waiting for transfers between devices, xor_butterfly(): other = lax.ppermute(stats, axis, [(i, i ^ step) for i in range(size)])  3.27 us
    ppermute x3, waiting for transfers between devices, xor_gather(): lax.ppermute(value, axis, [(i, i ^ k) for i in range(size)])  2.5 us
    ppermute x3, waiting for transfers between devices, per_device(): lax.ppermute(stats, 'blk', [(i, i ^ k) for i in range(n_blk)])  2.28 us
    unnamed x17, local copies, waits for them, and re-layouts  2.11 us
    ppermute x2, starting transfers between devices, xor_butterfly(): other = lax.ppermute(stats, axis, [(i, i ^ step) for i in range(size)])  1.57 us
    pallas_call x1, Pallas kernels, pack_rows(): pl.pallas_call(pack_kernel, out_shape=jax.ShapeDtypeStruct((slots, width...  1.57 us
  transfers between devices with their start and end apart: 8, of which 7 were waited for; matrix products, arithmetic and copies ran while one was open for 11% of the time, Pallas kernels for 0%

profile of v15, /device:TPU:0, one launch (start us, length us, event | category | flops | bytes accessed | tf_op | source)
XLA Modules:
  0.0 34.1 jit_solution(5546784210569616840)
XLA Ops:
  0.6 0.0 copy-start.2
  0.6 0.0 copy-start.3
  0.7 0.0 copy-start.4
  0.7 1.6 %shard_map.104 = bf16[8,4224]{1,0:T(8,128)(2,1)} custom-call(s32[4]{0:T(128)} %sizes_ref.1, f32[4]{0:T(128)} %scales_ref.1, s32[8]{0:T(128)} %bins_ref.1, bf16[8,4096]{1,0:T(8,128)(2,1)} %images_ref.1), custom_call_target="tpu_custom_call" | custom-call | tf_op jit(solution)/shard_map/pallas_call | solution.py:152
  2.2 3.0 %collective-permute-start = (bf16[8,4224]{1,0:T(8,128)(2,1)}, bf16[8,4224]{1,0:T(8,128)(2,1)S(1)}, u32[]{:S(2)}, u32[]{:S(2)}) collective-permute-start(bf16[8,4224]{1,0:T(8,128)(2,1)} %shard_map.104), channel_id=1, source_target_pairs={{0,4},{4,0},{8,12},{12,8},{1,5},{5,1},{9,13},{13,9},{2,6},{6,2},{1... | collective-permute-start | bytes 202760 | tf_op jit(solution)/shard_map/ppermute | solution.py:162
  5.3 2.6 %collective-permute-start.1 = (bf16[8,4224]{1,0:T(8,128)(2,1)}, bf16[8,4224]{1,0:T(8,128)(2,1)S(1)}, u32[]{:S(2)}, u32[]{:S(2)}) collective-permute-start(bf16[8,4224]{1,0:T(8,128)(2,1)} %shard_map.104), channel_id=1, source_target_pairs={{0,8},{4,12},{8,0},{12,4},{1,9},{5,13},{9,1},{13,5},{2,10},{6,14},... | collective-permute-start | bytes 202760 | tf_op jit(solution)/shard_map/ppermute | solution.py:162
  7.8 0.0 collective-permute-start.2
  7.8 1.0 %convert_element_type.26 = f32[8,4224]{1,0:T(8,128)S(1)} convert(bf16[8,4224]{1,0:T(8,128)(2,1)} %shard_map.104) | non-fusion elementwise | flops 33792 | bytes 202752 | tf_op jit(solution)/shard_map/convert_element_type | solution.py:235
  8.8 0.2 slice_reduce_fusion.3
  9.0 1.1 %bitcast_convert_fusion = f32[50,4096]{1,0:T(8,128)S(1)} fusion(bf16[1,50,4096]{2,1,0:T(8,128)(2,1)} %param.10), kind=kLoop, calls=%fused_computation.23 | loop fusion | flops 204800 | bytes 1228800 | tf_op jit(solution)/shard_map/convert_element_type | solution.py:65
  10.1 0.0 copy-done.4
  10.1 0.0 copy-start.5
  10.2 0.5 %fusion.8 = f32[16,50]{1,0:T(8,128)S(1)} fusion(f32[50,4096]{1,0:T(8,128)S(1)} %bitcast_convert_fusion, f32[16,2048]{1,0:T(8,128)S(1)} %copy-done.4), kind=kOutput, calls=%fused_computation.19 | convolution fusion | flops 20000768 | bytes 953472 | tf_op jit(solution)/shard_map/dot_general | solution.py:70
  10.6 0.2 fusion.17
  10.9 0.1 slice_multiply_fusion.4
  11.0 0.0 copy-done.2
  11.0 0.0 copy-done.3
  11.0 0.3 multiply_convert_fusion.3
  11.3 0.0 copy-done.5
  11.3 0.4 %fusion.6 = f32[8,16,50]{2,1,0:T(8,128)S(1)} fusion(bf16[8,16,2048]{2,1,0:T(8,128)(2,1)S(1)} %get-tuple-element.23, bf16[8,16,2048]{2,1,0:T(8,128)(2,1)S(1)} %get-tuple-element.22, bf16[1,50,4096]{2,1,0:T(8,128)(2,1)S(1)} %copy-done.5, f32[8,50]{1,0:T(8,128)S(1)} %slice_multiply_fusion.4, f32[8]{0:T(128)S(1)} %get-tuple-element.11), kind=kOutput, calls=%fused_computation.12 | convolution fusion | flops 54538752 | bytes 1485408 | tf_op jit(solution)/shard_map/dot_general | solution.py:75
  11.7 0.0 collective-permute-done
  11.7 1.1 %collective-permute-done.1 = bf16[8,4224]{1,0:T(8,128)(2,1)S(1)} collective-permute-done((bf16[8,4224]{1,0:T(8,128)(2,1)}, bf16[8,4224]{1,0:T(8,128)(2,1)S(1)}, u32[]{:S(2)}, u32[]{:S(2)}) %collective-permute-start.1) | collective-permute-done | bytes 67616 | tf_op jit(solution)/shard_map/ppermute | solution.py:162
  12.9 1.4 %collective-permute-done.2 = bf16[8,4224]{1,0:T(8,128)(2,1)S(1)} collective-permute-done((bf16[8,4224]{1,0:T(8,128)(2,1)}, bf16[8,4224]{1,0:T(8,128)(2,1)S(1)}, u32[]{:S(2)}, u32[]{:S(2)}) %collective-permute-start.2) | collective-permute-done | bytes 67616 | tf_op jit(solution)/shard_map/ppermute | solution.py:162
  14.3 0.2 slice_reduce_fusion.1
  14.5 0.3 fusion.16
  14.9 0.1 slice_multiply_fusion.3
  14.9 1.1 %multiply_convert_fusion.1 = (bf16[24,16,2048]{2,1,0:T(8,128)(2,1)S(1)}, bf16[24,16,2048]{2,1,0:T(8,128)(2,1)S(1)}) fusion(f32[24,2048]{1,0:T(8,128)S(1)} %slice.208, f32[16,2048]{1,0:T(8,128)S(1)} %copy-done.2, f32[24,2048]{1,0:T(8,128)S(1)} %get-tuple-element.25, f32[16,2048]{1,0:T(8,128)S(1)} %copy-done.3, f32[24,2048]{1,0:T(8,128)S(1)} %get-tuple-element.24), kind=kLoop, calls=%fused_computation.7 | loop fusion | flops 7864320 | bytes 3997696 | tf_op jit(solution)/shard_map/convert
  16.0 0.0 copy-start
  16.0 0.0 copy-start.6
  16.0 1.0 %fusion.5 = f32[24,16,50]{2,1,0:T(8,128)S(1)} fusion(bf16[24,16,2048]{2,1,0:T(8,128)(2,1)S(1)} %get-tuple-element.21, bf16[24,16,2048]{2,1,0:T(8,128)(2,1)S(1)} %get-tuple-element.20, bf16[1,50,4096]{2,1,0:T(8,128)(2,1)S(1)} %copy-done.5, f32[24,50]{1,0:T(8,128)S(1)} %slice_multiply_fusion.3, f32[24]{0:T(128)S(1)} %get-tuple-element.14), kind=kOutput, calls=%fused_computation.10 | convolution fusion | flops 163616256 | bytes 3637024 | tf_op jit(solution)/shard_map/dot_general | solution.py:75
  17.0 0.2 copy-done
  17.2 0.1 reshape.142
  17.4 0.2 broadcast_reduce_fusion
  17.5 0.1 stack.32
  17.6 0.1 squeeze.13
  17.7 0.0 collective-permute-start.3
  17.7 1.2 %collective-permute-done.3 = f32[2,4,8]{2,1,0:T(4,128)S(1)} collective-permute-done((f32[2,4,8]{2,1,0:T(4,128)S(1)}, f32[2,4,8]{2,1,0:T(4,128)S(1)}, u32[]{:S(2)}, u32[]{:S(2)}) %collective-permute-start.3) | collective-permute-done | bytes 288 | tf_op jit(solution)/shard_map/ppermute | solution.py:177
  18.9 1.6 %collective-permute-start.4 = (f32[2,4,8]{2,1,0:T(4,128)S(1)}, f32[2,4,8]{2,1,0:T(4,128)S(1)}, u32[]{:S(2)}, u32[]{:S(2)}) collective-permute-start(f32[2,4,8]{2,1,0:T(4,128)S(1)} %pad_maximum_fusion.17), channel_id=1, source_target_pairs={{0,2},{1,3},{2,0},{3,1},{4,6},{5,7},{6,4},{7,5},{8,10},{9,11},{10,... | collective-permute-start | bytes 776 | tf_op jit(solution)/shard_map/ppermute | solution.py:177
  20.4 0.0 copy-done.6
  20.5 2.1 %collective-permute-done.4 = f32[2,4,8]{2,1,0:T(4,128)S(1)} collective-permute-done((f32[2,4,8]{2,1,0:T(4,128)S(1)}, f32[2,4,8]{2,1,0:T(4,128)S(1)}, u32[]{:S(2)}, u32[]{:S(2)}) %collective-permute-start.4) | collective-permute-done | bytes 288 | tf_op jit(solution)/shard_map/ppermute | solution.py:177
  22.6 1.9 %collective-permute-start.7 = (f32[2,4,8]{2,1,0:T(4,128)S(1)}, f32[2,4,8]{2,1,0:T(4,128)S(1)}, u32[]{:S(2)}, u32[]{:S(2)}) collective-permute-start(f32[2,4,8]{2,1,0:T(4,128)S(1)} %get-tuple-element.31), channel_id=1, source_target_pairs={{0,12},{4,8},{8,4},{12,0},{1,13},{5,9},{9,5},{13,1},{2,14},{6,10},... | collective-permute-start | bytes 776 | tf_op jit(solution)/shard_map/ppermute | solution.py:266
  24.5 0.1 fusion.38
  24.6 0.4 %collective-permute-start.5 = (f32[2,4,8]{2,1,0:T(4,128)S(1)}, f32[2,4,8]{2,1,0:T(4,128)S(1)}, u32[]{:S(2)}, u32[]{:S(2)}) collective-permute-start(f32[2,4,8]{2,1,0:T(4,128)S(1)} %get-tuple-element.31), channel_id=1, source_target_pairs={{0,4},{4,0},{8,12},{12,8},{1,5},{5,1},{9,13},{13,9},{2,6},{6,2},{1... | collective-permute-start | bytes 776 | tf_op jit(solution)/shard_map/ppermute | solution.py:266
  24.9 2.2 %collective-permute-start.6 = (f32[2,4,8]{2,1,0:T(4,128)S(1)}, f32[2,4,8]{2,1,0:T(4,128)S(1)}, u32[]{:S(2)}, u32[]{:S(2)}) collective-permute-start(f32[2,4,8]{2,1,0:T(4,128)S(1)} %get-tuple-element.31), channel_id=1, source_target_pairs={{0,8},{4,12},{8,0},{12,4},{1,9},{5,13},{9,1},{13,5},{2,10},{6,14},... | collective-permute-start | bytes 776 | tf_op jit(solution)/shard_map/ppermute | solution.py:266
  27.1 0.9 %collective-permute-done.7 = f32[2,4,8]{2,1,0:T(4,128)S(1)} collective-permute-done((f32[2,4,8]{2,1,0:T(4,128)S(1)}, f32[2,4,8]{2,1,0:T(4,128)S(1)}, u32[]{:S(2)}, u32[]{:S(2)}) %collective-permute-start.7) | collective-permute-done | bytes 288 | tf_op jit(solution)/shard_map/ppermute | solution.py:266
  28.1 0.1 collective-permute-done.5
  28.2 1.2 %collective-permute-done.6 = f32[2,4,8]{2,1,0:T(4,128)S(1)} collective-permute-done((f32[2,4,8]{2,1,0:T(4,128)S(1)}, f32[2,4,8]{2,1,0:T(4,128)S(1)}, u32[]{:S(2)}, u32[]{:S(2)}) %collective-permute-start.6) | collective-permute-done | bytes 288 | tf_op jit(solution)/shard_map/ppermute | solution.py:266
  29.5 0.1 sub.72
  29.6 0.1 div.13
  29.7 0.5 %compare_select_fusion = f32[8]{0:T(128)} fusion(f32[8]{0:T(128)S(1)} %get-tuple-element.10, f32[4,8]{1,0:T(4,128)S(1)} %fusion.21, f32[4,8]{1,0:T(4,128)S(1)} %slice_reduce_fusion.2), kind=kLoop, calls=%fused_computation.78 | loop fusion | flops 24 | bytes 128 | tf_op jit(solution)/shard_map/jit(_where)/select_n | solution.py:285
  30.2 0.0 copy-start.1
  30.2 0.2 fusion.37
  30.4 0.4 %convolution_bitcast_fusion.1 = f32[50,4096]{1,0:T(8,128)S(1)} fusion(bf16[8,16,2048]{2,1,0:T(8,128)(2,1)S(1)} %get-tuple-element.23, bf16[8,16,2048]{2,1,0:T(8,128)(2,1)S(1)} %get-tuple-element.22, f32[32]{0:T(128)S(1)} %get-tuple-element.17, f32[32]{0:T(128)S(1)} %get-tuple-element.42, f32[32]{0:T(128)S(1)} %div.13, f32[32]{0:T(128)S(1)} %sub.72, ...), kind=kOutput, calls=%fused_computation.4 | convolution fusion | flops 54679552 | bytes 1970688 | tf_op jit(solution)/shard_map/dot_general | solution.py:194
  30.8 0.6 %fusion.12 = f32[50,2048]{1,0:T(8,128)S(1)} fusion(f32[24,2048]{1,0:T(8,128)S(1)} %slice.208, f32[8,2048]{1,0:T(8,128)S(1)} %slice.199, f32[32,50]{1,0:T(8,128)S(1)} %fusion.37, f32[32]{0:T(128)S(1)} %get-tuple-element.16), kind=kOutput, calls=%fused_computation.26 | convolution fusion | flops 39454272 | bytes 678272 | tf_op jit(solution)/shard_map/dot_general | solution.py:203
  31.4 0.2 copy-done.1
  31.6 0.8 %fusion.2 = f32[1,50,4096]{2,1,0:T(8,128)S(1)} fusion(f32[50,4096]{1,0:T(8,128)S(1)} %convolution_bitcast_fusion.1, bf16[24,16,2048]{2,1,0:T(8,128)(2,1)S(1)} %copy-done.1, bf16[24,16,2048]{2,1,0:T(8,128)(2,1)S(1)} %get-tuple-element.20, f32[50,2048]{1,0:T(8,128)S(1)} %fusion.12, f32[4096]{0:T(1024)S(1)} %pad_maximum_fusion.15, ...), kind=kOutput, calls=%fused_computation.3 | convolution fusion | flops 164550656 | bytes 5313024 | tf_op jit(solution)/shard_map/dot_general | solution.py:194
  32.4 1.7 %copy.16 = f32[1,50,4096]{2,0,1:T(1,128)} copy(f32[1,50,4096]{2,1,0:T(8,128)S(1)} %fusion.2) | data formatting | bytes 1638400
  (25 shorter events, 0.3 us)
Async XLA Ops:
  0.6 10.3 %copy-start.2 = (f32[16,2048]{1,0:T(8,128)S(1)}, f32[16,2048]{1,0:T(8,128)}, u32[]{:S(2)}) copy-start(f32[16,2048]{1,0:T(8,128)} %constant.6.clone) | copy-start | bytes 393220
  0.6 10.3 %copy-start.3 = (f32[16,2048]{1,0:T(8,128)S(1)}, f32[16,2048]{1,0:T(8,128)}, u32[]{:S(2)}) copy-start(f32[16,2048]{1,0:T(8,128)} %constant.5.clone) | copy-start | bytes 393220
  0.7 9.5 %copy-start.4 = (f32[16,2048]{1,0:T(8,128)S(1)}, f32[16,2048]{1,0:T(8,128)}, u32[]{:S(2)}) copy-start(f32[16,2048]{1,0:T(8,128)} %param.11) | copy-start | bytes 393220
  2.2 9.5 %collective-permute-start = (bf16[8,4224]{1,0:T(8,128)(2,1)}, bf16[8,4224]{1,0:T(8,128)(2,1)S(1)}, u32[]{:S(2)}, u32[]{:S(2)}) collective-permute-start(bf16[8,4224]{1,0:T(8,128)(2,1)} %shard_map.104), channel_id=1, source_target_pairs={{0,4},{4,0},{8,12},{12,8},{1,5},{5,1},{9,13},{13,9},{2,6},{6,2},{1... | collective-permute-start | bytes 202760 | tf_op jit(solution)/shard_map/ppermute | solution.py:162
  5.3 7.6 %collective-permute-start.1 = (bf16[8,4224]{1,0:T(8,128)(2,1)}, bf16[8,4224]{1,0:T(8,128)(2,1)S(1)}, u32[]{:S(2)}, u32[]{:S(2)}) collective-permute-start(bf16[8,4224]{1,0:T(8,128)(2,1)} %shard_map.104), channel_id=1, source_target_pairs={{0,8},{4,12},{8,0},{12,4},{1,9},{5,13},{9,1},{13,5},{2,10},{6,14},... | collective-permute-start | bytes 202760 | tf_op jit(solution)/shard_map/ppermute | solution.py:162
  7.8 6.4 %collective-permute-start.2 = (bf16[8,4224]{1,0:T(8,128)(2,1)}, bf16[8,4224]{1,0:T(8,128)(2,1)S(1)}, u32[]{:S(2)}, u32[]{:S(2)}) collective-permute-start(bf16[8,4224]{1,0:T(8,128)(2,1)} %shard_map.104), channel_id=1, source_target_pairs={{0,12},{4,8},{8,4},{12,0},{1,13},{5,9},{9,5},{13,1},{2,14},{6,10},... | collective-permute-start | bytes 202760 | tf_op jit(solution)/shard_map/ppermute | solution.py:162
  10.1 1.1 %copy-start.5 = (bf16[1,50,4096]{2,1,0:T(8,128)(2,1)S(1)}, bf16[1,50,4096]{2,1,0:T(8,128)(2,1)}, u32[]{:S(2)}) copy-start(bf16[1,50,4096]{2,1,0:T(8,128)(2,1)} %param.10) | copy-start | bytes 1228804
  16.0 1.2 %copy-start = (bf16[24,16,2048]{2,1,0:T(8,128)(2,1)}, bf16[24,16,2048]{2,1,0:T(8,128)(2,1)S(1)}, u32[]{:S(2)}) copy-start(bf16[24,16,2048]{2,1,0:T(8,128)(2,1)S(1)} %get-tuple-element.21) | copy-start | bytes 4718596
  16.0 4.4 %copy-start.6 = (f32[2048]{0:T(1024)S(1)}, f32[2048]{0:T(1024)}, u32[]{:S(2)}) copy-start(f32[2048]{0:T(1024)} %param.12) | copy-start | bytes 24580
  17.7 1.2 %collective-permute-start.3 = (f32[2,4,8]{2,1,0:T(4,128)S(1)}, f32[2,4,8]{2,1,0:T(4,128)S(1)}, u32[]{:S(2)}, u32[]{:S(2)}) collective-permute-start(f32[2,4,8]{2,1,0:T(4,128)S(1)} %pad_maximum_fusion.16), channel_id=1, source_target_pairs={{0,1},{1,0},{2,3},{3,2},{4,5},{5,4},{6,7},{7,6},{8,9},{9,8},{10,11... | collective-permute-start | bytes 776 | tf_op jit(solution)/shard_map/ppermute | solution.py:177
  18.9 3.7 %collective-permute-start.4 = (f32[2,4,8]{2,1,0:T(4,128)S(1)}, f32[2,4,8]{2,1,0:T(4,128)S(1)}, u32[]{:S(2)}, u32[]{:S(2)}) collective-permute-start(f32[2,4,8]{2,1,0:T(4,128)S(1)} %pad_maximum_fusion.17), channel_id=1, source_target_pairs={{0,2},{1,3},{2,0},{3,1},{4,6},{5,7},{6,4},{7,5},{8,10},{9,11},{10,... | collective-permute-start | bytes 776 | tf_op jit(solution)/shard_map/ppermute | solution.py:177
  22.6 5.5 %collective-permute-start.7 = (f32[2,4,8]{2,1,0:T(4,128)S(1)}, f32[2,4,8]{2,1,0:T(4,128)S(1)}, u32[]{:S(2)}, u32[]{:S(2)}) collective-permute-start(f32[2,4,8]{2,1,0:T(4,128)S(1)} %get-tuple-element.31), channel_id=1, source_target_pairs={{0,12},{4,8},{8,4},{12,0},{1,13},{5,9},{9,5},{13,1},{2,14},{6,10},... | collective-permute-start | bytes 776 | tf_op jit(solution)/shard_map/ppermute | solution.py:266
  24.6 3.6 %collective-permute-start.5 = (f32[2,4,8]{2,1,0:T(4,128)S(1)}, f32[2,4,8]{2,1,0:T(4,128)S(1)}, u32[]{:S(2)}, u32[]{:S(2)}) collective-permute-start(f32[2,4,8]{2,1,0:T(4,128)S(1)} %get-tuple-element.31), channel_id=1, source_target_pairs={{0,4},{4,0},{8,12},{12,8},{1,5},{5,1},{9,13},{13,9},{2,6},{6,2},{1... | collective-permute-start | bytes 776 | tf_op jit(solution)/shard_map/ppermute | solution.py:266
  24.9 4.5 %collective-permute-start.6 = (f32[2,4,8]{2,1,0:T(4,128)S(1)}, f32[2,4,8]{2,1,0:T(4,128)S(1)}, u32[]{:S(2)}, u32[]{:S(2)}) collective-permute-start(f32[2,4,8]{2,1,0:T(4,128)S(1)} %get-tuple-element.31), channel_id=1, source_target_pairs={{0,8},{4,12},{8,0},{12,4},{1,9},{5,13},{9,1},{13,5},{2,10},{6,14},... | collective-permute-start | bytes 776 | tf_op jit(solution)/shard_map/ppermute | solution.py:266
  30.2 1.4 %copy-start.1 = (bf16[24,16,2048]{2,1,0:T(8,128)(2,1)S(1)}, bf16[24,16,2048]{2,1,0:T(8,128)(2,1)}, u32[]{:S(2)}) copy-start(bf16[24,16,2048]{2,1,0:T(8,128)(2,1)} %copy-done) | copy-start | bytes 4718596

commit v16 on v15

--- a/solution.py
+++ b/solution.py
@@ -261,13 +261,13 @@
 
     if small:
         stats = jnp.stack([peak_all, totals_all]).reshape(2, n_blk, batch_size)
-        stats = xor_butterfly(stats, "cls", n_cls)
         parts = [stats] + [
             xor_reorder(lax.ppermute(stats, "blk", [(i, i ^ k) for i in range(n_blk)]), k, 1)
             for k in range(1, n_blk)
         ]
         parts = jnp.stack(parts)
-        peak_all, totals_all = combine_many(parts[:, 0], parts[:, 1])
+        stats = jnp.stack(combine_many(parts[:, 0], parts[:, 1]))
+        peak_all, totals_all = xor_butterfly(stats, "cls", n_cls)
         peak_all = peak_all.reshape(-1)
         totals_all = totals_all.reshape(-1)
         peak_score = peak_all[:batch_size]

time: 34.4 us -> 34.3 us (level)
  waiting for transfers between devices: 8.04 us -> 7.47 us
  local copies, waits for them, and re-layouts: 2.65 us -> 3.15 us
    ppermute x2, waiting for transfers between devices: 3.27 us -> 2.86 us  [xor_butterfly(): other = lax.ppermute(stats, axis, [(i, i ^ step) for i in range(size)])]
    unnamed x17 -> x18, local copies, waits for them, and re-layouts: 2.11 us -> 2.11 us
  transfers between devices with their start and end apart: 8 -> 8, of which waited for: 7 -> 6; matrix products, arithmetic and copies ran while one was open for 11% -> 13% of each run, Pallas kernels for 0% -> 0%
where the time goes in v16:
time: 34.3 us; the launch traced here: 34.1 us
  starting transfers between devices  11.6 us (34%)
  waiting for transfers between devices  7.47 us (22%)
  other arithmetic  5.16 us (15%)
  matrix products  4.21 us (12%)
  local copies, waits for them, and re-layouts  3.15 us (9%)
  Pallas kernels  1.57 us (5%)
  between operations  0.89 us (3%)
    ppermute x3, starting transfers between devices, xor_gather(): lax.ppermute(value, axis, [(i, i ^ k) for i in range(size)])  5.62 us
    ppermute x3, starting transfers between devices, per_device(): lax.ppermute(stats, 'blk', [(i, i ^ k) for i in range(n_blk)])  4.39 us
    ppermute x2, waiting for transfers between devices, xor_butterfly(): other = lax.ppermute(stats, axis, [(i, i ^ step) for i in range(size)])  2.86 us
    ppermute x3, waiting for transfers between devices, xor_gather(): lax.ppermute(value, axis, [(i, i ^ k) for i in range(size)])  2.5 us
    ppermute x3, waiting for transfers between devices, per_device(): lax.ppermute(stats, 'blk', [(i, i ^ k) for i in range(n_blk)])  2.12 us
    unnamed x18, local copies, waits for them, and re-layouts  2.11 us
    ppermute x2, starting transfers between devices, xor_butterfly(): other = lax.ppermute(stats, axis, [(i, i ^ step) for i in range(size)])  1.63 us
    pallas_call x1, Pallas kernels, pack_rows(): pl.pallas_call(pack_kernel, out_shape=jax.ShapeDtypeStruct((slots, width...  1.57 us
  transfers between devices with their start and end apart: 8, of which 6 were waited for; matrix products, arithmetic and copies ran while one was open for 13% of the time, Pallas kernels for 0%

profile of v16, /device:TPU:0, one launch (start us, length us, event | category | flops | bytes accessed | tf_op | source)
XLA Modules:
  0.0 34.1 jit_solution(14437297407379011271)
XLA Ops:
  0.6 0.0 copy-start.2
  0.6 0.0 copy-start.3
  0.7 0.0 copy-start.4
  0.7 1.6 %shard_map.104 = bf16[8,4224]{1,0:T(8,128)(2,1)} custom-call(s32[4]{0:T(128)} %sizes_ref.1, f32[4]{0:T(128)} %scales_ref.1, s32[8]{0:T(128)} %bins_ref.1, bf16[8,4096]{1,0:T(8,128)(2,1)} %images_ref.1), custom_call_target="tpu_custom_call" | custom-call | tf_op jit(solution)/shard_map/pallas_call | solution.py:152
  2.2 3.0 %collective-permute-start = (bf16[8,4224]{1,0:T(8,128)(2,1)}, bf16[8,4224]{1,0:T(8,128)(2,1)S(1)}, u32[]{:S(2)}, u32[]{:S(2)}) collective-permute-start(bf16[8,4224]{1,0:T(8,128)(2,1)} %shard_map.104), channel_id=1, source_target_pairs={{0,4},{4,0},{8,12},{12,8},{1,5},{5,1},{9,13},{13,9},{2,6},{6,2},{1... | collective-permute-start | bytes 202760 | tf_op jit(solution)/shard_map/ppermute | solution.py:162
  5.3 2.6 %collective-permute-start.1 = (bf16[8,4224]{1,0:T(8,128)(2,1)}, bf16[8,4224]{1,0:T(8,128)(2,1)S(1)}, u32[]{:S(2)}, u32[]{:S(2)}) collective-permute-start(bf16[8,4224]{1,0:T(8,128)(2,1)} %shard_map.104), channel_id=1, source_target_pairs={{0,8},{4,12},{8,0},{12,4},{1,9},{5,13},{9,1},{13,5},{2,10},{6,14},... | collective-permute-start | bytes 202760 | tf_op jit(solution)/shard_map/ppermute | solution.py:162
  7.8 0.0 collective-permute-start.2
  7.8 1.0 %convert_element_type.26 = f32[8,4224]{1,0:T(8,128)S(1)} convert(bf16[8,4224]{1,0:T(8,128)(2,1)} %shard_map.104) | non-fusion elementwise | flops 33792 | bytes 202752 | tf_op jit(solution)/shard_map/convert_element_type | solution.py:235
  8.8 0.2 slice_reduce_fusion.3
  9.0 1.1 %bitcast_convert_fusion = f32[50,4096]{1,0:T(8,128)S(1)} fusion(bf16[1,50,4096]{2,1,0:T(8,128)(2,1)} %param.10), kind=kLoop, calls=%fused_computation.23 | loop fusion | flops 204800 | bytes 1228800 | tf_op jit(solution)/shard_map/convert_element_type | solution.py:65
  10.1 0.0 copy-done.4
  10.1 0.0 copy-start.5
  10.2 0.5 %fusion.8 = f32[16,50]{1,0:T(8,128)S(1)} fusion(f32[50,4096]{1,0:T(8,128)S(1)} %bitcast_convert_fusion, f32[16,2048]{1,0:T(8,128)S(1)} %copy-done.4), kind=kOutput, calls=%fused_computation.19 | convolution fusion | flops 20000768 | bytes 953472 | tf_op jit(solution)/shard_map/dot_general | solution.py:70
  10.6 0.2 fusion.17
  10.9 0.1 slice_multiply_fusion.4
  11.0 0.0 copy-done.2
  11.0 0.0 copy-done.3
  11.0 0.3 multiply_convert_fusion.3
  11.3 0.0 copy-done.5
  11.3 0.4 %fusion.6 = f32[8,16,50]{2,1,0:T(8,128)S(1)} fusion(bf16[8,16,2048]{2,1,0:T(8,128)(2,1)S(1)} %get-tuple-element.23, bf16[8,16,2048]{2,1,0:T(8,128)(2,1)S(1)} %get-tuple-element.22, bf16[1,50,4096]{2,1,0:T(8,128)(2,1)S(1)} %copy-done.5, f32[8,50]{1,0:T(8,128)S(1)} %slice_multiply_fusion.4, f32[8]{0:T(128)S(1)} %get-tuple-element.11), kind=kOutput, calls=%fused_computation.12 | convolution fusion | flops 54538752 | bytes 1485408 | tf_op jit(solution)/shard_map/dot_general | solution.py:75
  11.7 0.0 collective-permute-done
  11.7 1.1 %collective-permute-done.1 = bf16[8,4224]{1,0:T(8,128)(2,1)S(1)} collective-permute-done((bf16[8,4224]{1,0:T(8,128)(2,1)}, bf16[8,4224]{1,0:T(8,128)(2,1)S(1)}, u32[]{:S(2)}, u32[]{:S(2)}) %collective-permute-start.1) | collective-permute-done | bytes 67616 | tf_op jit(solution)/shard_map/ppermute | solution.py:162
  12.9 1.4 %collective-permute-done.2 = bf16[8,4224]{1,0:T(8,128)(2,1)S(1)} collective-permute-done((bf16[8,4224]{1,0:T(8,128)(2,1)}, bf16[8,4224]{1,0:T(8,128)(2,1)S(1)}, u32[]{:S(2)}, u32[]{:S(2)}) %collective-permute-start.2) | collective-permute-done | bytes 67616 | tf_op jit(solution)/shard_map/ppermute | solution.py:162
  14.3 0.2 slice_reduce_fusion.1
  14.5 0.3 fusion.16
  14.9 0.1 slice_multiply_fusion.3
  14.9 1.1 %multiply_convert_fusion.1 = (bf16[24,16,2048]{2,1,0:T(8,128)(2,1)S(1)}, bf16[24,16,2048]{2,1,0:T(8,128)(2,1)S(1)}) fusion(f32[24,2048]{1,0:T(8,128)S(1)} %slice.203, f32[16,2048]{1,0:T(8,128)S(1)} %copy-done.2, f32[24,2048]{1,0:T(8,128)S(1)} %get-tuple-element.25, f32[16,2048]{1,0:T(8,128)S(1)} %copy-done.3, f32[24,2048]{1,0:T(8,128)S(1)} %get-tuple-element.24), kind=kLoop, calls=%fused_computation.7 | loop fusion | flops 7864320 | bytes 3997696 | tf_op jit(solution)/shard_map/convert
  16.0 0.0 copy-start
  16.0 0.0 copy-start.6
  16.0 1.0 %fusion.5 = f32[24,16,50]{2,1,0:T(8,128)S(1)} fusion(bf16[24,16,2048]{2,1,0:T(8,128)(2,1)S(1)} %get-tuple-element.21, bf16[24,16,2048]{2,1,0:T(8,128)(2,1)S(1)} %get-tuple-element.20, bf16[1,50,4096]{2,1,0:T(8,128)(2,1)S(1)} %copy-done.5, f32[24,50]{1,0:T(8,128)S(1)} %slice_multiply_fusion.3, f32[24]{0:T(128)S(1)} %get-tuple-element.14), kind=kOutput, calls=%fused_computation.10 | convolution fusion | flops 163616256 | bytes 3637024 | tf_op jit(solution)/shard_map/dot_general | solution.py:75
  17.0 0.2 copy-done
  17.2 0.1 reshape.190
  17.4 0.2 broadcast_reduce_fusion
  17.5 0.1 stack.44
  17.6 0.1 stack.45
  17.7 1.8 %collective-permute-start.5 = (f32[2,4,8]{2,1,0:T(4,128)S(1)}, f32[2,4,8]{2,1,0:T(4,128)S(1)}, u32[]{:S(2)}, u32[]{:S(2)}) collective-permute-start(f32[2,4,8]{2,1,0:T(4,128)S(1)} %constant_dynamic-update-slice_fusion.3), channel_id=1, source_target_pairs={{0,12},{4,8},{8,4},{12,0},{1,13},{5,9},{9,5},{13,1},{2,14},{6,10},... | collective-permute-start | bytes 776 | tf_op jit(solution)/shard_map/ppermute | solution.py:265
  19.5 0.0 copy-done.6
  19.6 0.4 %collective-permute-start.3 = (f32[2,4,8]{2,1,0:T(4,128)S(1)}, f32[2,4,8]{2,1,0:T(4,128)S(1)}, u32[]{:S(2)}, u32[]{:S(2)}) collective-permute-start(f32[2,4,8]{2,1,0:T(4,128)S(1)} %constant_dynamic-update-slice_fusion.3), channel_id=1, source_target_pairs={{0,4},{4,0},{8,12},{12,8},{1,5},{5,1},{9,13},{13,9},{2,6},{6,2},{1... | collective-permute-start | bytes 776 | tf_op jit(solution)/shard_map/ppermute | solution.py:265
  19.9 2.2 %collective-permute-start.4 = (f32[2,4,8]{2,1,0:T(4,128)S(1)}, f32[2,4,8]{2,1,0:T(4,128)S(1)}, u32[]{:S(2)}, u32[]{:S(2)}) collective-permute-start(f32[2,4,8]{2,1,0:T(4,128)S(1)} %constant_dynamic-update-slice_fusion.3), channel_id=1, source_target_pairs={{0,8},{4,12},{8,0},{12,4},{1,9},{5,13},{9,1},{13,5},{2,10},{6,14},... | collective-permute-start | bytes 776 | tf_op jit(solution)/shard_map/ppermute | solution.py:265
  22.1 0.1 stack.42
  22.2 0.1 stack.41
  22.3 0.8 %collective-permute-done.5 = f32[2,4,8]{2,1,0:T(4,128)S(1)} collective-permute-done((f32[2,4,8]{2,1,0:T(4,128)S(1)}, f32[2,4,8]{2,1,0:T(4,128)S(1)}, u32[]{:S(2)}, u32[]{:S(2)}) %collective-permute-start.5) | collective-permute-done | bytes 288 | tf_op jit(solution)/shard_map/ppermute | solution.py:265
  23.1 0.0 collective-permute-done.3
  23.2 1.2 %collective-permute-done.4 = f32[2,4,8]{2,1,0:T(4,128)S(1)} collective-permute-done((f32[2,4,8]{2,1,0:T(4,128)S(1)}, f32[2,4,8]{2,1,0:T(4,128)S(1)}, u32[]{:S(2)}, u32[]{:S(2)}) %collective-permute-start.4) | collective-permute-done | bytes 288 | tf_op jit(solution)/shard_map/ppermute | solution.py:265
  24.5 0.1 collective-permute-start.6
  24.6 0.1 fusion.40
  24.7 0.1 reduce_sum.21
  24.7 1.0 %collective-permute-done.6 = f32[2,4,8]{2,1,0:T(4,128)S(1)} collective-permute-done((f32[2,4,8]{2,1,0:T(4,128)S(1)}, f32[2,4,8]{2,1,0:T(4,128)S(1)}, u32[]{:S(2)}, u32[]{:S(2)}) %collective-permute-start.6) | collective-permute-done | bytes 288 | tf_op jit(solution)/shard_map/ppermute | solution.py:177
  25.8 1.6 %collective-permute-start.7 = (f32[2,4,8]{2,1,0:T(4,128)S(1)}, f32[2,4,8]{2,1,0:T(4,128)S(1)}, u32[]{:S(2)}, u32[]{:S(2)}) collective-permute-start(f32[2,4,8]{2,1,0:T(4,128)S(1)} %pad_maximum_fusion.17), channel_id=1, source_target_pairs={{0,2},{1,3},{2,0},{3,1},{4,6},{5,7},{6,4},{7,5},{8,10},{9,11},{10,... | collective-permute-start | bytes 776 | tf_op jit(solution)/shard_map/ppermute | solution.py:177
  27.3 0.1 reduce_max.12
  27.4 0.1 squeeze.48
  27.5 0.1 squeeze.46
  27.6 1.9 %collective-permute-done.7 = f32[2,4,8]{2,1,0:T(4,128)S(1)} collective-permute-done((f32[2,4,8]{2,1,0:T(4,128)S(1)}, f32[2,4,8]{2,1,0:T(4,128)S(1)}, u32[]{:S(2)}, u32[]{:S(2)}) %collective-permute-start.7) | collective-permute-done | bytes 288 | tf_op jit(solution)/shard_map/ppermute | solution.py:177
  29.4 0.1 squeeze.49
  29.5 0.1 squeeze.47
  29.6 0.0 copy-start.1
  29.6 0.2 fusion.39
  29.8 0.4 %convolution_bitcast_fusion.1 = f32[50,4096]{1,0:T(8,128)S(1)} fusion(bf16[8,16,2048]{2,1,0:T(8,128)(2,1)S(1)} %get-tuple-element.23, bf16[8,16,2048]{2,1,0:T(8,128)(2,1)S(1)} %get-tuple-element.22, f32[32]{0:T(128)S(1)} %get-tuple-element.17, f32[32]{0:T(128)S(1)} %get-tuple-element.46, f32[32]{0:T(128)S(1)} %get-tuple-element.18, ...), kind=kOutput, calls=%fused_computation.4 | convolution fusion | flops 54679552 | bytes 1970688 | tf_op jit(solution)/shard_map/dot_general | solution.py:194
  30.2 0.6 %fusion.12 = f32[50,2048]{1,0:T(8,128)S(1)} fusion(f32[24,2048]{1,0:T(8,128)S(1)} %slice.203, f32[8,2048]{1,0:T(8,128)S(1)} %slice.194, f32[32,50]{1,0:T(8,128)S(1)} %fusion.39, f32[32]{0:T(128)S(1)} %get-tuple-element.16), kind=kOutput, calls=%fused_computation.26 | convolution fusion | flops 39454272 | bytes 678272 | tf_op jit(solution)/shard_map/dot_general | solution.py:203
  30.9 0.2 copy-done.1
  31.0 0.8 %fusion.2 = f32[1,50,4096]{2,1,0:T(8,128)S(1)} fusion(f32[50,4096]{1,0:T(8,128)S(1)} %convolution_bitcast_fusion.1, bf16[24,16,2048]{2,1,0:T(8,128)(2,1)S(1)} %copy-done.1, bf16[24,16,2048]{2,1,0:T(8,128)(2,1)S(1)} %get-tuple-element.20, f32[50,2048]{1,0:T(8,128)S(1)} %fusion.12, f32[4096]{0:T(1024)S(1)} %pad_maximum_fusion.15, ...), kind=kOutput, calls=%fused_computation.3 | convolution fusion | flops 164550656 | bytes 5313024 | tf_op jit(solution)/shard_map/dot_general | solution.py:194
  31.8 1.7 %copy.16 = f32[1,50,4096]{2,0,1:T(1,128)} copy(f32[1,50,4096]{2,1,0:T(8,128)S(1)} %fusion.2) | data formatting | bytes 1638400
  33.6 0.5 %compare_select_fusion = f32[8]{0:T(128)} fusion(f32[8]{0:T(128)S(1)} %get-tuple-element.10, f32[4,8]{1,0:T(4,128)S(1)} %get-tuple-element.29, f32[4,8]{1,0:T(4,128)S(1)} %get-tuple-element.28), kind=kLoop, calls=%fused_computation.87 | loop fusion | flops 24 | bytes 128 | tf_op jit(solution)/shard_map/jit(_where)/select_n | solution.py:285
  (28 shorter events, 0.3 us)
Async XLA Ops:
  0.6 10.3 %copy-start.2 = (f32[16,2048]{1,0:T(8,128)S(1)}, f32[16,2048]{1,0:T(8,128)}, u32[]{:S(2)}) copy-start(f32[16,2048]{1,0:T(8,128)} %constant.6.clone) | copy-start | bytes 393220
  0.6 10.3 %copy-start.3 = (f32[16,2048]{1,0:T(8,128)S(1)}, f32[16,2048]{1,0:T(8,128)}, u32[]{:S(2)}) copy-start(f32[16,2048]{1,0:T(8,128)} %constant.5.clone) | copy-start | bytes 393220
  0.7 9.5 %copy-start.4 = (f32[16,2048]{1,0:T(8,128)S(1)}, f32[16,2048]{1,0:T(8,128)}, u32[]{:S(2)}) copy-start(f32[16,2048]{1,0:T(8,128)} %param.11) | copy-start | bytes 393220
  2.2 9.5 %collective-permute-start = (bf16[8,4224]{1,0:T(8,128)(2,1)}, bf16[8,4224]{1,0:T(8,128)(2,1)S(1)}, u32[]{:S(2)}, u32[]{:S(2)}) collective-permute-start(bf16[8,4224]{1,0:T(8,128)(2,1)} %shard_map.104), channel_id=1, source_target_pairs={{0,4},{4,0},{8,12},{12,8},{1,5},{5,1},{9,13},{13,9},{2,6},{6,2},{1... | collective-permute-start | bytes 202760 | tf_op jit(solution)/shard_map/ppermute | solution.py:162
  5.3 7.6 %collective-permute-start.1 = (bf16[8,4224]{1,0:T(8,128)(2,1)}, bf16[8,4224]{1,0:T(8,128)(2,1)S(1)}, u32[]{:S(2)}, u32[]{:S(2)}) collective-permute-start(bf16[8,4224]{1,0:T(8,128)(2,1)} %shard_map.104), channel_id=1, source_target_pairs={{0,8},{4,12},{8,0},{12,4},{1,9},{5,13},{9,1},{13,5},{2,10},{6,14},... | collective-permute-start | bytes 202760 | tf_op jit(solution)/shard_map/ppermute | solution.py:162
  7.8 6.4 %collective-permute-start.2 = (bf16[8,4224]{1,0:T(8,128)(2,1)}, bf16[8,4224]{1,0:T(8,128)(2,1)S(1)}, u32[]{:S(2)}, u32[]{:S(2)}) collective-permute-start(bf16[8,4224]{1,0:T(8,128)(2,1)} %shard_map.104), channel_id=1, source_target_pairs={{0,12},{4,8},{8,4},{12,0},{1,13},{5,9},{9,5},{13,1},{2,14},{6,10},... | collective-permute-start | bytes 202760 | tf_op jit(solution)/shard_map/ppermute | solution.py:162
  10.1 1.1 %copy-start.5 = (bf16[1,50,4096]{2,1,0:T(8,128)(2,1)S(1)}, bf16[1,50,4096]{2,1,0:T(8,128)(2,1)}, u32[]{:S(2)}) copy-start(bf16[1,50,4096]{2,1,0:T(8,128)(2,1)} %param.10) | copy-start | bytes 1228804
  16.0 1.2 %copy-start = (bf16[24,16,2048]{2,1,0:T(8,128)(2,1)}, bf16[24,16,2048]{2,1,0:T(8,128)(2,1)S(1)}, u32[]{:S(2)}) copy-start(bf16[24,16,2048]{2,1,0:T(8,128)(2,1)S(1)} %get-tuple-element.21) | copy-start | bytes 4718596
  16.0 3.5 %copy-start.6 = (f32[2048]{0:T(1024)S(1)}, f32[2048]{0:T(1024)}, u32[]{:S(2)}) copy-start(f32[2048]{0:T(1024)} %param.12) | copy-start | bytes 24580
  17.7 5.4 %collective-permute-start.5 = (f32[2,4,8]{2,1,0:T(4,128)S(1)}, f32[2,4,8]{2,1,0:T(4,128)S(1)}, u32[]{:S(2)}, u32[]{:S(2)}) collective-permute-start(f32[2,4,8]{2,1,0:T(4,128)S(1)} %constant_dynamic-update-slice_fusion.3), channel_id=1, source_target_pairs={{0,12},{4,8},{8,4},{12,0},{1,13},{5,9},{9,5},{13,1},{2,14},{6,10},... | collective-permute-start | bytes 776 | tf_op jit(solution)/shard_map/ppermute | solution.py:265
  19.6 3.6 %collective-permute-start.3 = (f32[2,4,8]{2,1,0:T(4,128)S(1)}, f32[2,4,8]{2,1,0:T(4,128)S(1)}, u32[]{:S(2)}, u32[]{:S(2)}) collective-permute-start(f32[2,4,8]{2,1,0:T(4,128)S(1)} %constant_dynamic-update-slice_fusion.3), channel_id=1, source_target_pairs={{0,4},{4,0},{8,12},{12,8},{1,5},{5,1},{9,13},{13,9},{2,6},{6,2},{1... | collective-permute-start | bytes 776 | tf_op jit(solution)/shard_map/ppermute | solution.py:265
  19.9 4.5 %collective-permute-start.4 = (f32[2,4,8]{2,1,0:T(4,128)S(1)}, f32[2,4,8]{2,1,0:T(4,128)S(1)}, u32[]{:S(2)}, u32[]{:S(2)}) collective-permute-start(f32[2,4,8]{2,1,0:T(4,128)S(1)} %constant_dynamic-update-slice_fusion.3), channel_id=1, source_target_pairs={{0,8},{4,12},{8,0},{12,4},{1,9},{5,13},{9,1},{13,5},{2,10},{6,14},... | collective-permute-start | bytes 776 | tf_op jit(solution)/shard_map/ppermute | solution.py:265
  24.5 1.2 %collective-permute-start.6 = (f32[2,4,8]{2,1,0:T(4,128)S(1)}, f32[2,4,8]{2,1,0:T(4,128)S(1)}, u32[]{:S(2)}, u32[]{:S(2)}) collective-permute-start(f32[2,4,8]{2,1,0:T(4,128)S(1)} %pad_maximum_fusion.16), channel_id=1, source_target_pairs={{0,1},{1,0},{2,3},{3,2},{4,5},{5,4},{6,7},{7,6},{8,9},{9,8},{10,11... | collective-permute-start | bytes 776 | tf_op jit(solution)/shard_map/ppermute | solution.py:177
  25.8 3.7 %collective-permute-start.7 = (f32[2,4,8]{2,1,0:T(4,128)S(1)}, f32[2,4,8]{2,1,0:T(4,128)S(1)}, u32[]{:S(2)}, u32[]{:S(2)}) collective-permute-start(f32[2,4,8]{2,1,0:T(4,128)S(1)} %pad_maximum_fusion.17), channel_id=1, source_target_pairs={{0,2},{1,3},{2,0},{3,1},{4,6},{5,7},{6,4},{7,5},{8,10},{9,11},{10,... | collective-permute-start | bytes 776 | tf_op jit(solution)/shard_map/ppermute | solution.py:177
  29.6 1.4 %copy-start.1 = (bf16[24,16,2048]{2,1,0:T(8,128)(2,1)S(1)}, bf16[24,16,2048]{2,1,0:T(8,128)(2,1)}, u32[]{:S(2)}) copy-start(bf16[24,16,2048]{2,1,0:T(8,128)(2,1)} %copy-done) | copy-start | bytes 4718596

commit v17 on v15

--- a/solution.py
+++ b/solution.py
@@ -118,7 +118,7 @@
     return (high, middle, rest - middle)
 
 
-def pack_kernel(sizes_ref, scales_ref, bins_ref, images_ref, out_ref):
+def pack_kernel(sizes_ref, scales_ref, bins_ref, images_ref, out_ref, half_ref):
     slots, width = images_ref.shape
     row = lax.broadcasted_iota(jnp.int32, (slots, META), 0)
     column = lax.broadcasted_iota(jnp.int32, (slots, META), 1)
@@ -137,23 +137,41 @@
     high = gain.astype(jnp.bfloat16).astype(jnp.float32)
     rest = gain - high
     middle = rest.astype(jnp.bfloat16).astype(jnp.float32)
-    fields = (high, middle, rest - middle, live, bins)
+    parity = lax.axis_index("cls") % 2
+    fields = (high, middle, rest - middle, live, bins, jnp.full((slots, META), parity, jnp.float32))
     meta = jnp.zeros((slots, META), jnp.float32)
     for index, field in enumerate(fields):
         meta = jnp.where(column == index, field, meta)
     out_ref[:, :width] = images_ref[...]
     out_ref[:, width:] = meta.astype(out_ref.dtype)
+    cut = half_ref.shape[1]
+
+    @pl.when(parity == 0)
+    def _():
+        half_ref[...] = images_ref[:, :cut]
+
+    @pl.when(parity == 1)
+    def _():
+        half_ref[:, : width - cut] = images_ref[:, cut:]
+        half_ref[:, width - cut : width - cut + META] = meta.astype(half_ref.dtype)
+        half_ref[:, width - cut + META :] = jnp.zeros(
+            (slots, 2 * cut - width - META), half_ref.dtype
+        )
 
 
 def pack_rows(particles, group_counts, group_scale, defocus_bin):
     slots, width = particles.shape
     scalar = pl.BlockSpec(memory_space=pltpu.SMEM)
     whole = pl.BlockSpec(memory_space=pltpu.VMEM)
+    cut = 128 * -(-(width + META) // 256)
     return pl.pallas_call(
         pack_kernel,
-        out_shape=jax.ShapeDtypeStruct((slots, width + META), particles.dtype),
+        out_shape=(
+            jax.ShapeDtypeStruct((slots, width + META), particles.dtype),
+            jax.ShapeDtypeStruct((slots, cut), particles.dtype),
+        ),
         in_specs=[scalar, scalar, scalar, whole],
-        out_specs=whole,
+        out_specs=(whole, whole),
     )(group_counts, group_scale, defocus_bin, particles)
 
 
@@ -227,12 +245,19 @@
     classes_here = ref_tile.shape[0]
     shifts_count = cosine_table.shape[0]
 
-    small = n_blk <= 4 and n_blk & (n_blk - 1) == 0 and n_cls & (n_cls - 1) == 0
+    small = n_blk <= 4 and n_blk & (n_blk - 1) == 0 and n_cls >= 2 and n_cls & (n_cls - 1) == 0
     tables = (jnp.concatenate([ctf_table, own_norms], axis=1), ref_tile, cosine_table, sine_table)
     if small:
-        packed = pack_rows(particles, group_counts, group_scale, defocus_bin)
-        others = xor_gather(packed, "blk", n_blk)[batch_size:]
+        packed, half = pack_rows(particles, group_counts, group_scale, defocus_bin)
+        mine = xor_gather(half, "blk", n_blk)[batch_size:]
+        theirs = lax.ppermute(mine, "cls", [(i, i ^ 1) for i in range(n_cls)])
         own_rows = lax.optimization_barrier(packed.astype(jnp.float32))
+        first = own_rows[0, width + 5] < 0.5
+        cut = half.shape[1]
+        others = jnp.concatenate(
+            [jnp.where(first, mine, theirs), jnp.where(first, theirs, mine)[:, : width + META - cut]],
+            axis=1,
+        )
         groups = []
         for rows in (own_rows, others):
             meta = rows[:, width : width + 5].astype(jnp.float32)

time: 34.4 us -> 35.1 us (1.020)
  waiting for transfers between devices: 8.04 us -> 7 us
  between operations: 0.88 us -> 1.58 us
  local copies, waits for them, and re-layouts: 2.65 us -> 3.24 us
  starting transfers between devices: 11.6 us -> 12.1 us
    ppermute x3, waiting for transfers between devices: 2.28 us -> 1.54 us  [per_device(): lax.ppermute(stats, 'blk', [(i, i ^ k) for i in range(n_blk)])]
    slice x0 -> x2, local copies, waits for them, and re-layouts: none -> 0.59 us  [the longest x1 0.58 us: per_device(): first = own_rows[0, width + 5] < 0.5]
    ppermute x2, starting transfers between devices: 1.57 us -> 2.06 us  [xor_butterfly(): other = lax.ppermute(stats, axis, [(i, i ^ step) for i in range(size)])]
  transfers between devices with their start and end apart: 8 -> 9, of which waited for: 7 -> 5; matrix products, arithmetic and copies ran while one was open for 11% -> 13% of each run, Pallas kernels for 0% -> 0%
where the time goes in v17:
time: 35.1 us; the launch traced here: 34.8 us
  starting transfers between devices  12.1 us (34%)
  waiting for transfers between devices  7 us (20%)
  other arithmetic  5.1 us (15%)
  matrix products  4.21 us (12%)
  local copies, waits for them, and re-layouts  3.24 us (9%)
  Pallas kernels  1.58 us (5%)
  between operations  1.58 us (5%)
    ppermute x3, starting transfers between devices, xor_gather(): lax.ppermute(value, axis, [(i, i ^ k) for i in range(size)])  5.62 us
    ppermute x3, starting transfers between devices, per_device(): lax.ppermute(stats, 'blk', [(i, i ^ k) for i in range(n_blk)])  4.45 us
    ppermute x2, waiting for transfers between devices, xor_butterfly(): other = lax.ppermute(stats, axis, [(i, i ^ step) for i in range(size)])  2.93 us
    ppermute x3, waiting for transfers between devices, xor_gather(): lax.ppermute(value, axis, [(i, i ^ k) for i in range(size)])  2.52 us
    unnamed x17, local copies, waits for them, and re-layouts  2.11 us
    ppermute x2, starting transfers between devices, xor_butterfly(): other = lax.ppermute(stats, axis, [(i, i ^ step) for i in range(size)])  2.06 us
    pallas_call x1, Pallas kernels, pack_rows(): pl.pallas_call(pack_kernel, out_shape=(jax.ShapeDtypeStruct((slots, width...  1.58 us
    ppermute x3, waiting for transfers between devices, per_device(): lax.ppermute(stats, 'blk', [(i, i ^ k) for i in range(n_blk)])  1.54 us
  transfers between devices with their start and end apart: 9, of which 5 were waited for; matrix products, arithmetic and copies ran while one was open for 13% of the time, Pallas kernels for 0%

profile of v17, /device:TPU:0, one launch (start us, length us, event | category | flops | bytes accessed | tf_op | source)
XLA Modules:
  0.0 34.8 jit_solution(14325849680355474663)
XLA Ops:
  0.6 0.0 copy-start.2
  0.6 0.0 copy-start.3
  0.7 0.0 copy-start.4
  0.7 1.6 %shard_map.104 = (bf16[8,4224]{1,0:T(8,128)(2,1)}, bf16[8,2176]{1,0:T(8,128)(2,1)}) custom-call(s32[4]{0:T(128)} %sizes_ref.1, f32[4]{0:T(128)} %scales_ref.1, s32[8]{0:T(128)} %bins_ref.1, bf16[8,4096]{1,0:T(8,128)(2,1)} %images_ref.1), custom_call_target="tpu_custom_call" | custom-call | tf_op jit(solution)/shard_map/pallas_call | solution.py:167
  2.2 3.0 %collective-permute-start = (bf16[8,2176]{1,0:T(8,128)(2,1)}, bf16[8,2176]{1,0:T(8,128)(2,1)S(1)}, u32[]{:S(2)}, u32[]{:S(2)}) collective-permute-start(bf16[8,2176]{1,0:T(8,128)(2,1)} %get-tuple-element.7), channel_id=1, source_target_pairs={{0,4},{4,0},{8,12},{12,8},{1,5},{5,1},{9,13},{13,9},{2,6},{6,2},{1... | collective-permute-start | bytes 104456 | tf_op jit(solution)/shard_map/ppermute | solution.py:180
  5.3 2.6 %collective-permute-start.1 = (bf16[8,2176]{1,0:T(8,128)(2,1)}, bf16[8,2176]{1,0:T(8,128)(2,1)S(1)}, u32[]{:S(2)}, u32[]{:S(2)}) collective-permute-start(bf16[8,2176]{1,0:T(8,128)(2,1)} %get-tuple-element.7), channel_id=1, source_target_pairs={{0,8},{4,12},{8,0},{12,4},{1,9},{5,13},{9,1},{13,5},{2,10},{6,14},... | collective-permute-start | bytes 104456 | tf_op jit(solution)/shard_map/ppermute | solution.py:180
  7.9 0.0 collective-permute-start.2
  7.9 0.9 %convert_element_type.26 = f32[8,4224]{1,0:T(8,128)S(1)} convert(bf16[8,4224]{1,0:T(8,128)(2,1)} %get-tuple-element.6) | non-fusion elementwise | flops 33792 | bytes 202752 | tf_op jit(solution)/shard_map/convert_element_type | solution.py:254
  8.8 0.2 slice_reduce_fusion.3
  9.0 1.1 %bitcast_convert_fusion = f32[50,4096]{1,0:T(8,128)S(1)} fusion(bf16[1,50,4096]{2,1,0:T(8,128)(2,1)} %param.10), kind=kLoop, calls=%fused_computation.23 | loop fusion | flops 204800 | bytes 1228800 | tf_op jit(solution)/shard_map/convert_element_type | solution.py:65
  10.1 0.0 copy-done.4
  10.1 0.0 copy-start.5
  10.1 0.5 %fusion.8 = f32[16,50]{1,0:T(8,128)S(1)} fusion(f32[50,4096]{1,0:T(8,128)S(1)} %bitcast_convert_fusion, f32[16,2048]{1,0:T(8,128)S(1)} %copy-done.4), kind=kOutput, calls=%fused_computation.19 | convolution fusion | flops 20000768 | bytes 953472 | tf_op jit(solution)/shard_map/dot_general | solution.py:70
  10.6 0.2 fusion.17
  10.8 0.0 copy-done.2
  10.9 0.0 copy-done.3
  10.9 0.3 multiply_convert_fusion.3
  11.2 0.1 slice_multiply_fusion.4
  11.3 0.0 collective-permute-done
  11.3 0.0 collective-permute-done.1
  11.3 2.5 %collective-permute-done.2 = bf16[8,2176]{1,0:T(8,128)(2,1)S(1)} collective-permute-done((bf16[8,2176]{1,0:T(8,128)(2,1)}, bf16[8,2176]{1,0:T(8,128)(2,1)S(1)}, u32[]{:S(2)}, u32[]{:S(2)}) %collective-permute-start.2) | collective-permute-done | bytes 34848 | tf_op jit(solution)/shard_map/ppermute | solution.py:180
  13.8 0.0 collective-permute-start.3
  13.8 0.0 copy-done.5
  13.8 0.4 %fusion.6 = f32[8,16,50]{2,1,0:T(8,128)S(1)} fusion(bf16[8,16,2048]{2,1,0:T(8,128)(2,1)S(1)} %get-tuple-element.27, bf16[8,16,2048]{2,1,0:T(8,128)(2,1)S(1)} %get-tuple-element.26, bf16[1,50,4096]{2,1,0:T(8,128)(2,1)S(1)} %copy-done.5, f32[8,50]{1,0:T(8,128)S(1)} %slice_multiply_fusion.4, f32[8]{0:T(128)S(1)} %get-tuple-element.16), kind=kOutput, calls=%fused_computation.12 | convolution fusion | flops 54538752 | bytes 1485408 | tf_op jit(solution)/shard_map/dot_general | solution.py:75
  14.2 0.6 %slice.211 = f32[1,1]{1,0:T(1,128)} slice(f32[8,4224]{1,0:T(8,128)S(1)} %convert_element_type.26), slice={[0:1], [4101:4102]} | slice | bytes 8 | tf_op jit(solution)/shard_map/slice | solution.py:255
  15.5 0.0 collective-permute-done.3
  15.5 0.2 slice_reduce_fusion.1
  15.8 0.3 fusion.16
  16.1 0.1 slice_multiply_fusion.3
  16.2 1.1 %multiply_convert_fusion.1 = (bf16[24,16,2048]{2,1,0:T(8,128)(2,1)S(1)}, bf16[24,16,2048]{2,1,0:T(8,128)(2,1)S(1)}) fusion(f32[24,2048]{1,0:T(8,128)S(1)} %slice.219, f32[16,2048]{1,0:T(8,128)S(1)} %copy-done.2, f32[24,2048]{1,0:T(8,128)S(1)} %get-tuple-element.33, f32[16,2048]{1,0:T(8,128)S(1)} %copy-done.3, f32[24,2048]{1,0:T(8,128)S(1)} %get-tuple-element.32), kind=kLoop, calls=%fused_computation.7 | loop fusion | flops 7864320 | bytes 3997696 | tf_op jit(solution)/shard_map/convert
  17.3 0.0 copy-start
  17.3 0.0 copy-start.6
  17.3 1.0 %fusion.5 = f32[24,16,50]{2,1,0:T(8,128)S(1)} fusion(bf16[24,16,2048]{2,1,0:T(8,128)(2,1)S(1)} %get-tuple-element.25, bf16[24,16,2048]{2,1,0:T(8,128)(2,1)S(1)} %get-tuple-element.24, bf16[1,50,4096]{2,1,0:T(8,128)(2,1)S(1)} %copy-done.5, f32[24,50]{1,0:T(8,128)S(1)} %slice_multiply_fusion.3, f32[24]{0:T(128)S(1)} %get-tuple-element.18), kind=kOutput, calls=%fused_computation.10 | convolution fusion | flops 163616256 | bytes 3637024 | tf_op jit(solution)/shard_map/dot_general | solution.py:75
  18.3 0.2 copy-done
  18.5 0.1 reshape.144
  18.6 0.2 broadcast_reduce_fusion
  18.8 0.1 stack.32
  18.9 0.1 squeeze.13
  19.0 0.5 %collective-permute-start.4 = (f32[2,4,8]{2,1,0:T(4,128)S(1)}, f32[2,4,8]{2,1,0:T(4,128)S(1)}, u32[]{:S(2)}, u32[]{:S(2)}) collective-permute-start(f32[2,4,8]{2,1,0:T(4,128)S(1)} %pad_maximum_fusion.17), channel_id=1, source_target_pairs={{0,1},{1,0},{2,3},{3,2},{4,5},{5,4},{6,7},{7,6},{8,9},{9,8},{10,11... | collective-permute-start | bytes 776 | tf_op jit(solution)/shard_map/ppermute | solution.py:195
  19.5 0.8 %collective-permute-done.4 = f32[2,4,8]{2,1,0:T(4,128)S(1)} collective-permute-done((f32[2,4,8]{2,1,0:T(4,128)S(1)}, f32[2,4,8]{2,1,0:T(4,128)S(1)}, u32[]{:S(2)}, u32[]{:S(2)}) %collective-permute-start.4) | collective-permute-done | bytes 288 | tf_op jit(solution)/shard_map/ppermute | solution.py:195
  20.3 1.6 %collective-permute-start.5 = (f32[2,4,8]{2,1,0:T(4,128)S(1)}, f32[2,4,8]{2,1,0:T(4,128)S(1)}, u32[]{:S(2)}, u32[]{:S(2)}) collective-permute-start(f32[2,4,8]{2,1,0:T(4,128)S(1)} %pad_maximum_fusion.18), channel_id=1, source_target_pairs={{0,2},{1,3},{2,0},{3,1},{4,6},{5,7},{6,4},{7,5},{8,10},{9,11},{10,... | collective-permute-start | bytes 776 | tf_op jit(solution)/shard_map/ppermute | solution.py:195
  21.9 0.0 copy-done.6
  21.9 2.1 %collective-permute-done.5 = f32[2,4,8]{2,1,0:T(4,128)S(1)} collective-permute-done((f32[2,4,8]{2,1,0:T(4,128)S(1)}, f32[2,4,8]{2,1,0:T(4,128)S(1)}, u32[]{:S(2)}, u32[]{:S(2)}) %collective-permute-start.5) | collective-permute-done | bytes 288 | tf_op jit(solution)/shard_map/ppermute | solution.py:195
  24.0 1.4 %collective-permute-start.8 = (f32[2,4,8]{2,1,0:T(4,128)S(1)}, f32[2,4,8]{2,1,0:T(4,128)S(1)}, u32[]{:S(2)}, u32[]{:S(2)}) collective-permute-start(f32[2,4,8]{2,1,0:T(4,128)S(1)} %get-tuple-element.37), channel_id=1, source_target_pairs={{0,12},{4,8},{8,4},{12,0},{1,13},{5,9},{9,5},{13,1},{2,14},{6,10},... | collective-permute-start | bytes 776 | tf_op jit(solution)/shard_map/ppermute | solution.py:291
  25.5 0.1 fusion.39
  25.5 0.0 collective-permute-start.6
  25.6 3.0 %collective-permute-start.7 = (f32[2,4,8]{2,1,0:T(4,128)S(1)}, f32[2,4,8]{2,1,0:T(4,128)S(1)}, u32[]{:S(2)}, u32[]{:S(2)}) collective-permute-start(f32[2,4,8]{2,1,0:T(4,128)S(1)} %get-tuple-element.37), channel_id=1, source_target_pairs={{0,8},{4,12},{8,0},{12,4},{1,9},{5,13},{9,1},{13,5},{2,10},{6,14},... | collective-permute-start | bytes 776 | tf_op jit(solution)/shard_map/ppermute | solution.py:291
  28.6 0.9 %collective-permute-done.8 = f32[2,4,8]{2,1,0:T(4,128)S(1)} collective-permute-done((f32[2,4,8]{2,1,0:T(4,128)S(1)}, f32[2,4,8]{2,1,0:T(4,128)S(1)}, u32[]{:S(2)}, u32[]{:S(2)}) %collective-permute-start.8) | collective-permute-done | bytes 288 | tf_op jit(solution)/shard_map/ppermute | solution.py:291
  29.5 0.0 collective-permute-done.6
  29.5 0.6 %collective-permute-done.7 = f32[2,4,8]{2,1,0:T(4,128)S(1)} collective-permute-done((f32[2,4,8]{2,1,0:T(4,128)S(1)}, f32[2,4,8]{2,1,0:T(4,128)S(1)}, u32[]{:S(2)}, u32[]{:S(2)}) %collective-permute-start.7) | collective-permute-done | bytes 288 | tf_op jit(solution)/shard_map/ppermute | solution.py:291
  30.2 0.1 sub.72
  30.3 0.1 div.13
  30.4 0.5 %compare_select_fusion = f32[8]{0:T(128)} fusion(f32[8]{0:T(128)S(1)} %get-tuple-element.14, f32[4,8]{1,0:T(4,128)S(1)} %fusion.22, f32[4,8]{1,0:T(4,128)S(1)} %slice_reduce_fusion.2), kind=kLoop, calls=%fused_computation.81 | loop fusion | flops 24 | bytes 128 | tf_op jit(solution)/shard_map/jit(_where)/select_n | solution.py:310
  30.9 0.0 copy-start.1
  30.9 0.2 fusion.38
  31.1 0.4 %convolution_bitcast_fusion.1 = f32[50,4096]{1,0:T(8,128)S(1)} fusion(bf16[8,16,2048]{2,1,0:T(8,128)(2,1)S(1)} %get-tuple-element.27, bf16[8,16,2048]{2,1,0:T(8,128)(2,1)S(1)} %get-tuple-element.26, f32[32]{0:T(128)S(1)} %get-tuple-element.21, f32[32]{0:T(128)S(1)} %get-tuple-element.48, f32[32]{0:T(128)S(1)} %div.13, f32[32]{0:T(128)S(1)} %sub.72, ...), kind=kOutput, calls=%fused_computation.4 | convolution fusion | flops 54679552 | bytes 1970688 | tf_op jit(solution)/shard_map/dot_general | solution.py:212
  31.5 0.6 %fusion.12 = f32[50,2048]{1,0:T(8,128)S(1)} fusion(f32[24,2048]{1,0:T(8,128)S(1)} %slice.219, f32[8,2048]{1,0:T(8,128)S(1)} %slice.209, f32[32,50]{1,0:T(8,128)S(1)} %fusion.38, f32[32]{0:T(128)S(1)} %get-tuple-element.20), kind=kOutput, calls=%fused_computation.26 | convolution fusion | flops 39454272 | bytes 678272 | tf_op jit(solution)/shard_map/dot_general | solution.py:221
  32.2 0.2 copy-done.1
  32.3 0.8 %fusion.2 = f32[1,50,4096]{2,1,0:T(8,128)S(1)} fusion(f32[50,4096]{1,0:T(8,128)S(1)} %convolution_bitcast_fusion.1, bf16[24,16,2048]{2,1,0:T(8,128)(2,1)S(1)} %copy-done.1, bf16[24,16,2048]{2,1,0:T(8,128)(2,1)S(1)} %get-tuple-element.24, f32[50,2048]{1,0:T(8,128)S(1)} %fusion.12, f32[4096]{0:T(1024)S(1)} %pad_maximum_fusion.16, ...), kind=kOutput, calls=%fused_computation.3 | convolution fusion | flops 164550656 | bytes 5313024 | tf_op jit(solution)/shard_map/dot_general | solution.py:212
  33.1 1.7 %copy.16 = f32[1,50,4096]{2,0,1:T(1,128)} copy(f32[1,50,4096]{2,1,0:T(8,128)S(1)} %fusion.2) | data formatting | bytes 1638400
  (27 shorter events, 0.3 us)
Async XLA Ops:
  0.6 10.2 %copy-start.2 = (f32[16,2048]{1,0:T(8,128)S(1)}, f32[16,2048]{1,0:T(8,128)}, u32[]{:S(2)}) copy-start(f32[16,2048]{1,0:T(8,128)} %constant.20.clone) | copy-start | bytes 393220
  0.6 10.2 %copy-start.3 = (f32[16,2048]{1,0:T(8,128)S(1)}, f32[16,2048]{1,0:T(8,128)}, u32[]{:S(2)}) copy-start(f32[16,2048]{1,0:T(8,128)} %constant.7.clone) | copy-start | bytes 393220
  0.7 9.4 %copy-start.4 = (f32[16,2048]{1,0:T(8,128)S(1)}, f32[16,2048]{1,0:T(8,128)}, u32[]{:S(2)}) copy-start(f32[16,2048]{1,0:T(8,128)} %param.11) | copy-start | bytes 393220
  2.2 9.0 %collective-permute-start = (bf16[8,2176]{1,0:T(8,128)(2,1)}, bf16[8,2176]{1,0:T(8,128)(2,1)S(1)}, u32[]{:S(2)}, u32[]{:S(2)}) collective-permute-start(bf16[8,2176]{1,0:T(8,128)(2,1)} %get-tuple-element.7), channel_id=1, source_target_pairs={{0,4},{4,0},{8,12},{12,8},{1,5},{5,1},{9,13},{13,9},{2,6},{6,2},{1... | collective-permute-start | bytes 104456 | tf_op jit(solution)/shard_map/ppermute | solution.py:180
  5.3 6.0 %collective-permute-start.1 = (bf16[8,2176]{1,0:T(8,128)(2,1)}, bf16[8,2176]{1,0:T(8,128)(2,1)S(1)}, u32[]{:S(2)}, u32[]{:S(2)}) collective-permute-start(bf16[8,2176]{1,0:T(8,128)(2,1)} %get-tuple-element.7), channel_id=1, source_target_pairs={{0,8},{4,12},{8,0},{12,4},{1,9},{5,13},{9,1},{13,5},{2,10},{6,14},... | collective-permute-start | bytes 104456 | tf_op jit(solution)/shard_map/ppermute | solution.py:180
  7.9 5.9 %collective-permute-start.2 = (bf16[8,2176]{1,0:T(8,128)(2,1)}, bf16[8,2176]{1,0:T(8,128)(2,1)S(1)}, u32[]{:S(2)}, u32[]{:S(2)}) collective-permute-start(bf16[8,2176]{1,0:T(8,128)(2,1)} %get-tuple-element.7), channel_id=1, source_target_pairs={{0,12},{4,8},{8,4},{12,0},{1,13},{5,9},{9,5},{13,1},{2,14},{6,10},... | collective-permute-start | bytes 104456 | tf_op jit(solution)/shard_map/ppermute | solution.py:180
  10.1 3.7 %copy-start.5 = (bf16[1,50,4096]{2,1,0:T(8,128)(2,1)S(1)}, bf16[1,50,4096]{2,1,0:T(8,128)(2,1)}, u32[]{:S(2)}) copy-start(bf16[1,50,4096]{2,1,0:T(8,128)(2,1)} %param.10) | copy-start | bytes 1228804
  13.8 1.7 %collective-permute-start.3 = (bf16[24,2176]{1,0:T(8,128)(2,1)S(1)}, bf16[24,2176]{1,0:T(8,128)(2,1)S(1)}, u32[]{:S(2)}, u32[]{:S(2)}) collective-permute-start(bf16[24,2176]{1,0:T(8,128)(2,1)S(1)} %constant_dynamic-update-slice_fusion), channel_id=1, source_target_pairs={{0,1},{1,0},{2,3},{3,2},{4,5},{5,4},{6,7},{7,6},{8,9},{9,8},{10,11... | collective-permute-start | bytes 313352 | tf_op jit(solution)/shard_map/ppermute | solution.py:253
  17.3 1.2 %copy-start = (bf16[24,16,2048]{2,1,0:T(8,128)(2,1)}, bf16[24,16,2048]{2,1,0:T(8,128)(2,1)S(1)}, u32[]{:S(2)}) copy-start(bf16[24,16,2048]{2,1,0:T(8,128)(2,1)S(1)} %get-tuple-element.25) | copy-start | bytes 4718596
  17.3 4.6 %copy-start.6 = (f32[2048]{0:T(1024)S(1)}, f32[2048]{0:T(1024)}, u32[]{:S(2)}) copy-start(f32[2048]{0:T(1024)} %param.12) | copy-start | bytes 24580
  19.0 1.3 %collective-permute-start.4 = (f32[2,4,8]{2,1,0:T(4,128)S(1)}, f32[2,4,8]{2,1,0:T(4,128)S(1)}, u32[]{:S(2)}, u32[]{:S(2)}) collective-permute-start(f32[2,4,8]{2,1,0:T(4,128)S(1)} %pad_maximum_fusion.17), channel_id=1, source_target_pairs={{0,1},{1,0},{2,3},{3,2},{4,5},{5,4},{6,7},{7,6},{8,9},{9,8},{10,11... | collective-permute-start | bytes 776 | tf_op jit(solution)/shard_map/ppermute | solution.py:195
  20.3 3.7 %collective-permute-start.5 = (f32[2,4,8]{2,1,0:T(4,128)S(1)}, f32[2,4,8]{2,1,0:T(4,128)S(1)}, u32[]{:S(2)}, u32[]{:S(2)}) collective-permute-start(f32[2,4,8]{2,1,0:T(4,128)S(1)} %pad_maximum_fusion.18), channel_id=1, source_target_pairs={{0,2},{1,3},{2,0},{3,1},{4,6},{5,7},{6,4},{7,5},{8,10},{9,11},{10,... | collective-permute-start | bytes 776 | tf_op jit(solution)/shard_map/ppermute | solution.py:195
  24.0 5.5 %collective-permute-start.8 = (f32[2,4,8]{2,1,0:T(4,128)S(1)}, f32[2,4,8]{2,1,0:T(4,128)S(1)}, u32[]{:S(2)}, u32[]{:S(2)}) collective-permute-start(f32[2,4,8]{2,1,0:T(4,128)S(1)} %get-tuple-element.37), channel_id=1, source_target_pairs={{0,12},{4,8},{8,4},{12,0},{1,13},{5,9},{9,5},{13,1},{2,14},{6,10},... | collective-permute-start | bytes 776 | tf_op jit(solution)/shard_map/ppermute | solution.py:291
  25.5 4.0 %collective-permute-start.6 = (f32[2,4,8]{2,1,0:T(4,128)S(1)}, f32[2,4,8]{2,1,0:T(4,128)S(1)}, u32[]{:S(2)}, u32[]{:S(2)}) collective-permute-start(f32[2,4,8]{2,1,0:T(4,128)S(1)} %get-tuple-element.37), channel_id=1, source_target_pairs={{0,4},{4,0},{8,12},{12,8},{1,5},{5,1},{9,13},{13,9},{2,6},{6,2},{1... | collective-permute-start | bytes 776 | tf_op jit(solution)/shard_map/ppermute | solution.py:291
  25.6 4.6 %collective-permute-start.7 = (f32[2,4,8]{2,1,0:T(4,128)S(1)}, f32[2,4,8]{2,1,0:T(4,128)S(1)}, u32[]{:S(2)}, u32[]{:S(2)}) collective-permute-start(f32[2,4,8]{2,1,0:T(4,128)S(1)} %get-tuple-element.37), channel_id=1, source_target_pairs={{0,8},{4,12},{8,0},{12,4},{1,9},{5,13},{9,1},{13,5},{2,10},{6,14},... | collective-permute-start | bytes 776 | tf_op jit(solution)/shard_map/ppermute | solution.py:291
  30.9 1.4 %copy-start.1 = (bf16[24,16,2048]{2,1,0:T(8,128)(2,1)S(1)}, bf16[24,16,2048]{2,1,0:T(8,128)(2,1)}, u32[]{:S(2)}) copy-start(bf16[24,16,2048]{2,1,0:T(8,128)(2,1)} %copy-done) | copy-start | bytes 4718596

commit v18 on v15

--- a/solution.py
+++ b/solution.py
@@ -282,7 +282,7 @@
     numerator, denominator = accumulate(
         pieces, all_scores, gain_all, ctf_rows, live_all, peak_all, totals_all
     )
-    log_evidence = jnp.where(live_mask > 0.5, peak_score + jnp.log(totals), 0.0)
+    log_evidence = jnp.where(live_all > 0.5, peak_all + jnp.log(totals_all), 0.0)[:batch_size]
     denominator = (
         jnp.concatenate([denominator, denominator], axis=1)
         + jnp.concatenate([spectral_reg, spectral_reg])[None, :]

time: 34.4 us -> 34.8 us (1.012)
  waiting for transfers between devices: 8.04 us -> 9.29 us
  starting transfers between devices: 11.6 us -> 10.7 us
    ppermute x3, waiting for transfers between devices: 2.28 us -> 3.53 us  [per_device(): lax.ppermute(stats, 'blk', [(i, i ^ k) for i in range(n_blk)])]
    ppermute x3, starting transfers between devices: 4.45 us -> 3.55 us  [per_device(): lax.ppermute(stats, 'blk', [(i, i ^ k) for i in range(n_blk)])]
  transfers between devices with their start and end apart: 8 -> 8, of which waited for: 7 -> 6; matrix products, arithmetic and copies ran while one was open for 11% -> 11% of each run, Pallas kernels for 0% -> 0%
where the time goes in v18:
time: 34.8 us; the launch traced here: 34.5 us
  starting transfers between devices  10.7 us (31%)
  waiting for transfers between devices  9.29 us (27%)
  other arithmetic  5.15 us (15%)
  matrix products  4.21 us (12%)
  local copies, waits for them, and re-layouts  2.65 us (8%)
  Pallas kernels  1.57 us (5%)
  between operations  0.89 us (3%)
    ppermute x3, starting transfers between devices, xor_gather(): lax.ppermute(value, axis, [(i, i ^ k) for i in range(size)])  5.62 us
    ppermute x3, starting transfers between devices, per_device(): lax.ppermute(stats, 'blk', [(i, i ^ k) for i in range(n_blk)])  3.55 us
    ppermute x3, waiting for transfers between devices, per_device(): lax.ppermute(stats, 'blk', [(i, i ^ k) for i in range(n_blk)])  3.53 us
    ppermute x2, waiting for transfers between devices, xor_butterfly(): other = lax.ppermute(stats, axis, [(i, i ^ step) for i in range(size)])  3.27 us
    ppermute x3, waiting for transfers between devices, xor_gather(): lax.ppermute(value, axis, [(i, i ^ k) for i in range(size)])  2.5 us
    unnamed x17, local copies, waits for them, and re-layouts  2.11 us
    ppermute x2, starting transfers between devices, xor_butterfly(): other = lax.ppermute(stats, axis, [(i, i ^ step) for i in range(size)])  1.57 us
    pallas_call x1, Pallas kernels, pack_rows(): pl.pallas_call(pack_kernel, out_shape=jax.ShapeDtypeStruct((slots, width...  1.57 us
  transfers between devices with their start and end apart: 8, of which 6 were waited for; matrix products, arithmetic and copies ran while one was open for 11% of the time, Pallas kernels for 0%

profile of v18, /device:TPU:0, one launch (start us, length us, event | category | flops | bytes accessed | tf_op | source)
XLA Modules:
  0.0 34.5 jit_solution(3801181488392930904)
XLA Ops:
  0.6 0.0 copy-start.2
  0.6 0.0 copy-start.3
  0.7 0.0 copy-start.4
  0.7 1.6 %shard_map.104 = bf16[8,4224]{1,0:T(8,128)(2,1)} custom-call(s32[4]{0:T(128)} %sizes_ref.1, f32[4]{0:T(128)} %scales_ref.1, s32[8]{0:T(128)} %bins_ref.1, bf16[8,4096]{1,0:T(8,128)(2,1)} %images_ref.1), custom_call_target="tpu_custom_call" | custom-call | tf_op jit(solution)/shard_map/pallas_call | solution.py:152
  2.2 3.0 %collective-permute-start = (bf16[8,4224]{1,0:T(8,128)(2,1)}, bf16[8,4224]{1,0:T(8,128)(2,1)S(1)}, u32[]{:S(2)}, u32[]{:S(2)}) collective-permute-start(bf16[8,4224]{1,0:T(8,128)(2,1)} %shard_map.104), channel_id=1, source_target_pairs={{0,4},{4,0},{8,12},{12,8},{1,5},{5,1},{9,13},{13,9},{2,6},{6,2},{1... | collective-permute-start | bytes 202760 | tf_op jit(solution)/shard_map/ppermute | solution.py:162
  5.3 2.6 %collective-permute-start.1 = (bf16[8,4224]{1,0:T(8,128)(2,1)}, bf16[8,4224]{1,0:T(8,128)(2,1)S(1)}, u32[]{:S(2)}, u32[]{:S(2)}) collective-permute-start(bf16[8,4224]{1,0:T(8,128)(2,1)} %shard_map.104), channel_id=1, source_target_pairs={{0,8},{4,12},{8,0},{12,4},{1,9},{5,13},{9,1},{13,5},{2,10},{6,14},... | collective-permute-start | bytes 202760 | tf_op jit(solution)/shard_map/ppermute | solution.py:162
  7.8 0.0 collective-permute-start.2
  7.8 1.0 %convert_element_type.26 = f32[8,4224]{1,0:T(8,128)S(1)} convert(bf16[8,4224]{1,0:T(8,128)(2,1)} %shard_map.104) | non-fusion elementwise | flops 33792 | bytes 202752 | tf_op jit(solution)/shard_map/convert_element_type | solution.py:235
  8.8 0.2 slice_reduce_fusion.3
  9.0 1.1 %bitcast_convert_fusion = f32[50,4096]{1,0:T(8,128)S(1)} fusion(bf16[1,50,4096]{2,1,0:T(8,128)(2,1)} %param.10), kind=kLoop, calls=%fused_computation.23 | loop fusion | flops 204800 | bytes 1228800 | tf_op jit(solution)/shard_map/convert_element_type | solution.py:65
  10.1 0.0 copy-done.4
  10.1 0.0 copy-start.5
  10.2 0.5 %fusion.8 = f32[16,50]{1,0:T(8,128)S(1)} fusion(f32[50,4096]{1,0:T(8,128)S(1)} %bitcast_convert_fusion, f32[16,2048]{1,0:T(8,128)S(1)} %copy-done.4), kind=kOutput, calls=%fused_computation.19 | convolution fusion | flops 20000768 | bytes 953472 | tf_op jit(solution)/shard_map/dot_general | solution.py:70
  10.6 0.2 fusion.17
  10.9 0.1 slice_multiply_fusion.4
  11.0 0.0 copy-done.2
  11.0 0.0 copy-done.3
  11.0 0.3 multiply_convert_fusion.3
  11.3 0.0 copy-done.5
  11.3 0.4 %fusion.6 = f32[8,16,50]{2,1,0:T(8,128)S(1)} fusion(bf16[8,16,2048]{2,1,0:T(8,128)(2,1)S(1)} %get-tuple-element.25, bf16[8,16,2048]{2,1,0:T(8,128)(2,1)S(1)} %get-tuple-element.24, bf16[1,50,4096]{2,1,0:T(8,128)(2,1)S(1)} %copy-done.5, f32[8,50]{1,0:T(8,128)S(1)} %slice_multiply_fusion.4, f32[8]{0:T(128)S(1)} %get-tuple-element.11), kind=kOutput, calls=%fused_computation.12 | convolution fusion | flops 54538752 | bytes 1485408 | tf_op jit(solution)/shard_map/dot_general | solution.py:75
  11.7 0.0 collective-permute-done
  11.7 1.1 %collective-permute-done.1 = bf16[8,4224]{1,0:T(8,128)(2,1)S(1)} collective-permute-done((bf16[8,4224]{1,0:T(8,128)(2,1)}, bf16[8,4224]{1,0:T(8,128)(2,1)S(1)}, u32[]{:S(2)}, u32[]{:S(2)}) %collective-permute-start.1) | collective-permute-done | bytes 67616 | tf_op jit(solution)/shard_map/ppermute | solution.py:162
  12.9 1.4 %collective-permute-done.2 = bf16[8,4224]{1,0:T(8,128)(2,1)S(1)} collective-permute-done((bf16[8,4224]{1,0:T(8,128)(2,1)}, bf16[8,4224]{1,0:T(8,128)(2,1)S(1)}, u32[]{:S(2)}, u32[]{:S(2)}) %collective-permute-start.2) | collective-permute-done | bytes 67616 | tf_op jit(solution)/shard_map/ppermute | solution.py:162
  14.3 0.2 slice_reduce_fusion.1
  14.5 0.3 fusion.16
  14.9 0.1 slice_multiply_fusion.3
  14.9 1.1 %multiply_convert_fusion.1 = (bf16[24,16,2048]{2,1,0:T(8,128)(2,1)S(1)}, bf16[24,16,2048]{2,1,0:T(8,128)(2,1)S(1)}) fusion(f32[24,2048]{1,0:T(8,128)S(1)} %slice.202, f32[16,2048]{1,0:T(8,128)S(1)} %copy-done.2, f32[24,2048]{1,0:T(8,128)S(1)} %get-tuple-element.27, f32[16,2048]{1,0:T(8,128)S(1)} %copy-done.3, f32[24,2048]{1,0:T(8,128)S(1)} %get-tuple-element.26), kind=kLoop, calls=%fused_computation.7 | loop fusion | flops 7864320 | bytes 3997696 | tf_op jit(solution)/shard_map/convert
  16.0 0.0 copy-start
  16.0 0.0 copy-start.6
  16.0 1.0 %fusion.5 = f32[24,16,50]{2,1,0:T(8,128)S(1)} fusion(bf16[24,16,2048]{2,1,0:T(8,128)(2,1)S(1)} %get-tuple-element.23, bf16[24,16,2048]{2,1,0:T(8,128)(2,1)S(1)} %get-tuple-element.22, bf16[1,50,4096]{2,1,0:T(8,128)(2,1)S(1)} %copy-done.5, f32[24,50]{1,0:T(8,128)S(1)} %slice_multiply_fusion.3, f32[24]{0:T(128)S(1)} %get-tuple-element.14), kind=kOutput, calls=%fused_computation.10 | convolution fusion | flops 163616256 | bytes 3637024 | tf_op jit(solution)/shard_map/dot_general | solution.py:75
  17.0 0.2 copy-done
  17.2 0.1 reshape.138
  17.4 0.2 broadcast_reduce_fusion
  17.5 0.1 stack.32
  17.6 0.1 squeeze.13
  17.7 0.0 collective-permute-start.3
  17.7 1.2 %collective-permute-done.3 = f32[2,4,8]{2,1,0:T(4,128)S(1)} collective-permute-done((f32[2,4,8]{2,1,0:T(4,128)S(1)}, f32[2,4,8]{2,1,0:T(4,128)S(1)}, u32[]{:S(2)}, u32[]{:S(2)}) %collective-permute-start.3) | collective-permute-done | bytes 288 | tf_op jit(solution)/shard_map/ppermute | solution.py:177
  18.9 1.6 %collective-permute-start.4 = (f32[2,4,8]{2,1,0:T(4,128)S(1)}, f32[2,4,8]{2,1,0:T(4,128)S(1)}, u32[]{:S(2)}, u32[]{:S(2)}) collective-permute-start(f32[2,4,8]{2,1,0:T(4,128)S(1)} %pad_maximum_fusion.17), channel_id=1, source_target_pairs={{0,2},{1,3},{2,0},{3,1},{4,6},{5,7},{6,4},{7,5},{8,10},{9,11},{10,... | collective-permute-start | bytes 776 | tf_op jit(solution)/shard_map/ppermute | solution.py:177
  20.5 2.1 %collective-permute-done.4 = f32[2,4,8]{2,1,0:T(4,128)S(1)} collective-permute-done((f32[2,4,8]{2,1,0:T(4,128)S(1)}, f32[2,4,8]{2,1,0:T(4,128)S(1)}, u32[]{:S(2)}, u32[]{:S(2)}) %collective-permute-start.4) | collective-permute-done | bytes 288 | tf_op jit(solution)/shard_map/ppermute | solution.py:177
  22.6 1.7 %collective-permute-start.6 = (f32[2,4,8]{2,1,0:T(4,128)S(1)}, f32[2,4,8]{2,1,0:T(4,128)S(1)}, u32[]{:S(2)}, u32[]{:S(2)}) collective-permute-start(f32[2,4,8]{2,1,0:T(4,128)S(1)} %get-tuple-element.33), channel_id=1, source_target_pairs={{0,8},{4,12},{8,0},{12,4},{1,9},{5,13},{9,1},{13,5},{2,10},{6,14},... | collective-permute-start | bytes 776 | tf_op jit(solution)/shard_map/ppermute | solution.py:266
  24.3 0.0 copy-done.6
  24.3 1.4 %collective-permute-start.7 = (f32[2,4,8]{2,1,0:T(4,128)S(1)}, f32[2,4,8]{2,1,0:T(4,128)S(1)}, u32[]{:S(2)}, u32[]{:S(2)}) collective-permute-start(f32[2,4,8]{2,1,0:T(4,128)S(1)} %get-tuple-element.33), channel_id=1, source_target_pairs={{0,12},{4,8},{8,4},{12,0},{1,13},{5,9},{9,5},{13,1},{2,14},{6,10},... | collective-permute-start | bytes 776 | tf_op jit(solution)/shard_map/ppermute | solution.py:266
  25.6 0.5 %collective-permute-start.5 = (f32[2,4,8]{2,1,0:T(4,128)S(1)}, f32[2,4,8]{2,1,0:T(4,128)S(1)}, u32[]{:S(2)}, u32[]{:S(2)}) collective-permute-start(f32[2,4,8]{2,1,0:T(4,128)S(1)} %get-tuple-element.33), channel_id=1, source_target_pairs={{0,4},{4,0},{8,12},{12,8},{1,5},{5,1},{9,13},{13,9},{2,6},{6,2},{1... | collective-permute-start | bytes 776 | tf_op jit(solution)/shard_map/ppermute | solution.py:266
  26.1 1.0 %collective-permute-done.6 = f32[2,4,8]{2,1,0:T(4,128)S(1)} collective-permute-done((f32[2,4,8]{2,1,0:T(4,128)S(1)}, f32[2,4,8]{2,1,0:T(4,128)S(1)}, u32[]{:S(2)}, u32[]{:S(2)}) %collective-permute-start.6) | collective-permute-done | bytes 288 | tf_op jit(solution)/shard_map/ppermute | solution.py:266
  27.2 2.5 %collective-permute-done.7 = f32[2,4,8]{2,1,0:T(4,128)S(1)} collective-permute-done((f32[2,4,8]{2,1,0:T(4,128)S(1)}, f32[2,4,8]{2,1,0:T(4,128)S(1)}, u32[]{:S(2)}, u32[]{:S(2)}) %collective-permute-start.7) | collective-permute-done | bytes 288 | tf_op jit(solution)/shard_map/ppermute | solution.py:266
  29.7 0.0 collective-permute-done.5
  29.8 0.1 sub.72
  29.9 0.1 div.13
  30.0 0.6 %compare_select_fusion = (f32[32]{0:T(128)}, f32[32]{0:T(128)S(1)}, f32[32]{0:T(128)S(1)}, f32[32]{0:T(128)S(1)}) fusion(f32[32]{0:T(128)S(1)} %sub.72, f32[32]{0:T(128)S(1)} %div.13, f32[24]{0:T(128)S(1)} %get-tuple-element.15, f32[8]{0:T(128)S(1)} %get-tuple-element.10, f32[24]{0:T(128)S(1)} %get-tuple-element.14, f32[8]{0:T(128)S(1)} %get-tuple-element.11), kind=kLoop, calls=%fused_computation.78 | loop fusion | flops 192 | bytes 1024 | tf_op jit(solution)/shard_map/jit(_where)/select_n | solution.py:285
  30.6 0.0 copy-start.1
  30.6 0.2 fusion.37
  30.8 0.4 %convolution_bitcast_fusion.1 = f32[50,4096]{1,0:T(8,128)S(1)} fusion(bf16[8,16,2048]{2,1,0:T(8,128)(2,1)S(1)} %get-tuple-element.25, bf16[8,16,2048]{2,1,0:T(8,128)(2,1)S(1)} %get-tuple-element.24, f32[32]{0:T(128)S(1)} %get-tuple-element.45, f32[32]{0:T(128)S(1)} %get-tuple-element.17, f32[32]{0:T(128)S(1)} %div.13, f32[32]{0:T(128)S(1)} %sub.72, ...), kind=kOutput, calls=%fused_computation.4 | convolution fusion | flops 54679552 | bytes 1970688 | tf_op jit(solution)/shard_map/dot_general | solution.py:194
  31.2 0.6 %fusion.12 = f32[50,2048]{1,0:T(8,128)S(1)} fusion(f32[24,2048]{1,0:T(8,128)S(1)} %slice.202, f32[8,2048]{1,0:T(8,128)S(1)} %slice.193, f32[32,50]{1,0:T(8,128)S(1)} %fusion.37, f32[32]{0:T(128)S(1)} %get-tuple-element.44), kind=kOutput, calls=%fused_computation.26 | convolution fusion | flops 39454272 | bytes 678272 | tf_op jit(solution)/shard_map/dot_general | solution.py:203
  31.8 0.2 copy-done.1
  32.0 0.8 %fusion.2 = f32[1,50,4096]{2,1,0:T(8,128)S(1)} fusion(f32[50,4096]{1,0:T(8,128)S(1)} %convolution_bitcast_fusion.1, bf16[24,16,2048]{2,1,0:T(8,128)(2,1)S(1)} %copy-done.1, bf16[24,16,2048]{2,1,0:T(8,128)(2,1)S(1)} %get-tuple-element.22, f32[50,2048]{1,0:T(8,128)S(1)} %fusion.12, f32[4096]{0:T(1024)S(1)} %pad_maximum_fusion.15, ...), kind=kOutput, calls=%fused_computation.3 | convolution fusion | flops 164550656 | bytes 5313024 | tf_op jit(solution)/shard_map/dot_general | solution.py:194
  32.8 1.7 %copy.16 = f32[1,50,4096]{2,0,1:T(1,128)} copy(f32[1,50,4096]{2,1,0:T(8,128)S(1)} %fusion.2) | data formatting | bytes 1638400
  (26 shorter events, 0.3 us)
Async XLA Ops:
  0.6 10.3 %copy-start.2 = (f32[16,2048]{1,0:T(8,128)S(1)}, f32[16,2048]{1,0:T(8,128)}, u32[]{:S(2)}) copy-start(f32[16,2048]{1,0:T(8,128)} %constant.6.clone) | copy-start | bytes 393220
  0.6 10.3 %copy-start.3 = (f32[16,2048]{1,0:T(8,128)S(1)}, f32[16,2048]{1,0:T(8,128)}, u32[]{:S(2)}) copy-start(f32[16,2048]{1,0:T(8,128)} %constant.5.clone) | copy-start | bytes 393220
  0.7 9.5 %copy-start.4 = (f32[16,2048]{1,0:T(8,128)S(1)}, f32[16,2048]{1,0:T(8,128)}, u32[]{:S(2)}) copy-start(f32[16,2048]{1,0:T(8,128)} %param.11) | copy-start | bytes 393220
  2.2 9.5 %collective-permute-start = (bf16[8,4224]{1,0:T(8,128)(2,1)}, bf16[8,4224]{1,0:T(8,128)(2,1)S(1)}, u32[]{:S(2)}, u32[]{:S(2)}) collective-permute-start(bf16[8,4224]{1,0:T(8,128)(2,1)} %shard_map.104), channel_id=1, source_target_pairs={{0,4},{4,0},{8,12},{12,8},{1,5},{5,1},{9,13},{13,9},{2,6},{6,2},{1... | collective-permute-start | bytes 202760 | tf_op jit(solution)/shard_map/ppermute | solution.py:162
  5.3 7.6 %collective-permute-start.1 = (bf16[8,4224]{1,0:T(8,128)(2,1)}, bf16[8,4224]{1,0:T(8,128)(2,1)S(1)}, u32[]{:S(2)}, u32[]{:S(2)}) collective-permute-start(bf16[8,4224]{1,0:T(8,128)(2,1)} %shard_map.104), channel_id=1, source_target_pairs={{0,8},{4,12},{8,0},{12,4},{1,9},{5,13},{9,1},{13,5},{2,10},{6,14},... | collective-permute-start | bytes 202760 | tf_op jit(solution)/shard_map/ppermute | solution.py:162
  7.8 6.4 %collective-permute-start.2 = (bf16[8,4224]{1,0:T(8,128)(2,1)}, bf16[8,4224]{1,0:T(8,128)(2,1)S(1)}, u32[]{:S(2)}, u32[]{:S(2)}) collective-permute-start(bf16[8,4224]{1,0:T(8,128)(2,1)} %shard_map.104), channel_id=1, source_target_pairs={{0,12},{4,8},{8,4},{12,0},{1,13},{5,9},{9,5},{13,1},{2,14},{6,10},... | collective-permute-start | bytes 202760 | tf_op jit(solution)/shard_map/ppermute | solution.py:162
  10.1 1.1 %copy-start.5 = (bf16[1,50,4096]{2,1,0:T(8,128)(2,1)S(1)}, bf16[1,50,4096]{2,1,0:T(8,128)(2,1)}, u32[]{:S(2)}) copy-start(bf16[1,50,4096]{2,1,0:T(8,128)(2,1)} %param.10) | copy-start | bytes 1228804
  16.0 1.2 %copy-start = (bf16[24,16,2048]{2,1,0:T(8,128)(2,1)}, bf16[24,16,2048]{2,1,0:T(8,128)(2,1)S(1)}, u32[]{:S(2)}) copy-start(bf16[24,16,2048]{2,1,0:T(8,128)(2,1)S(1)} %get-tuple-element.23) | copy-start | bytes 4718596
  16.0 8.2 %copy-start.6 = (f32[2048]{0:T(1024)S(1)}, f32[2048]{0:T(1024)}, u32[]{:S(2)}) copy-start(f32[2048]{0:T(1024)} %param.12) | copy-start | bytes 24580
  17.7 1.2 %collective-permute-start.3 = (f32[2,4,8]{2,1,0:T(4,128)S(1)}, f32[2,4,8]{2,1,0:T(4,128)S(1)}, u32[]{:S(2)}, u32[]{:S(2)}) collective-permute-start(f32[2,4,8]{2,1,0:T(4,128)S(1)} %pad_maximum_fusion.16), channel_id=1, source_target_pairs={{0,1},{1,0},{2,3},{3,2},{4,5},{5,4},{6,7},{7,6},{8,9},{9,8},{10,11... | collective-permute-start | bytes 776 | tf_op jit(solution)/shard_map/ppermute | solution.py:177
  18.9 3.7 %collective-permute-start.4 = (f32[2,4,8]{2,1,0:T(4,128)S(1)}, f32[2,4,8]{2,1,0:T(4,128)S(1)}, u32[]{:S(2)}, u32[]{:S(2)}) collective-permute-start(f32[2,4,8]{2,1,0:T(4,128)S(1)} %pad_maximum_fusion.17), channel_id=1, source_target_pairs={{0,2},{1,3},{2,0},{3,1},{4,6},{5,7},{6,4},{7,5},{8,10},{9,11},{10,... | collective-permute-start | bytes 776 | tf_op jit(solution)/shard_map/ppermute | solution.py:177
  22.6 4.6 %collective-permute-start.6 = (f32[2,4,8]{2,1,0:T(4,128)S(1)}, f32[2,4,8]{2,1,0:T(4,128)S(1)}, u32[]{:S(2)}, u32[]{:S(2)}) collective-permute-start(f32[2,4,8]{2,1,0:T(4,128)S(1)} %get-tuple-element.33), channel_id=1, source_target_pairs={{0,8},{4,12},{8,0},{12,4},{1,9},{5,13},{9,1},{13,5},{2,10},{6,14},... | collective-permute-start | bytes 776 | tf_op jit(solution)/shard_map/ppermute | solution.py:266
  24.3 5.4 %collective-permute-start.7 = (f32[2,4,8]{2,1,0:T(4,128)S(1)}, f32[2,4,8]{2,1,0:T(4,128)S(1)}, u32[]{:S(2)}, u32[]{:S(2)}) collective-permute-start(f32[2,4,8]{2,1,0:T(4,128)S(1)} %get-tuple-element.33), channel_id=1, source_target_pairs={{0,12},{4,8},{8,4},{12,0},{1,13},{5,9},{9,5},{13,1},{2,14},{6,10},... | collective-permute-start | bytes 776 | tf_op jit(solution)/shard_map/ppermute | solution.py:266
  25.6 4.1 %collective-permute-start.5 = (f32[2,4,8]{2,1,0:T(4,128)S(1)}, f32[2,4,8]{2,1,0:T(4,128)S(1)}, u32[]{:S(2)}, u32[]{:S(2)}) collective-permute-start(f32[2,4,8]{2,1,0:T(4,128)S(1)} %get-tuple-element.33), channel_id=1, source_target_pairs={{0,4},{4,0},{8,12},{12,8},{1,5},{5,1},{9,13},{13,9},{2,6},{6,2},{1... | collective-permute-start | bytes 776 | tf_op jit(solution)/shard_map/ppermute | solution.py:266
  30.6 1.4 %copy-start.1 = (bf16[24,16,2048]{2,1,0:T(8,128)(2,1)S(1)}, bf16[24,16,2048]{2,1,0:T(8,128)(2,1)}, u32[]{:S(2)}) copy-start(bf16[24,16,2048]{2,1,0:T(8,128)(2,1)} %copy-done) | copy-start | bytes 4718596

commit v19 on v15

--- a/solution.py
+++ b/solution.py
@@ -51,11 +51,10 @@
 
 def shifted_rows(images, ctf_rows, cosine_table, sine_table):
     half_width = ctf_rows.shape[1]
-    real_part = images[:, :half_width].astype(jnp.float32)[:, None, :]
-    imag_part = images[:, half_width:].astype(jnp.float32)[:, None, :]
-    ctf_wide = ctf_rows[:, None, :]
-    new_real = (real_part * cosine_table + imag_part * sine_table) * ctf_wide
-    new_imag = (imag_part * cosine_table - real_part * sine_table) * ctf_wide
+    real_part = (images[:, :half_width].astype(jnp.float32) * ctf_rows)[:, None, :]
+    imag_part = (images[:, half_width:].astype(jnp.float32) * ctf_rows)[:, None, :]
+    new_real = real_part * cosine_table + imag_part * sine_table
+    new_imag = imag_part * cosine_table - real_part * sine_table
     joined = jnp.concatenate([new_real, new_imag], axis=2).astype(jnp.bfloat16)
     return joined.reshape(images.shape[0] * cosine_table.shape[0], 2 * half_width)
 

time: 34.4 us -> 34.3 us (level)
    unnamed x17 -> x19, local copies, waits for them, and re-layouts: 2.11 us -> 2.11 us
where the time goes in v19:
time: 34.3 us; the launch traced here: 34.1 us
  starting transfers between devices  11.6 us (34%)
  waiting for transfers between devices  8.11 us (24%)
  other arithmetic  5.06 us (15%)
  matrix products  4.21 us (12%)
  local copies, waits for them, and re-layouts  2.62 us (8%)
  Pallas kernels  1.57 us (5%)
  between operations  0.87 us (3%)
    ppermute x3, starting transfers between devices, xor_gather(): lax.ppermute(value, axis, [(i, i ^ k) for i in range(size)])  5.62 us
    ppermute x3, starting transfers between devices, per_device(): lax.ppermute(stats, 'blk', [(i, i ^ k) for i in range(n_blk)])  4.45 us
    ppermute x2, waiting for transfers between devices, xor_butterfly(): other = lax.ppermute(stats, axis, [(i, i ^ step) for i in range(size)])  3.26 us
    ppermute x3, waiting for transfers between devices, xor_gather(): lax.ppermute(value, axis, [(i, i ^ k) for i in range(size)])  2.54 us
    ppermute x3, waiting for transfers between devices, per_device(): lax.ppermute(stats, 'blk', [(i, i ^ k) for i in range(n_blk)])  2.3 us
    unnamed x19, local copies, waits for them, and re-layouts  2.11 us
    ppermute x2, starting transfers between devices, xor_butterfly(): other = lax.ppermute(stats, axis, [(i, i ^ step) for i in range(size)])  1.57 us
    pallas_call x1, Pallas kernels, pack_rows(): pl.pallas_call(pack_kernel, out_shape=jax.ShapeDtypeStruct((slots, width...  1.57 us
  transfers between devices with their start and end apart: 8, of which 7 were waited for; matrix products, arithmetic and copies ran while one was open for 11% of the time, Pallas kernels for 0%

profile of v19, /device:TPU:0, one launch (start us, length us, event | category | flops | bytes accessed | tf_op | source)
XLA Modules:
  0.0 34.1 jit_solution(3657226684395064453)
XLA Ops:
  0.6 0.0 copy-start.3
  0.6 0.0 copy-start.4
  0.7 0.0 copy-start.2
  0.7 1.6 %shard_map.104 = bf16[8,4224]{1,0:T(8,128)(2,1)} custom-call(s32[4]{0:T(128)} %sizes_ref.1, f32[4]{0:T(128)} %scales_ref.1, s32[8]{0:T(128)} %bins_ref.1, bf16[8,4096]{1,0:T(8,128)(2,1)} %images_ref.1), custom_call_target="tpu_custom_call" | custom-call | tf_op jit(solution)/shard_map/pallas_call | solution.py:151
  2.2 3.0 %collective-permute-start = (bf16[8,4224]{1,0:T(8,128)(2,1)}, bf16[8,4224]{1,0:T(8,128)(2,1)S(1)}, u32[]{:S(2)}, u32[]{:S(2)}) collective-permute-start(bf16[8,4224]{1,0:T(8,128)(2,1)} %shard_map.104), channel_id=1, source_target_pairs={{0,4},{4,0},{8,12},{12,8},{1,5},{5,1},{9,13},{13,9},{2,6},{6,2},{1... | collective-permute-start | bytes 202760 | tf_op jit(solution)/shard_map/ppermute | solution.py:161
  5.3 2.6 %collective-permute-start.1 = (bf16[8,4224]{1,0:T(8,128)(2,1)}, bf16[8,4224]{1,0:T(8,128)(2,1)S(1)}, u32[]{:S(2)}, u32[]{:S(2)}) collective-permute-start(bf16[8,4224]{1,0:T(8,128)(2,1)} %shard_map.104), channel_id=1, source_target_pairs={{0,8},{4,12},{8,0},{12,4},{1,9},{5,13},{9,1},{13,5},{2,10},{6,14},... | collective-permute-start | bytes 202760 | tf_op jit(solution)/shard_map/ppermute | solution.py:161
  7.8 0.0 collective-permute-start.2
  7.8 1.0 %convert_element_type.26 = f32[8,4224]{1,0:T(8,128)S(1)} convert(bf16[8,4224]{1,0:T(8,128)(2,1)} %shard_map.104) | non-fusion elementwise | flops 33792 | bytes 202752 | tf_op jit(solution)/shard_map/convert_element_type | solution.py:234
  8.8 1.1 %bitcast_convert_fusion = f32[50,4096]{1,0:T(8,128)S(1)} fusion(bf16[1,50,4096]{2,1,0:T(8,128)(2,1)} %param.10), kind=kLoop, calls=%fused_computation.23 | loop fusion | flops 204800 | bytes 1228800 | tf_op jit(solution)/shard_map/convert_element_type | solution.py:64
  9.9 0.0 copy-start.6
  9.9 0.2 slice_reduce_fusion.3
  10.1 0.0 copy-done.2
  10.1 0.5 %fusion.8 = f32[16,50]{1,0:T(8,128)S(1)} fusion(f32[50,4096]{1,0:T(8,128)S(1)} %bitcast_convert_fusion, f32[16,2048]{1,0:T(8,128)S(1)} %copy-done.2), kind=kOutput, calls=%fused_computation.19 | convolution fusion | flops 20000768 | bytes 953472 | tf_op jit(solution)/shard_map/dot_general | solution.py:69
  10.6 0.2 fusion.17
  10.9 0.1 slice_multiply_fusion.6
  11.0 0.0 copy-done.3
  11.0 0.0 copy-done.4
  11.0 0.2 add_convert_fusion.1
  11.2 0.0 copy-done.6
  11.2 0.0 copy-start.5
  11.2 0.4 %fusion.6 = f32[8,16,50]{2,1,0:T(8,128)S(1)} fusion(bf16[8,16,2048]{2,1,0:T(8,128)(2,1)S(1)} %get-tuple-element.25, bf16[8,16,2048]{2,1,0:T(8,128)(2,1)S(1)} %get-tuple-element.24, bf16[1,50,4096]{2,1,0:T(8,128)(2,1)S(1)} %copy-done.6, f32[8,50]{1,0:T(8,128)S(1)} %slice_multiply_fusion.6, f32[8]{0:T(128)S(1)} %get-tuple-element.12), kind=kOutput, calls=%fused_computation.12 | convolution fusion | flops 54538752 | bytes 1485408 | tf_op jit(solution)/shard_map/dot_general | solution.py:74
  11.7 0.0 collective-permute-done
  11.7 1.2 %collective-permute-done.1 = bf16[8,4224]{1,0:T(8,128)(2,1)S(1)} collective-permute-done((bf16[8,4224]{1,0:T(8,128)(2,1)}, bf16[8,4224]{1,0:T(8,128)(2,1)S(1)}, u32[]{:S(2)}, u32[]{:S(2)}) %collective-permute-start.1) | collective-permute-done | bytes 67616 | tf_op jit(solution)/shard_map/ppermute | solution.py:161
  12.9 1.4 %collective-permute-done.2 = bf16[8,4224]{1,0:T(8,128)(2,1)S(1)} collective-permute-done((bf16[8,4224]{1,0:T(8,128)(2,1)}, bf16[8,4224]{1,0:T(8,128)(2,1)S(1)}, u32[]{:S(2)}, u32[]{:S(2)}) %collective-permute-start.2) | collective-permute-done | bytes 67616 | tf_op jit(solution)/shard_map/ppermute | solution.py:161
  14.3 0.2 slice_reduce_fusion.1
  14.5 0.3 fusion.16
  14.8 0.1 convert_multiply_fusion.1
  14.9 0.1 slice_multiply_fusion.5
  14.9 0.0 copy-done.5
  14.9 1.0 %add_convert_fusion = (bf16[24,16,2048]{2,1,0:T(8,128)(2,1)S(1)}, bf16[24,16,2048]{2,1,0:T(8,128)(2,1)S(1)}) fusion(f32[16,2048]{1,0:T(8,128)S(1)} %copy-done.3, f32[24,2048]{1,0:T(8,128)S(1)} %get-tuple-element.23, f32[16,2048]{1,0:T(8,128)S(1)} %copy-done.5, f32[24,2048]{1,0:T(8,128)S(1)} %get-tuple-element.22), kind=kLoop, calls=%fused_computation.7 | loop fusion | flops 6291456 | bytes 3801088 | tf_op jit(solution)/shard_map/convert
  16.0 0.0 copy-start
  16.0 0.0 copy-start.7
  16.0 1.0 %fusion.5 = f32[24,16,50]{2,1,0:T(8,128)S(1)} fusion(bf16[24,16,2048]{2,1,0:T(8,128)(2,1)S(1)} %get-tuple-element.21, bf16[24,16,2048]{2,1,0:T(8,128)(2,1)S(1)} %get-tuple-element.20, bf16[1,50,4096]{2,1,0:T(8,128)(2,1)S(1)} %copy-done.6, f32[24,50]{1,0:T(8,128)S(1)} %slice_multiply_fusion.5, f32[24]{0:T(128)S(1)} %get-tuple-element.14), kind=kOutput, calls=%fused_computation.10 | convolution fusion | flops 163616256 | bytes 3637024 | tf_op jit(solution)/shard_map/dot_general | solution.py:74
  16.9 0.2 copy-done
  17.1 0.1 reshape.140
  17.3 0.2 broadcast_reduce_fusion
  17.5 0.1 stack.32
  17.5 0.1 squeeze.13
  17.6 0.0 collective-permute-start.3
  17.7 1.2 %collective-permute-done.3 = f32[2,4,8]{2,1,0:T(4,128)S(1)} collective-permute-done((f32[2,4,8]{2,1,0:T(4,128)S(1)}, f32[2,4,8]{2,1,0:T(4,128)S(1)}, u32[]{:S(2)}, u32[]{:S(2)}) %collective-permute-start.3) | collective-permute-done | bytes 288 | tf_op jit(solution)/shard_map/ppermute | solution.py:176
  18.8 1.6 %collective-permute-start.4 = (f32[2,4,8]{2,1,0:T(4,128)S(1)}, f32[2,4,8]{2,1,0:T(4,128)S(1)}, u32[]{:S(2)}, u32[]{:S(2)}) collective-permute-start(f32[2,4,8]{2,1,0:T(4,128)S(1)} %pad_maximum_fusion.17), channel_id=1, source_target_pairs={{0,2},{1,3},{2,0},{3,1},{4,6},{5,7},{6,4},{7,5},{8,10},{9,11},{10,... | collective-permute-start | bytes 776 | tf_op jit(solution)/shard_map/ppermute | solution.py:176
  20.4 0.0 copy-done.7
  20.4 2.1 %collective-permute-done.4 = f32[2,4,8]{2,1,0:T(4,128)S(1)} collective-permute-done((f32[2,4,8]{2,1,0:T(4,128)S(1)}, f32[2,4,8]{2,1,0:T(4,128)S(1)}, u32[]{:S(2)}, u32[]{:S(2)}) %collective-permute-start.4) | collective-permute-done | bytes 288 | tf_op jit(solution)/shard_map/ppermute | solution.py:176
  22.5 1.9 %collective-permute-start.7 = (f32[2,4,8]{2,1,0:T(4,128)S(1)}, f32[2,4,8]{2,1,0:T(4,128)S(1)}, u32[]{:S(2)}, u32[]{:S(2)}) collective-permute-start(f32[2,4,8]{2,1,0:T(4,128)S(1)} %get-tuple-element.33), channel_id=1, source_target_pairs={{0,12},{4,8},{8,4},{12,0},{1,13},{5,9},{9,5},{13,1},{2,14},{6,10},... | collective-permute-start | bytes 776 | tf_op jit(solution)/shard_map/ppermute | solution.py:265
  24.4 0.1 fusion.38
  24.5 0.4 %collective-permute-start.5 = (f32[2,4,8]{2,1,0:T(4,128)S(1)}, f32[2,4,8]{2,1,0:T(4,128)S(1)}, u32[]{:S(2)}, u32[]{:S(2)}) collective-permute-start(f32[2,4,8]{2,1,0:T(4,128)S(1)} %get-tuple-element.33), channel_id=1, source_target_pairs={{0,4},{4,0},{8,12},{12,8},{1,5},{5,1},{9,13},{13,9},{2,6},{6,2},{1... | collective-permute-start | bytes 776 | tf_op jit(solution)/shard_map/ppermute | solution.py:265
  24.9 2.2 %collective-permute-start.6 = (f32[2,4,8]{2,1,0:T(4,128)S(1)}, f32[2,4,8]{2,1,0:T(4,128)S(1)}, u32[]{:S(2)}, u32[]{:S(2)}) collective-permute-start(f32[2,4,8]{2,1,0:T(4,128)S(1)} %get-tuple-element.33), channel_id=1, source_target_pairs={{0,8},{4,12},{8,0},{12,4},{1,9},{5,13},{9,1},{13,5},{2,10},{6,14},... | collective-permute-start | bytes 776 | tf_op jit(solution)/shard_map/ppermute | solution.py:265
  27.0 0.9 %collective-permute-done.7 = f32[2,4,8]{2,1,0:T(4,128)S(1)} collective-permute-done((f32[2,4,8]{2,1,0:T(4,128)S(1)}, f32[2,4,8]{2,1,0:T(4,128)S(1)}, u32[]{:S(2)}, u32[]{:S(2)}) %collective-permute-start.7) | collective-permute-done | bytes 288 | tf_op jit(solution)/shard_map/ppermute | solution.py:265
  28.0 0.1 collective-permute-done.5
  28.1 1.3 %collective-permute-done.6 = f32[2,4,8]{2,1,0:T(4,128)S(1)} collective-permute-done((f32[2,4,8]{2,1,0:T(4,128)S(1)}, f32[2,4,8]{2,1,0:T(4,128)S(1)}, u32[]{:S(2)}, u32[]{:S(2)}) %collective-permute-start.6) | collective-permute-done | bytes 288 | tf_op jit(solution)/shard_map/ppermute | solution.py:265
  29.5 0.1 sub.72
  29.5 0.1 div.13
  29.6 0.5 %compare_select_fusion = f32[8]{0:T(128)} fusion(f32[8]{0:T(128)S(1)} %get-tuple-element.10, f32[4,8]{1,0:T(4,128)S(1)} %fusion.21, f32[4,8]{1,0:T(4,128)S(1)} %slice_reduce_fusion.2), kind=kLoop, calls=%fused_computation.80 | loop fusion | flops 24 | bytes 128 | tf_op jit(solution)/shard_map/jit(_where)/select_n | solution.py:284
  30.1 0.0 copy-start.1
  30.1 0.2 fusion.37
  30.3 0.4 %convolution_bitcast_fusion.1 = f32[50,4096]{1,0:T(8,128)S(1)} fusion(bf16[8,16,2048]{2,1,0:T(8,128)(2,1)S(1)} %get-tuple-element.25, bf16[8,16,2048]{2,1,0:T(8,128)(2,1)S(1)} %get-tuple-element.24, f32[32]{0:T(128)S(1)} %get-tuple-element.17, f32[32]{0:T(128)S(1)} %get-tuple-element.44, f32[32]{0:T(128)S(1)} %div.13, f32[32]{0:T(128)S(1)} %sub.72, ...), kind=kOutput, calls=%fused_computation.4 | convolution fusion | flops 54679552 | bytes 1970688 | tf_op jit(solution)/shard_map/dot_general | solution.py:193
  30.7 0.6 %fusion.12 = f32[50,2048]{1,0:T(8,128)S(1)} fusion(f32[24,2048]{1,0:T(8,128)S(1)} %get-tuple-element.26, f32[8,2048]{1,0:T(8,128)S(1)} %get-tuple-element.29, f32[32,50]{1,0:T(8,128)S(1)} %fusion.37, f32[32]{0:T(128)S(1)} %get-tuple-element.16), kind=kOutput, calls=%fused_computation.26 | convolution fusion | flops 39454272 | bytes 678272 | tf_op jit(solution)/shard_map/dot_general | solution.py:202
  31.4 0.2 copy-done.1
  31.6 0.8 %fusion.2 = f32[1,50,4096]{2,1,0:T(8,128)S(1)} fusion(f32[50,4096]{1,0:T(8,128)S(1)} %convolution_bitcast_fusion.1, bf16[24,16,2048]{2,1,0:T(8,128)(2,1)S(1)} %copy-done.1, bf16[24,16,2048]{2,1,0:T(8,128)(2,1)S(1)} %get-tuple-element.20, f32[50,2048]{1,0:T(8,128)S(1)} %fusion.12, f32[4096]{0:T(1024)S(1)} %pad_maximum_fusion.15, ...), kind=kOutput, calls=%fused_computation.3 | convolution fusion | flops 164550656 | bytes 5313024 | tf_op jit(solution)/shard_map/dot_general | solution.py:193
  32.3 1.7 %copy.16 = f32[1,50,4096]{2,0,1:T(1,128)} copy(f32[1,50,4096]{2,1,0:T(8,128)S(1)} %fusion.2) | data formatting | bytes 1638400
  (22 shorter events, 0.2 us)
Async XLA Ops:
  0.6 10.3 %copy-start.3 = (f32[16,2048]{1,0:T(8,128)S(1)}, f32[16,2048]{1,0:T(8,128)}, u32[]{:S(2)}) copy-start(f32[16,2048]{1,0:T(8,128)} %constant.6.clone) | copy-start | bytes 393220
  0.6 10.3 %copy-start.4 = (f32[16,2048]{1,0:T(8,128)S(1)}, f32[16,2048]{1,0:T(8,128)}, u32[]{:S(2)}) copy-start(f32[16,2048]{1,0:T(8,128)} %constant.5.clone) | copy-start | bytes 393220
  0.7 9.5 %copy-start.2 = (f32[16,2048]{1,0:T(8,128)S(1)}, f32[16,2048]{1,0:T(8,128)}, u32[]{:S(2)}) copy-start(f32[16,2048]{1,0:T(8,128)} %param.11) | copy-start | bytes 393220
  2.2 9.4 %collective-permute-start = (bf16[8,4224]{1,0:T(8,128)(2,1)}, bf16[8,4224]{1,0:T(8,128)(2,1)S(1)}, u32[]{:S(2)}, u32[]{:S(2)}) collective-permute-start(bf16[8,4224]{1,0:T(8,128)(2,1)} %shard_map.104), channel_id=1, source_target_pairs={{0,4},{4,0},{8,12},{12,8},{1,5},{5,1},{9,13},{13,9},{2,6},{6,2},{1... | collective-permute-start | bytes 202760 | tf_op jit(solution)/shard_map/ppermute | solution.py:161
  5.3 7.6 %collective-permute-start.1 = (bf16[8,4224]{1,0:T(8,128)(2,1)}, bf16[8,4224]{1,0:T(8,128)(2,1)S(1)}, u32[]{:S(2)}, u32[]{:S(2)}) collective-permute-start(bf16[8,4224]{1,0:T(8,128)(2,1)} %shard_map.104), channel_id=1, source_target_pairs={{0,8},{4,12},{8,0},{12,4},{1,9},{5,13},{9,1},{13,5},{2,10},{6,14},... | collective-permute-start | bytes 202760 | tf_op jit(solution)/shard_map/ppermute | solution.py:161
  7.8 6.4 %collective-permute-start.2 = (bf16[8,4224]{1,0:T(8,128)(2,1)}, bf16[8,4224]{1,0:T(8,128)(2,1)S(1)}, u32[]{:S(2)}, u32[]{:S(2)}) collective-permute-start(bf16[8,4224]{1,0:T(8,128)(2,1)} %shard_map.104), channel_id=1, source_target_pairs={{0,12},{4,8},{8,4},{12,0},{1,13},{5,9},{9,5},{13,1},{2,14},{6,10},... | collective-permute-start | bytes 202760 | tf_op jit(solution)/shard_map/ppermute | solution.py:161
  9.9 1.3 %copy-start.6 = (bf16[1,50,4096]{2,1,0:T(8,128)(2,1)S(1)}, bf16[1,50,4096]{2,1,0:T(8,128)(2,1)}, u32[]{:S(2)}) copy-start(bf16[1,50,4096]{2,1,0:T(8,128)(2,1)} %param.10) | copy-start | bytes 1228804
  11.2 3.7 %copy-start.5 = (f32[16,2048]{1,0:T(8,128)S(1)}, f32[16,2048]{1,0:T(8,128)}, u32[]{:S(2)}) copy-start(f32[16,2048]{1,0:T(8,128)} %constant.5.clone) | copy-start | bytes 393220
  16.0 1.2 %copy-start = (bf16[24,16,2048]{2,1,0:T(8,128)(2,1)}, bf16[24,16,2048]{2,1,0:T(8,128)(2,1)S(1)}, u32[]{:S(2)}) copy-start(bf16[24,16,2048]{2,1,0:T(8,128)(2,1)S(1)} %get-tuple-element.21) | copy-start | bytes 4718596
  16.0 4.4 %copy-start.7 = (f32[2048]{0:T(1024)S(1)}, f32[2048]{0:T(1024)}, u32[]{:S(2)}) copy-start(f32[2048]{0:T(1024)} %param.12) | copy-start | bytes 24580
  17.6 1.2 %collective-permute-start.3 = (f32[2,4,8]{2,1,0:T(4,128)S(1)}, f32[2,4,8]{2,1,0:T(4,128)S(1)}, u32[]{:S(2)}, u32[]{:S(2)}) collective-permute-start(f32[2,4,8]{2,1,0:T(4,128)S(1)} %pad_maximum_fusion.16), channel_id=1, source_target_pairs={{0,1},{1,0},{2,3},{3,2},{4,5},{5,4},{6,7},{7,6},{8,9},{9,8},{10,11... | collective-permute-start | bytes 776 | tf_op jit(solution)/shard_map/ppermute | solution.py:176
  18.8 3.7 %collective-permute-start.4 = (f32[2,4,8]{2,1,0:T(4,128)S(1)}, f32[2,4,8]{2,1,0:T(4,128)S(1)}, u32[]{:S(2)}, u32[]{:S(2)}) collective-permute-start(f32[2,4,8]{2,1,0:T(4,128)S(1)} %pad_maximum_fusion.17), channel_id=1, source_target_pairs={{0,2},{1,3},{2,0},{3,1},{4,6},{5,7},{6,4},{7,5},{8,10},{9,11},{10,... | collective-permute-start | bytes 776 | tf_op jit(solution)/shard_map/ppermute | solution.py:176
  22.5 5.5 %collective-permute-start.7 = (f32[2,4,8]{2,1,0:T(4,128)S(1)}, f32[2,4,8]{2,1,0:T(4,128)S(1)}, u32[]{:S(2)}, u32[]{:S(2)}) collective-permute-start(f32[2,4,8]{2,1,0:T(4,128)S(1)} %get-tuple-element.33), channel_id=1, source_target_pairs={{0,12},{4,8},{8,4},{12,0},{1,13},{5,9},{9,5},{13,1},{2,14},{6,10},... | collective-permute-start | bytes 776 | tf_op jit(solution)/shard_map/ppermute | solution.py:265
  24.5 3.6 %collective-permute-start.5 = (f32[2,4,8]{2,1,0:T(4,128)S(1)}, f32[2,4,8]{2,1,0:T(4,128)S(1)}, u32[]{:S(2)}, u32[]{:S(2)}) collective-permute-start(f32[2,4,8]{2,1,0:T(4,128)S(1)} %get-tuple-element.33), channel_id=1, source_target_pairs={{0,4},{4,0},{8,12},{12,8},{1,5},{5,1},{9,13},{13,9},{2,6},{6,2},{1... | collective-permute-start | bytes 776 | tf_op jit(solution)/shard_map/ppermute | solution.py:265
  24.9 4.5 %collective-permute-start.6 = (f32[2,4,8]{2,1,0:T(4,128)S(1)}, f32[2,4,8]{2,1,0:T(4,128)S(1)}, u32[]{:S(2)}, u32[]{:S(2)}) collective-permute-start(f32[2,4,8]{2,1,0:T(4,128)S(1)} %get-tuple-element.33), channel_id=1, source_target_pairs={{0,8},{4,12},{8,0},{12,4},{1,9},{5,13},{9,1},{13,5},{2,10},{6,14},... | collective-permute-start | bytes 776 | tf_op jit(solution)/shard_map/ppermute | solution.py:265
  30.1 1.4 %copy-start.1 = (bf16[24,16,2048]{2,1,0:T(8,128)(2,1)S(1)}, bf16[24,16,2048]{2,1,0:T(8,128)(2,1)}, u32[]{:S(2)}) copy-start(bf16[24,16,2048]{2,1,0:T(8,128)(2,1)} %copy-done) | copy-start | bytes 4718596

commit v20 on v15

--- a/solution.py
+++ b/solution.py
@@ -201,7 +201,7 @@
         start += count
     summed = jnp.sum(weights, axis=1) * (gain_rows * gain_rows)[:, None]
     denominator = lax.dot_general(
-        summed, ctf_rows * ctf_rows, (((0,), (0,)), ((), ())), precision=HIGHEST
+        summed, ctf_rows * ctf_rows, (((0,), (0,)), ((), ())), precision=lax.Precision.HIGH
     )
     return (numerator, denominator)
 

time: 34.4 us -> 34.4 us (level)
  no operation moved by 1% of the time
where the time goes in v20:
time: 34.4 us; the launch traced here: 34.1 us
  starting transfers between devices  11.6 us (34%)
  waiting for transfers between devices  8.04 us (23%)
  other arithmetic  5.14 us (15%)
  matrix products  4.03 us (12%)
  local copies, waits for them, and re-layouts  2.83 us (8%)
  Pallas kernels  1.57 us (5%)
  between operations  0.88 us (3%)
    ppermute x3, starting transfers between devices, xor_gather(): lax.ppermute(value, axis, [(i, i ^ k) for i in range(size)])  5.62 us
    ppermute x3, starting transfers between devices, per_device(): lax.ppermute(stats, 'blk', [(i, i ^ k) for i in range(n_blk)])  4.45 us
    ppermute x2, waiting for transfers between devices, xor_butterfly(): other = lax.ppermute(stats, axis, [(i, i ^ step) for i in range(size)])  3.27 us
    ppermute x3, waiting for transfers between devices, xor_gather(): lax.ppermute(value, axis, [(i, i ^ k) for i in range(size)])  2.5 us
    unnamed x17, local copies, waits for them, and re-layouts  2.29 us
    ppermute x3, waiting for transfers between devices, per_device(): lax.ppermute(stats, 'blk', [(i, i ^ k) for i in range(n_blk)])  2.28 us
    ppermute x2, starting transfers between devices, xor_butterfly(): other = lax.ppermute(stats, axis, [(i, i ^ step) for i in range(size)])  1.57 us
    pallas_call x1, Pallas kernels, pack_rows(): pl.pallas_call(pack_kernel, out_shape=jax.ShapeDtypeStruct((slots, width...  1.57 us
  transfers between devices with their start and end apart: 8, of which 7 were waited for; matrix products, arithmetic and copies ran while one was open for 11% of the time, Pallas kernels for 0%

profile of v20, /device:TPU:0, one launch (start us, length us, event | category | flops | bytes accessed | tf_op | source)
XLA Modules:
  0.0 34.1 jit_solution(6100797887806588611)
XLA Ops:
  0.6 0.0 copy-start.2
  0.6 0.0 copy-start.3
  0.7 0.0 copy-start.4
  0.7 1.6 %shard_map.104 = bf16[8,4224]{1,0:T(8,128)(2,1)} custom-call(s32[4]{0:T(128)} %sizes_ref.1, f32[4]{0:T(128)} %scales_ref.1, s32[8]{0:T(128)} %bins_ref.1, bf16[8,4096]{1,0:T(8,128)(2,1)} %images_ref.1), custom_call_target="tpu_custom_call" | custom-call | tf_op jit(solution)/shard_map/pallas_call | solution.py:152
  2.2 3.0 %collective-permute-start = (bf16[8,4224]{1,0:T(8,128)(2,1)}, bf16[8,4224]{1,0:T(8,128)(2,1)S(1)}, u32[]{:S(2)}, u32[]{:S(2)}) collective-permute-start(bf16[8,4224]{1,0:T(8,128)(2,1)} %shard_map.104), channel_id=1, source_target_pairs={{0,4},{4,0},{8,12},{12,8},{1,5},{5,1},{9,13},{13,9},{2,6},{6,2},{1... | collective-permute-start | bytes 202760 | tf_op jit(solution)/shard_map/ppermute | solution.py:162
  5.3 2.6 %collective-permute-start.1 = (bf16[8,4224]{1,0:T(8,128)(2,1)}, bf16[8,4224]{1,0:T(8,128)(2,1)S(1)}, u32[]{:S(2)}, u32[]{:S(2)}) collective-permute-start(bf16[8,4224]{1,0:T(8,128)(2,1)} %shard_map.104), channel_id=1, source_target_pairs={{0,8},{4,12},{8,0},{12,4},{1,9},{5,13},{9,1},{13,5},{2,10},{6,14},... | collective-permute-start | bytes 202760 | tf_op jit(solution)/shard_map/ppermute | solution.py:162
  7.8 0.0 collective-permute-start.2
  7.8 1.0 %convert_element_type.26 = f32[8,4224]{1,0:T(8,128)S(1)} convert(bf16[8,4224]{1,0:T(8,128)(2,1)} %shard_map.104) | non-fusion elementwise | flops 33792 | bytes 202752 | tf_op jit(solution)/shard_map/convert_element_type | solution.py:235
  8.8 0.2 slice_reduce_fusion.3
  9.0 1.1 %bitcast_convert_fusion = f32[50,4096]{1,0:T(8,128)S(1)} fusion(bf16[1,50,4096]{2,1,0:T(8,128)(2,1)} %param.10), kind=kLoop, calls=%fused_computation.23 | loop fusion | flops 204800 | bytes 1228800 | tf_op jit(solution)/shard_map/convert_element_type | solution.py:65
  10.1 0.0 copy-done.4
  10.1 0.0 copy-start.5
  10.2 0.5 %fusion.8 = f32[16,50]{1,0:T(8,128)S(1)} fusion(f32[50,4096]{1,0:T(8,128)S(1)} %bitcast_convert_fusion, f32[16,2048]{1,0:T(8,128)S(1)} %copy-done.4), kind=kOutput, calls=%fused_computation.19 | convolution fusion | flops 20000768 | bytes 953472 | tf_op jit(solution)/shard_map/dot_general | solution.py:70
  10.6 0.2 fusion.17
  10.9 0.1 slice_multiply_fusion.4
  11.0 0.0 copy-done.2
  11.0 0.0 copy-done.3
  11.0 0.3 multiply_convert_fusion.3
  11.3 0.0 copy-done.5
  11.3 0.4 %fusion.6 = f32[8,16,50]{2,1,0:T(8,128)S(1)} fusion(bf16[8,16,2048]{2,1,0:T(8,128)(2,1)S(1)} %get-tuple-element.23, bf16[8,16,2048]{2,1,0:T(8,128)(2,1)S(1)} %get-tuple-element.22, bf16[1,50,4096]{2,1,0:T(8,128)(2,1)S(1)} %copy-done.5, f32[8,50]{1,0:T(8,128)S(1)} %slice_multiply_fusion.4, f32[8]{0:T(128)S(1)} %get-tuple-element.11), kind=kOutput, calls=%fused_computation.12 | convolution fusion | flops 54538752 | bytes 1485408 | tf_op jit(solution)/shard_map/dot_general | solution.py:75
  11.7 0.0 collective-permute-done
  11.7 1.1 %collective-permute-done.1 = bf16[8,4224]{1,0:T(8,128)(2,1)S(1)} collective-permute-done((bf16[8,4224]{1,0:T(8,128)(2,1)}, bf16[8,4224]{1,0:T(8,128)(2,1)S(1)}, u32[]{:S(2)}, u32[]{:S(2)}) %collective-permute-start.1) | collective-permute-done | bytes 67616 | tf_op jit(solution)/shard_map/ppermute | solution.py:162
  12.9 1.4 %collective-permute-done.2 = bf16[8,4224]{1,0:T(8,128)(2,1)S(1)} collective-permute-done((bf16[8,4224]{1,0:T(8,128)(2,1)}, bf16[8,4224]{1,0:T(8,128)(2,1)S(1)}, u32[]{:S(2)}, u32[]{:S(2)}) %collective-permute-start.2) | collective-permute-done | bytes 67616 | tf_op jit(solution)/shard_map/ppermute | solution.py:162
  14.3 0.2 slice_reduce_fusion.1
  14.5 0.3 fusion.16
  14.9 0.1 slice_multiply_fusion.3
  14.9 1.1 %multiply_convert_fusion.1 = (bf16[24,16,2048]{2,1,0:T(8,128)(2,1)S(1)}, bf16[24,16,2048]{2,1,0:T(8,128)(2,1)S(1)}) fusion(f32[24,2048]{1,0:T(8,128)S(1)} %slice.208, f32[16,2048]{1,0:T(8,128)S(1)} %copy-done.2, f32[24,2048]{1,0:T(8,128)S(1)} %get-tuple-element.25, f32[16,2048]{1,0:T(8,128)S(1)} %copy-done.3, f32[24,2048]{1,0:T(8,128)S(1)} %get-tuple-element.24), kind=kLoop, calls=%fused_computation.7 | loop fusion | flops 7864320 | bytes 3997696 | tf_op jit(solution)/shard_map/convert
  16.0 0.0 copy-start
  16.0 0.0 copy-start.6
  16.0 1.0 %fusion.5 = f32[24,16,50]{2,1,0:T(8,128)S(1)} fusion(bf16[24,16,2048]{2,1,0:T(8,128)(2,1)S(1)} %get-tuple-element.21, bf16[24,16,2048]{2,1,0:T(8,128)(2,1)S(1)} %get-tuple-element.20, bf16[1,50,4096]{2,1,0:T(8,128)(2,1)S(1)} %copy-done.5, f32[24,50]{1,0:T(8,128)S(1)} %slice_multiply_fusion.3, f32[24]{0:T(128)S(1)} %get-tuple-element.14), kind=kOutput, calls=%fused_computation.10 | convolution fusion | flops 163616256 | bytes 3637024 | tf_op jit(solution)/shard_map/dot_general | solution.py:75
  17.0 0.2 copy-done
  17.2 0.1 reshape.142
  17.4 0.2 broadcast_reduce_fusion
  17.5 0.1 stack.32
  17.6 0.1 squeeze.13
  17.7 0.0 collective-permute-start.3
  17.7 1.2 %collective-permute-done.3 = f32[2,4,8]{2,1,0:T(4,128)S(1)} collective-permute-done((f32[2,4,8]{2,1,0:T(4,128)S(1)}, f32[2,4,8]{2,1,0:T(4,128)S(1)}, u32[]{:S(2)}, u32[]{:S(2)}) %collective-permute-start.3) | collective-permute-done | bytes 288 | tf_op jit(solution)/shard_map/ppermute | solution.py:177
  18.9 1.6 %collective-permute-start.4 = (f32[2,4,8]{2,1,0:T(4,128)S(1)}, f32[2,4,8]{2,1,0:T(4,128)S(1)}, u32[]{:S(2)}, u32[]{:S(2)}) collective-permute-start(f32[2,4,8]{2,1,0:T(4,128)S(1)} %pad_maximum_fusion.17), channel_id=1, source_target_pairs={{0,2},{1,3},{2,0},{3,1},{4,6},{5,7},{6,4},{7,5},{8,10},{9,11},{10,... | collective-permute-start | bytes 776 | tf_op jit(solution)/shard_map/ppermute | solution.py:177
  20.4 0.0 copy-done.6
  20.5 2.1 %collective-permute-done.4 = f32[2,4,8]{2,1,0:T(4,128)S(1)} collective-permute-done((f32[2,4,8]{2,1,0:T(4,128)S(1)}, f32[2,4,8]{2,1,0:T(4,128)S(1)}, u32[]{:S(2)}, u32[]{:S(2)}) %collective-permute-start.4) | collective-permute-done | bytes 288 | tf_op jit(solution)/shard_map/ppermute | solution.py:177
  22.6 1.9 %collective-permute-start.7 = (f32[2,4,8]{2,1,0:T(4,128)S(1)}, f32[2,4,8]{2,1,0:T(4,128)S(1)}, u32[]{:S(2)}, u32[]{:S(2)}) collective-permute-start(f32[2,4,8]{2,1,0:T(4,128)S(1)} %get-tuple-element.31), channel_id=1, source_target_pairs={{0,12},{4,8},{8,4},{12,0},{1,13},{5,9},{9,5},{13,1},{2,14},{6,10},... | collective-permute-start | bytes 776 | tf_op jit(solution)/shard_map/ppermute | solution.py:266
  24.5 0.1 fusion.38
  24.6 0.4 %collective-permute-start.5 = (f32[2,4,8]{2,1,0:T(4,128)S(1)}, f32[2,4,8]{2,1,0:T(4,128)S(1)}, u32[]{:S(2)}, u32[]{:S(2)}) collective-permute-start(f32[2,4,8]{2,1,0:T(4,128)S(1)} %get-tuple-element.31), channel_id=1, source_target_pairs={{0,4},{4,0},{8,12},{12,8},{1,5},{5,1},{9,13},{13,9},{2,6},{6,2},{1... | collective-permute-start | bytes 776 | tf_op jit(solution)/shard_map/ppermute | solution.py:266
  24.9 2.2 %collective-permute-start.6 = (f32[2,4,8]{2,1,0:T(4,128)S(1)}, f32[2,4,8]{2,1,0:T(4,128)S(1)}, u32[]{:S(2)}, u32[]{:S(2)}) collective-permute-start(f32[2,4,8]{2,1,0:T(4,128)S(1)} %get-tuple-element.31), channel_id=1, source_target_pairs={{0,8},{4,12},{8,0},{12,4},{1,9},{5,13},{9,1},{13,5},{2,10},{6,14},... | collective-permute-start | bytes 776 | tf_op jit(solution)/shard_map/ppermute | solution.py:266
  27.1 0.9 %collective-permute-done.7 = f32[2,4,8]{2,1,0:T(4,128)S(1)} collective-permute-done((f32[2,4,8]{2,1,0:T(4,128)S(1)}, f32[2,4,8]{2,1,0:T(4,128)S(1)}, u32[]{:S(2)}, u32[]{:S(2)}) %collective-permute-start.7) | collective-permute-done | bytes 288 | tf_op jit(solution)/shard_map/ppermute | solution.py:266
  28.1 0.1 collective-permute-done.5
  28.2 1.2 %collective-permute-done.6 = f32[2,4,8]{2,1,0:T(4,128)S(1)} collective-permute-done((f32[2,4,8]{2,1,0:T(4,128)S(1)}, f32[2,4,8]{2,1,0:T(4,128)S(1)}, u32[]{:S(2)}, u32[]{:S(2)}) %collective-permute-start.6) | collective-permute-done | bytes 288 | tf_op jit(solution)/shard_map/ppermute | solution.py:266
  29.5 0.1 sub.72
  29.6 0.1 div.13
  29.7 0.5 %compare_select_fusion = f32[8]{0:T(128)} fusion(f32[8]{0:T(128)S(1)} %get-tuple-element.10, f32[4,8]{1,0:T(4,128)S(1)} %fusion.21, f32[4,8]{1,0:T(4,128)S(1)} %slice_reduce_fusion.2), kind=kLoop, calls=%fused_computation.78 | loop fusion | flops 24 | bytes 128 | tf_op jit(solution)/shard_map/jit(_where)/select_n | solution.py:285
  30.2 0.0 copy-start.1
  30.2 0.2 fusion.37
  30.4 0.4 %convolution_bitcast_fusion.1 = f32[50,4096]{1,0:T(8,128)S(1)} fusion(bf16[8,16,2048]{2,1,0:T(8,128)(2,1)S(1)} %get-tuple-element.23, bf16[8,16,2048]{2,1,0:T(8,128)(2,1)S(1)} %get-tuple-element.22, f32[32]{0:T(128)S(1)} %get-tuple-element.17, f32[32]{0:T(128)S(1)} %get-tuple-element.42, f32[32]{0:T(128)S(1)} %div.13, f32[32]{0:T(128)S(1)} %sub.72, ...), kind=kOutput, calls=%fused_computation.4 | convolution fusion | flops 54679552 | bytes 1970688 | tf_op jit(solution)/shard_map/dot_general | solution.py:194
  30.8 0.5 %fusion.12 = f32[50,2048]{1,0:T(8,128)S(1)} fusion(f32[24,2048]{1,0:T(8,128)S(1)} %slice.208, f32[8,2048]{1,0:T(8,128)S(1)} %slice.199, f32[32,50]{1,0:T(8,128)S(1)} %fusion.37, f32[32]{0:T(128)S(1)} %get-tuple-element.16), kind=kOutput, calls=%fused_computation.26 | convolution fusion | flops 19793472 | bytes 678272 | tf_op jit(solution)/shard_map/dot_general | solution.py:203
  31.3 0.3 copy-done.1
  31.6 0.8 %fusion.2 = f32[1,50,4096]{2,1,0:T(8,128)S(1)} fusion(f32[50,4096]{1,0:T(8,128)S(1)} %convolution_bitcast_fusion.1, bf16[24,16,2048]{2,1,0:T(8,128)(2,1)S(1)} %copy-done.1, bf16[24,16,2048]{2,1,0:T(8,128)(2,1)S(1)} %get-tuple-element.20, f32[50,2048]{1,0:T(8,128)S(1)} %fusion.12, f32[4096]{0:T(1024)S(1)} %pad_maximum_fusion.15, ...), kind=kOutput, calls=%fused_computation.3 | convolution fusion | flops 164550656 | bytes 5313024 | tf_op jit(solution)/shard_map/dot_general | solution.py:194
  32.4 1.7 %copy.16 = f32[1,50,4096]{2,0,1:T(1,128)} copy(f32[1,50,4096]{2,1,0:T(8,128)S(1)} %fusion.2) | data formatting | bytes 1638400
  (25 shorter events, 0.3 us)
Async XLA Ops:
  0.6 10.3 %copy-start.2 = (f32[16,2048]{1,0:T(8,128)S(1)}, f32[16,2048]{1,0:T(8,128)}, u32[]{:S(2)}) copy-start(f32[16,2048]{1,0:T(8,128)} %constant.6.clone) | copy-start | bytes 393220
  0.6 10.3 %copy-start.3 = (f32[16,2048]{1,0:T(8,128)S(1)}, f32[16,2048]{1,0:T(8,128)}, u32[]{:S(2)}) copy-start(f32[16,2048]{1,0:T(8,128)} %constant.5.clone) | copy-start | bytes 393220
  0.7 9.5 %copy-start.4 = (f32[16,2048]{1,0:T(8,128)S(1)}, f32[16,2048]{1,0:T(8,128)}, u32[]{:S(2)}) copy-start(f32[16,2048]{1,0:T(8,128)} %param.11) | copy-start | bytes 393220
  2.2 9.5 %collective-permute-start = (bf16[8,4224]{1,0:T(8,128)(2,1)}, bf16[8,4224]{1,0:T(8,128)(2,1)S(1)}, u32[]{:S(2)}, u32[]{:S(2)}) collective-permute-start(bf16[8,4224]{1,0:T(8,128)(2,1)} %shard_map.104), channel_id=1, source_target_pairs={{0,4},{4,0},{8,12},{12,8},{1,5},{5,1},{9,13},{13,9},{2,6},{6,2},{1... | collective-permute-start | bytes 202760 | tf_op jit(solution)/shard_map/ppermute | solution.py:162
  5.3 7.6 %collective-permute-start.1 = (bf16[8,4224]{1,0:T(8,128)(2,1)}, bf16[8,4224]{1,0:T(8,128)(2,1)S(1)}, u32[]{:S(2)}, u32[]{:S(2)}) collective-permute-start(bf16[8,4224]{1,0:T(8,128)(2,1)} %shard_map.104), channel_id=1, source_target_pairs={{0,8},{4,12},{8,0},{12,4},{1,9},{5,13},{9,1},{13,5},{2,10},{6,14},... | collective-permute-start | bytes 202760 | tf_op jit(solution)/shard_map/ppermute | solution.py:162
  7.8 6.4 %collective-permute-start.2 = (bf16[8,4224]{1,0:T(8,128)(2,1)}, bf16[8,4224]{1,0:T(8,128)(2,1)S(1)}, u32[]{:S(2)}, u32[]{:S(2)}) collective-permute-start(bf16[8,4224]{1,0:T(8,128)(2,1)} %shard_map.104), channel_id=1, source_target_pairs={{0,12},{4,8},{8,4},{12,0},{1,13},{5,9},{9,5},{13,1},{2,14},{6,10},... | collective-permute-start | bytes 202760 | tf_op jit(solution)/shard_map/ppermute | solution.py:162
  10.1 1.1 %copy-start.5 = (bf16[1,50,4096]{2,1,0:T(8,128)(2,1)S(1)}, bf16[1,50,4096]{2,1,0:T(8,128)(2,1)}, u32[]{:S(2)}) copy-start(bf16[1,50,4096]{2,1,0:T(8,128)(2,1)} %param.10) | copy-start | bytes 1228804
  16.0 1.2 %copy-start = (bf16[24,16,2048]{2,1,0:T(8,128)(2,1)}, bf16[24,16,2048]{2,1,0:T(8,128)(2,1)S(1)}, u32[]{:S(2)}) copy-start(bf16[24,16,2048]{2,1,0:T(8,128)(2,1)S(1)} %get-tuple-element.21) | copy-start | bytes 4718596
  16.0 4.4 %copy-start.6 = (f32[2048]{0:T(1024)S(1)}, f32[2048]{0:T(1024)}, u32[]{:S(2)}) copy-start(f32[2048]{0:T(1024)} %param.12) | copy-start | bytes 24580
  17.7 1.2 %collective-permute-start.3 = (f32[2,4,8]{2,1,0:T(4,128)S(1)}, f32[2,4,8]{2,1,0:T(4,128)S(1)}, u32[]{:S(2)}, u32[]{:S(2)}) collective-permute-start(f32[2,4,8]{2,1,0:T(4,128)S(1)} %pad_maximum_fusion.16), channel_id=1, source_target_pairs={{0,1},{1,0},{2,3},{3,2},{4,5},{5,4},{6,7},{7,6},{8,9},{9,8},{10,11... | collective-permute-start | bytes 776 | tf_op jit(solution)/shard_map/ppermute | solution.py:177
  18.9 3.7 %collective-permute-start.4 = (f32[2,4,8]{2,1,0:T(4,128)S(1)}, f32[2,4,8]{2,1,0:T(4,128)S(1)}, u32[]{:S(2)}, u32[]{:S(2)}) collective-permute-start(f32[2,4,8]{2,1,0:T(4,128)S(1)} %pad_maximum_fusion.17), channel_id=1, source_target_pairs={{0,2},{1,3},{2,0},{3,1},{4,6},{5,7},{6,4},{7,5},{8,10},{9,11},{10,... | collective-permute-start | bytes 776 | tf_op jit(solution)/shard_map/ppermute | solution.py:177
  22.6 5.5 %collective-permute-start.7 = (f32[2,4,8]{2,1,0:T(4,128)S(1)}, f32[2,4,8]{2,1,0:T(4,128)S(1)}, u32[]{:S(2)}, u32[]{:S(2)}) collective-permute-start(f32[2,4,8]{2,1,0:T(4,128)S(1)} %get-tuple-element.31), channel_id=1, source_target_pairs={{0,12},{4,8},{8,4},{12,0},{1,13},{5,9},{9,5},{13,1},{2,14},{6,10},... | collective-permute-start | bytes 776 | tf_op jit(solution)/shard_map/ppermute | solution.py:266
  24.6 3.6 %collective-permute-start.5 = (f32[2,4,8]{2,1,0:T(4,128)S(1)}, f32[2,4,8]{2,1,0:T(4,128)S(1)}, u32[]{:S(2)}, u32[]{:S(2)}) collective-permute-start(f32[2,4,8]{2,1,0:T(4,128)S(1)} %get-tuple-element.31), channel_id=1, source_target_pairs={{0,4},{4,0},{8,12},{12,8},{1,5},{5,1},{9,13},{13,9},{2,6},{6,2},{1... | collective-permute-start | bytes 776 | tf_op jit(solution)/shard_map/ppermute | solution.py:266
  24.9 4.5 %collective-permute-start.6 = (f32[2,4,8]{2,1,0:T(4,128)S(1)}, f32[2,4,8]{2,1,0:T(4,128)S(1)}, u32[]{:S(2)}, u32[]{:S(2)}) collective-permute-start(f32[2,4,8]{2,1,0:T(4,128)S(1)} %get-tuple-element.31), channel_id=1, source_target_pairs={{0,8},{4,12},{8,0},{12,4},{1,9},{5,13},{9,1},{13,5},{2,10},{6,14},... | collective-permute-start | bytes 776 | tf_op jit(solution)/shard_map/ppermute | solution.py:266
  30.2 1.4 %copy-start.1 = (bf16[24,16,2048]{2,1,0:T(8,128)(2,1)S(1)}, bf16[24,16,2048]{2,1,0:T(8,128)(2,1)}, u32[]{:S(2)}) copy-start(bf16[24,16,2048]{2,1,0:T(8,128)(2,1)} %copy-done) | copy-start | bytes 4718596

commit v21 on v15

--- a/solution.py
+++ b/solution.py
@@ -172,11 +172,11 @@
 
 
 def xor_butterfly(stats, axis, size):
-    step = 1
-    while step < size:
+    step = size // 2
+    while step >= 1:
         other = lax.ppermute(stats, axis, [(i, i ^ step) for i in range(size)])
         stats = jnp.stack(combine_stats(stats, other))
-        step *= 2
+        step //= 2
     return stats
 
 

time: 34.4 us -> 34.4 us (level)
  no operation moved by 1% of the time
where the time goes in v21:
time: 34.4 us; the launch traced here: 34.1 us
  starting transfers between devices  11.6 us (34%)
  waiting for transfers between devices  8.03 us (23%)
  other arithmetic  5.15 us (15%)
  matrix products  4.21 us (12%)
  local copies, waits for them, and re-layouts  2.65 us (8%)
  Pallas kernels  1.57 us (5%)
  between operations  0.89 us (3%)
    ppermute x3, starting transfers between devices, xor_gather(): lax.ppermute(value, axis, [(i, i ^ k) for i in range(size)])  5.62 us
    ppermute x3, starting transfers between devices, per_device(): lax.ppermute(stats, 'blk', [(i, i ^ k) for i in range(n_blk)])  4.45 us
    ppermute x2, waiting for transfers between devices, xor_butterfly(): other = lax.ppermute(stats, axis, [(i, i ^ step) for i in range(size)])  3.25 us
    ppermute x3, waiting for transfers between devices, xor_gather(): lax.ppermute(value, axis, [(i, i ^ k) for i in range(size)])  2.5 us
    ppermute x3, waiting for transfers between devices, per_device(): lax.ppermute(stats, 'blk', [(i, i ^ k) for i in range(n_blk)])  2.28 us
    unnamed x17, local copies, waits for them, and re-layouts  2.11 us
    ppermute x2, starting transfers between devices, xor_butterfly(): other = lax.ppermute(stats, axis, [(i, i ^ step) for i in range(size)])  1.57 us
    pallas_call x1, Pallas kernels, pack_rows(): pl.pallas_call(pack_kernel, out_shape=jax.ShapeDtypeStruct((slots, width...  1.57 us
  transfers between devices with their start and end apart: 8, of which 7 were waited for; matrix products, arithmetic and copies ran while one was open for 11% of the time, Pallas kernels for 0%

profile of v21, /device:TPU:0, one launch (start us, length us, event | category | flops | bytes accessed | tf_op | source)
XLA Modules:
  0.0 34.1 jit_solution(2564298339008851552)
XLA Ops:
  0.6 0.0 copy-start.2
  0.6 0.0 copy-start.3
  0.7 0.0 copy-start.4
  0.7 1.6 %shard_map.104 = bf16[8,4224]{1,0:T(8,128)(2,1)} custom-call(s32[4]{0:T(128)} %sizes_ref.1, f32[4]{0:T(128)} %scales_ref.1, s32[8]{0:T(128)} %bins_ref.1, bf16[8,4096]{1,0:T(8,128)(2,1)} %images_ref.1), custom_call_target="tpu_custom_call" | custom-call | tf_op jit(solution)/shard_map/pallas_call | solution.py:152
  2.2 3.0 %collective-permute-start = (bf16[8,4224]{1,0:T(8,128)(2,1)}, bf16[8,4224]{1,0:T(8,128)(2,1)S(1)}, u32[]{:S(2)}, u32[]{:S(2)}) collective-permute-start(bf16[8,4224]{1,0:T(8,128)(2,1)} %shard_map.104), channel_id=1, source_target_pairs={{0,4},{4,0},{8,12},{12,8},{1,5},{5,1},{9,13},{13,9},{2,6},{6,2},{1... | collective-permute-start | bytes 202760 | tf_op jit(solution)/shard_map/ppermute | solution.py:162
  5.3 2.6 %collective-permute-start.1 = (bf16[8,4224]{1,0:T(8,128)(2,1)}, bf16[8,4224]{1,0:T(8,128)(2,1)S(1)}, u32[]{:S(2)}, u32[]{:S(2)}) collective-permute-start(bf16[8,4224]{1,0:T(8,128)(2,1)} %shard_map.104), channel_id=1, source_target_pairs={{0,8},{4,12},{8,0},{12,4},{1,9},{5,13},{9,1},{13,5},{2,10},{6,14},... | collective-permute-start | bytes 202760 | tf_op jit(solution)/shard_map/ppermute | solution.py:162
  7.8 0.0 collective-permute-start.2
  7.8 1.0 %convert_element_type.26 = f32[8,4224]{1,0:T(8,128)S(1)} convert(bf16[8,4224]{1,0:T(8,128)(2,1)} %shard_map.104) | non-fusion elementwise | flops 33792 | bytes 202752 | tf_op jit(solution)/shard_map/convert_element_type | solution.py:235
  8.8 0.2 slice_reduce_fusion.3
  9.0 1.1 %bitcast_convert_fusion = f32[50,4096]{1,0:T(8,128)S(1)} fusion(bf16[1,50,4096]{2,1,0:T(8,128)(2,1)} %param.10), kind=kLoop, calls=%fused_computation.23 | loop fusion | flops 204800 | bytes 1228800 | tf_op jit(solution)/shard_map/convert_element_type | solution.py:65
  10.1 0.0 copy-done.4
  10.1 0.0 copy-start.5
  10.2 0.5 %fusion.8 = f32[16,50]{1,0:T(8,128)S(1)} fusion(f32[50,4096]{1,0:T(8,128)S(1)} %bitcast_convert_fusion, f32[16,2048]{1,0:T(8,128)S(1)} %copy-done.4), kind=kOutput, calls=%fused_computation.19 | convolution fusion | flops 20000768 | bytes 953472 | tf_op jit(solution)/shard_map/dot_general | solution.py:70
  10.6 0.2 fusion.17
  10.9 0.1 slice_multiply_fusion.4
  11.0 0.0 copy-done.2
  11.0 0.0 copy-done.3
  11.0 0.3 multiply_convert_fusion.3
  11.3 0.0 copy-done.5
  11.3 0.4 %fusion.6 = f32[8,16,50]{2,1,0:T(8,128)S(1)} fusion(bf16[8,16,2048]{2,1,0:T(8,128)(2,1)S(1)} %get-tuple-element.23, bf16[8,16,2048]{2,1,0:T(8,128)(2,1)S(1)} %get-tuple-element.22, bf16[1,50,4096]{2,1,0:T(8,128)(2,1)S(1)} %copy-done.5, f32[8,50]{1,0:T(8,128)S(1)} %slice_multiply_fusion.4, f32[8]{0:T(128)S(1)} %get-tuple-element.11), kind=kOutput, calls=%fused_computation.12 | convolution fusion | flops 54538752 | bytes 1485408 | tf_op jit(solution)/shard_map/dot_general | solution.py:75
  11.7 0.0 collective-permute-done
  11.7 1.1 %collective-permute-done.1 = bf16[8,4224]{1,0:T(8,128)(2,1)S(1)} collective-permute-done((bf16[8,4224]{1,0:T(8,128)(2,1)}, bf16[8,4224]{1,0:T(8,128)(2,1)S(1)}, u32[]{:S(2)}, u32[]{:S(2)}) %collective-permute-start.1) | collective-permute-done | bytes 67616 | tf_op jit(solution)/shard_map/ppermute | solution.py:162
  12.9 1.4 %collective-permute-done.2 = bf16[8,4224]{1,0:T(8,128)(2,1)S(1)} collective-permute-done((bf16[8,4224]{1,0:T(8,128)(2,1)}, bf16[8,4224]{1,0:T(8,128)(2,1)S(1)}, u32[]{:S(2)}, u32[]{:S(2)}) %collective-permute-start.2) | collective-permute-done | bytes 67616 | tf_op jit(solution)/shard_map/ppermute | solution.py:162
  14.3 0.2 slice_reduce_fusion.1
  14.5 0.3 fusion.16
  14.9 0.1 slice_multiply_fusion.3
  14.9 1.1 %multiply_convert_fusion.1 = (bf16[24,16,2048]{2,1,0:T(8,128)(2,1)S(1)}, bf16[24,16,2048]{2,1,0:T(8,128)(2,1)S(1)}) fusion(f32[24,2048]{1,0:T(8,128)S(1)} %slice.208, f32[16,2048]{1,0:T(8,128)S(1)} %copy-done.2, f32[24,2048]{1,0:T(8,128)S(1)} %get-tuple-element.25, f32[16,2048]{1,0:T(8,128)S(1)} %copy-done.3, f32[24,2048]{1,0:T(8,128)S(1)} %get-tuple-element.24), kind=kLoop, calls=%fused_computation.7 | loop fusion | flops 7864320 | bytes 3997696 | tf_op jit(solution)/shard_map/convert
  16.0 0.0 copy-start
  16.0 0.0 copy-start.6
  16.0 1.0 %fusion.5 = f32[24,16,50]{2,1,0:T(8,128)S(1)} fusion(bf16[24,16,2048]{2,1,0:T(8,128)(2,1)S(1)} %get-tuple-element.21, bf16[24,16,2048]{2,1,0:T(8,128)(2,1)S(1)} %get-tuple-element.20, bf16[1,50,4096]{2,1,0:T(8,128)(2,1)S(1)} %copy-done.5, f32[24,50]{1,0:T(8,128)S(1)} %slice_multiply_fusion.3, f32[24]{0:T(128)S(1)} %get-tuple-element.14), kind=kOutput, calls=%fused_computation.10 | convolution fusion | flops 163616256 | bytes 3637024 | tf_op jit(solution)/shard_map/dot_general | solution.py:75
  17.0 0.2 copy-done
  17.2 0.1 reshape.142
  17.4 0.2 broadcast_reduce_fusion
  17.5 0.1 stack.32
  17.6 0.1 squeeze.13
  17.7 1.5 %collective-permute-start.3 = (f32[2,4,8]{2,1,0:T(4,128)S(1)}, f32[2,4,8]{2,1,0:T(4,128)S(1)}, u32[]{:S(2)}, u32[]{:S(2)}) collective-permute-start(f32[2,4,8]{2,1,0:T(4,128)S(1)} %pad_maximum_fusion.16), channel_id=1, source_target_pairs={{0,2},{1,3},{2,0},{3,1},{4,6},{5,7},{6,4},{7,5},{8,10},{9,11},{10,... | collective-permute-start | bytes 776 | tf_op jit(solution)/shard_map/ppermute | solution.py:177
  19.2 2.1 %collective-permute-done.3 = f32[2,4,8]{2,1,0:T(4,128)S(1)} collective-permute-done((f32[2,4,8]{2,1,0:T(4,128)S(1)}, f32[2,4,8]{2,1,0:T(4,128)S(1)}, u32[]{:S(2)}, u32[]{:S(2)}) %collective-permute-start.3) | collective-permute-done | bytes 288 | tf_op jit(solution)/shard_map/ppermute | solution.py:177
  21.3 0.1 collective-permute-start.4
  21.4 0.0 copy-done.6
  21.4 1.1 %collective-permute-done.4 = f32[2,4,8]{2,1,0:T(4,128)S(1)} collective-permute-done((f32[2,4,8]{2,1,0:T(4,128)S(1)}, f32[2,4,8]{2,1,0:T(4,128)S(1)}, u32[]{:S(2)}, u32[]{:S(2)}) %collective-permute-start.4) | collective-permute-done | bytes 288 | tf_op jit(solution)/shard_map/ppermute | solution.py:177
  22.6 1.9 %collective-permute-start.7 = (f32[2,4,8]{2,1,0:T(4,128)S(1)}, f32[2,4,8]{2,1,0:T(4,128)S(1)}, u32[]{:S(2)}, u32[]{:S(2)}) collective-permute-start(f32[2,4,8]{2,1,0:T(4,128)S(1)} %get-tuple-element.31), channel_id=1, source_target_pairs={{0,12},{4,8},{8,4},{12,0},{1,13},{5,9},{9,5},{13,1},{2,14},{6,10},... | collective-permute-start | bytes 776 | tf_op jit(solution)/shard_map/ppermute | solution.py:266
  24.5 0.1 fusion.38
  24.6 0.4 %collective-permute-start.5 = (f32[2,4,8]{2,1,0:T(4,128)S(1)}, f32[2,4,8]{2,1,0:T(4,128)S(1)}, u32[]{:S(2)}, u32[]{:S(2)}) collective-permute-start(f32[2,4,8]{2,1,0:T(4,128)S(1)} %get-tuple-element.31), channel_id=1, source_target_pairs={{0,4},{4,0},{8,12},{12,8},{1,5},{5,1},{9,13},{13,9},{2,6},{6,2},{1... | collective-permute-start | bytes 776 | tf_op jit(solution)/shard_map/ppermute | solution.py:266
  24.9 2.2 %collective-permute-start.6 = (f32[2,4,8]{2,1,0:T(4,128)S(1)}, f32[2,4,8]{2,1,0:T(4,128)S(1)}, u32[]{:S(2)}, u32[]{:S(2)}) collective-permute-start(f32[2,4,8]{2,1,0:T(4,128)S(1)} %get-tuple-element.31), channel_id=1, source_target_pairs={{0,8},{4,12},{8,0},{12,4},{1,9},{5,13},{9,1},{13,5},{2,10},{6,14},... | collective-permute-start | bytes 776 | tf_op jit(solution)/shard_map/ppermute | solution.py:266
  27.1 0.9 %collective-permute-done.7 = f32[2,4,8]{2,1,0:T(4,128)S(1)} collective-permute-done((f32[2,4,8]{2,1,0:T(4,128)S(1)}, f32[2,4,8]{2,1,0:T(4,128)S(1)}, u32[]{:S(2)}, u32[]{:S(2)}) %collective-permute-start.7) | collective-permute-done | bytes 288 | tf_op jit(solution)/shard_map/ppermute | solution.py:266
  28.1 0.1 collective-permute-done.5
  28.2 1.2 %collective-permute-done.6 = f32[2,4,8]{2,1,0:T(4,128)S(1)} collective-permute-done((f32[2,4,8]{2,1,0:T(4,128)S(1)}, f32[2,4,8]{2,1,0:T(4,128)S(1)}, u32[]{:S(2)}, u32[]{:S(2)}) %collective-permute-start.6) | collective-permute-done | bytes 288 | tf_op jit(solution)/shard_map/ppermute | solution.py:266
  29.5 0.1 sub.72
  29.6 0.1 div.13
  29.7 0.5 %compare_select_fusion = f32[8]{0:T(128)} fusion(f32[8]{0:T(128)S(1)} %get-tuple-element.10, f32[4,8]{1,0:T(4,128)S(1)} %fusion.21, f32[4,8]{1,0:T(4,128)S(1)} %slice_reduce_fusion.2), kind=kLoop, calls=%fused_computation.78 | loop fusion | flops 24 | bytes 128 | tf_op jit(solution)/shard_map/jit(_where)/select_n | solution.py:285
  30.2 0.0 copy-start.1
  30.2 0.2 fusion.37
  30.4 0.4 %convolution_bitcast_fusion.1 = f32[50,4096]{1,0:T(8,128)S(1)} fusion(bf16[8,16,2048]{2,1,0:T(8,128)(2,1)S(1)} %get-tuple-element.23, bf16[8,16,2048]{2,1,0:T(8,128)(2,1)S(1)} %get-tuple-element.22, f32[32]{0:T(128)S(1)} %get-tuple-element.17, f32[32]{0:T(128)S(1)} %get-tuple-element.42, f32[32]{0:T(128)S(1)} %div.13, f32[32]{0:T(128)S(1)} %sub.72, ...), kind=kOutput, calls=%fused_computation.4 | convolution fusion | flops 54679552 | bytes 1970688 | tf_op jit(solution)/shard_map/dot_general | solution.py:194
  30.8 0.6 %fusion.12 = f32[50,2048]{1,0:T(8,128)S(1)} fusion(f32[24,2048]{1,0:T(8,128)S(1)} %slice.208, f32[8,2048]{1,0:T(8,128)S(1)} %slice.199, f32[32,50]{1,0:T(8,128)S(1)} %fusion.37, f32[32]{0:T(128)S(1)} %get-tuple-element.16), kind=kOutput, calls=%fused_computation.26 | convolution fusion | flops 39454272 | bytes 678272 | tf_op jit(solution)/shard_map/dot_general | solution.py:203
  31.4 0.2 copy-done.1
  31.6 0.8 %fusion.2 = f32[1,50,4096]{2,1,0:T(8,128)S(1)} fusion(f32[50,4096]{1,0:T(8,128)S(1)} %convolution_bitcast_fusion.1, bf16[24,16,2048]{2,1,0:T(8,128)(2,1)S(1)} %copy-done.1, bf16[24,16,2048]{2,1,0:T(8,128)(2,1)S(1)} %get-tuple-element.20, f32[50,2048]{1,0:T(8,128)S(1)} %fusion.12, f32[4096]{0:T(1024)S(1)} %pad_maximum_fusion.15, ...), kind=kOutput, calls=%fused_computation.3 | convolution fusion | flops 164550656 | bytes 5313024 | tf_op jit(solution)/shard_map/dot_general | solution.py:194
  32.4 1.7 %copy.16 = f32[1,50,4096]{2,0,1:T(1,128)} copy(f32[1,50,4096]{2,1,0:T(8,128)S(1)} %fusion.2) | data formatting | bytes 1638400
  (25 shorter events, 0.3 us)
Async XLA Ops:
  0.6 10.3 %copy-start.2 = (f32[16,2048]{1,0:T(8,128)S(1)}, f32[16,2048]{1,0:T(8,128)}, u32[]{:S(2)}) copy-start(f32[16,2048]{1,0:T(8,128)} %constant.6.clone) | copy-start | bytes 393220
  0.6 10.3 %copy-start.3 = (f32[16,2048]{1,0:T(8,128)S(1)}, f32[16,2048]{1,0:T(8,128)}, u32[]{:S(2)}) copy-start(f32[16,2048]{1,0:T(8,128)} %constant.5.clone) | copy-start | bytes 393220
  0.7 9.5 %copy-start.4 = (f32[16,2048]{1,0:T(8,128)S(1)}, f32[16,2048]{1,0:T(8,128)}, u32[]{:S(2)}) copy-start(f32[16,2048]{1,0:T(8,128)} %param.11) | copy-start | bytes 393220
  2.2 9.5 %collective-permute-start = (bf16[8,4224]{1,0:T(8,128)(2,1)}, bf16[8,4224]{1,0:T(8,128)(2,1)S(1)}, u32[]{:S(2)}, u32[]{:S(2)}) collective-permute-start(bf16[8,4224]{1,0:T(8,128)(2,1)} %shard_map.104), channel_id=1, source_target_pairs={{0,4},{4,0},{8,12},{12,8},{1,5},{5,1},{9,13},{13,9},{2,6},{6,2},{1... | collective-permute-start | bytes 202760 | tf_op jit(solution)/shard_map/ppermute | solution.py:162
  5.3 7.6 %collective-permute-start.1 = (bf16[8,4224]{1,0:T(8,128)(2,1)}, bf16[8,4224]{1,0:T(8,128)(2,1)S(1)}, u32[]{:S(2)}, u32[]{:S(2)}) collective-permute-start(bf16[8,4224]{1,0:T(8,128)(2,1)} %shard_map.104), channel_id=1, source_target_pairs={{0,8},{4,12},{8,0},{12,4},{1,9},{5,13},{9,1},{13,5},{2,10},{6,14},... | collective-permute-start | bytes 202760 | tf_op jit(solution)/shard_map/ppermute | solution.py:162
  7.8 6.4 %collective-permute-start.2 = (bf16[8,4224]{1,0:T(8,128)(2,1)}, bf16[8,4224]{1,0:T(8,128)(2,1)S(1)}, u32[]{:S(2)}, u32[]{:S(2)}) collective-permute-start(bf16[8,4224]{1,0:T(8,128)(2,1)} %shard_map.104), channel_id=1, source_target_pairs={{0,12},{4,8},{8,4},{12,0},{1,13},{5,9},{9,5},{13,1},{2,14},{6,10},... | collective-permute-start | bytes 202760 | tf_op jit(solution)/shard_map/ppermute | solution.py:162
  10.1 1.1 %copy-start.5 = (bf16[1,50,4096]{2,1,0:T(8,128)(2,1)S(1)}, bf16[1,50,4096]{2,1,0:T(8,128)(2,1)}, u32[]{:S(2)}) copy-start(bf16[1,50,4096]{2,1,0:T(8,128)(2,1)} %param.10) | copy-start | bytes 1228804
  16.0 1.2 %copy-start = (bf16[24,16,2048]{2,1,0:T(8,128)(2,1)}, bf16[24,16,2048]{2,1,0:T(8,128)(2,1)S(1)}, u32[]{:S(2)}) copy-start(bf16[24,16,2048]{2,1,0:T(8,128)(2,1)S(1)} %get-tuple-element.21) | copy-start | bytes 4718596
  16.0 5.4 %copy-start.6 = (f32[2048]{0:T(1024)S(1)}, f32[2048]{0:T(1024)}, u32[]{:S(2)}) copy-start(f32[2048]{0:T(1024)} %param.12) | copy-start | bytes 24580
  17.7 3.6 %collective-permute-start.3 = (f32[2,4,8]{2,1,0:T(4,128)S(1)}, f32[2,4,8]{2,1,0:T(4,128)S(1)}, u32[]{:S(2)}, u32[]{:S(2)}) collective-permute-start(f32[2,4,8]{2,1,0:T(4,128)S(1)} %pad_maximum_fusion.16), channel_id=1, source_target_pairs={{0,2},{1,3},{2,0},{3,1},{4,6},{5,7},{6,4},{7,5},{8,10},{9,11},{10,... | collective-permute-start | bytes 776 | tf_op jit(solution)/shard_map/ppermute | solution.py:177
  21.3 1.2 %collective-permute-start.4 = (f32[2,4,8]{2,1,0:T(4,128)S(1)}, f32[2,4,8]{2,1,0:T(4,128)S(1)}, u32[]{:S(2)}, u32[]{:S(2)}) collective-permute-start(f32[2,4,8]{2,1,0:T(4,128)S(1)} %pad_maximum_fusion.17), channel_id=1, source_target_pairs={{0,1},{1,0},{2,3},{3,2},{4,5},{5,4},{6,7},{7,6},{8,9},{9,8},{10,11... | collective-permute-start | bytes 776 | tf_op jit(solution)/shard_map/ppermute | solution.py:177
  22.6 5.5 %collective-permute-start.7 = (f32[2,4,8]{2,1,0:T(4,128)S(1)}, f32[2,4,8]{2,1,0:T(4,128)S(1)}, u32[]{:S(2)}, u32[]{:S(2)}) collective-permute-start(f32[2,4,8]{2,1,0:T(4,128)S(1)} %get-tuple-element.31), channel_id=1, source_target_pairs={{0,12},{4,8},{8,4},{12,0},{1,13},{5,9},{9,5},{13,1},{2,14},{6,10},... | collective-permute-start | bytes 776 | tf_op jit(solution)/shard_map/ppermute | solution.py:266
  24.6 3.6 %collective-permute-start.5 = (f32[2,4,8]{2,1,0:T(4,128)S(1)}, f32[2,4,8]{2,1,0:T(4,128)S(1)}, u32[]{:S(2)}, u32[]{:S(2)}) collective-permute-start(f32[2,4,8]{2,1,0:T(4,128)S(1)} %get-tuple-element.31), channel_id=1, source_target_pairs={{0,4},{4,0},{8,12},{12,8},{1,5},{5,1},{9,13},{13,9},{2,6},{6,2},{1... | collective-permute-start | bytes 776 | tf_op jit(solution)/shard_map/ppermute | solution.py:266
  24.9 4.5 %collective-permute-start.6 = (f32[2,4,8]{2,1,0:T(4,128)S(1)}, f32[2,4,8]{2,1,0:T(4,128)S(1)}, u32[]{:S(2)}, u32[]{:S(2)}) collective-permute-start(f32[2,4,8]{2,1,0:T(4,128)S(1)} %get-tuple-element.31), channel_id=1, source_target_pairs={{0,8},{4,12},{8,0},{12,4},{1,9},{5,13},{9,1},{13,5},{2,10},{6,14},... | collective-permute-start | bytes 776 | tf_op jit(solution)/shard_map/ppermute | solution.py:266
  30.2 1.4 %copy-start.1 = (bf16[24,16,2048]{2,1,0:T(8,128)(2,1)S(1)}, bf16[24,16,2048]{2,1,0:T(8,128)(2,1)}, u32[]{:S(2)}) copy-start(bf16[24,16,2048]{2,1,0:T(8,128)(2,1)} %copy-done) | copy-start | bytes 4718596

commit v22 on v15

--- a/solution.py
+++ b/solution.py
@@ -6,6 +6,7 @@
 from jax import lax
 from jax.experimental import pallas as pl
 from jax.experimental.pallas import tpu as pltpu
+from jax.experimental.layout import Layout, with_layout_constraint
 from jax.sharding import PartitionSpec as P
 
 KX = 32
@@ -287,7 +288,9 @@
         jnp.concatenate([denominator, denominator], axis=1)
         + jnp.concatenate([spectral_reg, spectral_reg])[None, :]
     )
-    class_average = (numerator / denominator)[None]
+    class_average = with_layout_constraint(
+        (numerator / denominator)[None], Layout(major_to_minor=(1, 0, 2))
+    )
     return (class_average, log_evidence)
 
 

time: 34.4 us -> 34.4 us (level)
    broadcast_in_dim x0 -> x1, local copies, waits for them, and re-layouts: none -> 1.8 us  [per_device(): (numerator / denominator)[None]]
    unnamed x17 -> x16, local copies, waits for them, and re-layouts: 2.11 us -> 0.38 us
where the time goes in v22:
time: 34.4 us; the launch traced here: 34.2 us
  starting transfers between devices  11.6 us (34%)
  waiting for transfers between devices  8.04 us (23%)
  other arithmetic  5.14 us (15%)
  matrix products  4.21 us (12%)
  local copies, waits for them, and re-layouts  2.72 us (8%)
  Pallas kernels  1.57 us (5%)
  between operations  0.88 us (3%)
    ppermute x3, starting transfers between devices, xor_gather(): lax.ppermute(value, axis, [(i, i ^ k) for i in range(size)])  5.62 us
    ppermute x3, starting transfers between devices, per_device(): lax.ppermute(stats, 'blk', [(i, i ^ k) for i in range(n_blk)])  4.45 us
    ppermute x2, waiting for transfers between devices, xor_butterfly(): other = lax.ppermute(stats, axis, [(i, i ^ step) for i in range(size)])  3.27 us
    ppermute x3, waiting for transfers between devices, xor_gather(): lax.ppermute(value, axis, [(i, i ^ k) for i in range(size)])  2.5 us
    ppermute x3, waiting for transfers between devices, per_device(): lax.ppermute(stats, 'blk', [(i, i ^ k) for i in range(n_blk)])  2.28 us
    broadcast_in_dim x1, local copies, waits for them, and re-layouts, per_device(): (numerator / denominator)[None]  1.8 us
    ppermute x2, starting transfers between devices, xor_butterfly(): other = lax.ppermute(stats, axis, [(i, i ^ step) for i in range(size)])  1.57 us
    pallas_call x1, Pallas kernels, pack_rows(): pl.pallas_call(pack_kernel, out_shape=jax.ShapeDtypeStruct((slots, width...  1.57 us
  transfers between devices with their start and end apart: 8, of which 7 were waited for; matrix products, arithmetic and copies ran while one was open for 11% of the time, Pallas kernels for 0%

profile of v22, /device:TPU:0, one launch (start us, length us, event | category | flops | bytes accessed | tf_op | source)
XLA Modules:
  0.0 34.2 jit_solution(2755267045414152078)
XLA Ops:
  0.6 0.0 copy-start.2
  0.6 0.0 copy-start.3
  0.7 0.0 copy-start.4
  0.7 1.6 %shard_map.104 = bf16[8,4224]{1,0:T(8,128)(2,1)} custom-call(s32[4]{0:T(128)} %sizes_ref.1, f32[4]{0:T(128)} %scales_ref.1, s32[8]{0:T(128)} %bins_ref.1, bf16[8,4096]{1,0:T(8,128)(2,1)} %images_ref.1), custom_call_target="tpu_custom_call" | custom-call | tf_op jit(solution)/shard_map/pallas_call | solution.py:153
  2.2 3.0 %collective-permute-start = (bf16[8,4224]{1,0:T(8,128)(2,1)}, bf16[8,4224]{1,0:T(8,128)(2,1)S(1)}, u32[]{:S(2)}, u32[]{:S(2)}) collective-permute-start(bf16[8,4224]{1,0:T(8,128)(2,1)} %shard_map.104), channel_id=1, source_target_pairs={{0,4},{4,0},{8,12},{12,8},{1,5},{5,1},{9,13},{13,9},{2,6},{6,2},{1... | collective-permute-start | bytes 202760 | tf_op jit(solution)/shard_map/ppermute | solution.py:163
  5.3 2.6 %collective-permute-start.1 = (bf16[8,4224]{1,0:T(8,128)(2,1)}, bf16[8,4224]{1,0:T(8,128)(2,1)S(1)}, u32[]{:S(2)}, u32[]{:S(2)}) collective-permute-start(bf16[8,4224]{1,0:T(8,128)(2,1)} %shard_map.104), channel_id=1, source_target_pairs={{0,8},{4,12},{8,0},{12,4},{1,9},{5,13},{9,1},{13,5},{2,10},{6,14},... | collective-permute-start | bytes 202760 | tf_op jit(solution)/shard_map/ppermute | solution.py:163
  7.8 0.0 collective-permute-start.2
  7.8 1.0 %convert_element_type.26 = f32[8,4224]{1,0:T(8,128)S(1)} convert(bf16[8,4224]{1,0:T(8,128)(2,1)} %shard_map.104) | non-fusion elementwise | flops 33792 | bytes 202752 | tf_op jit(solution)/shard_map/convert_element_type | solution.py:236
  8.8 0.2 slice_reduce_fusion.3
  9.0 1.1 %bitcast_convert_fusion = f32[50,4096]{1,0:T(8,128)S(1)} fusion(bf16[1,50,4096]{2,1,0:T(8,128)(2,1)} %param.10), kind=kLoop, calls=%fused_computation.22 | loop fusion | flops 204800 | bytes 1228800 | tf_op jit(solution)/shard_map/convert_element_type | solution.py:66
  10.1 0.0 copy-done.4
  10.1 0.0 copy-start.5
  10.2 0.5 %fusion.7 = f32[16,50]{1,0:T(8,128)S(1)} fusion(f32[50,4096]{1,0:T(8,128)S(1)} %bitcast_convert_fusion, f32[16,2048]{1,0:T(8,128)S(1)} %copy-done.4), kind=kOutput, calls=%fused_computation.18 | convolution fusion | flops 20000768 | bytes 953472 | tf_op jit(solution)/shard_map/dot_general | solution.py:71
  10.6 0.2 fusion.16
  10.9 0.1 slice_multiply_fusion.4
  11.0 0.0 copy-done.2
  11.0 0.0 copy-done.3
  11.0 0.3 multiply_convert_fusion.3
  11.3 0.0 copy-done.5
  11.3 0.4 %fusion.5 = f32[8,16,50]{2,1,0:T(8,128)S(1)} fusion(bf16[8,16,2048]{2,1,0:T(8,128)(2,1)S(1)} %get-tuple-element.19, bf16[8,16,2048]{2,1,0:T(8,128)(2,1)S(1)} %get-tuple-element.18, bf16[1,50,4096]{2,1,0:T(8,128)(2,1)S(1)} %copy-done.5, f32[8,50]{1,0:T(8,128)S(1)} %slice_multiply_fusion.4, f32[8]{0:T(128)S(1)} %get-tuple-element.7), kind=kOutput, calls=%fused_computation.11 | convolution fusion | flops 54538752 | bytes 1485408 | tf_op jit(solution)/shard_map/dot_general | solution.py:76
  11.7 0.0 collective-permute-done
  11.7 1.1 %collective-permute-done.1 = bf16[8,4224]{1,0:T(8,128)(2,1)S(1)} collective-permute-done((bf16[8,4224]{1,0:T(8,128)(2,1)}, bf16[8,4224]{1,0:T(8,128)(2,1)S(1)}, u32[]{:S(2)}, u32[]{:S(2)}) %collective-permute-start.1) | collective-permute-done | bytes 67616 | tf_op jit(solution)/shard_map/ppermute | solution.py:163
  12.9 1.4 %collective-permute-done.2 = bf16[8,4224]{1,0:T(8,128)(2,1)S(1)} collective-permute-done((bf16[8,4224]{1,0:T(8,128)(2,1)}, bf16[8,4224]{1,0:T(8,128)(2,1)S(1)}, u32[]{:S(2)}, u32[]{:S(2)}) %collective-permute-start.2) | collective-permute-done | bytes 67616 | tf_op jit(solution)/shard_map/ppermute | solution.py:163
  14.3 0.2 slice_reduce_fusion.1
  14.5 0.3 fusion.15
  14.9 0.1 slice_multiply_fusion.3
  14.9 1.1 %multiply_convert_fusion.1 = (bf16[24,16,2048]{2,1,0:T(8,128)(2,1)S(1)}, bf16[24,16,2048]{2,1,0:T(8,128)(2,1)S(1)}) fusion(f32[24,2048]{1,0:T(8,128)S(1)} %slice.208, f32[16,2048]{1,0:T(8,128)S(1)} %copy-done.2, f32[24,2048]{1,0:T(8,128)S(1)} %get-tuple-element.21, f32[16,2048]{1,0:T(8,128)S(1)} %copy-done.3, f32[24,2048]{1,0:T(8,128)S(1)} %get-tuple-element.20), kind=kLoop, calls=%fused_computation.6 | loop fusion | flops 7864320 | bytes 3997696 | tf_op jit(solution)/shard_map/convert
  16.0 0.0 copy-start
  16.0 0.0 copy-start.6
  16.0 1.0 %fusion.4 = f32[24,16,50]{2,1,0:T(8,128)S(1)} fusion(bf16[24,16,2048]{2,1,0:T(8,128)(2,1)S(1)} %get-tuple-element.17, bf16[24,16,2048]{2,1,0:T(8,128)(2,1)S(1)} %get-tuple-element.16, bf16[1,50,4096]{2,1,0:T(8,128)(2,1)S(1)} %copy-done.5, f32[24,50]{1,0:T(8,128)S(1)} %slice_multiply_fusion.3, f32[24]{0:T(128)S(1)} %get-tuple-element.10), kind=kOutput, calls=%fused_computation.9 | convolution fusion | flops 163616256 | bytes 3637024 | tf_op jit(solution)/shard_map/dot_general | solution.py:76
  17.0 0.2 copy-done
  17.2 0.1 reshape.142
  17.4 0.2 broadcast_reduce_fusion
  17.5 0.1 stack.32
  17.6 0.1 squeeze.13
  17.7 0.0 collective-permute-start.3
  17.7 1.2 %collective-permute-done.3 = f32[2,4,8]{2,1,0:T(4,128)S(1)} collective-permute-done((f32[2,4,8]{2,1,0:T(4,128)S(1)}, f32[2,4,8]{2,1,0:T(4,128)S(1)}, u32[]{:S(2)}, u32[]{:S(2)}) %collective-permute-start.3) | collective-permute-done | bytes 288 | tf_op jit(solution)/shard_map/ppermute | solution.py:178
  18.9 1.6 %collective-permute-start.4 = (f32[2,4,8]{2,1,0:T(4,128)S(1)}, f32[2,4,8]{2,1,0:T(4,128)S(1)}, u32[]{:S(2)}, u32[]{:S(2)}) collective-permute-start(f32[2,4,8]{2,1,0:T(4,128)S(1)} %pad_maximum_fusion.17), channel_id=1, source_target_pairs={{0,2},{1,3},{2,0},{3,1},{4,6},{5,7},{6,4},{7,5},{8,10},{9,11},{10,... | collective-permute-start | bytes 776 | tf_op jit(solution)/shard_map/ppermute | solution.py:178
  20.4 0.0 copy-done.6
  20.5 2.1 %collective-permute-done.4 = f32[2,4,8]{2,1,0:T(4,128)S(1)} collective-permute-done((f32[2,4,8]{2,1,0:T(4,128)S(1)}, f32[2,4,8]{2,1,0:T(4,128)S(1)}, u32[]{:S(2)}, u32[]{:S(2)}) %collective-permute-start.4) | collective-permute-done | bytes 288 | tf_op jit(solution)/shard_map/ppermute | solution.py:178
  22.6 1.9 %collective-permute-start.7 = (f32[2,4,8]{2,1,0:T(4,128)S(1)}, f32[2,4,8]{2,1,0:T(4,128)S(1)}, u32[]{:S(2)}, u32[]{:S(2)}) collective-permute-start(f32[2,4,8]{2,1,0:T(4,128)S(1)} %get-tuple-element.27), channel_id=1, source_target_pairs={{0,12},{4,8},{8,4},{12,0},{1,13},{5,9},{9,5},{13,1},{2,14},{6,10},... | collective-permute-start | bytes 776 | tf_op jit(solution)/shard_map/ppermute | solution.py:267
  24.5 0.1 fusion.37
  24.6 0.4 %collective-permute-start.5 = (f32[2,4,8]{2,1,0:T(4,128)S(1)}, f32[2,4,8]{2,1,0:T(4,128)S(1)}, u32[]{:S(2)}, u32[]{:S(2)}) collective-permute-start(f32[2,4,8]{2,1,0:T(4,128)S(1)} %get-tuple-element.27), channel_id=1, source_target_pairs={{0,4},{4,0},{8,12},{12,8},{1,5},{5,1},{9,13},{13,9},{2,6},{6,2},{1... | collective-permute-start | bytes 776 | tf_op jit(solution)/shard_map/ppermute | solution.py:267
  24.9 2.2 %collective-permute-start.6 = (f32[2,4,8]{2,1,0:T(4,128)S(1)}, f32[2,4,8]{2,1,0:T(4,128)S(1)}, u32[]{:S(2)}, u32[]{:S(2)}) collective-permute-start(f32[2,4,8]{2,1,0:T(4,128)S(1)} %get-tuple-element.27), channel_id=1, source_target_pairs={{0,8},{4,12},{8,0},{12,4},{1,9},{5,13},{9,1},{13,5},{2,10},{6,14},... | collective-permute-start | bytes 776 | tf_op jit(solution)/shard_map/ppermute | solution.py:267
  27.1 0.9 %collective-permute-done.7 = f32[2,4,8]{2,1,0:T(4,128)S(1)} collective-permute-done((f32[2,4,8]{2,1,0:T(4,128)S(1)}, f32[2,4,8]{2,1,0:T(4,128)S(1)}, u32[]{:S(2)}, u32[]{:S(2)}) %collective-permute-start.7) | collective-permute-done | bytes 288 | tf_op jit(solution)/shard_map/ppermute | solution.py:267
  28.1 0.1 collective-permute-done.5
  28.2 1.2 %collective-permute-done.6 = f32[2,4,8]{2,1,0:T(4,128)S(1)} collective-permute-done((f32[2,4,8]{2,1,0:T(4,128)S(1)}, f32[2,4,8]{2,1,0:T(4,128)S(1)}, u32[]{:S(2)}, u32[]{:S(2)}) %collective-permute-start.6) | collective-permute-done | bytes 288 | tf_op jit(solution)/shard_map/ppermute | solution.py:267
  29.5 0.1 sub.72
  29.6 0.1 div.13
  29.7 0.5 %compare_select_fusion = f32[8]{0:T(128)} fusion(f32[8]{0:T(128)S(1)} %get-tuple-element.6, f32[4,8]{1,0:T(4,128)S(1)} %fusion.20, f32[4,8]{1,0:T(4,128)S(1)} %slice_reduce_fusion.2), kind=kLoop, calls=%fused_computation.77 | loop fusion | flops 24 | bytes 128 | tf_op jit(solution)/shard_map/jit(_where)/select_n | solution.py:286
  30.2 0.0 copy-start.1
  30.2 0.2 fusion.36
  30.4 0.4 %convolution_bitcast_fusion.1 = f32[50,4096]{1,0:T(8,128)S(1)} fusion(bf16[8,16,2048]{2,1,0:T(8,128)(2,1)S(1)} %get-tuple-element.19, bf16[8,16,2048]{2,1,0:T(8,128)(2,1)S(1)} %get-tuple-element.18, f32[32]{0:T(128)S(1)} %get-tuple-element.13, f32[32]{0:T(128)S(1)} %get-tuple-element.38, f32[32]{0:T(128)S(1)} %div.13, f32[32]{0:T(128)S(1)} %sub.72, ...), kind=kOutput, calls=%fused_computation.3 | convolution fusion | flops 54679552 | bytes 1970688 | tf_op jit(solution)/shard_map/dot_general | solution.py:195
  30.8 0.6 %fusion.11 = f32[50,2048]{1,0:T(8,128)S(1)} fusion(f32[24,2048]{1,0:T(8,128)S(1)} %slice.208, f32[8,2048]{1,0:T(8,128)S(1)} %slice.199, f32[32,50]{1,0:T(8,128)S(1)} %fusion.36, f32[32]{0:T(128)S(1)} %get-tuple-element.12), kind=kOutput, calls=%fused_computation.25 | convolution fusion | flops 39454272 | bytes 678272 | tf_op jit(solution)/shard_map/dot_general | solution.py:204
  31.4 0.2 copy-done.1
  31.6 0.8 %fusion.1 = f32[50,4096]{1,0:T(8,128)S(1)} fusion(f32[50,4096]{1,0:T(8,128)S(1)} %convolution_bitcast_fusion.1, bf16[24,16,2048]{2,1,0:T(8,128)(2,1)S(1)} %copy-done.1, bf16[24,16,2048]{2,1,0:T(8,128)(2,1)S(1)} %get-tuple-element.16, f32[50,2048]{1,0:T(8,128)S(1)} %fusion.11, f32[4096]{0:T(1024)S(1)} %pad_maximum_fusion.15, f32[32]{0:T(128)S(1)} %get-tuple-element.13, ...), kind=kOutput, calls=%fused_computation.2 | convolution fusion | flops 164550656 | bytes 5313024 | tf_op jit(solution)/shard_map/dot_general | solution.py:195
  32.4 1.8 %broadcast_in_dim.8 = f32[1,50,4096]{2,0,1:T(1,128)} reshape(f32[50,4096]{1,0:T(8,128)S(1)} %fusion.1) | data formatting | bytes 1638400 | tf_op jit(solution)/shard_map/broadcast_in_dim | solution.py:292
  (25 shorter events, 0.3 us)
Async XLA Ops:
  0.6 10.3 %copy-start.2 = (f32[16,2048]{1,0:T(8,128)S(1)}, f32[16,2048]{1,0:T(8,128)}, u32[]{:S(2)}) copy-start(f32[16,2048]{1,0:T(8,128)} %constant.6.clone) | copy-start | bytes 393220
  0.6 10.3 %copy-start.3 = (f32[16,2048]{1,0:T(8,128)S(1)}, f32[16,2048]{1,0:T(8,128)}, u32[]{:S(2)}) copy-start(f32[16,2048]{1,0:T(8,128)} %constant.5.clone) | copy-start | bytes 393220
  0.7 9.5 %copy-start.4 = (f32[16,2048]{1,0:T(8,128)S(1)}, f32[16,2048]{1,0:T(8,128)}, u32[]{:S(2)}) copy-start(f32[16,2048]{1,0:T(8,128)} %param.11) | copy-start | bytes 393220
  2.2 9.5 %collective-permute-start = (bf16[8,4224]{1,0:T(8,128)(2,1)}, bf16[8,4224]{1,0:T(8,128)(2,1)S(1)}, u32[]{:S(2)}, u32[]{:S(2)}) collective-permute-start(bf16[8,4224]{1,0:T(8,128)(2,1)} %shard_map.104), channel_id=1, source_target_pairs={{0,4},{4,0},{8,12},{12,8},{1,5},{5,1},{9,13},{13,9},{2,6},{6,2},{1... | collective-permute-start | bytes 202760 | tf_op jit(solution)/shard_map/ppermute | solution.py:163
  5.3 7.6 %collective-permute-start.1 = (bf16[8,4224]{1,0:T(8,128)(2,1)}, bf16[8,4224]{1,0:T(8,128)(2,1)S(1)}, u32[]{:S(2)}, u32[]{:S(2)}) collective-permute-start(bf16[8,4224]{1,0:T(8,128)(2,1)} %shard_map.104), channel_id=1, source_target_pairs={{0,8},{4,12},{8,0},{12,4},{1,9},{5,13},{9,1},{13,5},{2,10},{6,14},... | collective-permute-start | bytes 202760 | tf_op jit(solution)/shard_map/ppermute | solution.py:163
  7.8 6.4 %collective-permute-start.2 = (bf16[8,4224]{1,0:T(8,128)(2,1)}, bf16[8,4224]{1,0:T(8,128)(2,1)S(1)}, u32[]{:S(2)}, u32[]{:S(2)}) collective-permute-start(bf16[8,4224]{1,0:T(8,128)(2,1)} %shard_map.104), channel_id=1, source_target_pairs={{0,12},{4,8},{8,4},{12,0},{1,13},{5,9},{9,5},{13,1},{2,14},{6,10},... | collective-permute-start | bytes 202760 | tf_op jit(solution)/shard_map/ppermute | solution.py:163
  10.1 1.1 %copy-start.5 = (bf16[1,50,4096]{2,1,0:T(8,128)(2,1)S(1)}, bf16[1,50,4096]{2,1,0:T(8,128)(2,1)}, u32[]{:S(2)}) copy-start(bf16[1,50,4096]{2,1,0:T(8,128)(2,1)} %param.10) | copy-start | bytes 1228804
  16.0 1.2 %copy-start = (bf16[24,16,2048]{2,1,0:T(8,128)(2,1)}, bf16[24,16,2048]{2,1,0:T(8,128)(2,1)S(1)}, u32[]{:S(2)}) copy-start(bf16[24,16,2048]{2,1,0:T(8,128)(2,1)S(1)} %get-tuple-element.17) | copy-start | bytes 4718596
  16.0 4.4 %copy-start.6 = (f32[2048]{0:T(1024)S(1)}, f32[2048]{0:T(1024)}, u32[]{:S(2)}) copy-start(f32[2048]{0:T(1024)} %param.12) | copy-start | bytes 24580
  17.7 1.2 %collective-permute-start.3 = (f32[2,4,8]{2,1,0:T(4,128)S(1)}, f32[2,4,8]{2,1,0:T(4,128)S(1)}, u32[]{:S(2)}, u32[]{:S(2)}) collective-permute-start(f32[2,4,8]{2,1,0:T(4,128)S(1)} %pad_maximum_fusion.16), channel_id=1, source_target_pairs={{0,1},{1,0},{2,3},{3,2},{4,5},{5,4},{6,7},{7,6},{8,9},{9,8},{10,11... | collective-permute-start | bytes 776 | tf_op jit(solution)/shard_map/ppermute | solution.py:178
  18.9 3.7 %collective-permute-start.4 = (f32[2,4,8]{2,1,0:T(4,128)S(1)}, f32[2,4,8]{2,1,0:T(4,128)S(1)}, u32[]{:S(2)}, u32[]{:S(2)}) collective-permute-start(f32[2,4,8]{2,1,0:T(4,128)S(1)} %pad_maximum_fusion.17), channel_id=1, source_target_pairs={{0,2},{1,3},{2,0},{3,1},{4,6},{5,7},{6,4},{7,5},{8,10},{9,11},{10,... | collective-permute-start | bytes 776 | tf_op jit(solution)/shard_map/ppermute | solution.py:178
  22.6 5.5 %collective-permute-start.7 = (f32[2,4,8]{2,1,0:T(4,128)S(1)}, f32[2,4,8]{2,1,0:T(4,128)S(1)}, u32[]{:S(2)}, u32[]{:S(2)}) collective-permute-start(f32[2,4,8]{2,1,0:T(4,128)S(1)} %get-tuple-element.27), channel_id=1, source_target_pairs={{0,12},{4,8},{8,4},{12,0},{1,13},{5,9},{9,5},{13,1},{2,14},{6,10},... | collective-permute-start | bytes 776 | tf_op jit(solution)/shard_map/ppermute | solution.py:267
  24.6 3.6 %collective-permute-start.5 = (f32[2,4,8]{2,1,0:T(4,128)S(1)}, f32[2,4,8]{2,1,0:T(4,128)S(1)}, u32[]{:S(2)}, u32[]{:S(2)}) collective-permute-start(f32[2,4,8]{2,1,0:T(4,128)S(1)} %get-tuple-element.27), channel_id=1, source_target_pairs={{0,4},{4,0},{8,12},{12,8},{1,5},{5,1},{9,13},{13,9},{2,6},{6,2},{1... | collective-permute-start | bytes 776 | tf_op jit(solution)/shard_map/ppermute | solution.py:267
  24.9 4.5 %collective-permute-start.6 = (f32[2,4,8]{2,1,0:T(4,128)S(1)}, f32[2,4,8]{2,1,0:T(4,128)S(1)}, u32[]{:S(2)}, u32[]{:S(2)}) collective-permute-start(f32[2,4,8]{2,1,0:T(4,128)S(1)} %get-tuple-element.27), channel_id=1, source_target_pairs={{0,8},{4,12},{8,0},{12,4},{1,9},{5,13},{9,1},{13,5},{2,10},{6,14},... | collective-permute-start | bytes 776 | tf_op jit(solution)/shard_map/ppermute | solution.py:267
  30.2 1.4 %copy-start.1 = (bf16[24,16,2048]{2,1,0:T(8,128)(2,1)S(1)}, bf16[24,16,2048]{2,1,0:T(8,128)(2,1)}, u32[]{:S(2)}) copy-start(bf16[24,16,2048]{2,1,0:T(8,128)(2,1)} %copy-done) | copy-start | bytes 4718596
